TPU v7x, 256 devices: a whole 4x4x8 slice. The times are simulated.
256 devices in a mesh: row: 16 (over y, x), col: 16 (over z, core).
Axes of the slice: x: 4, y: 4, z: 8, core: 2. Of those that a mesh axis runs over, the one named last changes fastest.
Arguments:
- q_seq: bfloat16 [2048, 6144], P('row', 'col'), may hold values from -4.5 to 4.5
- k_seq: bfloat16 [2048, 6144], P('row', 'col'), may hold values from -4.5 to 4.5
- v_seq: bfloat16 [2048, 6144], P('row', 'col'), may hold values from -6 to 6
- resid: bfloat16 [2048, 6144], P('row', 'col'), may hold values from -90 to 90
- ln_gain: float32 [6144], replicated, may hold values from 0.1 to 1.9
- w_up: bfloat16 [6144, 24576], P('row', 'col'), may hold values from -0.078125 to 0.078125
Outputs:
- hidden: bfloat16 [2048, 24576], P('row', 'col')
All inputs are finite; a program needn't handle non-finite values.
Results may differ from a plain program's by a relative error of at most 0.0051.
Values may be sent and summed in bfloat16 or wider, within the bound.
No kernel may reach another device: no remote copies, remote signals or barrier semaphores. Data moves between devices by JAX's collectives and lax.ppermute only.
A program may use at most 64 MiB of HBM per device.

v0:
```python
import math

import jax
import jax.numpy as jnp
from jax import lax
from jax.sharding import PartitionSpec as P

HD = 128


def attention_block(query, keys, values):
    seq, width = query.shape
    heads = width // HD
    qshaped = query.reshape(seq, heads, HD)
    kshaped = keys.reshape(seq, heads, HD)
    vshaped = values.reshape(seq, heads, HD)
    scores = jnp.einsum("qhd,khd->hqk", qshaped, kshaped, preferred_element_type=jnp.float32)
    scores = scores * (1.0 / math.sqrt(HD))
    rows_idx = lax.broadcasted_iota(jnp.int32, (seq, seq), 0)
    cols_idx = lax.broadcasted_iota(jnp.int32, (seq, seq), 1)
    scores = jnp.where((rows_idx >= cols_idx)[None], scores, -1e30)
    highest = jnp.max(scores, axis=-1, keepdims=True)
    expo = jnp.exp(scores - highest)
    prob = (expo / jnp.sum(expo, axis=-1, keepdims=True)).astype(jnp.bfloat16)
    output = jnp.einsum("hqk,khd->qhd", prob, vshaped, preferred_element_type=jnp.float32)
    return output.astype(jnp.bfloat16).reshape(seq, width)


def scale_rows(stream, mean, spread, gain):
    return ((stream - mean) * lax.rsqrt(spread + 1e-05) * gain[None, :]).astype(jnp.bfloat16)


def per_device(q_seq, k_seq, v_seq, resid, ln_gain, w_up):
    attended = attention_block(q_seq, k_seq, v_seq)
    returned, res_tokens = (
        lax.all_to_all(attended, "col", split_axis=0, concat_axis=1, tiled=True),
        lax.all_to_all(resid, "col", split_axis=0, concat_axis=1, tiled=True),
    )
    stream = res_tokens.astype(jnp.float32) + returned.astype(jnp.float32)
    full_width = stream.shape[1]
    mean = jnp.sum(stream, axis=1, keepdims=True) / full_width
    spread = jnp.sum(stream * stream, axis=1, keepdims=True) / full_width - mean * mean
    normed_tokens = scale_rows(stream, mean, spread, ln_gain)
    normed = lax.all_to_all(normed_tokens, "col", split_axis=1, concat_axis=0, tiled=True)
    whole = lax.all_gather(normed, "col", axis=1, tiled=True)
    product = jnp.dot(
        whole, lax.all_gather(w_up, "row", axis=0, tiled=True), preferred_element_type=jnp.float32
    )
    return jax.nn.gelu(product, approximate=True).astype(jnp.bfloat16)


def solution(mesh):
    placed = (
        P("row", "col"),
        P("row", "col"),
        P("row", "col"),
        P("row", "col"),
        P(),
        P("row", "col"),
    )
    return jax.shard_map(
        per_device, mesh=mesh, in_specs=placed, out_specs=P("row", "col"), check_vma=False
    )
```

profile of v0, /device:TPU:6, one launch (start us, length us, event | category | flops | bytes accessed | tf_op | source)
XLA Modules:
  0.0 228.8 jit_solution(653046495785371151)
XLA Ops:
  6.5 0.0 copy-start
  6.5 8.7 %all-to-all-start = ((bf16[16,8,384]{2,1,0:T(8,128)(2,1)}), bf16[16,8,384]{2,1,0:T(8,128)(2,1)S(1)}, u32[]{:S(2)}, u32[]{:S(2)}) async-start(bf16[16,8,384]{2,1,0:T(8,128)(2,1)} %bitcast.21), calls=%async_computation | async-start | bytes 196608 | tf_op jit(solution)/shard_map/all_to_all | solution.py:37
  15.3 1.0 copy.11
  16.3 1.0 copy.12
  17.3 0.2 fusion.2
  17.5 0.1 fusion.17
  17.6 1.0 copy.15
  18.6 0.3 fusion.4
  18.9 0.1 copy.18
  19.0 0.7 all_to_all.34
  19.7 3.9 %all-to-all-done = bf16[16,8,384]{2,1,0:T(8,128)(2,1)S(1)} async-done(((bf16[16,8,384]{2,1,0:T(8,128)(2,1)}), bf16[16,8,384]{2,1,0:T(8,128)(2,1)S(1)}, u32[]{:S(2)}, u32[]{:S(2)}) %all-to-all-start) | async-done | bytes 98336 | tf_op jit(solution)/shard_map/all_to_all | solution.py:37
  23.6 3.5 %all-to-all-start.1 = ((bf16[16,8,384]{2,1,0:T(8,128)(2,1)}), bf16[16,8,384]{2,1,0:T(8,128)(2,1)S(1)}, u32[]{:S(2)}, u32[]{:S(2)}) async-start(bf16[16,8,384]{2,1,0:T(8,128)(2,1)} %all_to_all.34), calls=%async_computation.1 | async-start | bytes 196608 | tf_op jit(solution)/shard_map/all_to_all | solution.py:36
  27.1 0.0 all-gather.3.cloned.1.call-start
  27.1 0.0 copy-done
  27.2 8.2 %all-to-all-done.1 = bf16[16,8,384]{2,1,0:T(8,128)(2,1)S(1)} async-done(((bf16[16,8,384]{2,1,0:T(8,128)(2,1)}), bf16[16,8,384]{2,1,0:T(8,128)(2,1)S(1)}, u32[]{:S(2)}, u32[]{:S(2)}) %all-to-all-start.1) | async-done | bytes 98336 | tf_op jit(solution)/shard_map/all_to_all | solution.py:36
  35.4 0.2 fusion.13
  35.6 0.1 fusion.14
  35.7 11.6 %all_to_all.42 = bf16[8,16,384]{2,0,1:T(8,128)(2,1)} all-to-all(bf16[8,16,384]{2,0,1:T(8,128)(2,1)S(1)} %fusion.14), channel_id=1, replica_groups=mesh['row'=16,'col'=16] {'col'}, dimensions={1} | all-to-all | bytes 196608 | tf_op jit(solution)/shard_map/all_to_all | solution.py:44
  47.2 0.0 all-gather.3.cloned.1.call-update
  47.3 0.0 all-gather.5.cloned.1.call-start
  47.3 0.7 all-gather.5.cloned.1.call-update
  48.0 35.4 %all-gather.3.cloned.1.call-done = bf16[128,6144]{1,0:T(8,128)(2,1)} async-done(((bf16[128,384]{1,0:T(8,128)(2,1)}), bf16[128,6144]{1,0:T(8,128)(2,1)}) %all-gather.3.cloned.1.call-update) | async-done | bytes 1572880 | tf_op jit(solution)/shard_map/all_gather | solution.py:45
  83.4 128.1 %all-gather.5.cloned.1.call-done = bf16[6144,1536]{1,0:T(8,128)(2,1)} async-done(((bf16[384,1536]{1,0:T(8,128)(2,1)}), bf16[6144,1536]{1,0:T(8,128)(2,1)}) %all-gather.5.cloned.1.call-update) | async-done | bytes 18874384 | tf_op jit(solution)/shard_map/all_gather | solution.py:47
  211.6 10.4 %fusion.12 = bf16[128,1536]{1,0:T(8,128)(2,1)} fusion(bf16[128,6144]{1,0:T(8,128)(2,1)} %all-gather.3.cloned.1.call-done, bf16[6144,1536]{1,0:T(8,128)(2,1)} %all-gather.5.cloned.1.call-done), kind=kOutput, calls=%fused_computation.15 | convolution fusion | flops 2417688576 | bytes 20840448 | tf_op jit(solution)/shard_map/dot_general | solution.py:46
  (3 shorter events, 0.0 us)
Async XLA Ops:
  6.5 20.6 %copy-start = (f32[6144]{0:T(1024)S(1)}, f32[6144]{0:T(1024)}, u32[]{:S(2)}) copy-start(f32[6144]{0:T(1024)} %param.10) | copy-start | bytes 73732
  6.5 17.0 %all-to-all-start = ((bf16[16,8,384]{2,1,0:T(8,128)(2,1)}), bf16[16,8,384]{2,1,0:T(8,128)(2,1)S(1)}, u32[]{:S(2)}, u32[]{:S(2)}) async-start(bf16[16,8,384]{2,1,0:T(8,128)(2,1)} %bitcast.21), calls=%async_computation | async-start | bytes 196608 | tf_op jit(solution)/shard_map/all_to_all | solution.py:37
  23.6 11.8 %all-to-all-start.1 = ((bf16[16,8,384]{2,1,0:T(8,128)(2,1)}), bf16[16,8,384]{2,1,0:T(8,128)(2,1)S(1)}, u32[]{:S(2)}, u32[]{:S(2)}) async-start(bf16[16,8,384]{2,1,0:T(8,128)(2,1)} %all_to_all.34), calls=%async_computation.1 | async-start | bytes 196608 | tf_op jit(solution)/shard_map/all_to_all | solution.py:36
  27.1 56.4 %all-gather.3.cloned.1.call-start = ((), (), s32[]{:S(2)}) async-start(), calls=%async_computation.3 | async-start | bytes 1671168 | tf_op jit(solution)/shard_map/all_gather | solution.py:45
  47.3 164.3 %all-gather.5.cloned.1.call-start = ((), (), s32[]{:S(2)}) async-start(), calls=%async_computation.4 | async-start | bytes 20054016 | tf_op jit(solution)/shard_map/all_gather | solution.py:47
Sparse Core Ops, SparseCore 0:
  47.4 36.0 all-gather.2
  85.9 125.6 all-gather.4
where the time goes:
time: 230 us; the launch traced here: 229 us
  waiting for transfers between devices  176 us (77%)
  between operations  13.5 us (6%)
  starting transfers between devices  12.3 us (5%)
  blocking collectives  11.6 us (5%)
  matrix products  10.9 us (5%)
  local copies, waits for them, and re-layouts  3.85 us (2%)
    all_gather x1, waiting for transfers between devices, per_device(): lax.all_gather(w_up, 'row', axis=0, tiled=True)  128 us
    all_gather x1, waiting for transfers between devices, per_device(): whole = lax.all_gather(normed, 'col', axis=1, tiled=True)  35.4 us
    all_to_all x1, blocking collectives, per_device(): lax.all_to_all(normed_tokens, 'col', split_axis=1, concat_axis=0, tiled=T...  11.6 us
    dot_general x1, matrix products, per_device(): jnp.dot(whole, lax.all_gather(w_up, 'row', axis=0, tiled=True), preferred...  10.4 us
    all_to_all x1, starting transfers between devices, per_device(): lax.all_to_all(resid, 'col', split_axis=0, concat_axis=1, tiled=True)  8.7 us
    all_to_all x1, waiting for transfers between devices, per_device(): lax.all_to_all(attended, 'col', split_axis=0, concat_axis=1, tiled=True)  8.2 us
  transfers between devices with their start and end apart: 4, of which 4 were waited for; matrix products, arithmetic and copies ran while one was open for 2% of the time, Pallas kernels for 0%

commit v1 on v0

v1 whole, which is shorter than its diff:
```python
import math

import jax
import jax.numpy as jnp
from jax import lax
from jax.sharding import Mesh, PartitionSpec as P

HD = 128


def attention_block(query, keys, values):
    seq, width = query.shape
    heads = width // HD
    qshaped = query.reshape(seq, heads, HD)
    kshaped = keys.reshape(seq, heads, HD)
    vshaped = values.reshape(seq, heads, HD)
    scores = jnp.einsum("qhd,khd->hqk", qshaped, kshaped, preferred_element_type=jnp.float32)
    scores = scores * (1.0 / math.sqrt(HD))
    rows_idx = lax.broadcasted_iota(jnp.int32, (seq, seq), 0)
    cols_idx = lax.broadcasted_iota(jnp.int32, (seq, seq), 1)
    scores = jnp.where((rows_idx >= cols_idx)[None], scores, -1e30)
    highest = jnp.max(scores, axis=-1, keepdims=True)
    expo = jnp.exp(scores - highest)
    prob = (expo / jnp.sum(expo, axis=-1, keepdims=True)).astype(jnp.bfloat16)
    output = jnp.einsum("hqk,khd->qhd", prob, vshaped, preferred_element_type=jnp.float32)
    return output.astype(jnp.bfloat16).reshape(seq, width)


def per_device(q_seq, k_seq, v_seq, resid, ln_gain, w_up, full_width):
    w_group = lax.all_gather(w_up, "rx", axis=0, tiled=True)
    attended = attention_block(q_seq, k_seq, v_seq)
    stream = resid.astype(jnp.float32) + attended.astype(jnp.float32)
    width = stream.shape[1]
    sums = jnp.concatenate(
        [jnp.sum(stream, axis=1, keepdims=True), jnp.sum(stream * stream, axis=1, keepdims=True)], axis=1
    )
    sums = lax.psum(sums, "col")
    mean = sums[:, 0:1] / full_width
    spread = sums[:, 1:2] / full_width - mean * mean
    col = lax.axis_index("col")
    gain = lax.dynamic_slice_in_dim(ln_gain, col * width, width)
    normed = ((stream - mean) * lax.rsqrt(spread + 1e-05) * gain[None, :]).astype(jnp.bfloat16)
    whole = lax.all_gather(normed, "col", axis=1, tiled=True)
    tokens = lax.all_to_all(whole, "ry", split_axis=1, concat_axis=0, tiled=True)
    partial = jnp.dot(tokens, w_group, preferred_element_type=jnp.float32)
    product = lax.psum_scatter(partial, "ry", scatter_dimension=0, tiled=True)
    return jax.nn.gelu(product, approximate=True).astype(jnp.bfloat16)


def solution(mesh):
    n_row, n_col = mesh.shape["row"], mesh.shape["col"]
    nx = len({d.coords[0] for d in mesh.devices[:, 0]})
    split = Mesh(mesh.devices.reshape(n_row // nx, nx, n_col), ("ry", "rx", "col"))
    rows = ("ry", "rx")
    placed = (
        P(rows, "col"),
        P(rows, "col"),
        P(rows, "col"),
        P(rows, "col"),
        P(),
        P(rows, "col"),
    )

    def body(q_seq, k_seq, v_seq, resid, ln_gain, w_up):
        return per_device(q_seq, k_seq, v_seq, resid, ln_gain, w_up, float(ln_gain.shape[0]))

    return jax.shard_map(body, mesh=split, in_specs=placed, out_specs=P(rows, "col"), check_vma=False)
```

time: 230 us -> 192 us (0.83)
  waiting for transfers between devices: 176 us -> 108 us
  blocking collectives: 11.6 us -> 54.2 us
  starting transfers between devices: 12.3 us -> 0.08 us
  matrix products: 10.9 us -> 7.04 us
  other arithmetic: 0.4 us -> 3.07 us
    all_gather x1, waiting for transfers between devices: 128 us -> 27.8 us  [per_device(): w_group = lax.all_gather(w_up, 'rx', axis=0, tiled=True)]
    reduce_scatter x0 -> x1, waiting for transfers between devices: none -> 43.1 us  [per_device(): product = lax.psum_scatter(partial, 'ry', scatter_dimension=0, tiled=True)]
    psum x0 -> x1, blocking collectives: none -> 28.8 us  [per_device(): sums = lax.psum(sums, 'col')]
    all_to_all x1, blocking collectives: 11.6 us -> 25.4 us  [per_device(): lax.all_to_all(whole, 'ry', split_axis=1, concat_axis=0, tiled=True)]
    all_to_all x2 -> x0, starting transfers between devices: 12.2 us -> none  [the longest x1 8.7 us: per_device(): lax.all_to_all(resid, 'col', split_axis=0, concat_axis=1, tiled=True)]
    all_to_all x2 -> x0, waiting for transfers between devices: 12.1 us -> none  [the longest x1 8.2 us: per_device(): lax.all_to_all(attended, 'col', split_axis=0, concat_axis=1, tiled=True)]
    dot_general x1, matrix products: 10.4 us -> 6.6 us  [per_device(): partial = jnp.dot(tokens, w_group, preferred_element_type=jnp.float32)]
    convert_element_type x1 -> x2, other arithmetic: 0.1 us -> 2.89 us  [the longest x1 2.13 us: per_device(): return jax.nn.gelu(product, approximate=True).astype(jnp.bfloat16)]
  transfers between devices with their start and end apart: 4 -> 3, of which waited for: 4 -> 3; matrix products, arithmetic and copies ran while one was open for 2% -> 0% of each run, Pallas kernels for 0% -> 0%
where the time goes in v1:
time: 192 us; the launch traced here: 191 us
  waiting for transfers between devices  108 us (56%)
  blocking collectives  54.2 us (28%)
  between operations  13.2 us (7%)
  matrix products  7.04 us (4%)
  local copies, waits for them, and re-layouts  5.51 us (3%)
  other arithmetic  3.07 us (2%)
    reduce_scatter x1, waiting for transfers between devices, per_device(): product = lax.psum_scatter(partial, 'ry', scatter_dimension=0, tiled=True)  43.1 us
    all_gather x1, waiting for transfers between devices, per_device(): whole = lax.all_gather(normed, 'col', axis=1, tiled=True)  36.1 us
    psum x1, blocking collectives, per_device(): sums = lax.psum(sums, 'col')  28.8 us
    all_gather x1, waiting for transfers between devices, per_device(): w_group = lax.all_gather(w_up, 'rx', axis=0, tiled=True)  27.8 us
    all_to_all x1, blocking collectives, per_device(): lax.all_to_all(whole, 'ry', split_axis=1, concat_axis=0, tiled=True)  25.4 us
    dot_general x1, matrix products, per_device(): partial = jnp.dot(tokens, w_group, preferred_element_type=jnp.float32)  6.6 us
    unnamed x4, local copies, waits for them, and re-layouts  4.04 us
  transfers between devices with their start and end apart: 3, of which 3 were waited for; matrix products, arithmetic and copies ran while one was open for 0% of the time, Pallas kernels for 0%

profile of v1, /device:TPU:6, one launch (start us, length us, event | category | flops | bytes accessed | tf_op | source)
XLA Modules:
  0.0 190.9 jit_solution(10350833693274371443)
XLA Ops:
  6.5 0.0 all-gather.3.cloned.1.call-start
  6.6 1.0 copy.19
  7.6 1.0 copy.20
  8.6 1.0 copy.21
  9.6 0.2 fusion.2
  9.8 0.1 fusion.17
  9.9 1.0 copy.24
  10.9 0.2 fusion.4
  11.1 0.1 fusion.14
  11.2 28.8 %psum.7 = f32[128,2]{0,1:T(2,128)S(1)} all-reduce(f32[128,2]{0,1:T(2,128)S(1)} %pad_maximum_fusion), channel_id=1, replica_groups=mesh['ry'=4,'rx'=4,'col'=16] {'col'}, use_global_device_ids=true, to_apply=%region_4.5 | all-reduce | flops 256 | bytes 2048 | tf_op jit(solution)/shard_map/psum | solution.py:37
  40.1 0.8 dynamic_slice.3
  40.8 0.8 multiply_convert_fusion
  41.6 0.0 all-gather.3.cloned.1.call-update
  41.6 0.0 all-gather.5.cloned.1.call-start
  41.7 0.7 all-gather.5.cloned.1.call-update
  42.4 0.0 reduce-scatter.2.cloned.1.call-start
  42.4 36.1 %all-gather.3.cloned.1.call-done = bf16[128,6144]{0,1:T(8,128)(2,1)} async-done(((bf16[128,384]{0,1:T(8,128)(2,1)}), bf16[128,6144]{0,1:T(8,128)(2,1)}) %all-gather.3.cloned.1.call-update) | async-done | bytes 1572880 | tf_op jit(solution)/shard_map/all_gather | solution.py:43
  78.5 25.4 %all_to_all.19 = bf16[128,4,1536]{0,2,1:T(8,128)(2,1)S(1)} all-to-all(bf16[128,4,1536]{0,2,1:T(8,128)(2,1)} %bitcast.30), channel_id=1, replica_groups=mesh['ry'=4,'rx'=4,'col'=16] {'ry'}, dimensions={1} | all-to-all | bytes 3145728 | tf_op jit(solution)/shard_map/all_to_all | solution.py:44
  104.0 0.7 copy.26
  104.7 27.8 %all-gather.5.cloned.1.call-done = bf16[1536,1536]{1,0:T(8,128)(2,1)} async-done(((bf16[384,1536]{1,0:T(8,128)(2,1)}), bf16[1536,1536]{1,0:T(8,128)(2,1)}) %all-gather.5.cloned.1.call-update) | async-done | bytes 4718608 | tf_op jit(solution)/shard_map/all_gather | solution.py:30
  132.5 6.6 %fusion.18 = f32[512,1536]{1,0:T(8,128)} fusion(bf16[512,1536]{1,0:T(8,128)(2,1)S(1)} %bitcast.31, bf16[1536,1536]{1,0:T(8,128)(2,1)} %all-gather.5.cloned.1.call-done), kind=kOutput, calls=%fused_computation.29 | convolution fusion | flops 2415919104 | bytes 9437184 | tf_op jit(solution)/shard_map/dot_general | solution.py:45
  139.1 0.0 reduce-scatter.2.cloned.1.call-update
  139.1 43.1 %reduce-scatter.2.cloned.1.call-done = f32[128,1536]{1,0:T(8,128)} async-done(((f32[512,1536]{1,0:T(8,128)}), f32[128,1536]{1,0:T(8,128)}) %reduce-scatter.2.cloned.1.call-update) | async-done | bytes 786448 | tf_op jit(solution)/shard_map/reduce_scatter | solution.py:46
  182.3 2.1 %fusion.12 = bf16[128,1536]{1,0:T(8,128)(2,1)} fusion(f32[128,1536]{1,0:T(8,128)} %reduce-scatter.2.cloned.1.call-done), kind=kLoop, calls=%fused_computation.15 | loop fusion | flops 1769472 | bytes 1179648 | tf_op jit(solution)/shard_map/convert_element_type | solution.py:47
  (3 shorter events, 0.0 us)
Async XLA Ops:
  6.5 72.0 %all-gather.3.cloned.1.call-start = ((), (), s32[]{:S(2)}) async-start(), calls=%async_computation.2 | async-start | bytes 1671168 | tf_op jit(solution)/shard_map/all_gather | solution.py:43
  41.6 90.9 %all-gather.5.cloned.1.call-start = ((), (), s32[]{:S(2)}) async-start(), calls=%async_computation.3 | async-start | bytes 5898240 | tf_op jit(solution)/shard_map/all_gather | solution.py:30
  42.4 139.9 %reduce-scatter.2.cloned.1.call-start = ((), (), s32[]{:S(2)}) async-start(), calls=%async_computation.4 | async-start | bytes 3932160 | tf_op jit(solution)/shard_map/reduce_scatter | solution.py:46
Sparse Core Ops, SparseCore 0:
  41.7 36.7 all-gather.2
  80.3 52.1 all-gather.4
  139.2 42.9 reduce-scatter.1

commit v2 on v1

--- a/solution.py
+++ b/solution.py
@@ -26,23 +26,22 @@
     return output.astype(jnp.bfloat16).reshape(seq, width)
 
 
-def per_device(q_seq, k_seq, v_seq, resid, ln_gain, w_up, full_width):
+def per_device(q_seq, k_seq, v_seq, resid, ln_gain, w_up):
     w_group = lax.all_gather(w_up, "rx", axis=0, tiled=True)
+    res_tokens = lax.all_to_all(resid, "col", split_axis=0, concat_axis=1, tiled=True)
     attended = attention_block(q_seq, k_seq, v_seq)
-    stream = resid.astype(jnp.float32) + attended.astype(jnp.float32)
-    width = stream.shape[1]
-    sums = jnp.concatenate(
-        [jnp.sum(stream, axis=1, keepdims=True), jnp.sum(stream * stream, axis=1, keepdims=True)], axis=1
-    )
-    sums = lax.psum(sums, "col")
-    mean = sums[:, 0:1] / full_width
-    spread = sums[:, 1:2] / full_width - mean * mean
-    col = lax.axis_index("col")
-    gain = lax.dynamic_slice_in_dim(ln_gain, col * width, width)
-    normed = ((stream - mean) * lax.rsqrt(spread + 1e-05) * gain[None, :]).astype(jnp.bfloat16)
-    whole = lax.all_gather(normed, "col", axis=1, tiled=True)
-    tokens = lax.all_to_all(whole, "ry", split_axis=1, concat_axis=0, tiled=True)
-    partial = jnp.dot(tokens, w_group, preferred_element_type=jnp.float32)
+    att_tokens = lax.all_to_all(attended, "col", split_axis=0, concat_axis=1, tiled=True)
+    stream = res_tokens.astype(jnp.float32) + att_tokens.astype(jnp.float32)
+    full_width = stream.shape[1]
+    mean = jnp.sum(stream, axis=1, keepdims=True) / full_width
+    spread = jnp.sum(stream * stream, axis=1, keepdims=True) / full_width - mean * mean
+    normed = ((stream - mean) * lax.rsqrt(spread + 1e-05) * ln_gain[None, :]).astype(jnp.bfloat16)
+    part = lax.all_to_all(normed, "ry", split_axis=1, concat_axis=0, tiled=True)
+    n_y = part.shape[0] // normed.shape[0]
+    part = part.reshape(n_y, normed.shape[0], part.shape[1])
+    tokens = lax.all_gather(part, "col", axis=0, tiled=False)
+    partial = jnp.einsum("cytf,fu->yctu", tokens, w_group, preferred_element_type=jnp.float32)
+    partial = partial.reshape(-1, partial.shape[-1])
     product = lax.psum_scatter(partial, "ry", scatter_dimension=0, tiled=True)
     return jax.nn.gelu(product, approximate=True).astype(jnp.bfloat16)
 
@@ -62,6 +61,6 @@
     )
 
     def body(q_seq, k_seq, v_seq, resid, ln_gain, w_up):
-        return per_device(q_seq, k_seq, v_seq, resid, ln_gain, w_up, float(ln_gain.shape[0]))
+        return per_device(q_seq, k_seq, v_seq, resid, ln_gain, w_up)
 
     return jax.shard_map(body, mesh=split, in_specs=placed, out_specs=P(rows, "col"), check_vma=False)

time: 192 us -> 194 us (1.010)
  blocking collectives: 54.2 us -> 10.2 us
  waiting for transfers between devices: 108 us -> 143 us
  starting transfers between devices: 0.08 us -> 12.2 us
    psum x1 -> x0, blocking collectives: 28.8 us -> none  [per_device(): sums = lax.psum(sums, 'col')]
    all_gather x1, waiting for transfers between devices: 27.8 us -> 54 us  [per_device(): w_group = lax.all_gather(w_up, 'rx', axis=0, tiled=True)]
    all_to_all x1, blocking collectives: 25.4 us -> 10.2 us  [per_device(): part = lax.all_to_all(normed, 'ry', split_axis=1, concat_axis=0, tiled=True)]
    all_to_all x0 -> x2, starting transfers between devices: none -> 12.1 us  [the longest x1 8.57 us: per_device(): lax.all_to_all(resid, 'col', split_axis=0, concat_axis=1, tiled=True)]
    all_to_all x0 -> x2, waiting for transfers between devices: none -> 11.3 us  [the longest x1 7.47 us: per_device(): lax.all_to_all(attended, 'col', split_axis=0, concat_axis=1, tiled=True)]
    all_gather x1, waiting for transfers between devices: 36.1 us -> 33.5 us  [per_device(): tokens = lax.all_gather(part, 'col', axis=0, tiled=False)]
    unnamed x4 -> x3, local copies, waits for them, and re-layouts: 4.04 us -> 3.03 us
  transfers between devices with their start and end apart: 3 -> 5, of which waited for: 3 -> 5; matrix products, arithmetic and copies ran while one was open for 0% -> 2% of each run, Pallas kernels for 0% -> 0%
where the time goes in v2:
time: 194 us; the launch traced here: 193 us
  waiting for transfers between devices  143 us (74%)
  between operations  13.2 us (7%)
  starting transfers between devices  12.2 us (6%)
  blocking collectives  10.2 us (5%)
  local copies, waits for them, and re-layouts  6.52 us (3%)
  matrix products  5.42 us (3%)
  other arithmetic  2.53 us (1%)
    all_gather x1, waiting for transfers between devices, per_device(): w_group = lax.all_gather(w_up, 'rx', axis=0, tiled=True)  54 us
    reduce_scatter x1, waiting for transfers between devices, per_device(): product = lax.psum_scatter(partial, 'ry', scatter_dimension=0, tiled=True)  43.1 us
    all_gather x1, waiting for transfers between devices, per_device(): tokens = lax.all_gather(part, 'col', axis=0, tiled=False)  33.5 us
    all_to_all x1, blocking collectives, per_device(): part = lax.all_to_all(normed, 'ry', split_axis=1, concat_axis=0, tiled=True)  10.2 us
    all_to_all x1, starting transfers between devices, per_device(): lax.all_to_all(resid, 'col', split_axis=0, concat_axis=1, tiled=True)  8.57 us
    all_to_all x1, waiting for transfers between devices, per_device(): lax.all_to_all(attended, 'col', split_axis=0, concat_axis=1, tiled=True)  7.47 us
    dot_general x1, matrix products, per_device(): jnp.einsum('cytf,fu->yctu', tokens, w_group, preferred_element_type=jnp.f...  4.93 us
  transfers between devices with their start and end apart: 5, of which 5 were waited for; matrix products, arithmetic and copies ran while one was open for 2% of the time, Pallas kernels for 0%

profile of v2, /device:TPU:6, one launch (start us, length us, event | category | flops | bytes accessed | tf_op | source)
XLA Modules:
  0.0 192.7 jit_solution(17831639695960104614)
XLA Ops:
  6.5 8.6 %all-to-all-start = ((bf16[16,8,384]{2,1,0:T(8,128)(2,1)}), bf16[16,8,384]{2,1,0:T(8,128)(2,1)S(1)}, u32[]{:S(2)}, u32[]{:S(2)}) async-start(bf16[16,8,384]{2,1,0:T(8,128)(2,1)} %bitcast.32), calls=%async_computation | async-start | bytes 196608 | tf_op jit(solution)/shard_map/all_to_all | solution.py:31
  15.1 1.0 copy.20
  16.1 1.0 copy.21
  17.2 0.2 fusion.7
  17.4 0.1 fusion.21
  17.5 1.0 copy.24
  18.5 0.3 fusion.9
  18.8 0.1 copy.27
  18.8 0.7 all_to_all.32
  19.6 3.9 %all-to-all-done = bf16[16,8,384]{2,1,0:T(8,128)(2,1)S(1)} async-done(((bf16[16,8,384]{2,1,0:T(8,128)(2,1)}), bf16[16,8,384]{2,1,0:T(8,128)(2,1)S(1)}, u32[]{:S(2)}, u32[]{:S(2)}) %all-to-all-start) | async-done | bytes 98336 | tf_op jit(solution)/shard_map/all_to_all | solution.py:31
  23.4 3.5 %all-to-all-start.1 = ((bf16[16,8,384]{2,1,0:T(8,128)(2,1)}), bf16[16,8,384]{2,1,0:T(8,128)(2,1)S(1)}, u32[]{:S(2)}, u32[]{:S(2)}) async-start(bf16[16,8,384]{2,1,0:T(8,128)(2,1)} %all_to_all.32), calls=%async_computation.1 | async-start | bytes 196608 | tf_op jit(solution)/shard_map/all_to_all | solution.py:33
  26.9 0.0 all-gather.6.cloned.1.call-start
  27.0 0.8 mul.66
  27.7 7.5 %all-to-all-done.1 = bf16[16,8,384]{2,1,0:T(8,128)(2,1)S(1)} async-done(((bf16[16,8,384]{2,1,0:T(8,128)(2,1)}), bf16[16,8,384]{2,1,0:T(8,128)(2,1)S(1)}, u32[]{:S(2)}, u32[]{:S(2)}) %all-to-all-start.1) | async-done | bytes 98336 | tf_op jit(solution)/shard_map/all_to_all | solution.py:33
  35.2 0.2 fusion.20
  35.4 0.1 multiply_convert_fusion
  35.5 10.2 %all_to_all.39 = bf16[8,4,1536]{2,0,1:T(8,128)(2,1)} all-to-all(bf16[8,4,1536]{2,0,1:T(8,128)(2,1)S(1)} %multiply_convert_fusion), channel_id=1, replica_groups=mesh['ry'=4,'rx'=4,'col'=16] {'ry'}, dimensions={1} | all-to-all | bytes 196608 | tf_op jit(solution)/shard_map/all_to_all | solution.py:39
  45.8 0.7 all-gather.4.cloned.1.call-update
  46.5 33.5 %all-gather.6.cloned.1.call-done = bf16[64,8,1536]{2,1,0:T(8,128)(2,1)} async-done(((bf16[4,8,1536]{2,1,0:T(8,128)(2,1)}), bf16[64,8,1536]{2,1,0:T(8,128)(2,1)}) %all-gather.6.cloned.1.call-update) | async-done | bytes 1572880 | tf_op jit(solution)/shard_map/all_gather | solution.py:42
  80.1 54.0 %all-gather.4.cloned.1.call-done = bf16[1536,1536]{1,0:T(8,128)(2,1)} async-done(((bf16[384,1536]{1,0:T(8,128)(2,1)}), bf16[1536,1536]{1,0:T(8,128)(2,1)}) %all-gather.4.cloned.1.call-update) | async-done | bytes 4718608 | tf_op jit(solution)/shard_map/all_gather | solution.py:30
  134.0 4.9 %fusion.3 = f32[4,16,8,1536]{3,2,0,1:T(8,128)S(1)} fusion(bf16[16,4,8,1536]{3,2,1,0:T(8,128)(2,1)} %bitcast.34, bf16[1536,1536]{1,0:T(8,128)(2,1)} %all-gather.4.cloned.1.call-done), kind=kOutput, calls=%fused_computation.3 | convolution fusion | flops 2415919104 | bytes 9437184 | tf_op jit(solution)/shard_map/cytf,fu->yctu/dot_general | solution.py:43
  139.0 1.9 copy.28
  140.9 43.1 %reduce-scatter.2.cloned.1.call-done = f32[128,1536]{1,0:T(8,128)} async-done(((f32[512,1536]{1,0:T(8,128)}), f32[128,1536]{1,0:T(8,128)}) %reduce-scatter.2.cloned.1.call-update) | async-done | bytes 786448 | tf_op jit(solution)/shard_map/reduce_scatter | solution.py:45
  184.0 2.1 %fusion.17 = bf16[128,1536]{1,0:T(8,128)(2,1)} fusion(f32[128,1536]{1,0:T(8,128)} %reduce-scatter.2.cloned.1.call-done), kind=kLoop, calls=%fused_computation.18 | loop fusion | flops 1769472 | bytes 1179648 | tf_op jit(solution)/shard_map/convert_element_type | solution.py:46
  (6 shorter events, 0.1 us)
Async XLA Ops:
  6.5 16.9 %all-to-all-start = ((bf16[16,8,384]{2,1,0:T(8,128)(2,1)}), bf16[16,8,384]{2,1,0:T(8,128)(2,1)S(1)}, u32[]{:S(2)}, u32[]{:S(2)}) async-start(bf16[16,8,384]{2,1,0:T(8,128)(2,1)} %bitcast.32), calls=%async_computation | async-start | bytes 196608 | tf_op jit(solution)/shard_map/all_to_all | solution.py:31
  23.4 11.8 %all-to-all-start.1 = ((bf16[16,8,384]{2,1,0:T(8,128)(2,1)}), bf16[16,8,384]{2,1,0:T(8,128)(2,1)S(1)}, u32[]{:S(2)}, u32[]{:S(2)}) async-start(bf16[16,8,384]{2,1,0:T(8,128)(2,1)} %all_to_all.32), calls=%async_computation.1 | async-start | bytes 196608 | tf_op jit(solution)/shard_map/all_to_all | solution.py:33
  26.9 53.1 %all-gather.6.cloned.1.call-start = ((), (), s32[]{:S(2)}) async-start(), calls=%async_computation.6 | async-start | bytes 1671168 | tf_op jit(solution)/shard_map/all_gather | solution.py:42
  45.7 88.3 %all-gather.4.cloned.1.call-start = ((), (), s32[]{:S(2)}) async-start(), calls=%async_computation.4 | async-start | bytes 5898240 | tf_op jit(solution)/shard_map/all_gather | solution.py:30
  46.5 137.6 %reduce-scatter.2.cloned.1.call-start = ((), (), s32[]{:S(2)}) async-start(), calls=%async_computation.5 | async-start | bytes 3932160 | tf_op jit(solution)/shard_map/reduce_scatter | solution.py:45
Sparse Core Ops, SparseCore 0:
  45.9 34.1 all-gather.5
  81.9 52.1 all-gather.3
  141.0 42.9 reduce-scatter.1

commit v3 on v2

--- a/solution.py
+++ b/solution.py
@@ -26,8 +26,24 @@
     return output.astype(jnp.bfloat16).reshape(seq, width)
 
 
-def per_device(q_seq, k_seq, v_seq, resid, ln_gain, w_up):
-    w_group = lax.all_gather(w_up, "rx", axis=0, tiled=True)
+def gather_ring(block, axis, n):
+    if n != 4:
+        whole = lax.all_gather(block, axis, axis=0, tiled=False)
+        me = lax.axis_index(axis)
+        order = (me + jnp.arange(n)) % n
+        return jnp.take(whole, order, axis=0).reshape((-1,) + block.shape[1:])
+    to_right = [(i, (i + 1) % n) for i in range(n)]
+    to_left = [(i, (i - 1) % n) for i in range(n)]
+    from_left = lax.ppermute(block, axis, to_right)
+    from_right = lax.ppermute(block, axis, to_left)
+    half = block.shape[0] // 2
+    far_low = lax.ppermute(from_left[:half], axis, to_right)
+    far_high = lax.ppermute(from_right[half:], axis, to_left)
+    return jnp.concatenate([block, from_right, far_low, far_high, from_left], axis=0)
+
+
+def per_device(q_seq, k_seq, v_seq, resid, ln_gain, w_up, n_x):
+    w_group = gather_ring(w_up, "rx", n_x)
     res_tokens = lax.all_to_all(resid, "col", split_axis=0, concat_axis=1, tiled=True)
     attended = attention_block(q_seq, k_seq, v_seq)
     att_tokens = lax.all_to_all(attended, "col", split_axis=0, concat_axis=1, tiled=True)
@@ -40,6 +56,9 @@
     n_y = part.shape[0] // normed.shape[0]
     part = part.reshape(n_y, normed.shape[0], part.shape[1])
     tokens = lax.all_gather(part, "col", axis=0, tiled=False)
+    block = w_up.shape[0]
+    doubled = jnp.concatenate([tokens, tokens], axis=3)
+    tokens = lax.dynamic_slice_in_dim(doubled, lax.axis_index("rx") * block, tokens.shape[3], axis=3)
     partial = jnp.einsum("cytf,fu->yctu", tokens, w_group, preferred_element_type=jnp.float32)
     partial = partial.reshape(-1, partial.shape[-1])
     product = lax.psum_scatter(partial, "ry", scatter_dimension=0, tiled=True)
@@ -61,6 +80,6 @@
     )
 
     def body(q_seq, k_seq, v_seq, resid, ln_gain, w_up):
-        return per_device(q_seq, k_seq, v_seq, resid, ln_gain, w_up)
+        return per_device(q_seq, k_seq, v_seq, resid, ln_gain, w_up, nx)
 
     return jax.shard_map(body, mesh=split, in_specs=placed, out_specs=P(rows, "col"), check_vma=False)

time: 194 us -> 154 us (0.79)
  waiting for transfers between devices: 143 us -> 78 us
  blocking collectives: 10.2 us -> 26.9 us
  local copies, waits for them, and re-layouts: 6.52 us -> 18.8 us
  starting transfers between devices: 12.2 us -> 7.72 us
    all_gather x1 -> x0, waiting for transfers between devices: 54 us -> none  [per_device(): w_group = lax.all_gather(w_up, 'rx', axis=0, tiled=True)]
    ppermute x0 -> x4, waiting for transfers between devices: none -> 35.2 us  [the longest x1 25 us: gather_ring(): from_left = lax.ppermute(block, axis, to_right)]
    all_gather x1, waiting for transfers between devices: 33.5 us -> 0.01 us  [per_device(): tokens = lax.all_gather(part, 'col', axis=0, tiled=False)]
    all_to_all x0 -> x1, blocking collectives: none -> 16.7 us  [per_device(): lax.all_to_all(attended, 'col', split_axis=0, concat_axis=1, tiled=True)]
    reduce_scatter x1, waiting for transfers between devices: 43.1 us -> 35.3 us  [per_device(): product = lax.psum_scatter(partial, 'ry', scatter_dimension=0, tiled=True)]
    all_to_all x1 -> x0, waiting for transfers between devices: 7.47 us -> none  [per_device(): lax.all_to_all(attended, 'col', split_axis=0, concat_axis=1, tiled=True)]
    unnamed x3 -> x9, local copies, waits for them, and re-layouts: 3.03 us -> 9.18 us
    all_to_all x1, starting transfers between devices: 8.57 us -> 3.51 us  [per_device(): lax.all_to_all(resid, 'col', split_axis=0, concat_axis=1, tiled=True)]
  transfers between devices with their start and end apart: 5 -> 7, of which waited for: 5 -> 5; matrix products, arithmetic and copies ran while one was open for 2% -> 6% of each run, Pallas kernels for 0% -> 0%
where the time goes in v3:
time: 154 us; the launch traced here: 153 us
  waiting for transfers between devices  78 us (51%)
  blocking collectives  26.9 us (17%)
  local copies, waits for them, and re-layouts  18.8 us (12%)
  between operations  13.5 us (9%)
  starting transfers between devices  7.72 us (5%)
  matrix products  5.08 us (3%)
  other arithmetic  2.55 us (2%)
    reduce_scatter x1, waiting for transfers between devices, per_device(): product = lax.psum_scatter(partial, 'ry', scatter_dimension=0, tiled=True)  35.3 us
    ppermute x1, waiting for transfers between devices, gather_ring(): from_left = lax.ppermute(block, axis, to_right)  25 us
    all_to_all x1, blocking collectives, per_device(): lax.all_to_all(attended, 'col', split_axis=0, concat_axis=1, tiled=True)  16.7 us
    all_to_all x1, blocking collectives, per_device(): part = lax.all_to_all(normed, 'ry', split_axis=1, concat_axis=0, tiled=True)  10.2 us
    unnamed x9, local copies, waits for them, and re-layouts  9.18 us
    ppermute x1, waiting for transfers between devices, gather_ring(): far_low = lax.ppermute(from_left[:half], axis, to_right)  8.75 us
    all_to_all x1, waiting for transfers between devices, per_device(): lax.all_to_all(resid, 'col', split_axis=0, concat_axis=1, tiled=True)  7.47 us
    dot_general x1, matrix products, per_device(): jnp.einsum('cytf,fu->yctu', tokens, w_group, preferred_element_type=jnp.f...  4.6 us
  transfers between devices with their start and end apart: 7, of which 5 were waited for; matrix products, arithmetic and copies ran while one was open for 6% of the time, Pallas kernels for 0%

profile of v3, /device:TPU:6, one launch (start us, length us, event | category | flops | bytes accessed | tf_op | source)
XLA Modules:
  0.0 152.6 jit_solution(7139897727542933133)
XLA Ops:
  6.6 1.1 copy.28
  7.7 1.0 copy.24
  8.7 1.0 copy.25
  10.5 16.7 %all_to_all.39 = bf16[16,8,384]{2,1,0:T(8,128)(2,1)S(1)} all-to-all(bf16[16,8,384]{2,1,0:T(8,128)(2,1)S(1)} %all_to_all.32), channel_id=1, replica_groups=mesh['ry'=4,'rx'=4,'col'=16] {'col'}, dimensions={0} | all-to-all | bytes 196608 | tf_op jit(solution)/shard_map/all_to_all | solution.py:49
  27.1 3.5 %all-to-all-start = ((bf16[16,8,384]{2,1,0:T(8,128)(2,1)}), bf16[16,8,384]{2,1,0:T(8,128)(2,1)S(1)}, u32[]{:S(2)}, u32[]{:S(2)}) async-start(bf16[16,8,384]{2,1,0:T(8,128)(2,1)} %bitcast.30), calls=%async_computation | async-start | bytes 196608 | tf_op jit(solution)/shard_map/all_to_all | solution.py:47
  31.5 7.5 %all-to-all-done = bf16[16,8,384]{2,1,0:T(8,128)(2,1)S(1)} async-done(((bf16[16,8,384]{2,1,0:T(8,128)(2,1)}), bf16[16,8,384]{2,1,0:T(8,128)(2,1)S(1)}, u32[]{:S(2)}, u32[]{:S(2)}) %all-to-all-start) | async-done | bytes 98336 | tf_op jit(solution)/shard_map/all_to_all | solution.py:47
  39.4 10.2 %all_to_all.40 = bf16[8,4,1536]{2,0,1:T(8,128)(2,1)} all-to-all(bf16[8,4,1536]{2,0,1:T(8,128)(2,1)S(1)} %copy.33), channel_id=1, replica_groups=mesh['ry'=4,'rx'=4,'col'=16] {'ry'}, dimensions={1} | all-to-all | bytes 196608 | tf_op jit(solution)/shard_map/all_to_all | solution.py:55
  50.2 1.5 %collective-permute-start = (bf16[384,1536]{1,0:T(8,128)(2,1)S(1)}, bf16[384,1536]{1,0:T(8,128)(2,1)S(1)}, u32[]{:S(2)}, u32[]{:S(2)}) collective-permute-start(bf16[384,1536]{1,0:T(8,128)(2,1)S(1)} %copy-done), channel_id=1, source_target_pairs={{0,48},{16,0},{32,16},{48,32},{1,49},{17,1},{33,17},{49,33},{2,50}... | collective-permute-start | bytes 3538952 | tf_op jit(solution)/shard_map/ppermute | solution.py:38
  51.8 25.0 %collective-permute-done.1 = bf16[384,1536]{1,0:T(8,128)(2,1)S(1)} collective-permute-done((bf16[384,1536]{1,0:T(8,128)(2,1)S(1)}, bf16[384,1536]{1,0:T(8,128)(2,1)S(1)}, u32[]{:S(2)}, u32[]{:S(2)}) %collective-permute-start.1) | collective-permute-done | bytes 1179680 | tf_op jit(solution)/shard_map/ppermute | solution.py:37
  76.8 0.9 slice.8
  77.7 1.7 %collective-permute-start.2 = (bf16[192,1536]{1,0:T(8,128)(2,1)}, bf16[192,1536]{1,0:T(8,128)(2,1)}, u32[]{:S(2)}, u32[]{:S(2)}) collective-permute-start(bf16[192,1536]{1,0:T(8,128)(2,1)} %slice.8), channel_id=1, source_target_pairs={{0,16},{16,32},{32,48},{48,0},{1,17},{17,33},{33,49},{49,1},{2,18}... | collective-permute-start | bytes 1769480 | tf_op jit(solution)/shard_map/ppermute | solution.py:40
  79.4 0.9 slice.9
  80.6 1.1 constant_dynamic-update-slice_fusion.4
  81.6 1.1 constant_dynamic-update-slice_fusion.3
  82.8 8.8 %collective-permute-done.2 = bf16[192,1536]{1,0:T(8,128)(2,1)} collective-permute-done((bf16[192,1536]{1,0:T(8,128)(2,1)}, bf16[192,1536]{1,0:T(8,128)(2,1)}, u32[]{:S(2)}, u32[]{:S(2)}) %collective-permute-start.2) | collective-permute-done | bytes 589856 | tf_op jit(solution)/shard_map/ppermute | solution.py:40
  91.5 1.9 %constant_dynamic-update-slice_fusion.2 = bf16[1536,1536]{1,0:T(8,128)(2,1)} fusion(bf16[1536,1536]{1,0:T(8,128)(2,1)} %constant_dynamic-update-slice_fusion.3, bf16[192,1536]{1,0:T(8,128)(2,1)} %collective-permute-done.2), kind=kLoop, calls=%fused_computation.32 | loop fusion | bytes 1179648
  93.5 1.5 collective-permute-done.3
  94.9 1.9 %constant_dynamic-update-slice_fusion.1 = bf16[1536,1536]{1,0:T(8,128)(2,1)} fusion(bf16[1536,1536]{1,0:T(8,128)(2,1)} %constant_dynamic-update-slice_fusion.2, bf16[192,1536]{1,0:T(8,128)(2,1)} %collective-permute-done.3), kind=kLoop, calls=%fused_computation.31 | loop fusion | bytes 1179648
  96.8 1.1 constant_dynamic-update-slice_fusion
  97.9 2.3 %copy.34 = bf16[16,4,8,1536]{3,0,2,1:T(8,128)(2,1)S(1)} copy(bf16[16,4,8,1536]{3,2,1,0:T(8,128)(2,1)} %bitcast.26) | data formatting | bytes 3145728 | tf_op jit(solution)/shard_map/all_gather | solution.py:58
  100.2 4.6 %fusion.3 = f32[4,16,8,1536]{3,1,2,0:T(8,128)S(1)} fusion(bf16[1536,1536]{1,0:T(8,128)(2,1)} %constant_dynamic-update-slice_fusion, s32[]{:T(128)S(6)} %select_n.8, bf16[16,4,8,1536]{3,0,2,1:T(8,128)(2,1)S(1)} %copy.34), kind=kOutput, calls=%fused_computation.3 | convolution fusion | flops 2419064832 | bytes 9437188 | tf_op jit(solution)/shard_map/cytf,fu->yctu/dot_general | solution.py:62
  104.8 3.5 %copy.36 = f32[4,16,8,1536]{3,2,1,0:T(8,128)} copy(f32[4,16,8,1536]{3,1,2,0:T(8,128)S(1)} %fusion.3) | data formatting | bytes 6291456 | tf_op jit(solution)/shard_map/cytf,fu->yctu/transpose | solution.py:62
  108.3 35.3 %reduce-scatter.2.cloned.1.call-done = f32[128,1536]{1,0:T(8,128)} async-done(((f32[512,1536]{1,0:T(8,128)}), f32[128,1536]{1,0:T(8,128)}) %reduce-scatter.2.cloned.1.call-update) | async-done | bytes 786448 | tf_op jit(solution)/shard_map/reduce_scatter | solution.py:64
  143.6 2.1 %fusion.19 = bf16[128,1536]{1,0:T(8,128)(2,1)} fusion(f32[128,1536]{1,0:T(8,128)} %reduce-scatter.2.cloned.1.call-done), kind=kLoop, calls=%fused_computation.21 | loop fusion | flops 1769472 | bytes 1179648 | tf_op jit(solution)/shard_map/convert_element_type | solution.py:65
  (23 shorter events, 3.0 us)
Async XLA Ops:
  6.5 43.1 %copy-start = (bf16[384,1536]{1,0:T(8,128)(2,1)S(1)}, bf16[384,1536]{1,0:T(8,128)(2,1)}, u32[]{:S(2)}) copy-start(bf16[384,1536]{1,0:T(8,128)(2,1)} %param.11) | copy-start | bytes 3538948
  27.1 11.8 %all-to-all-start = ((bf16[16,8,384]{2,1,0:T(8,128)(2,1)}), bf16[16,8,384]{2,1,0:T(8,128)(2,1)S(1)}, u32[]{:S(2)}, u32[]{:S(2)}) async-start(bf16[16,8,384]{2,1,0:T(8,128)(2,1)} %bitcast.30), calls=%async_computation | async-start | bytes 196608 | tf_op jit(solution)/shard_map/all_to_all | solution.py:47
  30.7 67.2 %all-gather.3.cloned.1.call-start = ((), (), s32[]{:S(2)}) async-start(), calls=%async_computation.5 | async-start | bytes 1671168 | tf_op jit(solution)/shard_map/all_gather | solution.py:58
  49.6 94.0 %reduce-scatter.2.cloned.1.call-start = ((), (), s32[]{:S(2)}) async-start(), calls=%async_computation.4 | async-start | bytes 3932160 | tf_op jit(solution)/shard_map/reduce_scatter | solution.py:64
  49.7 27.1 %collective-permute-start.1 = (bf16[384,1536]{1,0:T(8,128)(2,1)S(1)}, bf16[384,1536]{1,0:T(8,128)(2,1)S(1)}, u32[]{:S(2)}, u32[]{:S(2)}) collective-permute-start(bf16[384,1536]{1,0:T(8,128)(2,1)S(1)} %copy-done), channel_id=1, source_target_pairs={{0,16},{16,32},{32,48},{48,0},{1,17},{17,33},{33,49},{49,1},{2,18}... | collective-permute-start | bytes 3538952 | tf_op jit(solution)/shard_map/ppermute | solution.py:37
  50.2 29.1 %collective-permute-start = (bf16[384,1536]{1,0:T(8,128)(2,1)S(1)}, bf16[384,1536]{1,0:T(8,128)(2,1)S(1)}, u32[]{:S(2)}, u32[]{:S(2)}) collective-permute-start(bf16[384,1536]{1,0:T(8,128)(2,1)S(1)} %copy-done), channel_id=1, source_target_pairs={{0,48},{16,0},{32,16},{48,32},{1,49},{17,1},{33,17},{49,33},{2,50}... | collective-permute-start | bytes 3538952 | tf_op jit(solution)/shard_map/ppermute | solution.py:38
  77.7 13.9 %collective-permute-start.2 = (bf16[192,1536]{1,0:T(8,128)(2,1)}, bf16[192,1536]{1,0:T(8,128)(2,1)}, u32[]{:S(2)}, u32[]{:S(2)}) collective-permute-start(bf16[192,1536]{1,0:T(8,128)(2,1)} %slice.8), channel_id=1, source_target_pairs={{0,16},{16,32},{32,48},{48,0},{1,17},{17,33},{33,49},{49,1},{2,18}... | collective-permute-start | bytes 1769480 | tf_op jit(solution)/shard_map/ppermute | solution.py:40
  80.2 14.7 %collective-permute-start.3 = (bf16[192,1536]{1,0:T(8,128)(2,1)}, bf16[192,1536]{1,0:T(8,128)(2,1)}, u32[]{:S(2)}, u32[]{:S(2)}) collective-permute-start(bf16[192,1536]{1,0:T(8,128)(2,1)} %slice.9), channel_id=1, source_target_pairs={{0,48},{16,0},{32,16},{48,32},{1,49},{17,1},{33,17},{49,33},{2,50}... | collective-permute-start | bytes 1769480 | tf_op jit(solution)/shard_map/ppermute | solution.py:41
Sparse Core Ops, SparseCore 0:
  49.7 34.1 all-gather.2
  108.4 35.1 reduce-scatter.1

commit v4 on v2

--- a/solution.py
+++ b/solution.py
@@ -3,6 +3,7 @@
 import jax
 import jax.numpy as jnp
 from jax import lax
+from jax.experimental import pallas as pl
 from jax.sharding import Mesh, PartitionSpec as P
 
 HD = 128
@@ -26,8 +27,48 @@
     return output.astype(jnp.bfloat16).reshape(seq, width)
 
 
-def per_device(q_seq, k_seq, v_seq, resid, ln_gain, w_up):
-    w_group = lax.all_gather(w_up, "rx", axis=0, tiled=True)
+def ring_pieces(block, axis):
+    n = 4
+    to_right = [(i, (i + 1) % n) for i in range(n)]
+    to_left = [(i, (i - 1) % n) for i in range(n)]
+    from_left = lax.ppermute(block, axis, to_right)
+    from_right = lax.ppermute(block, axis, to_left)
+    half = block.shape[1] // 2
+    far_low = lax.ppermute(from_left[:, :half], axis, to_right)
+    far_high = lax.ppermute(from_right[:, half:], axis, to_left)
+    return block, from_right, far_low, far_high, from_left
+
+
+def pieces_kernel(a_ref, w0_ref, w1_ref, w2lo_ref, w2hi_ref, w3_ref, o_ref):
+    k = w0_ref.shape[0]
+    half = w2lo_ref.shape[1]
+    a = a_ref[...]
+    base = jnp.dot(a[:, 0:k], w0_ref[...], preferred_element_type=jnp.float32)
+    base = base + jnp.dot(a[:, k:2 * k], w1_ref[...], preferred_element_type=jnp.float32)
+    base = base + jnp.dot(a[:, 3 * k:4 * k], w3_ref[...], preferred_element_type=jnp.float32)
+    far = a[:, 2 * k:3 * k]
+    o_ref[:, 0:half] = base[:, 0:half] + jnp.dot(far, w2lo_ref[...], preferred_element_type=jnp.float32)
+    o_ref[:, half:] = base[:, half:] + jnp.dot(far, w2hi_ref[...], preferred_element_type=jnp.float32)
+
+
+def dot_pieces(a, pieces, tile=128):
+    m, kk = a.shape
+    n = pieces[0].shape[1]
+    full = lambda p: pl.BlockSpec(p.shape, lambda i: (0, 0))
+    return pl.pallas_call(
+        pieces_kernel,
+        grid=(m // tile,),
+        in_specs=[pl.BlockSpec((tile, kk), lambda i: (i, 0))] + [full(p) for p in pieces],
+        out_specs=pl.BlockSpec((tile, n), lambda i: (i, 0)),
+        out_shape=jax.ShapeDtypeStruct((m, n), jnp.float32),
+        cost_estimate=pl.CostEstimate(
+            flops=2 * m * kk * n, transcendentals=0, bytes_accessed=a.size * 2 + sum(p.size * 2 for p in pieces) + m * n * 4
+        ),
+    )(a, *pieces)
+
+
+def per_device(q_seq, k_seq, v_seq, resid, ln_gain, w_up, n_x):
+    pieces = ring_pieces(w_up, "rx")
     res_tokens = lax.all_to_all(resid, "col", split_axis=0, concat_axis=1, tiled=True)
     attended = attention_block(q_seq, k_seq, v_seq)
     att_tokens = lax.all_to_all(attended, "col", split_axis=0, concat_axis=1, tiled=True)
@@ -36,12 +77,16 @@
     mean = jnp.sum(stream, axis=1, keepdims=True) / full_width
     spread = jnp.sum(stream * stream, axis=1, keepdims=True) / full_width - mean * mean
     normed = ((stream - mean) * lax.rsqrt(spread + 1e-05) * ln_gain[None, :]).astype(jnp.bfloat16)
-    part = lax.all_to_all(normed, "ry", split_axis=1, concat_axis=0, tiled=True)
-    n_y = part.shape[0] // normed.shape[0]
-    part = part.reshape(n_y, normed.shape[0], part.shape[1])
-    tokens = lax.all_gather(part, "col", axis=0, tiled=False)
-    partial = jnp.einsum("cytf,fu->yctu", tokens, w_group, preferred_element_type=jnp.float32)
-    partial = partial.reshape(-1, partial.shape[-1])
+    chunk, block = normed.shape[0], w_up.shape[0]
+    n_y = full_width // (n_x * block)
+    grouped = normed.reshape(chunk, n_y, n_x, block)
+    doubled = jnp.concatenate([grouped, grouped], axis=2)
+    rolled = lax.dynamic_slice_in_dim(doubled, lax.axis_index("rx"), n_x, axis=2).reshape(chunk, full_width)
+    part = lax.all_to_all(rolled, "ry", split_axis=1, concat_axis=0, tiled=True)
+    part = part.reshape(n_y, chunk, part.shape[1])
+    tokens = lax.all_gather(part, "col", axis=1, tiled=True)
+    tokens = tokens.reshape(-1, tokens.shape[-1])
+    partial = dot_pieces(tokens, pieces)
     product = lax.psum_scatter(partial, "ry", scatter_dimension=0, tiled=True)
     return jax.nn.gelu(product, approximate=True).astype(jnp.bfloat16)
 
@@ -61,6 +106,6 @@
     )
 
     def body(q_seq, k_seq, v_seq, resid, ln_gain, w_up):
-        return per_device(q_seq, k_seq, v_seq, resid, ln_gain, w_up)
+        return per_device(q_seq, k_seq, v_seq, resid, ln_gain, w_up, nx)
 
     return jax.shard_map(body, mesh=split, in_specs=placed, out_specs=P(rows, "col"), check_vma=False)

time: 194 us -> 144 us (0.74)
  waiting for transfers between devices: 143 us -> 84.9 us
  Pallas kernels: 0 us -> 7.63 us
  starting transfers between devices: 12.2 us -> 19 us
  matrix products: 5.42 us -> 0.49 us
  local copies, waits for them, and re-layouts: 6.52 us -> 3.86 us
    all_gather x2 -> x1, waiting for transfers between devices: 87.5 us -> 0.01 us  [per_device(): tokens = lax.all_gather(part, 'col', axis=1, tiled=True)]
    ppermute x0 -> x4, waiting for transfers between devices: none -> 36.4 us  [the longest x1 25 us: ring_pieces(): from_right = lax.ppermute(block, axis, to_left)]
    pallas_call x0 -> x1, Pallas kernels: none -> 7.63 us  [dot_pieces(): pl.pallas_call(pieces_kernel, grid=(m // tile,), in_specs=[pl.BlockSpec((...]
    reduce_scatter x1, waiting for transfers between devices: 43.1 us -> 35.6 us  [per_device(): product = lax.psum_scatter(partial, 'ry', scatter_dimension=0, tiled=True)]
    ppermute x0 -> x4, starting transfers between devices: none -> 6.68 us  [the longest x1 3.28 us: ring_pieces(): far_low = lax.ppermute(from_left[:, :half], axis, to_right)]
    dot_general x1 -> x0, matrix products: 4.93 us -> none  [per_device(): jnp.einsum('cytf,fu->yctu', tokens, w_group, preferred_element_type=jnp.f...]
  transfers between devices with their start and end apart: 5 -> 8, of which waited for: 5 -> 5; matrix products, arithmetic and copies ran while one was open for 2% -> 2% of each run, Pallas kernels for 0% -> 0%
where the time goes in v4:
time: 144 us; the launch traced here: 142 us
  waiting for transfers between devices  84.9 us (59%)
  starting transfers between devices  19 us (13%)
  between operations  13.6 us (9%)
  blocking collectives  10.2 us (7%)
  Pallas kernels  7.63 us (5%)
  local copies, waits for them, and re-layouts  3.86 us (3%)
  other arithmetic  2.59 us (2%)
    reduce_scatter x1, waiting for transfers between devices, per_device(): product = lax.psum_scatter(partial, 'ry', scatter_dimension=0, tiled=True)  35.6 us
    ppermute x1, waiting for transfers between devices, ring_pieces(): from_right = lax.ppermute(block, axis, to_left)  25 us
    ppermute x1, waiting for transfers between devices, ring_pieces(): far_high = lax.ppermute(from_right[:, half:], axis, to_left)  11.4 us
    all_to_all x1, blocking collectives, per_device(): part = lax.all_to_all(rolled, 'ry', split_axis=1, concat_axis=0, tiled=True)  10.2 us
    all_to_all x1, starting transfers between devices, per_device(): lax.all_to_all(resid, 'col', split_axis=0, concat_axis=1, tiled=True)  8.7 us
    all_to_all x1, waiting for transfers between devices, per_device(): lax.all_to_all(attended, 'col', split_axis=0, concat_axis=1, tiled=True)  8.19 us
    pallas_call x1, Pallas kernels, dot_pieces(): pl.pallas_call(pieces_kernel, grid=(m // tile,), in_specs=[pl.BlockSpec((...  7.63 us
    all_to_all x1, waiting for transfers between devices, per_device(): lax.all_to_all(resid, 'col', split_axis=0, concat_axis=1, tiled=True)  4.7 us
  transfers between devices with their start and end apart: 8, of which 5 were waited for; matrix products, arithmetic and copies ran while one was open for 2% of the time, Pallas kernels for 0%

profile of v4, /device:TPU:6, one launch (start us, length us, event | category | flops | bytes accessed | tf_op | source)
XLA Modules:
  0.0 142.2 jit_solution(9923411950639215733)
XLA Ops:
  6.5 8.7 %all-to-all-start = ((bf16[16,8,384]{2,1,0:T(8,128)(2,1)}), bf16[16,8,384]{2,1,0:T(8,128)(2,1)S(1)}, u32[]{:S(2)}, u32[]{:S(2)}) async-start(bf16[16,8,384]{2,1,0:T(8,128)(2,1)} %bitcast.23), calls=%async_computation | async-start | bytes 196608 | tf_op jit(solution)/shard_map/all_to_all | solution.py:72
  15.3 1.0 copy.11
  16.3 1.0 copy.12
  17.3 0.2 fusion.2
  17.6 0.1 copy.15
  17.8 0.3 fusion.4
  18.0 0.1 copy.18
  18.1 0.7 all_to_all.34
  18.9 4.7 %all-to-all-done = bf16[16,8,384]{2,1,0:T(8,128)(2,1)S(1)} async-done(((bf16[16,8,384]{2,1,0:T(8,128)(2,1)}), bf16[16,8,384]{2,1,0:T(8,128)(2,1)S(1)}, u32[]{:S(2)}, u32[]{:S(2)}) %all-to-all-start) | async-done | bytes 98336 | tf_op jit(solution)/shard_map/all_to_all | solution.py:72
  23.6 3.5 %all-to-all-start.1 = ((bf16[16,8,384]{2,1,0:T(8,128)(2,1)}), bf16[16,8,384]{2,1,0:T(8,128)(2,1)S(1)}, u32[]{:S(2)}, u32[]{:S(2)}) async-start(bf16[16,8,384]{2,1,0:T(8,128)(2,1)} %all_to_all.34), calls=%async_computation.1 | async-start | bytes 196608 | tf_op jit(solution)/shard_map/all_to_all | solution.py:74
  27.2 8.2 %all-to-all-done.1 = bf16[16,8,384]{2,1,0:T(8,128)(2,1)S(1)} async-done(((bf16[16,8,384]{2,1,0:T(8,128)(2,1)}), bf16[16,8,384]{2,1,0:T(8,128)(2,1)S(1)}, u32[]{:S(2)}, u32[]{:S(2)}) %all-to-all-start.1) | async-done | bytes 98336 | tf_op jit(solution)/shard_map/all_to_all | solution.py:74
  35.4 0.2 fusion.16
  35.6 0.1 multiply_convert_fusion
  35.7 10.2 %all_to_all.42 = bf16[8,4,1536]{2,0,1:T(8,128)(2,1)} all-to-all(bf16[8,4,1536]{2,0,1:T(8,128)(2,1)S(1)} %bitcast.20), channel_id=1, replica_groups=mesh['ry'=4,'rx'=4,'col'=16] {'ry'}, dimensions={1} | all-to-all | bytes 196608 | tf_op jit(solution)/shard_map/all_to_all | solution.py:85
  46.0 0.9 collective-permute-start
  46.9 2.4 %collective-permute-start.1 = (bf16[384,1536]{1,0:T(8,128)(2,1)S(1)}, bf16[384,1536]{1,0:T(8,128)(2,1)S(1)}, u32[]{:S(2)}, u32[]{:S(2)}) collective-permute-start(bf16[384,1536]{1,0:T(8,128)(2,1)S(1)} %copy-done.2), channel_id=1, source_target_pairs={{0,16},{16,32},{32,48},{48,0},{1,17},{17,33},{33,49},{49,1},{2,18}... | collective-permute-start | bytes 3538952 | tf_op jit(solution)/shard_map/ppermute | solution.py:34
  49.3 25.0 %collective-permute-done.w1_ref = bf16[384,1536]{1,0:T(8,128)(2,1)S(1)} collective-permute-done((bf16[384,1536]{1,0:T(8,128)(2,1)S(1)}, bf16[384,1536]{1,0:T(8,128)(2,1)S(1)}, u32[]{:S(2)}, u32[]{:S(2)}) %collective-permute-start) | collective-permute-done | bytes 1179680 | tf_op jit(solution)/shard_map/ppermute | solution.py:35
  74.3 0.1 collective-permute-start.3
  74.5 3.3 %collective-permute-start.2 = (bf16[384,768]{1,0:T(8,128)(2,1)S(1)}, bf16[384,768]{1,0:T(8,128)(2,1)S(1)}, u32[]{:S(2)}, u32[]{:S(2)}) collective-permute-start(bf16[384,768]{1,0:T(8,128)(2,1)S(1)} %slice.8), channel_id=1, source_target_pairs={{0,16},{16,32},{32,48},{48,0},{1,17},{17,33},{33,49},{49,1},{2,18}... | collective-permute-start | bytes 1769480 | tf_op jit(solution)/shard_map/ppermute | solution.py:37
  77.8 11.4 %collective-permute-done.3.w2hi_ref = bf16[384,768]{1,0:T(8,128)(2,1)} collective-permute-done((bf16[384,768]{1,0:T(8,128)(2,1)S(1)}, bf16[384,768]{1,0:T(8,128)(2,1)}, u32[]{:S(2)}, u32[]{:S(2)}) %collective-permute-start.3) | collective-permute-done | bytes 589856 | tf_op jit(solution)/shard_map/ppermute | solution.py:38
  89.2 0.8 copy-done.3
  90.0 7.6 %shard_map.64 = f32[512,1536]{1,0:T(8,128)} custom-call(bf16[512,1536]{1,0:T(8,128)(2,1)} %bitcast.17, bf16[384,1536]{1,0:T(8,128)(2,1)} %w0_ref.1, bf16[384,1536]{1,0:T(8,128)(2,1)} %copy-done, bf16[384,768]{1,0:T(8,128)(2,1)} %copy-done.3, bf16[384,768]{1,0:T(8,128)(2,1)} %collective-permute-done.3.w2hi_ref, bf16[384,1536]{1,0:T(8,128)(2,1)} %copy-done.1), custom_call_target="tpu_custom_call" | custom-call | flops 2415919104 | bytes 9437184 | tf_op jit(solution)/shard_map/pallas_call | solution.py:58
  97.6 35.6 %reduce-scatter.2.cloned.1.call-done = f32[128,1536]{1,0:T(8,128)} async-done(((f32[512,1536]{1,0:T(8,128)}), f32[128,1536]{1,0:T(8,128)}) %reduce-scatter.2.cloned.1.call-update) | async-done | bytes 786448 | tf_op jit(solution)/shard_map/reduce_scatter | solution.py:90
  133.2 2.1 %fusion.12 = bf16[128,1536]{1,0:T(8,128)(2,1)} fusion(f32[128,1536]{1,0:T(8,128)} %reduce-scatter.2.cloned.1.call-done), kind=kLoop, calls=%fused_computation.15 | loop fusion | flops 1769472 | bytes 1179648 | tf_op jit(solution)/shard_map/convert_element_type | solution.py:91
  (25 shorter events, 0.4 us)
Async XLA Ops:
  6.5 11.1 %copy-start.4 = (bf16[128,384]{1,0:T(8,128)(2,1)S(1)}, bf16[128,384]{1,0:T(8,128)(2,1)}, u32[]{:S(2)}) copy-start(bf16[128,384]{1,0:T(8,128)(2,1)} %param.8) | copy-start | bytes 294916
  6.5 17.0 %all-to-all-start = ((bf16[16,8,384]{2,1,0:T(8,128)(2,1)}), bf16[16,8,384]{2,1,0:T(8,128)(2,1)S(1)}, u32[]{:S(2)}, u32[]{:S(2)}) async-start(bf16[16,8,384]{2,1,0:T(8,128)(2,1)} %bitcast.23), calls=%async_computation | async-start | bytes 196608 | tf_op jit(solution)/shard_map/all_to_all | solution.py:72
  17.3 9.8 %copy-start.5 = (f32[6144]{0:T(1024)S(1)}, f32[6144]{0:T(1024)}, u32[]{:S(2)}) copy-start(f32[6144]{0:T(1024)} %param.10) | copy-start | bytes 73732
  18.0 28.0 %copy-start.2 = (bf16[384,1536]{1,0:T(8,128)(2,1)S(1)}, bf16[384,1536]{1,0:T(8,128)(2,1)}, u32[]{:S(2)}) copy-start(bf16[384,1536]{1,0:T(8,128)(2,1)} %w0_ref.1) | copy-start | bytes 3538948
  23.6 11.8 %all-to-all-start.1 = ((bf16[16,8,384]{2,1,0:T(8,128)(2,1)}), bf16[16,8,384]{2,1,0:T(8,128)(2,1)S(1)}, u32[]{:S(2)}, u32[]{:S(2)}) async-start(bf16[16,8,384]{2,1,0:T(8,128)(2,1)} %all_to_all.34), calls=%async_computation.1 | async-start | bytes 196608 | tf_op jit(solution)/shard_map/all_to_all | solution.py:74
  27.1 62.1 %all-gather.2.cloned.1.call-start = ((), (), s32[]{:S(2)}) async-start(), calls=%async_computation.4 | async-start | bytes 1671168 | tf_op jit(solution)/shard_map/all_gather | solution.py:87
  45.9 87.3 %reduce-scatter.2.cloned.1.call-start = ((), (), s32[]{:S(2)}) async-start(), calls=%async_computation.5 | async-start | bytes 3932160 | tf_op jit(solution)/shard_map/reduce_scatter | solution.py:90
  46.0 28.3 %collective-permute-start = (bf16[384,1536]{1,0:T(8,128)(2,1)S(1)}, bf16[384,1536]{1,0:T(8,128)(2,1)S(1)}, u32[]{:S(2)}, u32[]{:S(2)}) collective-permute-start(bf16[384,1536]{1,0:T(8,128)(2,1)S(1)} %copy-done.2), channel_id=1, source_target_pairs={{0,48},{16,0},{32,16},{48,32},{1,49},{17,1},{33,17},{49,33},{2,50}... | collective-permute-start | bytes 3538952 | tf_op jit(solution)/shard_map/ppermute | solution.py:35
  46.9 27.5 %collective-permute-start.1 = (bf16[384,1536]{1,0:T(8,128)(2,1)S(1)}, bf16[384,1536]{1,0:T(8,128)(2,1)S(1)}, u32[]{:S(2)}, u32[]{:S(2)}) collective-permute-start(bf16[384,1536]{1,0:T(8,128)(2,1)S(1)} %copy-done.2), channel_id=1, source_target_pairs={{0,16},{16,32},{32,48},{48,0},{1,17},{17,33},{33,49},{49,1},{2,18}... | collective-permute-start | bytes 3538952 | tf_op jit(solution)/shard_map/ppermute | solution.py:34
  74.3 14.9 %copy-start = (bf16[384,1536]{1,0:T(8,128)(2,1)}, bf16[384,1536]{1,0:T(8,128)(2,1)S(1)}, u32[]{:S(2)}) copy-start(bf16[384,1536]{1,0:T(8,128)(2,1)S(1)} %collective-permute-done.w1_ref) | copy-start | bytes 3538948
  74.3 14.8 %collective-permute-start.3 = (bf16[384,768]{1,0:T(8,128)(2,1)S(1)}, bf16[384,768]{1,0:T(8,128)(2,1)}, u32[]{:S(2)}, u32[]{:S(2)}) collective-permute-start(bf16[384,768]{1,0:T(8,128)(2,1)S(1)} %slice.9), channel_id=1, source_target_pairs={{0,48},{16,0},{32,16},{48,32},{1,49},{17,1},{33,17},{49,33},{2,50}... | collective-permute-start | bytes 1769480 | tf_op jit(solution)/shard_map/ppermute | solution.py:38
  74.4 14.7 %copy-start.1 = (bf16[384,1536]{1,0:T(8,128)(2,1)}, bf16[384,1536]{1,0:T(8,128)(2,1)S(1)}, u32[]{:S(2)}) copy-start(bf16[384,1536]{1,0:T(8,128)(2,1)S(1)} %collective-permute-done.1.w3_ref) | copy-start | bytes 3538948
  74.5 14.7 %collective-permute-start.2 = (bf16[384,768]{1,0:T(8,128)(2,1)S(1)}, bf16[384,768]{1,0:T(8,128)(2,1)S(1)}, u32[]{:S(2)}, u32[]{:S(2)}) collective-permute-start(bf16[384,768]{1,0:T(8,128)(2,1)S(1)} %slice.8), channel_id=1, source_target_pairs={{0,16},{16,32},{32,48},{48,0},{1,17},{17,33},{33,49},{49,1},{2,18}... | collective-permute-start | bytes 1769480 | tf_op jit(solution)/shard_map/ppermute | solution.py:37
  89.2 0.8 copy-start.3
Sparse Core Ops, SparseCore 0:
  46.1 34.2 all-gather.1
  97.7 35.4 reduce-scatter.1

commit v5 on v4

--- a/solution.py
+++ b/solution.py
@@ -27,12 +27,19 @@
     return output.astype(jnp.bfloat16).reshape(seq, width)
 
 
-def ring_pieces(block, axis):
+def ring_first(block, axis, anchor):
     n = 4
     to_right = [(i, (i + 1) % n) for i in range(n)]
     to_left = [(i, (i - 1) % n) for i in range(n)]
     from_left = lax.ppermute(block, axis, to_right)
     from_right = lax.ppermute(block, axis, to_left)
+    return lax.optimization_barrier((from_left, from_right, anchor))
+
+
+def ring_second(block, from_left, from_right, axis):
+    n = 4
+    to_right = [(i, (i + 1) % n) for i in range(n)]
+    to_left = [(i, (i - 1) % n) for i in range(n)]
     half = block.shape[1] // 2
     far_low = lax.ppermute(from_left[:, :half], axis, to_right)
     far_high = lax.ppermute(from_right[:, half:], axis, to_left)
@@ -68,15 +75,20 @@
 
 
 def per_device(q_seq, k_seq, v_seq, resid, ln_gain, w_up, n_x):
-    pieces = ring_pieces(w_up, "rx")
     res_tokens = lax.all_to_all(resid, "col", split_axis=0, concat_axis=1, tiled=True)
     attended = attention_block(q_seq, k_seq, v_seq)
+    rows = w_up.shape[0] // 2
+    left_a, right_a, attended = ring_first(w_up[:rows], "rx", attended)
     att_tokens = lax.all_to_all(attended, "col", split_axis=0, concat_axis=1, tiled=True)
     stream = res_tokens.astype(jnp.float32) + att_tokens.astype(jnp.float32)
     full_width = stream.shape[1]
     mean = jnp.sum(stream, axis=1, keepdims=True) / full_width
     spread = jnp.sum(stream * stream, axis=1, keepdims=True) / full_width - mean * mean
     normed = ((stream - mean) * lax.rsqrt(spread + 1e-05) * ln_gain[None, :]).astype(jnp.bfloat16)
+    left_b, right_b, normed = ring_first(w_up[rows:], "rx", normed)
+    from_left = jnp.concatenate([left_a, left_b], axis=0)
+    from_right = jnp.concatenate([right_a, right_b], axis=0)
+    pieces = ring_second(w_up, from_left, from_right, "rx")
     chunk, block = normed.shape[0], w_up.shape[0]
     n_y = full_width // (n_x * block)
     grouped = normed.reshape(chunk, n_y, n_x, block)

time: 144 us -> 157 us (1.090)
  waiting for transfers between devices: 84.9 us -> 94 us
  starting transfers between devices: 19 us -> 24.8 us
    all_gather x1, waiting for transfers between devices: 0.01 us -> 23.6 us  [per_device(): tokens = lax.all_gather(part, 'col', axis=1, tiled=True)]
    ppermute x4 -> x6, waiting for transfers between devices: 36.4 us -> 22.6 us  [the longest x2 11.9 us: ring_first(): from_right = lax.ppermute(block, axis, to_left)]
    reduce_scatter x1, waiting for transfers between devices: 35.6 us -> 39.8 us  [per_device(): product = lax.psum_scatter(partial, 'ry', scatter_dimension=0, tiled=True)]
    ppermute x4 -> x6, starting transfers between devices: 6.68 us -> 10.7 us  [the longest x2 5.63 us: ring_first(): from_left = lax.ppermute(block, axis, to_right)]
    all_to_all x1, waiting for transfers between devices: 8.19 us -> 4.95 us  [per_device(): lax.all_to_all(attended, 'col', split_axis=0, concat_axis=1, tiled=True)]
    unnamed x15 -> x21, local copies, waits for them, and re-layouts: 2.95 us -> 0.48 us
    all_to_all x1, starting transfers between devices: 3.51 us -> 5.48 us  [per_device(): lax.all_to_all(attended, 'col', split_axis=0, concat_axis=1, tiled=True)]
    all_to_all x1, waiting for transfers between devices: 4.7 us -> 3.09 us  [per_device(): lax.all_to_all(resid, 'col', split_axis=0, concat_axis=1, tiled=True)]
  transfers between devices with their start and end apart: 8 -> 10, of which waited for: 5 -> 8; matrix products, arithmetic and copies ran while one was open for 2% -> 1% of each run, Pallas kernels for 0% -> 0%
where the time goes in v5:
time: 157 us; the launch traced here: 156 us
  waiting for transfers between devices  94 us (60%)
  starting transfers between devices  24.8 us (16%)
  between operations  13.6 us (9%)
  blocking collectives  10.2 us (6%)
  Pallas kernels  7.65 us (5%)
  local copies, waits for them, and re-layouts  2.75 us (2%)
  other arithmetic  2.57 us (2%)
    reduce_scatter x1, waiting for transfers between devices, per_device(): product = lax.psum_scatter(partial, 'ry', scatter_dimension=0, tiled=True)  39.8 us
    all_gather x1, waiting for transfers between devices, per_device(): tokens = lax.all_gather(part, 'col', axis=1, tiled=True)  23.6 us
    ppermute x2, waiting for transfers between devices, ring_first(): from_right = lax.ppermute(block, axis, to_left)  11.9 us
    ppermute x1, waiting for transfers between devices, ring_second(): far_high = lax.ppermute(from_right[:, half:], axis, to_left)  10.6 us
    all_to_all x1, blocking collectives, per_device(): part = lax.all_to_all(rolled, 'ry', split_axis=1, concat_axis=0, tiled=True)  10.2 us
    all_to_all x1, starting transfers between devices, per_device(): lax.all_to_all(resid, 'col', split_axis=0, concat_axis=1, tiled=True)  8.57 us
    pallas_call x1, Pallas kernels, dot_pieces(): pl.pallas_call(pieces_kernel, grid=(m // tile,), in_specs=[pl.BlockSpec((...  7.65 us
    ppermute x2, starting transfers between devices, ring_first(): from_left = lax.ppermute(block, axis, to_right)  5.63 us
  transfers between devices with their start and end apart: 10, of which 8 were waited for; matrix products, arithmetic and copies ran while one was open for 1% of the time, Pallas kernels for 0%

profile of v5, /device:TPU:6, one launch (start us, length us, event | category | flops | bytes accessed | tf_op | source)
XLA Modules:
  0.0 156.0 jit_solution(8249167375887808175)
XLA Ops:
  6.5 1.4 fusion.16
  7.9 0.9 collective-permute-start.3
  8.8 2.4 %collective-permute-start.2 = (bf16[192,1536]{1,0:T(8,128)(2,1)S(1)}, bf16[192,1536]{1,0:T(8,128)(2,1)S(1)}, u32[]{:S(2)}, u32[]{:S(2)}) collective-permute-start(bf16[192,1536]{1,0:T(8,128)(2,1)S(1)} %get-tuple-element.19), channel_id=1, source_target_pairs={{0,16},{16,32},{32,48},{48,0},{1,17},{17,33},{33,49},{49,1},{2,18}... | collective-permute-start | bytes 1769480 | tf_op jit(solution)/shard_map/ppermute | solution.py:34
  11.2 8.6 %all-to-all-start = ((bf16[16,8,384]{2,1,0:T(8,128)(2,1)}), bf16[16,8,384]{2,1,0:T(8,128)(2,1)S(1)}, u32[]{:S(2)}, u32[]{:S(2)}) async-start(bf16[16,8,384]{2,1,0:T(8,128)(2,1)} %bitcast), calls=%async_computation | async-start | bytes 196608 | tf_op jit(solution)/shard_map/all_to_all | solution.py:78
  19.8 0.1 copy.12
  20.2 0.2 fusion.2
  20.6 0.2 convolution_convert_fusion
  20.8 3.5 %collective-permute-done.3 = bf16[192,1536]{1,0:T(8,128)(2,1)S(1)} collective-permute-done((bf16[192,1536]{1,0:T(8,128)(2,1)S(1)}, bf16[192,1536]{1,0:T(8,128)(2,1)S(1)}, u32[]{:S(2)}, u32[]{:S(2)}) %collective-permute-start.3) | collective-permute-done | bytes 589856 | tf_op jit(solution)/shard_map/ppermute | solution.py:35
  24.3 0.8 copy.18
  25.0 3.1 %all-to-all-done = bf16[16,8,384]{2,1,0:T(8,128)(2,1)S(1)} async-done(((bf16[16,8,384]{2,1,0:T(8,128)(2,1)}), bf16[16,8,384]{2,1,0:T(8,128)(2,1)S(1)}, u32[]{:S(2)}, u32[]{:S(2)}) %all-to-all-start) | async-done | bytes 98336 | tf_op jit(solution)/shard_map/all_to_all | solution.py:78
  28.1 5.5 %all-to-all-start.1 = ((bf16[16,8,384]{2,1,0:T(8,128)(2,1)}), bf16[16,8,384]{2,1,0:T(8,128)(2,1)S(1)}, u32[]{:S(2)}, u32[]{:S(2)}) async-start(bf16[16,8,384]{2,1,0:T(8,128)(2,1)} %bitcast.6), calls=%async_computation.1 | async-start | bytes 196608 | tf_op jit(solution)/shard_map/all_to_all | solution.py:82
  33.7 3.2 %collective-permute-start = (bf16[192,1536]{1,0:T(8,128)(2,1)S(1)}, bf16[192,1536]{1,0:T(8,128)(2,1)S(1)}, u32[]{:S(2)}, u32[]{:S(2)}) collective-permute-start(bf16[192,1536]{1,0:T(8,128)(2,1)S(1)} %get-tuple-element.20), channel_id=1, source_target_pairs={{0,16},{16,32},{32,48},{48,0},{1,17},{17,33},{33,49},{49,1},{2,18}... | collective-permute-start | bytes 1769480 | tf_op jit(solution)/shard_map/ppermute | solution.py:34
  37.0 5.0 %all-to-all-done.1 = bf16[16,8,384]{2,1,0:T(8,128)(2,1)S(1)} async-done(((bf16[16,8,384]{2,1,0:T(8,128)(2,1)}), bf16[16,8,384]{2,1,0:T(8,128)(2,1)S(1)}, u32[]{:S(2)}, u32[]{:S(2)}) %all-to-all-start.1) | async-done | bytes 98336 | tf_op jit(solution)/shard_map/all_to_all | solution.py:82
  41.9 0.2 fusion.15
  42.2 8.4 %collective-permute-done.1 = bf16[192,1536]{1,0:T(8,128)(2,1)S(1)} collective-permute-done((bf16[192,1536]{1,0:T(8,128)(2,1)S(1)}, bf16[192,1536]{1,0:T(8,128)(2,1)S(1)}, u32[]{:S(2)}, u32[]{:S(2)}) %collective-permute-start.1) | collective-permute-done | bytes 589856 | tf_op jit(solution)/shard_map/ppermute | solution.py:35
  50.7 10.2 %all_to_all.42 = bf16[8,4,1536]{2,0,1:T(8,128)(2,1)} all-to-all(bf16[8,4,1536]{2,0,1:T(8,128)(2,1)S(1)} %bitcast.23), channel_id=1, replica_groups=mesh['ry'=4,'rx'=4,'col'=16] {'ry'}, dimensions={1} | all-to-all | bytes 196608 | tf_op jit(solution)/shard_map/all_to_all | solution.py:97
  61.1 1.2 collective-permute-start.5
  62.4 2.8 %collective-permute-start.4 = (bf16[384,768]{1,0:T(8,128)(2,1)S(1)}, bf16[384,768]{1,0:T(8,128)(2,1)S(1)}, u32[]{:S(2)}, u32[]{:S(2)}) collective-permute-start(bf16[384,768]{1,0:T(8,128)(2,1)S(1)} %slice.16), channel_id=1, source_target_pairs={{0,16},{16,32},{32,48},{48,0},{1,17},{17,33},{33,49},{49,1},{2,18}... | collective-permute-start | bytes 1769480 | tf_op jit(solution)/shard_map/ppermute | solution.py:44
  65.3 10.6 %collective-permute-done.5.w2hi_ref = bf16[384,768]{1,0:T(8,128)(2,1)S(1)} collective-permute-done((bf16[384,768]{1,0:T(8,128)(2,1)S(1)}, bf16[384,768]{1,0:T(8,128)(2,1)S(1)}, u32[]{:S(2)}, u32[]{:S(2)}) %collective-permute-start.5) | collective-permute-done | bytes 589856 | tf_op jit(solution)/shard_map/ppermute | solution.py:45
  75.8 0.1 collective-permute-done.4.w2lo_ref
  76.0 23.6 %all-gather.2.cloned.1.call-done = bf16[4,128,1536]{2,1,0:T(8,128)(2,1)} async-done(((bf16[4,8,1536]{2,1,0:T(8,128)(2,1)}), bf16[4,128,1536]{2,1,0:T(8,128)(2,1)}) %all-gather.2.cloned.1.call-update) | async-done | bytes 1572880 | tf_op jit(solution)/shard_map/all_gather | solution.py:99
  99.6 7.6 %shard_map.64 = f32[512,1536]{1,0:T(8,128)} custom-call(bf16[512,1536]{1,0:T(8,128)(2,1)} %bitcast.20, bf16[384,1536]{1,0:T(8,128)(2,1)} %w0_ref.1, bf16[384,1536]{1,0:T(8,128)(2,1)} %copy-done.1, bf16[384,768]{1,0:T(8,128)(2,1)} %copy-done.3, bf16[384,768]{1,0:T(8,128)(2,1)} %copy-done.2, bf16[384,1536]{1,0:T(8,128)(2,1)} %copy-done), custom_call_target="tpu_custom_call" | custom-call | flops 2415919104 | bytes 9437184 | tf_op jit(solution)/shard_map/pallas_call | solution.py:65
  107.3 39.8 %reduce-scatter.2.cloned.1.call-done = f32[128,1536]{1,0:T(8,128)} async-done(((f32[512,1536]{1,0:T(8,128)}), f32[128,1536]{1,0:T(8,128)}) %reduce-scatter.2.cloned.1.call-update) | async-done | bytes 786448 | tf_op jit(solution)/shard_map/reduce_scatter | solution.py:102
  147.0 2.1 %fusion.11 = bf16[128,1536]{1,0:T(8,128)(2,1)} fusion(f32[128,1536]{1,0:T(8,128)} %reduce-scatter.2.cloned.1.call-done), kind=kLoop, calls=%fused_computation.14 | loop fusion | flops 1769472 | bytes 1179648 | tf_op jit(solution)/shard_map/convert_element_type | solution.py:103
  (36 shorter events, 1.0 us)
Async XLA Ops:
  6.5 13.3 %copy-start.4 = (bf16[128,384]{1,0:T(8,128)(2,1)S(1)}, bf16[128,384]{1,0:T(8,128)(2,1)}, u32[]{:S(2)}) copy-start(bf16[128,384]{1,0:T(8,128)(2,1)} %param.6) | copy-start | bytes 294916
  6.5 13.4 %copy-start.5 = (bf16[128,384]{1,0:T(8,128)(2,1)S(1)}, bf16[128,384]{1,0:T(8,128)(2,1)}, u32[]{:S(2)}) copy-start(bf16[128,384]{1,0:T(8,128)(2,1)} %param.7) | copy-start | bytes 294916
  6.5 13.6 %copy-start.6 = (bf16[128,384]{1,0:T(8,128)(2,1)S(1)}, bf16[128,384]{1,0:T(8,128)(2,1)}, u32[]{:S(2)}) copy-start(bf16[128,384]{1,0:T(8,128)(2,1)} %param.8) | copy-start | bytes 294916
  7.9 16.4 %collective-permute-start.3 = (bf16[192,1536]{1,0:T(8,128)(2,1)S(1)}, bf16[192,1536]{1,0:T(8,128)(2,1)S(1)}, u32[]{:S(2)}, u32[]{:S(2)}) collective-permute-start(bf16[192,1536]{1,0:T(8,128)(2,1)S(1)} %get-tuple-element.19), channel_id=1, source_target_pairs={{0,48},{16,0},{32,16},{48,32},{1,49},{17,1},{33,17},{49,33},{2,50}... | collective-permute-start | bytes 1769480 | tf_op jit(solution)/shard_map/ppermute | solution.py:35
  8.8 15.5 %collective-permute-start.2 = (bf16[192,1536]{1,0:T(8,128)(2,1)S(1)}, bf16[192,1536]{1,0:T(8,128)(2,1)S(1)}, u32[]{:S(2)}, u32[]{:S(2)}) collective-permute-start(bf16[192,1536]{1,0:T(8,128)(2,1)S(1)} %get-tuple-element.19), channel_id=1, source_target_pairs={{0,16},{16,32},{32,48},{48,0},{1,17},{17,33},{33,49},{49,1},{2,18}... | collective-permute-start | bytes 1769480 | tf_op jit(solution)/shard_map/ppermute | solution.py:34
  11.2 16.9 %all-to-all-start = ((bf16[16,8,384]{2,1,0:T(8,128)(2,1)}), bf16[16,8,384]{2,1,0:T(8,128)(2,1)S(1)}, u32[]{:S(2)}, u32[]{:S(2)}) async-start(bf16[16,8,384]{2,1,0:T(8,128)(2,1)} %bitcast), calls=%async_computation | async-start | bytes 196608 | tf_op jit(solution)/shard_map/all_to_all | solution.py:78
  20.2 21.9 %copy-start.7 = (f32[6144]{0:T(1024)S(1)}, f32[6144]{0:T(1024)}, u32[]{:S(2)}) copy-start(f32[6144]{0:T(1024)} %param.10) | copy-start | bytes 73732
  28.1 13.8 %all-to-all-start.1 = ((bf16[16,8,384]{2,1,0:T(8,128)(2,1)}), bf16[16,8,384]{2,1,0:T(8,128)(2,1)S(1)}, u32[]{:S(2)}, u32[]{:S(2)}) async-start(bf16[16,8,384]{2,1,0:T(8,128)(2,1)} %bitcast.6), calls=%async_computation.1 | async-start | bytes 196608 | tf_op jit(solution)/shard_map/all_to_all | solution.py:82
  33.6 66.0 %all-gather.2.cloned.1.call-start = ((), (), s32[]{:S(2)}) async-start(), calls=%async_computation.4 | async-start | bytes 1671168 | tf_op jit(solution)/shard_map/all_gather | solution.py:99
  33.6 16.9 %collective-permute-start.1 = (bf16[192,1536]{1,0:T(8,128)(2,1)S(1)}, bf16[192,1536]{1,0:T(8,128)(2,1)S(1)}, u32[]{:S(2)}, u32[]{:S(2)}) collective-permute-start(bf16[192,1536]{1,0:T(8,128)(2,1)S(1)} %get-tuple-element.20), channel_id=1, source_target_pairs={{0,48},{16,0},{32,16},{48,32},{1,49},{17,1},{33,17},{49,33},{2,50}... | collective-permute-start | bytes 1769480 | tf_op jit(solution)/shard_map/ppermute | solution.py:35
  33.7 16.9 %collective-permute-start = (bf16[192,1536]{1,0:T(8,128)(2,1)S(1)}, bf16[192,1536]{1,0:T(8,128)(2,1)S(1)}, u32[]{:S(2)}, u32[]{:S(2)}) collective-permute-start(bf16[192,1536]{1,0:T(8,128)(2,1)S(1)} %get-tuple-element.20), channel_id=1, source_target_pairs={{0,16},{16,32},{32,48},{48,0},{1,17},{17,33},{33,49},{49,1},{2,18}... | collective-permute-start | bytes 1769480 | tf_op jit(solution)/shard_map/ppermute | solution.py:34
  60.9 86.2 %reduce-scatter.2.cloned.1.call-start = ((), (), s32[]{:S(2)}) async-start(), calls=%async_computation.5 | async-start | bytes 3932160 | tf_op jit(solution)/shard_map/reduce_scatter | solution.py:102
  61.0 1.3 copy-start.1
  61.1 14.7 %collective-permute-start.5 = (bf16[384,768]{1,0:T(8,128)(2,1)S(1)}, bf16[384,768]{1,0:T(8,128)(2,1)S(1)}, u32[]{:S(2)}, u32[]{:S(2)}) collective-permute-start(bf16[384,768]{1,0:T(8,128)(2,1)S(1)} %slice.17), channel_id=1, source_target_pairs={{0,48},{16,0},{32,16},{48,32},{1,49},{17,1},{33,17},{49,33},{2,50}... | collective-permute-start | bytes 1769480 | tf_op jit(solution)/shard_map/ppermute | solution.py:45
  62.4 37.2 %copy-start = (bf16[384,1536]{1,0:T(8,128)(2,1)}, bf16[384,1536]{1,0:T(8,128)(2,1)S(1)}, u32[]{:S(2)}) copy-start(bf16[384,1536]{1,0:T(8,128)(2,1)S(1)} %constant_dynamic-update-slice_fusion.2.w3_ref) | copy-start | bytes 3538948
  62.4 13.5 %collective-permute-start.4 = (bf16[384,768]{1,0:T(8,128)(2,1)S(1)}, bf16[384,768]{1,0:T(8,128)(2,1)S(1)}, u32[]{:S(2)}, u32[]{:S(2)}) collective-permute-start(bf16[384,768]{1,0:T(8,128)(2,1)S(1)} %slice.16), channel_id=1, source_target_pairs={{0,16},{16,32},{32,48},{48,0},{1,17},{17,33},{33,49},{49,1},{2,18}... | collective-permute-start | bytes 1769480 | tf_op jit(solution)/shard_map/ppermute | solution.py:44
  75.8 23.7 %copy-start.2 = (bf16[384,768]{1,0:T(8,128)(2,1)}, bf16[384,768]{1,0:T(8,128)(2,1)S(1)}, u32[]{:S(2)}) copy-start(bf16[384,768]{1,0:T(8,128)(2,1)S(1)} %collective-permute-done.5.w2hi_ref) | copy-start | bytes 1769476
  76.0 23.6 %copy-start.3 = (bf16[384,768]{1,0:T(8,128)(2,1)}, bf16[384,768]{1,0:T(8,128)(2,1)S(1)}, u32[]{:S(2)}) copy-start(bf16[384,768]{1,0:T(8,128)(2,1)S(1)} %collective-permute-done.4.w2lo_ref) | copy-start | bytes 1769476
Sparse Core Ops, SparseCore 0:
  61.0 38.5 all-gather.1
  107.4 39.6 reduce-scatter.1

commit v6 on v4

--- a/solution.py
+++ b/solution.py
@@ -69,15 +69,17 @@
 
 def per_device(q_seq, k_seq, v_seq, resid, ln_gain, w_up, n_x):
     pieces = ring_pieces(w_up, "rx")
-    res_tokens = lax.all_to_all(resid, "col", split_axis=0, concat_axis=1, tiled=True)
     attended = attention_block(q_seq, k_seq, v_seq)
-    att_tokens = lax.all_to_all(attended, "col", split_axis=0, concat_axis=1, tiled=True)
-    stream = res_tokens.astype(jnp.float32) + att_tokens.astype(jnp.float32)
+    both = jnp.stack([resid, attended], axis=1)
+    both = lax.all_to_all(both, "col", split_axis=0, concat_axis=1, tiled=True)
+    chunk = both.shape[0]
+    both = both.reshape(chunk, -1, 2, resid.shape[1])
+    stream = (both[:, :, 0].astype(jnp.float32) + both[:, :, 1].astype(jnp.float32)).reshape(chunk, -1)
     full_width = stream.shape[1]
     mean = jnp.sum(stream, axis=1, keepdims=True) / full_width
     spread = jnp.sum(stream * stream, axis=1, keepdims=True) / full_width - mean * mean
     normed = ((stream - mean) * lax.rsqrt(spread + 1e-05) * ln_gain[None, :]).astype(jnp.bfloat16)
-    chunk, block = normed.shape[0], w_up.shape[0]
+    block = w_up.shape[0]
     n_y = full_width // (n_x * block)
     grouped = normed.reshape(chunk, n_y, n_x, block)
     doubled = jnp.concatenate([grouped, grouped], axis=2)

time: 144 us -> 139 us (0.965)
  starting transfers between devices: 19 us -> 14.6 us
  waiting for transfers between devices: 84.9 us -> 82 us
  local copies, waits for them, and re-layouts: 3.86 us -> 6.01 us
    all_to_all x2 -> x1, starting transfers between devices: 12.2 us -> 8.7 us  [per_device(): both = lax.all_to_all(both, 'col', split_axis=0, concat_axis=1, tiled=True)]
    all_to_all x2 -> x1, waiting for transfers between devices: 12.9 us -> 9.87 us  [per_device(): both = lax.all_to_all(both, 'col', split_axis=0, concat_axis=1, tiled=True)]
    unnamed x15 -> x18, local copies, waits for them, and re-layouts: 2.95 us -> 4.92 us
  transfers between devices with their start and end apart: 8 -> 7, of which waited for: 5 -> 4; matrix products, arithmetic and copies ran while one was open for 2% -> 0% of each run, Pallas kernels for 0% -> 0%
where the time goes in v6:
time: 139 us; the launch traced here: 138 us
  waiting for transfers between devices  82 us (59%)
  starting transfers between devices  14.6 us (11%)
  between operations  13.6 us (10%)
  blocking collectives  10.2 us (7%)
  Pallas kernels  7.64 us (5%)
  local copies, waits for them, and re-layouts  6.01 us (4%)
  other arithmetic  3.01 us (2%)
    reduce_scatter x1, waiting for transfers between devices, per_device(): product = lax.psum_scatter(partial, 'ry', scatter_dimension=0, tiled=True)  35.3 us
    ppermute x1, waiting for transfers between devices, ring_pieces(): from_right = lax.ppermute(block, axis, to_left)  25.3 us
    ppermute x1, waiting for transfers between devices, ring_pieces(): far_high = lax.ppermute(from_right[:, half:], axis, to_left)  11.6 us
    all_to_all x1, blocking collectives, per_device(): part = lax.all_to_all(rolled, 'ry', split_axis=1, concat_axis=0, tiled=True)  10.2 us
    all_to_all x1, waiting for transfers between devices, per_device(): both = lax.all_to_all(both, 'col', split_axis=0, concat_axis=1, tiled=True)  9.87 us
    all_to_all x1, starting transfers between devices, per_device(): both = lax.all_to_all(both, 'col', split_axis=0, concat_axis=1, tiled=True)  8.7 us
    pallas_call x1, Pallas kernels, dot_pieces(): pl.pallas_call(pieces_kernel, grid=(m // tile,), in_specs=[pl.BlockSpec((...  7.64 us
    unnamed x18, local copies, waits for them, and re-layouts  4.92 us
  transfers between devices with their start and end apart: 7, of which 4 were waited for; matrix products, arithmetic and copies ran while one was open for 0% of the time, Pallas kernels for 0%

profile of v6, /device:TPU:6, one launch (start us, length us, event | category | flops | bytes accessed | tf_op | source)
XLA Modules:
  0.0 137.6 jit_solution(9615862242598361863)
XLA Ops:
  6.6 1.0 copy.26
  7.6 1.0 copy.27
  8.6 0.2 fusion.2
  8.9 1.0 copy.30
  10.0 0.2 convolution_convert_fusion
  10.2 0.1 copy.32
  10.3 0.9 copy.33
  11.2 8.7 %all-to-all-start = ((bf16[128,2,384]{2,1,0:T(2,128)(2,1)}), bf16[128,2,384]{2,1,0:T(2,128)(2,1)S(1)}, u32[]{:S(2)}, u32[]{:S(2)}) async-start(bf16[128,2,384]{2,1,0:T(2,128)(2,1)} %copy.33), calls=%async_computation | async-start | bytes 393216 | tf_op jit(solution)/shard_map/all_to_all | solution.py:74
  20.0 9.9 %all-to-all-done = bf16[128,2,384]{2,1,0:T(2,128)(2,1)S(1)} async-done(((bf16[128,2,384]{2,1,0:T(2,128)(2,1)}), bf16[128,2,384]{2,1,0:T(2,128)(2,1)S(1)}, u32[]{:S(2)}, u32[]{:S(2)}) %all-to-all-start) | async-done | bytes 196640 | tf_op jit(solution)/shard_map/all_to_all | solution.py:74
  29.9 0.6 fusion.19
  30.5 0.1 fusion.15
  30.7 10.2 %all_to_all.31 = bf16[8,4,1536]{2,0,1:T(8,128)(2,1)} all-to-all(bf16[8,4,1536]{2,0,1:T(8,128)(2,1)S(1)} %bitcast.31), channel_id=1, replica_groups=mesh['ry'=4,'rx'=4,'col'=16] {'ry'}, dimensions={1} | all-to-all | bytes 196608 | tf_op jit(solution)/shard_map/all_to_all | solution.py:87
  41.0 0.9 collective-permute-start
  41.9 2.4 %collective-permute-start.1 = (bf16[384,1536]{1,0:T(8,128)(2,1)S(1)}, bf16[384,1536]{1,0:T(8,128)(2,1)S(1)}, u32[]{:S(2)}, u32[]{:S(2)}) collective-permute-start(bf16[384,1536]{1,0:T(8,128)(2,1)S(1)} %copy-done.2), channel_id=1, source_target_pairs={{0,16},{16,32},{32,48},{48,0},{1,17},{17,33},{33,49},{49,1},{2,18}... | collective-permute-start | bytes 3538952 | tf_op jit(solution)/shard_map/ppermute | solution.py:34
  44.3 25.3 %collective-permute-done.w1_ref = bf16[384,1536]{1,0:T(8,128)(2,1)S(1)} collective-permute-done((bf16[384,1536]{1,0:T(8,128)(2,1)S(1)}, bf16[384,1536]{1,0:T(8,128)(2,1)S(1)}, u32[]{:S(2)}, u32[]{:S(2)}) %collective-permute-start) | collective-permute-done | bytes 1179680 | tf_op jit(solution)/shard_map/ppermute | solution.py:35
  69.6 0.1 collective-permute-start.3
  69.8 0.8 copy-done
  70.6 2.4 %collective-permute-start.2 = (bf16[384,768]{1,0:T(8,128)(2,1)S(1)}, bf16[384,768]{1,0:T(8,128)(2,1)S(1)}, u32[]{:S(2)}, u32[]{:S(2)}) collective-permute-start(bf16[384,768]{1,0:T(8,128)(2,1)S(1)} %slice.18), channel_id=1, source_target_pairs={{0,16},{16,32},{32,48},{48,0},{1,17},{17,33},{33,49},{49,1},{2,18}... | collective-permute-start | bytes 1769480 | tf_op jit(solution)/shard_map/ppermute | solution.py:37
  73.1 11.6 %collective-permute-done.3.w2hi_ref = bf16[384,768]{1,0:T(8,128)(2,1)S(1)} collective-permute-done((bf16[384,768]{1,0:T(8,128)(2,1)S(1)}, bf16[384,768]{1,0:T(8,128)(2,1)S(1)}, u32[]{:S(2)}, u32[]{:S(2)}) %collective-permute-start.3) | collective-permute-done | bytes 589856 | tf_op jit(solution)/shard_map/ppermute | solution.py:38
  84.7 0.8 copy-done.3
  85.5 0.2 copy-done.4
  85.7 7.6 %shard_map.64 = f32[512,1536]{1,0:T(8,128)} custom-call(bf16[512,1536]{1,0:T(8,128)(2,1)} %bitcast.28, bf16[384,1536]{1,0:T(8,128)(2,1)} %w0_ref.1, bf16[384,1536]{1,0:T(8,128)(2,1)} %copy-done, bf16[384,768]{1,0:T(8,128)(2,1)} %copy-done.4, bf16[384,768]{1,0:T(8,128)(2,1)} %copy-done.3, bf16[384,1536]{1,0:T(8,128)(2,1)} %copy-done.1), custom_call_target="tpu_custom_call" | custom-call | flops 2415919104 | bytes 9437184 | tf_op jit(solution)/shard_map/pallas_call | solution.py:58
  93.3 35.3 %reduce-scatter.2.cloned.1.call-done = f32[128,1536]{1,0:T(8,128)} async-done(((f32[512,1536]{1,0:T(8,128)}), f32[128,1536]{1,0:T(8,128)}) %reduce-scatter.2.cloned.1.call-update) | async-done | bytes 786448 | tf_op jit(solution)/shard_map/reduce_scatter | solution.py:92
  128.6 2.1 %fusion.11 = bf16[128,1536]{1,0:T(8,128)(2,1)} fusion(f32[128,1536]{1,0:T(8,128)} %reduce-scatter.2.cloned.1.call-done), kind=kLoop, calls=%fused_computation.14 | loop fusion | flops 1769472 | bytes 1179648 | tf_op jit(solution)/shard_map/convert_element_type | solution.py:93
  (27 shorter events, 0.5 us)
Async XLA Ops:
  6.5 3.8 %copy-start.5 = (bf16[128,384]{1,0:T(8,128)(2,1)S(1)}, bf16[128,384]{1,0:T(8,128)(2,1)}, u32[]{:S(2)}) copy-start(bf16[128,384]{1,0:T(8,128)(2,1)} %param.9) | copy-start | bytes 294916
  9.9 10.0 %copy-start.6 = (f32[6144]{0:T(1024)S(1)}, f32[6144]{0:T(1024)}, u32[]{:S(2)}) copy-start(f32[6144]{0:T(1024)} %param.10) | copy-start | bytes 73732
  11.2 29.8 %copy-start.2 = (bf16[384,1536]{1,0:T(8,128)(2,1)S(1)}, bf16[384,1536]{1,0:T(8,128)(2,1)}, u32[]{:S(2)}) copy-start(bf16[384,1536]{1,0:T(8,128)(2,1)} %w0_ref.1) | copy-start | bytes 3538948
  11.2 18.7 %all-to-all-start = ((bf16[128,2,384]{2,1,0:T(2,128)(2,1)}), bf16[128,2,384]{2,1,0:T(2,128)(2,1)S(1)}, u32[]{:S(2)}, u32[]{:S(2)}) async-start(bf16[128,2,384]{2,1,0:T(2,128)(2,1)} %copy.33), calls=%async_computation | async-start | bytes 393216 | tf_op jit(solution)/shard_map/all_to_all | solution.py:74
  19.9 64.7 %all-gather.2.cloned.1.call-start = ((), (), s32[]{:S(2)}) async-start(), calls=%async_computation.3 | async-start | bytes 1671168 | tf_op jit(solution)/shard_map/all_gather | solution.py:89
  40.9 87.7 %reduce-scatter.2.cloned.1.call-start = ((), (), s32[]{:S(2)}) async-start(), calls=%async_computation.4 | async-start | bytes 3932160 | tf_op jit(solution)/shard_map/reduce_scatter | solution.py:92
  41.0 28.6 %collective-permute-start = (bf16[384,1536]{1,0:T(8,128)(2,1)S(1)}, bf16[384,1536]{1,0:T(8,128)(2,1)S(1)}, u32[]{:S(2)}, u32[]{:S(2)}) collective-permute-start(bf16[384,1536]{1,0:T(8,128)(2,1)S(1)} %copy-done.2), channel_id=1, source_target_pairs={{0,48},{16,0},{32,16},{48,32},{1,49},{17,1},{33,17},{49,33},{2,50}... | collective-permute-start | bytes 3538952 | tf_op jit(solution)/shard_map/ppermute | solution.py:35
  41.9 27.8 %collective-permute-start.1 = (bf16[384,1536]{1,0:T(8,128)(2,1)S(1)}, bf16[384,1536]{1,0:T(8,128)(2,1)S(1)}, u32[]{:S(2)}, u32[]{:S(2)}) collective-permute-start(bf16[384,1536]{1,0:T(8,128)(2,1)S(1)} %copy-done.2), channel_id=1, source_target_pairs={{0,16},{16,32},{32,48},{48,0},{1,17},{17,33},{33,49},{49,1},{2,18}... | collective-permute-start | bytes 3538952 | tf_op jit(solution)/shard_map/ppermute | solution.py:34
  69.6 1.1 copy-start
  69.6 15.0 %collective-permute-start.3 = (bf16[384,768]{1,0:T(8,128)(2,1)S(1)}, bf16[384,768]{1,0:T(8,128)(2,1)S(1)}, u32[]{:S(2)}, u32[]{:S(2)}) collective-permute-start(bf16[384,768]{1,0:T(8,128)(2,1)S(1)} %slice.19), channel_id=1, source_target_pairs={{0,48},{16,0},{32,16},{48,32},{1,49},{17,1},{33,17},{49,33},{2,50}... | collective-permute-start | bytes 1769480 | tf_op jit(solution)/shard_map/ppermute | solution.py:38
  69.7 15.0 %copy-start.1 = (bf16[384,1536]{1,0:T(8,128)(2,1)}, bf16[384,1536]{1,0:T(8,128)(2,1)S(1)}, u32[]{:S(2)}) copy-start(bf16[384,1536]{1,0:T(8,128)(2,1)S(1)} %collective-permute-done.1.w3_ref) | copy-start | bytes 3538948
  70.6 14.0 %collective-permute-start.2 = (bf16[384,768]{1,0:T(8,128)(2,1)S(1)}, bf16[384,768]{1,0:T(8,128)(2,1)S(1)}, u32[]{:S(2)}, u32[]{:S(2)}) collective-permute-start(bf16[384,768]{1,0:T(8,128)(2,1)S(1)} %slice.18), channel_id=1, source_target_pairs={{0,16},{16,32},{32,48},{48,0},{1,17},{17,33},{33,49},{49,1},{2,18}... | collective-permute-start | bytes 1769480 | tf_op jit(solution)/shard_map/ppermute | solution.py:37
  84.7 0.8 copy-start.3
  84.7 1.0 copy-start.4
Sparse Core Ops, SparseCore 0:
  41.1 34.6 all-gather.1
  93.4 35.0 reduce-scatter.1

commit v7 on v6

--- a/solution.py
+++ b/solution.py
@@ -27,28 +27,23 @@
     return output.astype(jnp.bfloat16).reshape(seq, width)
 
 
-def ring_pieces(block, axis):
+def ring_neighbours(block, axis):
     n = 4
     to_right = [(i, (i + 1) % n) for i in range(n)]
     to_left = [(i, (i - 1) % n) for i in range(n)]
     from_left = lax.ppermute(block, axis, to_right)
     from_right = lax.ppermute(block, axis, to_left)
-    half = block.shape[1] // 2
-    far_low = lax.ppermute(from_left[:, :half], axis, to_right)
-    far_high = lax.ppermute(from_right[:, half:], axis, to_left)
-    return block, from_right, far_low, far_high, from_left
+    return from_left, from_right
 
 
-def pieces_kernel(a_ref, w0_ref, w1_ref, w2lo_ref, w2hi_ref, w3_ref, o_ref):
+def pieces_kernel(a_ref, w0_ref, w1_ref, w2_ref, w3_ref, o_ref):
     k = w0_ref.shape[0]
-    half = w2lo_ref.shape[1]
     a = a_ref[...]
-    base = jnp.dot(a[:, 0:k], w0_ref[...], preferred_element_type=jnp.float32)
-    base = base + jnp.dot(a[:, k:2 * k], w1_ref[...], preferred_element_type=jnp.float32)
-    base = base + jnp.dot(a[:, 3 * k:4 * k], w3_ref[...], preferred_element_type=jnp.float32)
-    far = a[:, 2 * k:3 * k]
-    o_ref[:, 0:half] = base[:, 0:half] + jnp.dot(far, w2lo_ref[...], preferred_element_type=jnp.float32)
-    o_ref[:, half:] = base[:, half:] + jnp.dot(far, w2hi_ref[...], preferred_element_type=jnp.float32)
+    acc = jnp.dot(a[:, 0:k], w0_ref[...], preferred_element_type=jnp.float32)
+    acc = acc + jnp.dot(a[:, k:2 * k], w1_ref[...], preferred_element_type=jnp.float32)
+    acc = acc + jnp.dot(a[:, 2 * k:3 * k], w2_ref[...], preferred_element_type=jnp.float32)
+    acc = acc + jnp.dot(a[:, 3 * k:4 * k], w3_ref[...], preferred_element_type=jnp.float32)
+    o_ref[...] = acc
 
 
 def dot_pieces(a, pieces, tile=128):
@@ -68,7 +63,11 @@
 
 
 def per_device(q_seq, k_seq, v_seq, resid, ln_gain, w_up, n_x):
-    pieces = ring_pieces(w_up, "rx")
+    pair = lax.all_gather(w_up, "rxh", axis=0, tiled=False)
+    far = lax.dynamic_index_in_dim(pair, 1 - lax.axis_index("rxh"), 0, keepdims=False)
+    from_left, from_right = ring_neighbours(w_up, ("rxh", "rxl"))
+    pieces = (w_up, from_right, far, from_left)
+    x_index = lax.axis_index("rxh") * 2 + lax.axis_index("rxl")
     attended = attention_block(q_seq, k_seq, v_seq)
     both = jnp.stack([resid, attended], axis=1)
     both = lax.all_to_all(both, "col", split_axis=0, concat_axis=1, tiled=True)
@@ -83,9 +82,11 @@
     n_y = full_width // (n_x * block)
     grouped = normed.reshape(chunk, n_y, n_x, block)
     doubled = jnp.concatenate([grouped, grouped], axis=2)
-    rolled = lax.dynamic_slice_in_dim(doubled, lax.axis_index("rx"), n_x, axis=2).reshape(chunk, full_width)
+    rolled = lax.dynamic_slice_in_dim(doubled, x_index, n_x, axis=2).reshape(chunk, full_width)
     part = lax.all_to_all(rolled, "ry", split_axis=1, concat_axis=0, tiled=True)
     part = part.reshape(n_y, chunk, part.shape[1])
+    far, part = lax.optimization_barrier((far, part))
+    pieces = (w_up, from_right, far, from_left)
     tokens = lax.all_gather(part, "col", axis=1, tiled=True)
     tokens = tokens.reshape(-1, tokens.shape[-1])
     partial = dot_pieces(tokens, pieces)
@@ -96,8 +97,9 @@
 def solution(mesh):
     n_row, n_col = mesh.shape["row"], mesh.shape["col"]
     nx = len({d.coords[0] for d in mesh.devices[:, 0]})
-    split = Mesh(mesh.devices.reshape(n_row // nx, nx, n_col), ("ry", "rx", "col"))
-    rows = ("ry", "rx")
+    assert nx == 4
+    split = Mesh(mesh.devices.reshape(n_row // nx, 2, nx // 2, n_col), ("ry", "rxh", "rxl", "col"))
+    rows = ("ry", "rxh", "rxl")
     placed = (
         P(rows, "col"),
         P(rows, "col"),

time: 139 us -> 154 us (1.11)
  waiting for transfers between devices: 82 us -> 107 us
  blocking collectives: 10.2 us -> 0 us
  starting transfers between devices: 14.6 us -> 16.4 us
    all_gather x0 -> x1, waiting for transfers between devices: none -> 19.4 us  [per_device(): pair = lax.all_gather(w_up, 'rxh', axis=0, tiled=False)]
    all_gather x1, waiting for transfers between devices: 0.02 us -> 11.3 us  [per_device(): tokens = lax.all_gather(part, 'col', axis=1, tiled=True)]
    ppermute x4 -> x2, waiting for transfers between devices: 36.9 us -> 25.7 us  [the longest x1 25.7 us: ring_neighbours(): from_right = lax.ppermute(block, axis, to_left)]
    all_to_all x1 -> x0, blocking collectives: 10.2 us -> none  [per_device(): part = lax.all_to_all(rolled, 'ry', split_axis=1, concat_axis=0, tiled=True)]
    all_to_all x0 -> x1, starting transfers between devices: none -> 4.46 us  [per_device(): part = lax.all_to_all(rolled, 'ry', split_axis=1, concat_axis=0, tiled=True)]
    reduce_scatter x1, waiting for transfers between devices: 35.3 us -> 39.6 us  [per_device(): product = lax.psum_scatter(partial, 'ry', scatter_dimension=0, tiled=True)]
    unnamed x18 -> x22, local copies, waits for them, and re-layouts: 4.92 us -> 1.21 us
    ppermute x4 -> x2, starting transfers between devices: 5.84 us -> 3.31 us  [the longest x1 3.22 us: ring_neighbours(): from_left = lax.ppermute(block, axis, to_right)]
  transfers between devices with their start and end apart: 7 -> 7, of which waited for: 4 -> 5; matrix products, arithmetic and copies ran while one was open for 0% -> 4% of each run, Pallas kernels for 0% -> 0%
where the time goes in v7:
time: 154 us; the launch traced here: 153 us
  waiting for transfers between devices  107 us (69%)
  starting transfers between devices  16.4 us (11%)
  between operations  13.3 us (9%)
  Pallas kernels  7.64 us (5%)
  local copies, waits for them, and re-layouts  4.74 us (3%)
  other arithmetic  3.65 us (2%)
    reduce_scatter x1, waiting for transfers between devices, per_device(): product = lax.psum_scatter(partial, 'ry', scatter_dimension=0, tiled=True)  39.6 us
    ppermute x1, waiting for transfers between devices, ring_neighbours(): from_right = lax.ppermute(block, axis, to_left)  25.7 us
    all_gather x1, waiting for transfers between devices, per_device(): pair = lax.all_gather(w_up, 'rxh', axis=0, tiled=False)  19.4 us
    all_gather x1, waiting for transfers between devices, per_device(): tokens = lax.all_gather(part, 'col', axis=1, tiled=True)  11.3 us
    all_to_all x1, waiting for transfers between devices, per_device(): both = lax.all_to_all(both, 'col', split_axis=0, concat_axis=1, tiled=True)  9.92 us
    all_to_all x1, starting transfers between devices, per_device(): both = lax.all_to_all(both, 'col', split_axis=0, concat_axis=1, tiled=True)  8.57 us
    pallas_call x1, Pallas kernels, dot_pieces(): pl.pallas_call(pieces_kernel, grid=(m // tile,), in_specs=[pl.BlockSpec((...  7.64 us
    all_to_all x1, starting transfers between devices, per_device(): part = lax.all_to_all(rolled, 'ry', split_axis=1, concat_axis=0, tiled=True)  4.46 us
  transfers between devices with their start and end apart: 7, of which 5 were waited for; matrix products, arithmetic and copies ran while one was open for 4% of the time, Pallas kernels for 0%

profile of v7, /device:TPU:6, one launch (start us, length us, event | category | flops | bytes accessed | tf_op | source)
XLA Modules:
  0.0 152.7 jit_solution(14115564358148333994)
XLA Ops:
  6.5 0.7 all-gather.6.cloned.1.call-update
  7.3 0.2 copy-done.4
  7.4 0.1 copy.26
  7.6 0.1 copy.27
  7.7 0.1 copy.30
  7.9 0.2 fusion.2
  8.2 0.2 convolution_convert_fusion
  8.4 0.1 copy.32
  8.6 0.9 copy.33
  9.4 8.6 %all-to-all-start = ((bf16[128,2,384]{2,1,0:T(2,128)(2,1)}), bf16[128,2,384]{2,1,0:T(2,128)(2,1)S(1)}, u32[]{:S(2)}, u32[]{:S(2)}) async-start(bf16[128,2,384]{2,1,0:T(2,128)(2,1)} %copy.33), calls=%async_computation | async-start | bytes 393216 | tf_op jit(solution)/shard_map/all_to_all | solution.py:73
  18.1 9.9 %all-to-all-done = bf16[128,2,384]{2,1,0:T(2,128)(2,1)S(1)} async-done(((bf16[128,2,384]{2,1,0:T(2,128)(2,1)}), bf16[128,2,384]{2,1,0:T(2,128)(2,1)S(1)}, u32[]{:S(2)}, u32[]{:S(2)}) %all-to-all-start) | async-done | bytes 196640 | tf_op jit(solution)/shard_map/all_to_all | solution.py:73
  28.0 0.6 fusion.19
  28.6 0.1 fusion.15
  28.7 0.7 fusion.16
  29.4 4.5 %all-to-all-start.1 = ((bf16[8,4,1536]{2,0,1:T(8,128)(2,1)}), bf16[8,4,1536]{2,0,1:T(8,128)(2,1)S(1)}, u32[]{:S(2)}, u32[]{:S(2)}) async-start(bf16[8,4,1536]{2,0,1:T(8,128)(2,1)} %bitcast.11), calls=%async_computation.1 | async-start | bytes 196608 | tf_op jit(solution)/shard_map/all_to_all | solution.py:86
  33.9 19.4 %all-gather.6.cloned.1.call-done = bf16[768,1536]{1,0:T(8,128)(2,1)} async-done(((bf16[384,1536]{1,0:T(8,128)(2,1)}), bf16[768,1536]{1,0:T(8,128)(2,1)}) %all-gather.6.cloned.1.call-update) | async-done | bytes 2359312 | tf_op jit(solution)/shard_map/all_gather | solution.py:66
  53.2 2.5 %dynamic-slice_bitcast_fusion.w2_ref = bf16[384,1536]{1,0:T(8,128)(2,1)} fusion(bf16[2,384,1536]{2,1,0:T(8,128)(2,1)} %bitcast.33, s32[]{:T(128)S(6)} %select_n.11), kind=kLoop, calls=%fused_computation.2 | loop fusion | bytes 2359300 | tf_op jit(solution)/shard_map/jit(dynamic_index_in_dim)/squeeze | solution.py:67
  55.7 0.6 copy-done.3
  56.6 3.2 %collective-permute-start.1 = (bf16[384,1536]{1,0:T(8,128)(2,1)S(1)}, bf16[384,1536]{1,0:T(8,128)(2,1)S(1)}, u32[]{:S(2)}, u32[]{:S(2)}) collective-permute-start(bf16[384,1536]{1,0:T(8,128)(2,1)S(1)} %copy-done), channel_id=1, source_target_pairs={{0,16},{16,32},{32,48},{48,0},{1,17},{17,33},{33,49},{49,1},{2,18}... | collective-permute-start | bytes 3538952 | tf_op jit(solution)/shard_map/ppermute | solution.py:34
  59.8 25.7 %collective-permute-done.w1_ref = bf16[384,1536]{1,0:T(8,128)(2,1)S(1)} collective-permute-done((bf16[384,1536]{1,0:T(8,128)(2,1)S(1)}, bf16[384,1536]{1,0:T(8,128)(2,1)S(1)}, u32[]{:S(2)}, u32[]{:S(2)}) %collective-permute-start) | collective-permute-done | bytes 1179680 | tf_op jit(solution)/shard_map/ppermute | solution.py:35
  85.5 11.3 %all-gather.4.cloned.1.call-done = bf16[4,128,1536]{2,1,0:T(8,128)(2,1)} async-done(((bf16[4,8,1536]{2,1,0:T(8,128)(2,1)}), bf16[4,128,1536]{2,1,0:T(8,128)(2,1)}) %all-gather.4.cloned.1.call-update) | async-done | bytes 1572880 | tf_op jit(solution)/shard_map/all_gather | solution.py:90
  96.8 7.6 %shard_map.64 = f32[512,1536]{1,0:T(8,128)} custom-call(bf16[512,1536]{1,0:T(8,128)(2,1)} %bitcast.31, bf16[384,1536]{1,0:T(8,128)(2,1)} %w0_ref.1, bf16[384,1536]{1,0:T(8,128)(2,1)} %copy-done.1, bf16[384,1536]{1,0:T(8,128)(2,1)} %dynamic-slice_bitcast_fusion.w2_ref, bf16[384,1536]{1,0:T(8,128)(2,1)} %copy-done.2), custom_call_target="tpu_custom_call" | custom-call | flops 2415919104 | bytes 9437184 | tf_op jit(solution)/shard_map/pallas_call | solution.py:53
  104.4 39.6 %reduce-scatter.2.cloned.1.call-done = f32[128,1536]{1,0:T(8,128)} async-done(((f32[512,1536]{1,0:T(8,128)}), f32[128,1536]{1,0:T(8,128)}) %reduce-scatter.2.cloned.1.call-update) | async-done | bytes 786448 | tf_op jit(solution)/shard_map/reduce_scatter | solution.py:93
  144.0 2.1 %fusion.11 = bf16[128,1536]{1,0:T(8,128)(2,1)} fusion(f32[128,1536]{1,0:T(8,128)} %reduce-scatter.2.cloned.1.call-done), kind=kLoop, calls=%fused_computation.15 | loop fusion | flops 1769472 | bytes 1179648 | tf_op jit(solution)/shard_map/convert_element_type | solution.py:94
  (30 shorter events, 0.4 us)
Async XLA Ops:
  6.5 0.9 copy-start.4
  6.5 1.0 copy-start.5
  6.5 1.2 copy-start.6
  6.5 46.7 %all-gather.6.cloned.1.call-start = ((), (), s32[]{:S(2)}) async-start(), calls=%async_computation.5 | async-start | bytes 3538944 | tf_op jit(solution)/shard_map/all_gather | solution.py:66
  7.4 1.1 copy-start.7
  8.2 9.9 %copy-start.8 = (f32[6144]{0:T(1024)S(1)}, f32[6144]{0:T(1024)}, u32[]{:S(2)}) copy-start(f32[6144]{0:T(1024)} %param.10) | copy-start | bytes 73732
  9.4 18.5 %all-to-all-start = ((bf16[128,2,384]{2,1,0:T(2,128)(2,1)}), bf16[128,2,384]{2,1,0:T(2,128)(2,1)S(1)}, u32[]{:S(2)}, u32[]{:S(2)}) async-start(bf16[128,2,384]{2,1,0:T(2,128)(2,1)} %copy.33), calls=%async_computation | async-start | bytes 393216 | tf_op jit(solution)/shard_map/all_to_all | solution.py:73
  29.4 26.3 %all-to-all-start.1 = ((bf16[8,4,1536]{2,0,1:T(8,128)(2,1)}), bf16[8,4,1536]{2,0,1:T(8,128)(2,1)S(1)}, u32[]{:S(2)}, u32[]{:S(2)}) async-start(bf16[8,4,1536]{2,0,1:T(8,128)(2,1)} %bitcast.11), calls=%async_computation.1 | async-start | bytes 196608 | tf_op jit(solution)/shard_map/all_to_all | solution.py:86
  33.9 62.9 %all-gather.4.cloned.1.call-start = ((), (), s32[]{:S(2)}) async-start(), calls=%async_computation.3 | async-start | bytes 1671168 | tf_op jit(solution)/shard_map/all_gather | solution.py:90
  53.2 3.2 %copy-start = (bf16[384,1536]{1,0:T(8,128)(2,1)S(1)}, bf16[384,1536]{1,0:T(8,128)(2,1)}, u32[]{:S(2)}) copy-start(bf16[384,1536]{1,0:T(8,128)(2,1)} %w0_ref.1) | copy-start | bytes 3538948
  55.7 0.6 copy-start.3
  56.4 87.6 %reduce-scatter.2.cloned.1.call-start = ((), (), s32[]{:S(2)}) async-start(), calls=%async_computation.4 | async-start | bytes 3932160 | tf_op jit(solution)/shard_map/reduce_scatter | solution.py:93
  56.5 29.0 %collective-permute-start = (bf16[384,1536]{1,0:T(8,128)(2,1)S(1)}, bf16[384,1536]{1,0:T(8,128)(2,1)S(1)}, u32[]{:S(2)}, u32[]{:S(2)}) collective-permute-start(bf16[384,1536]{1,0:T(8,128)(2,1)S(1)} %copy-done), channel_id=1, source_target_pairs={{0,48},{16,0},{32,16},{48,32},{1,49},{17,1},{33,17},{49,33},{2,50}... | collective-permute-start | bytes 3538952 | tf_op jit(solution)/shard_map/ppermute | solution.py:35
  56.6 28.9 %collective-permute-start.1 = (bf16[384,1536]{1,0:T(8,128)(2,1)S(1)}, bf16[384,1536]{1,0:T(8,128)(2,1)S(1)}, u32[]{:S(2)}, u32[]{:S(2)}) collective-permute-start(bf16[384,1536]{1,0:T(8,128)(2,1)S(1)} %copy-done), channel_id=1, source_target_pairs={{0,16},{16,32},{32,48},{48,0},{1,17},{17,33},{33,49},{49,1},{2,18}... | collective-permute-start | bytes 3538952 | tf_op jit(solution)/shard_map/ppermute | solution.py:34
  85.5 11.3 %copy-start.1 = (bf16[384,1536]{1,0:T(8,128)(2,1)}, bf16[384,1536]{1,0:T(8,128)(2,1)S(1)}, u32[]{:S(2)}) copy-start(bf16[384,1536]{1,0:T(8,128)(2,1)S(1)} %collective-permute-done.w1_ref) | copy-start | bytes 3538948
  85.5 11.3 %copy-start.2 = (bf16[384,1536]{1,0:T(8,128)(2,1)}, bf16[384,1536]{1,0:T(8,128)(2,1)S(1)}, u32[]{:S(2)}) copy-start(bf16[384,1536]{1,0:T(8,128)(2,1)S(1)} %collective-permute-done.1.w3_ref) | copy-start | bytes 3538948
Sparse Core Ops, SparseCore 0:
  9.2 44.0 all-gather.5
  56.5 40.1 all-gather.3
  104.5 39.4 reduce-scatter.1

commit v8 on v6

--- a/solution.py
+++ b/solution.py
@@ -31,40 +31,59 @@
     n = 4
     to_right = [(i, (i + 1) % n) for i in range(n)]
     to_left = [(i, (i - 1) % n) for i in range(n)]
-    from_left = lax.ppermute(block, axis, to_right)
-    from_right = lax.ppermute(block, axis, to_left)
-    half = block.shape[1] // 2
-    far_low = lax.ppermute(from_left[:, :half], axis, to_right)
-    far_high = lax.ppermute(from_right[:, half:], axis, to_left)
-    return block, from_right, far_low, far_high, from_left
+    width = block.shape[1] // 2
+    near, far = [], []
+    lefts, rights = [], []
+    for c in range(2):
+        piece = block[:, c * width:(c + 1) * width]
+        lefts.append(lax.ppermute(piece, axis, to_right))
+        rights.append(lax.ppermute(piece, axis, to_left))
+    half = width // 2
+    for c in range(2):
+        far.append(lax.ppermute(lefts[c][:, :half], axis, to_right))
+        far.append(lax.ppermute(rights[c][:, half:], axis, to_left))
+    return (block, rights[0], rights[1], lefts[0], lefts[1]), tuple(far)
 
 
-def pieces_kernel(a_ref, w0_ref, w1_ref, w2lo_ref, w2hi_ref, w3_ref, o_ref):
+def near_kernel(a_ref, w0_ref, r0_ref, r1_ref, l0_ref, l1_ref, o_ref):
     k = w0_ref.shape[0]
-    half = w2lo_ref.shape[1]
+    width = r0_ref.shape[1]
     a = a_ref[...]
     base = jnp.dot(a[:, 0:k], w0_ref[...], preferred_element_type=jnp.float32)
-    base = base + jnp.dot(a[:, k:2 * k], w1_ref[...], preferred_element_type=jnp.float32)
-    base = base + jnp.dot(a[:, 3 * k:4 * k], w3_ref[...], preferred_element_type=jnp.float32)
-    far = a[:, 2 * k:3 * k]
-    o_ref[:, 0:half] = base[:, 0:half] + jnp.dot(far, w2lo_ref[...], preferred_element_type=jnp.float32)
-    o_ref[:, half:] = base[:, half:] + jnp.dot(far, w2hi_ref[...], preferred_element_type=jnp.float32)
+    own_right = a[:, k:2 * k]
+    own_left = a[:, 3 * k:4 * k]
+    for c, (r_ref, l_ref) in enumerate(((r0_ref, l0_ref), (r1_ref, l1_ref))):
+        cols = slice(c * width, (c + 1) * width)
+        side = jnp.dot(own_right, r_ref[...], preferred_element_type=jnp.float32)
+        side = side + jnp.dot(own_left, l_ref[...], preferred_element_type=jnp.float32)
+        o_ref[:, cols] = base[:, cols] + side
 
 
-def dot_pieces(a, pieces, tile=128):
+def far_kernel(a_ref, f0_ref, f1_ref, f2_ref, f3_ref, acc_ref, o_ref):
+    k = a_ref.shape[1] // 4
+    width = f0_ref.shape[1]
+    far = a_ref[:, 2 * k:3 * k]
+    for c, f_ref in enumerate((f0_ref, f1_ref, f2_ref, f3_ref)):
+        cols = slice(c * width, (c + 1) * width)
+        o_ref[:, cols] = acc_ref[:, cols] + jnp.dot(far, f_ref[...], preferred_element_type=jnp.float32)
+
+
+def tiled_call(kernel, a, pieces, extra=(), tile=128):
     m, kk = a.shape
-    n = pieces[0].shape[1]
+    n = 4 * pieces[0].shape[1] if kernel is far_kernel else pieces[0].shape[1]
     full = lambda p: pl.BlockSpec(p.shape, lambda i: (0, 0))
+    rows = lambda width: pl.BlockSpec((tile, width), lambda i: (i, 0))
+    flops = 2 * m * sum(p.shape[0] * p.shape[1] for p in pieces)
+    moved = a.size * 2 + sum(p.size * 2 for p in pieces) + m * n * 4 * (1 + len(extra))
     return pl.pallas_call(
-        pieces_kernel,
+        kernel,
         grid=(m // tile,),
-        in_specs=[pl.BlockSpec((tile, kk), lambda i: (i, 0))] + [full(p) for p in pieces],
-        out_specs=pl.BlockSpec((tile, n), lambda i: (i, 0)),
+        in_specs=[rows(kk)] + [full(p) for p in pieces] + [rows(n) for _ in extra],
+        out_specs=rows(n),
         out_shape=jax.ShapeDtypeStruct((m, n), jnp.float32),
-        cost_estimate=pl.CostEstimate(
-            flops=2 * m * kk * n, transcendentals=0, bytes_accessed=a.size * 2 + sum(p.size * 2 for p in pieces) + m * n * 4
-        ),
-    )(a, *pieces)
+        input_output_aliases={1 + len(pieces): 0} if extra else {},
+        cost_estimate=pl.CostEstimate(flops=flops, transcendentals=0, bytes_accessed=moved),
+    )(a, *pieces, *extra)
 
 
 def per_device(q_seq, k_seq, v_seq, resid, ln_gain, w_up, n_x):
@@ -88,7 +107,9 @@
     part = part.reshape(n_y, chunk, part.shape[1])
     tokens = lax.all_gather(part, "col", axis=1, tiled=True)
     tokens = tokens.reshape(-1, tokens.shape[-1])
-    partial = dot_pieces(tokens, pieces)
+    near, far = pieces
+    partial = tiled_call(near_kernel, tokens, near)
+    partial = tiled_call(far_kernel, tokens, far, extra=(partial,))
     product = lax.psum_scatter(partial, "ry", scatter_dimension=0, tiled=True)
     return jax.nn.gelu(product, approximate=True).astype(jnp.bfloat16)
 

time: 139 us -> 140 us (level)
  waiting for transfers between devices: 82 us -> 67.9 us
  starting transfers between devices: 14.6 us -> 21.7 us
  Pallas kernels: 7.64 us -> 12.3 us
  local copies, waits for them, and re-layouts: 6.01 us -> 9.04 us
    ppermute x4 -> x8, waiting for transfers between devices: 36.9 us -> 18.8 us  [the longest x2 18.8 us: ring_pieces(): rights.append(lax.ppermute(piece, axis, to_left))]
    ppermute x4 -> x8, starting transfers between devices: 5.84 us -> 13 us  [the longest x2 6.47 us: ring_pieces(): far.append(lax.ppermute(lefts[c][:, :half], axis, to_right))]
    pallas_call x1 -> x2, Pallas kernels: 7.64 us -> 12.3 us  [tiled_call(): pl.pallas_call(kernel, grid=(m // tile,), in_specs=[rows(kk)] + [full(p)...]
    reduce_scatter x1, waiting for transfers between devices: 35.3 us -> 39.2 us  [per_device(): product = lax.psum_scatter(partial, 'ry', scatter_dimension=0, tiled=True)]
    slice x2 -> x5, local copies, waits for them, and re-layouts: 0.08 us -> 3.28 us  [the longest x2 1.61 us: ring_pieces(): far.append(lax.ppermute(lefts[c][:, :half], axis, to_right))]
    unnamed x18 -> x26, local copies, waits for them, and re-layouts: 4.92 us -> 4.74 us
  transfers between devices with their start and end apart: 7 -> 11, of which waited for: 4 -> 4; matrix products, arithmetic and copies ran while one was open for 0% -> 2% of each run, Pallas kernels for 0% -> 5%
where the time goes in v8:
time: 140 us; the launch traced here: 138 us
  waiting for transfers between devices  67.9 us (49%)
  starting transfers between devices  21.7 us (16%)
  between operations  13.6 us (10%)
  Pallas kernels  12.3 us (9%)
  blocking collectives  10.2 us (7%)
  local copies, waits for them, and re-layouts  9.04 us (6%)
  other arithmetic  3.01 us (2%)
    reduce_scatter x1, waiting for transfers between devices, per_device(): product = lax.psum_scatter(partial, 'ry', scatter_dimension=0, tiled=True)  39.2 us
    ppermute x2, waiting for transfers between devices, ring_pieces(): rights.append(lax.ppermute(piece, axis, to_left))  18.8 us
    pallas_call x2, Pallas kernels, tiled_call(): pl.pallas_call(kernel, grid=(m // tile,), in_specs=[rows(kk)] + [full(p)...  12.3 us
    all_to_all x1, blocking collectives, per_device(): part = lax.all_to_all(rolled, 'ry', split_axis=1, concat_axis=0, tiled=True)  10.2 us
    all_to_all x1, waiting for transfers between devices, per_device(): both = lax.all_to_all(both, 'col', split_axis=0, concat_axis=1, tiled=True)  9.87 us
    all_to_all x1, starting transfers between devices, per_device(): both = lax.all_to_all(both, 'col', split_axis=0, concat_axis=1, tiled=True)  8.57 us
    ppermute x2, starting transfers between devices, ring_pieces(): far.append(lax.ppermute(lefts[c][:, :half], axis, to_right))  6.47 us
    ppermute x2, starting transfers between devices, ring_pieces(): lefts.append(lax.ppermute(piece, axis, to_right))  5.64 us
  transfers between devices with their start and end apart: 11, of which 4 were waited for; matrix products, arithmetic and copies ran while one was open for 2% of the time, Pallas kernels for 5%

profile of v8, /device:TPU:6, one launch (start us, length us, event | category | flops | bytes accessed | tf_op | source)
XLA Modules:
  0.0 138.2 jit_solution(11387538679388470284)
XLA Ops:
  6.6 1.0 copy.27
  7.6 1.0 copy.28
  8.9 1.0 copy.31
  10.3 0.9 copy.34
  11.2 8.6 %all-to-all-start = ((bf16[128,2,384]{2,1,0:T(2,128)(2,1)}), bf16[128,2,384]{2,1,0:T(2,128)(2,1)S(1)}, u32[]{:S(2)}, u32[]{:S(2)}) async-start(bf16[128,2,384]{2,1,0:T(2,128)(2,1)} %copy.34), calls=%async_computation | async-start | bytes 393216 | tf_op jit(solution)/shard_map/all_to_all | solution.py:93
  19.9 9.9 %all-to-all-done = bf16[128,2,384]{2,1,0:T(2,128)(2,1)S(1)} async-done(((bf16[128,2,384]{2,1,0:T(2,128)(2,1)}), bf16[128,2,384]{2,1,0:T(2,128)(2,1)S(1)}, u32[]{:S(2)}, u32[]{:S(2)}) %all-to-all-start) | async-done | bytes 196640 | tf_op jit(solution)/shard_map/all_to_all | solution.py:93
  30.6 10.2 %all_to_all.31 = bf16[8,4,1536]{2,0,1:T(8,128)(2,1)} all-to-all(bf16[8,4,1536]{2,0,1:T(8,128)(2,1)S(1)} %bitcast.32), channel_id=1, replica_groups=mesh['ry'=4,'rx'=4,'col'=16] {'ry'}, dimensions={1} | all-to-all | bytes 196608 | tf_op jit(solution)/shard_map/all_to_all | solution.py:106
  41.0 0.9 collective-permute-start.6
  41.9 2.4 %collective-permute-start.4 = (bf16[384,768]{1,0:T(8,128)(2,1)S(1)}, bf16[384,768]{1,0:T(8,128)(2,1)S(1)}, u32[]{:S(2)}, u32[]{:S(2)}) collective-permute-start(bf16[384,768]{1,0:T(8,128)(2,1)S(1)} %get-tuple-element.8), channel_id=1, source_target_pairs={{0,16},{16,32},{32,48},{48,0},{1,17},{17,33},{33,49},{49,1},{2,18}... | collective-permute-start | bytes 1769480 | tf_op jit(solution)/shard_map/ppermute | solution.py:39
  44.3 3.2 %collective-permute-start = (bf16[384,768]{1,0:T(8,128)(2,1)S(1)}, bf16[384,768]{1,0:T(8,128)(2,1)S(1)}, u32[]{:S(2)}, u32[]{:S(2)}) collective-permute-start(bf16[384,768]{1,0:T(8,128)(2,1)S(1)} %get-tuple-element.9), channel_id=1, source_target_pairs={{0,16},{16,32},{32,48},{48,0},{1,17},{17,33},{33,49},{49,1},{2,18}... | collective-permute-start | bytes 1769480 | tf_op jit(solution)/shard_map/ppermute | solution.py:39
  47.5 11.0 %collective-permute-done.6.r1_ref = bf16[384,768]{1,0:T(8,128)(2,1)S(1)} collective-permute-done((bf16[384,768]{1,0:T(8,128)(2,1)S(1)}, bf16[384,768]{1,0:T(8,128)(2,1)S(1)}, u32[]{:S(2)}, u32[]{:S(2)}) %collective-permute-start.6) | collective-permute-done | bytes 589856 | tf_op jit(solution)/shard_map/ppermute | solution.py:40
  58.5 0.8 slice.37
  59.3 0.8 slice.36
  60.1 3.2 %collective-permute-start.5 = (bf16[384,384]{1,0:T(8,128)(2,1)}, bf16[384,384]{1,0:T(8,128)(2,1)S(1)}, u32[]{:S(2)}, u32[]{:S(2)}) collective-permute-start(bf16[384,384]{1,0:T(8,128)(2,1)} %slice.36), channel_id=1, source_target_pairs={{0,16},{16,32},{32,48},{48,0},{1,17},{17,33},{33,49},{49,1},{2,18}... | collective-permute-start | bytes 884744 | tf_op jit(solution)/shard_map/ppermute | solution.py:43
  63.4 7.8 %collective-permute-done.2.r0_ref = bf16[384,768]{1,0:T(8,128)(2,1)S(1)} collective-permute-done((bf16[384,768]{1,0:T(8,128)(2,1)S(1)}, bf16[384,768]{1,0:T(8,128)(2,1)S(1)}, u32[]{:S(2)}, u32[]{:S(2)}) %collective-permute-start.2) | collective-permute-done | bytes 589856 | tf_op jit(solution)/shard_map/ppermute | solution.py:40
  71.2 0.8 slice.35
  72.0 0.8 slice.34
  72.8 3.2 %collective-permute-start.1 = (bf16[384,384]{1,0:T(8,128)(2,1)}, bf16[384,384]{1,0:T(8,128)(2,1)S(1)}, u32[]{:S(2)}, u32[]{:S(2)}) collective-permute-start(bf16[384,384]{1,0:T(8,128)(2,1)} %slice.34), channel_id=1, source_target_pairs={{0,16},{16,32},{32,48},{48,0},{1,17},{17,33},{33,49},{49,1},{2,18}... | collective-permute-start | bytes 884744 | tf_op jit(solution)/shard_map/ppermute | solution.py:43
  76.0 6.7 %shard_map.64.acc_ref = f32[512,1536]{1,0:T(8,128)} custom-call(bf16[512,1536]{1,0:T(8,128)(2,1)} %bitcast.27, bf16[384,1536]{1,0:T(8,128)(2,1)} %w0_ref.1, bf16[384,768]{1,0:T(8,128)(2,1)} %copy-done.3, bf16[384,768]{1,0:T(8,128)(2,1)} %copy-done.1, bf16[384,768]{1,0:T(8,128)(2,1)} %copy-done.4, bf16[384,768]{1,0:T(8,128)(2,1)} %copy-done.2), custom_call_target="tpu_custom_call" | custom-call | flops 1811939328 | bytes 8257536 | tf_op jit(solution)/shard_map/pallas_call | solution.py:78
  82.7 0.7 copy-done.5
  83.7 0.7 copy-done.8
  84.4 5.6 %shard_map.65 = f32[512,1536]{1,0:T(8,128)} custom-call(bf16[512,1536]{1,0:T(8,128)(2,1)} %bitcast.28, bf16[384,384]{1,0:T(8,128)(2,1)} %copy-done.8, bf16[384,384]{1,0:T(8,128)(2,1)} %copy-done.7, bf16[384,384]{1,0:T(8,128)(2,1)} %copy-done.6, bf16[384,384]{1,0:T(8,128)(2,1)} %copy-done.5, ...), custom_call_target="tpu_custom_call", output_to_operand_aliasing={{}: (5, {})} | custom-call | flops 603979776 | bytes 9043968 | tf_op jit(solution)/shard_map/pallas_call | solution.py:78
  90.0 39.2 %reduce-scatter.2.cloned.1.call-done = f32[128,1536]{1,0:T(8,128)} async-done(((f32[512,1536]{1,0:T(8,128)}), f32[128,1536]{1,0:T(8,128)}) %reduce-scatter.2.cloned.1.call-update) | async-done | bytes 786448 | tf_op jit(solution)/shard_map/reduce_scatter | solution.py:113
  129.3 2.1 %fusion.11 = bf16[128,1536]{1,0:T(8,128)(2,1)} fusion(f32[128,1536]{1,0:T(8,128)} %reduce-scatter.2.cloned.1.call-done), kind=kLoop, calls=%fused_computation.14 | loop fusion | flops 1769472 | bytes 1179648 | tf_op jit(solution)/shard_map/convert_element_type | solution.py:114
  (47 shorter events, 2.0 us)
Async XLA Ops:
  6.5 3.8 %copy-start.9 = (bf16[128,384]{1,0:T(8,128)(2,1)S(1)}, bf16[128,384]{1,0:T(8,128)(2,1)}, u32[]{:S(2)}) copy-start(bf16[128,384]{1,0:T(8,128)(2,1)} %param.9) | copy-start | bytes 294916
  8.6 11.2 %copy-start.10 = (f32[6144]{0:T(1024)S(1)}, f32[6144]{0:T(1024)}, u32[]{:S(2)}) copy-start(f32[6144]{0:T(1024)} %param.10) | copy-start | bytes 73732
  10.3 30.6 %copy-start = (bf16[384,1536]{1,0:T(8,128)(2,1)S(1)}, bf16[384,1536]{1,0:T(8,128)(2,1)}, u32[]{:S(2)}) copy-start(bf16[384,1536]{1,0:T(8,128)(2,1)} %w0_ref.1) | copy-start | bytes 3538948
  11.2 18.5 %all-to-all-start = ((bf16[128,2,384]{2,1,0:T(2,128)(2,1)}), bf16[128,2,384]{2,1,0:T(2,128)(2,1)S(1)}, u32[]{:S(2)}, u32[]{:S(2)}) async-start(bf16[128,2,384]{2,1,0:T(2,128)(2,1)} %copy.34), calls=%async_computation | async-start | bytes 393216 | tf_op jit(solution)/shard_map/all_to_all | solution.py:93
  19.8 56.2 %all-gather.2.cloned.1.call-start = ((), (), s32[]{:S(2)}) async-start(), calls=%async_computation.3 | async-start | bytes 1671168 | tf_op jit(solution)/shard_map/all_gather | solution.py:108
  40.8 88.4 %reduce-scatter.2.cloned.1.call-start = ((), (), s32[]{:S(2)}) async-start(), calls=%async_computation.4 | async-start | bytes 3932160 | tf_op jit(solution)/shard_map/reduce_scatter | solution.py:113
  41.0 17.6 %collective-permute-start.6 = (bf16[384,768]{1,0:T(8,128)(2,1)S(1)}, bf16[384,768]{1,0:T(8,128)(2,1)S(1)}, u32[]{:S(2)}, u32[]{:S(2)}) collective-permute-start(bf16[384,768]{1,0:T(8,128)(2,1)S(1)} %get-tuple-element.8), channel_id=1, source_target_pairs={{0,48},{16,0},{32,16},{48,32},{1,49},{17,1},{33,17},{49,33},{2,50}... | collective-permute-start | bytes 1769480 | tf_op jit(solution)/shard_map/ppermute | solution.py:40
  41.9 17.5 %collective-permute-start.4 = (bf16[384,768]{1,0:T(8,128)(2,1)S(1)}, bf16[384,768]{1,0:T(8,128)(2,1)S(1)}, u32[]{:S(2)}, u32[]{:S(2)}) collective-permute-start(bf16[384,768]{1,0:T(8,128)(2,1)S(1)} %get-tuple-element.8), channel_id=1, source_target_pairs={{0,16},{16,32},{32,48},{48,0},{1,17},{17,33},{33,49},{49,1},{2,18}... | collective-permute-start | bytes 1769480 | tf_op jit(solution)/shard_map/ppermute | solution.py:39
  44.3 26.9 %collective-permute-start.2 = (bf16[384,768]{1,0:T(8,128)(2,1)S(1)}, bf16[384,768]{1,0:T(8,128)(2,1)S(1)}, u32[]{:S(2)}, u32[]{:S(2)}) collective-permute-start(bf16[384,768]{1,0:T(8,128)(2,1)S(1)} %get-tuple-element.9), channel_id=1, source_target_pairs={{0,48},{16,0},{32,16},{48,32},{1,49},{17,1},{33,17},{49,33},{2,50}... | collective-permute-start | bytes 1769480 | tf_op jit(solution)/shard_map/ppermute | solution.py:40
  44.3 27.7 %collective-permute-start = (bf16[384,768]{1,0:T(8,128)(2,1)S(1)}, bf16[384,768]{1,0:T(8,128)(2,1)S(1)}, u32[]{:S(2)}, u32[]{:S(2)}) collective-permute-start(bf16[384,768]{1,0:T(8,128)(2,1)S(1)} %get-tuple-element.9), channel_id=1, source_target_pairs={{0,16},{16,32},{32,48},{48,0},{1,17},{17,33},{33,49},{49,1},{2,18}... | collective-permute-start | bytes 1769480 | tf_op jit(solution)/shard_map/ppermute | solution.py:39
  58.5 17.5 %copy-start.1 = (bf16[384,768]{1,0:T(8,128)(2,1)}, bf16[384,768]{1,0:T(8,128)(2,1)S(1)}, u32[]{:S(2)}) copy-start(bf16[384,768]{1,0:T(8,128)(2,1)S(1)} %collective-permute-done.6.r1_ref) | copy-start | bytes 1769476
  59.3 23.4 %collective-permute-start.7 = (bf16[384,384]{1,0:T(8,128)(2,1)}, bf16[384,384]{1,0:T(8,128)(2,1)S(1)}, u32[]{:S(2)}, u32[]{:S(2)}) collective-permute-start(bf16[384,384]{1,0:T(8,128)(2,1)} %slice.37), channel_id=1, source_target_pairs={{0,48},{16,0},{32,16},{48,32},{1,49},{17,1},{33,17},{49,33},{2,50}... | collective-permute-start | bytes 884744 | tf_op jit(solution)/shard_map/ppermute | solution.py:44
  59.3 16.7 %copy-start.2 = (bf16[384,768]{1,0:T(8,128)(2,1)}, bf16[384,768]{1,0:T(8,128)(2,1)S(1)}, u32[]{:S(2)}) copy-start(bf16[384,768]{1,0:T(8,128)(2,1)S(1)} %collective-permute-done.4.l1_ref) | copy-start | bytes 1769476
  60.1 22.5 %collective-permute-start.5 = (bf16[384,384]{1,0:T(8,128)(2,1)}, bf16[384,384]{1,0:T(8,128)(2,1)S(1)}, u32[]{:S(2)}, u32[]{:S(2)}) collective-permute-start(bf16[384,384]{1,0:T(8,128)(2,1)} %slice.36), channel_id=1, source_target_pairs={{0,16},{16,32},{32,48},{48,0},{1,17},{17,33},{33,49},{49,1},{2,18}... | collective-permute-start | bytes 884744 | tf_op jit(solution)/shard_map/ppermute | solution.py:43
  71.2 4.8 %copy-start.3 = (bf16[384,768]{1,0:T(8,128)(2,1)}, bf16[384,768]{1,0:T(8,128)(2,1)S(1)}, u32[]{:S(2)}) copy-start(bf16[384,768]{1,0:T(8,128)(2,1)S(1)} %collective-permute-done.2.r0_ref) | copy-start | bytes 1769476
  72.0 10.8 %collective-permute-start.3 = (bf16[384,384]{1,0:T(8,128)(2,1)}, bf16[384,384]{1,0:T(8,128)(2,1)S(1)}, u32[]{:S(2)}, u32[]{:S(2)}) collective-permute-start(bf16[384,384]{1,0:T(8,128)(2,1)} %slice.35), channel_id=1, source_target_pairs={{0,48},{16,0},{32,16},{48,32},{1,49},{17,1},{33,17},{49,33},{2,50}... | collective-permute-start | bytes 884744 | tf_op jit(solution)/shard_map/ppermute | solution.py:44
  72.0 4.0 %copy-start.4 = (bf16[384,768]{1,0:T(8,128)(2,1)}, bf16[384,768]{1,0:T(8,128)(2,1)S(1)}, u32[]{:S(2)}) copy-start(bf16[384,768]{1,0:T(8,128)(2,1)S(1)} %collective-permute-done.l0_ref) | copy-start | bytes 1769476
  72.8 10.0 %collective-permute-start.1 = (bf16[384,384]{1,0:T(8,128)(2,1)}, bf16[384,384]{1,0:T(8,128)(2,1)S(1)}, u32[]{:S(2)}, u32[]{:S(2)}) collective-permute-start(bf16[384,384]{1,0:T(8,128)(2,1)} %slice.34), channel_id=1, source_target_pairs={{0,16},{16,32},{32,48},{48,0},{1,17},{17,33},{33,49},{49,1},{2,18}... | collective-permute-start | bytes 884744 | tf_op jit(solution)/shard_map/ppermute | solution.py:43
  82.7 0.7 copy-start.5
  82.7 0.8 copy-start.6
  82.7 0.9 copy-start.7
  83.7 0.7 copy-start.8
Sparse Core Ops, SparseCore 0:
  40.9 34.6 all-gather.1
  90.1 39.0 reduce-scatter.1

commit v9 on v8

--- a/solution.py
+++ b/solution.py
@@ -27,22 +27,23 @@
     return output.astype(jnp.bfloat16).reshape(seq, width)
 
 
-def ring_pieces(block, axis):
+def ring_near(block, axis, chunk, anchor):
     n = 4
-    to_right = [(i, (i + 1) % n) for i in range(n)]
-    to_left = [(i, (i - 1) % n) for i in range(n)]
     width = block.shape[1] // 2
-    near, far = [], []
-    lefts, rights = [], []
-    for c in range(2):
-        piece = block[:, c * width:(c + 1) * width]
-        lefts.append(lax.ppermute(piece, axis, to_right))
-        rights.append(lax.ppermute(piece, axis, to_left))
-    half = width // 2
-    for c in range(2):
-        far.append(lax.ppermute(lefts[c][:, :half], axis, to_right))
-        far.append(lax.ppermute(rights[c][:, half:], axis, to_left))
-    return (block, rights[0], rights[1], lefts[0], lefts[1]), tuple(far)
+    piece = block[:, chunk * width:(chunk + 1) * width]
+    from_left = lax.ppermute(piece, axis, [(i, (i + 1) % n) for i in range(n)])
+    from_right = lax.ppermute(piece, axis, [(i, (i - 1) % n) for i in range(n)])
+    return lax.optimization_barrier((from_left, from_right, anchor))
+
+
+def ring_far(lefts, rights, axis):
+    n = 4
+    half = lefts[0].shape[1] // 2
+    far = []
+    for from_left, from_right in zip(lefts, rights):
+        far.append(lax.ppermute(from_left[:, :half], axis, [(i, (i + 1) % n) for i in range(n)]))
+        far.append(lax.ppermute(from_right[:, half:], axis, [(i, (i - 1) % n) for i in range(n)]))
+    return tuple(far)
 
 
 def near_kernel(a_ref, w0_ref, r0_ref, r1_ref, l0_ref, l1_ref, o_ref):
@@ -87,7 +88,6 @@
 
 
 def per_device(q_seq, k_seq, v_seq, resid, ln_gain, w_up, n_x):
-    pieces = ring_pieces(w_up, "rx")
     attended = attention_block(q_seq, k_seq, v_seq)
     both = jnp.stack([resid, attended], axis=1)
     both = lax.all_to_all(both, "col", split_axis=0, concat_axis=1, tiled=True)
@@ -105,9 +105,12 @@
     rolled = lax.dynamic_slice_in_dim(doubled, lax.axis_index("rx"), n_x, axis=2).reshape(chunk, full_width)
     part = lax.all_to_all(rolled, "ry", split_axis=1, concat_axis=0, tiled=True)
     part = part.reshape(n_y, chunk, part.shape[1])
+    left0, right0, part = ring_near(w_up, "rx", 0, part)
+    left1, right1, part = ring_near(w_up, "rx", 1, part)
+    far = ring_far((left0, left1), (right0, right1), "rx")
+    near = (w_up, right0, right1, left0, left1)
     tokens = lax.all_gather(part, "col", axis=1, tiled=True)
     tokens = tokens.reshape(-1, tokens.shape[-1])
-    near, far = pieces
     partial = tiled_call(near_kernel, tokens, near)
     partial = tiled_call(far_kernel, tokens, far, extra=(partial,))
     product = lax.psum_scatter(partial, "ry", scatter_dimension=0, tiled=True)

time: 140 us -> 155 us (1.11)
  waiting for transfers between devices: 67.9 us -> 82.8 us
    all_gather x1, waiting for transfers between devices: 0.01 us -> 30.9 us  [per_device(): tokens = lax.all_gather(part, 'col', axis=1, tiled=True)]
    ppermute x8, waiting for transfers between devices: 18.8 us -> 9.7 us  [the longest x2 9.68 us: ring_near(): from_right = lax.ppermute(piece, axis, [(i, (i - 1) % n) for i in range(n)])]
    all_to_all x1, waiting for transfers between devices: 9.87 us -> 2.5 us  [per_device(): both = lax.all_to_all(both, 'col', split_axis=0, concat_axis=1, tiled=True)]
  transfers between devices with their start and end apart: 11 -> 11, of which waited for: 4 -> 4; matrix products, arithmetic and copies ran while one was open for 2% -> 3% of each run, Pallas kernels for 5% -> 4%
where the time goes in v9:
time: 155 us; the launch traced here: 154 us
  waiting for transfers between devices  82.8 us (53%)
  starting transfers between devices  21.6 us (14%)
  between operations  13.6 us (9%)
  Pallas kernels  12.3 us (8%)
  blocking collectives  10.2 us (7%)
  local copies, waits for them, and re-layouts  9.82 us (6%)
  other arithmetic  3.01 us (2%)
    reduce_scatter x1, waiting for transfers between devices, per_device(): product = lax.psum_scatter(partial, 'ry', scatter_dimension=0, tiled=True)  39.6 us
    all_gather x1, waiting for transfers between devices, per_device(): tokens = lax.all_gather(part, 'col', axis=1, tiled=True)  30.9 us
    pallas_call x2, Pallas kernels, tiled_call(): pl.pallas_call(kernel, grid=(m // tile,), in_specs=[rows(kk)] + [full(p)...  12.3 us
    all_to_all x1, blocking collectives, per_device(): part = lax.all_to_all(rolled, 'ry', split_axis=1, concat_axis=0, tiled=True)  10.2 us
    ppermute x2, waiting for transfers between devices, ring_near(): from_right = lax.ppermute(piece, axis, [(i, (i - 1) % n) for i in range(n)])  9.68 us
    all_to_all x1, starting transfers between devices, per_device(): both = lax.all_to_all(both, 'col', split_axis=0, concat_axis=1, tiled=True)  8.57 us
    ppermute x2, starting transfers between devices, ring_far(): lax.ppermute(from_left[:, :half], axis, [(i, (i + 1) % n) for i in range(...  6.47 us
    ppermute x2, starting transfers between devices, ring_near(): from_left = lax.ppermute(piece, axis, [(i, (i + 1) % n) for i in range(n)])  5.64 us
  transfers between devices with their start and end apart: 11, of which 4 were waited for; matrix products, arithmetic and copies ran while one was open for 3% of the time, Pallas kernels for 4%

profile of v9, /device:TPU:6, one launch (start us, length us, event | category | flops | bytes accessed | tf_op | source)
XLA Modules:
  0.0 153.7 jit_solution(6175802865176655960)
XLA Ops:
  6.6 1.0 copy.27
  7.6 1.0 copy.28
  8.9 1.0 copy.31
  10.4 0.9 copy.34
  11.3 8.6 %all-to-all-start = ((bf16[128,2,384]{2,1,0:T(2,128)(2,1)}), bf16[128,2,384]{2,1,0:T(2,128)(2,1)S(1)}, u32[]{:S(2)}, u32[]{:S(2)}) async-start(bf16[128,2,384]{2,1,0:T(2,128)(2,1)} %copy.34), calls=%async_computation | async-start | bytes 393216 | tf_op jit(solution)/shard_map/all_to_all | solution.py:93
  19.9 0.9 fusion.21
  20.8 0.8 collective-permute-start.3
  21.6 2.4 %collective-permute-start.2 = (bf16[384,768]{1,0:T(8,128)(2,1)}, bf16[384,768]{1,0:T(8,128)(2,1)S(1)}, u32[]{:S(2)}, u32[]{:S(2)}) collective-permute-start(bf16[384,768]{1,0:T(8,128)(2,1)} %get-tuple-element.20), channel_id=1, source_target_pairs={{0,16},{16,32},{32,48},{48,0},{1,17},{17,33},{33,49},{49,1},{2,18}... | collective-permute-start | bytes 1769480 | tf_op jit(solution)/shard_map/ppermute | solution.py:34
  24.0 3.2 %collective-permute-start = (bf16[384,768]{1,0:T(8,128)(2,1)S(1)}, bf16[384,768]{1,0:T(8,128)(2,1)S(1)}, u32[]{:S(2)}, u32[]{:S(2)}) collective-permute-start(bf16[384,768]{1,0:T(8,128)(2,1)S(1)} %get-tuple-element.21), channel_id=1, source_target_pairs={{0,16},{16,32},{32,48},{48,0},{1,17},{17,33},{33,49},{49,1},{2,18}... | collective-permute-start | bytes 1769480 | tf_op jit(solution)/shard_map/ppermute | solution.py:34
  27.3 2.5 %all-to-all-done = bf16[128,2,384]{2,1,0:T(2,128)(2,1)S(1)} async-done(((bf16[128,2,384]{2,1,0:T(2,128)(2,1)}), bf16[128,2,384]{2,1,0:T(2,128)(2,1)S(1)}, u32[]{:S(2)}, u32[]{:S(2)}) %all-to-all-start) | async-done | bytes 196640 | tf_op jit(solution)/shard_map/all_to_all | solution.py:93
  30.6 10.2 %all_to_all.31 = bf16[8,4,1536]{2,0,1:T(8,128)(2,1)} all-to-all(bf16[8,4,1536]{2,0,1:T(8,128)(2,1)S(1)} %bitcast.32), channel_id=1, replica_groups=mesh['ry'=4,'rx'=4,'col'=16] {'ry'}, dimensions={1} | all-to-all | bytes 196608 | tf_op jit(solution)/shard_map/all_to_all | solution.py:106
  40.8 9.7 %collective-permute-done.1.r1_ref = bf16[384,768]{1,0:T(8,128)(2,1)S(1)} collective-permute-done((bf16[384,768]{1,0:T(8,128)(2,1)S(1)}, bf16[384,768]{1,0:T(8,128)(2,1)S(1)}, u32[]{:S(2)}, u32[]{:S(2)}) %collective-permute-start.1) | collective-permute-done | bytes 589856 | tf_op jit(solution)/shard_map/ppermute | solution.py:35
  50.6 0.9 slice.28
  51.5 0.7 slice.29
  52.3 3.2 %collective-permute-start.4 = (bf16[384,384]{1,0:T(8,128)(2,1)}, bf16[384,384]{1,0:T(8,128)(2,1)S(1)}, u32[]{:S(2)}, u32[]{:S(2)}) collective-permute-start(bf16[384,384]{1,0:T(8,128)(2,1)} %slice.28), channel_id=1, source_target_pairs={{0,16},{16,32},{32,48},{48,0},{1,17},{17,33},{33,49},{49,1},{2,18}... | collective-permute-start | bytes 884744 | tf_op jit(solution)/shard_map/ppermute | solution.py:44
  55.5 0.8 slice.30
  56.2 0.8 slice.31
  57.0 3.2 %collective-permute-start.6 = (bf16[384,384]{1,0:T(8,128)(2,1)}, bf16[384,384]{1,0:T(8,128)(2,1)S(1)}, u32[]{:S(2)}, u32[]{:S(2)}) collective-permute-start(bf16[384,384]{1,0:T(8,128)(2,1)} %slice.30), channel_id=1, source_target_pairs={{0,16},{16,32},{32,48},{48,0},{1,17},{17,33},{33,49},{49,1},{2,18}... | collective-permute-start | bytes 884744 | tf_op jit(solution)/shard_map/ppermute | solution.py:44
  60.2 30.9 %all-gather.2.cloned.1.call-done = bf16[4,128,1536]{2,1,0:T(8,128)(2,1)} async-done(((bf16[4,8,1536]{2,1,0:T(8,128)(2,1)}), bf16[4,128,1536]{2,1,0:T(8,128)(2,1)}) %all-gather.2.cloned.1.call-update) | async-done | bytes 1572880 | tf_op jit(solution)/shard_map/all_gather | solution.py:112
  91.2 6.7 %shard_map.64.acc_ref = f32[512,1536]{1,0:T(8,128)} custom-call(bf16[512,1536]{1,0:T(8,128)(2,1)} %bitcast.27, bf16[384,1536]{1,0:T(8,128)(2,1)} %w0_ref.1, bf16[384,768]{1,0:T(8,128)(2,1)} %copy-done.1, bf16[384,768]{1,0:T(8,128)(2,1)} %copy-done.3, bf16[384,768]{1,0:T(8,128)(2,1)} %copy-done.2, bf16[384,768]{1,0:T(8,128)(2,1)} %copy-done.4), custom_call_target="tpu_custom_call" | custom-call | flops 1811939328 | bytes 8257536 | tf_op jit(solution)/shard_map/pallas_call | solution.py:79
  98.8 0.7 copy-done.8
  99.5 5.6 %shard_map.65 = f32[512,1536]{1,0:T(8,128)} custom-call(bf16[512,1536]{1,0:T(8,128)(2,1)} %bitcast.28, bf16[384,384]{1,0:T(8,128)(2,1)} %copy-done.6, bf16[384,384]{1,0:T(8,128)(2,1)} %copy-done.5, bf16[384,384]{1,0:T(8,128)(2,1)} %copy-done.8, bf16[384,384]{1,0:T(8,128)(2,1)} %copy-done.7, ...), custom_call_target="tpu_custom_call", output_to_operand_aliasing={{}: (5, {})} | custom-call | flops 603979776 | bytes 9043968 | tf_op jit(solution)/shard_map/pallas_call | solution.py:79
  105.2 39.6 %reduce-scatter.2.cloned.1.call-done = f32[128,1536]{1,0:T(8,128)} async-done(((f32[512,1536]{1,0:T(8,128)}), f32[128,1536]{1,0:T(8,128)}) %reduce-scatter.2.cloned.1.call-update) | async-done | bytes 786448 | tf_op jit(solution)/shard_map/reduce_scatter | solution.py:116
  144.8 2.1 %fusion.11 = bf16[128,1536]{1,0:T(8,128)(2,1)} fusion(f32[128,1536]{1,0:T(8,128)} %reduce-scatter.2.cloned.1.call-done), kind=kLoop, calls=%fused_computation.14 | loop fusion | flops 1769472 | bytes 1179648 | tf_op jit(solution)/shard_map/convert_element_type | solution.py:117
  (47 shorter events, 2.5 us)
Async XLA Ops:
  6.5 3.8 %copy-start.9 = (bf16[128,384]{1,0:T(8,128)(2,1)S(1)}, bf16[128,384]{1,0:T(8,128)(2,1)}, u32[]{:S(2)}) copy-start(bf16[128,384]{1,0:T(8,128)(2,1)} %param.9) | copy-start | bytes 294916
  8.6 11.3 %copy-start = (bf16[384,1536]{1,0:T(8,128)(2,1)S(1)}, bf16[384,1536]{1,0:T(8,128)(2,1)}, u32[]{:S(2)}) copy-start(bf16[384,1536]{1,0:T(8,128)(2,1)} %w0_ref.1) | copy-start | bytes 3538948
  10.4 16.9 %copy-start.10 = (f32[6144]{0:T(1024)S(1)}, f32[6144]{0:T(1024)}, u32[]{:S(2)}) copy-start(f32[6144]{0:T(1024)} %param.10) | copy-start | bytes 73732
  11.3 18.5 %all-to-all-start = ((bf16[128,2,384]{2,1,0:T(2,128)(2,1)}), bf16[128,2,384]{2,1,0:T(2,128)(2,1)S(1)}, u32[]{:S(2)}, u32[]{:S(2)}) async-start(bf16[128,2,384]{2,1,0:T(2,128)(2,1)} %copy.34), calls=%async_computation | async-start | bytes 393216 | tf_op jit(solution)/shard_map/all_to_all | solution.py:93
  19.8 71.3 %all-gather.2.cloned.1.call-start = ((), (), s32[]{:S(2)}) async-start(), calls=%async_computation.3 | async-start | bytes 1671168 | tf_op jit(solution)/shard_map/all_gather | solution.py:112
  20.8 20.0 %collective-permute-start.3 = (bf16[384,768]{1,0:T(8,128)(2,1)}, bf16[384,768]{1,0:T(8,128)(2,1)S(1)}, u32[]{:S(2)}, u32[]{:S(2)}) collective-permute-start(bf16[384,768]{1,0:T(8,128)(2,1)} %get-tuple-element.20), channel_id=1, source_target_pairs={{0,48},{16,0},{32,16},{48,32},{1,49},{17,1},{33,17},{49,33},{2,50}... | collective-permute-start | bytes 1769480 | tf_op jit(solution)/shard_map/ppermute | solution.py:35
  21.6 19.2 %collective-permute-start.2 = (bf16[384,768]{1,0:T(8,128)(2,1)}, bf16[384,768]{1,0:T(8,128)(2,1)S(1)}, u32[]{:S(2)}, u32[]{:S(2)}) collective-permute-start(bf16[384,768]{1,0:T(8,128)(2,1)} %get-tuple-element.20), channel_id=1, source_target_pairs={{0,16},{16,32},{32,48},{48,0},{1,17},{17,33},{33,49},{49,1},{2,18}... | collective-permute-start | bytes 1769480 | tf_op jit(solution)/shard_map/ppermute | solution.py:34
  24.0 26.5 %collective-permute-start.1 = (bf16[384,768]{1,0:T(8,128)(2,1)S(1)}, bf16[384,768]{1,0:T(8,128)(2,1)S(1)}, u32[]{:S(2)}, u32[]{:S(2)}) collective-permute-start(bf16[384,768]{1,0:T(8,128)(2,1)S(1)} %get-tuple-element.21), channel_id=1, source_target_pairs={{0,48},{16,0},{32,16},{48,32},{1,49},{17,1},{33,17},{49,33},{2,50}... | collective-permute-start | bytes 1769480 | tf_op jit(solution)/shard_map/ppermute | solution.py:35
  24.0 26.5 %collective-permute-start = (bf16[384,768]{1,0:T(8,128)(2,1)S(1)}, bf16[384,768]{1,0:T(8,128)(2,1)S(1)}, u32[]{:S(2)}, u32[]{:S(2)}) collective-permute-start(bf16[384,768]{1,0:T(8,128)(2,1)S(1)} %get-tuple-element.21), channel_id=1, source_target_pairs={{0,16},{16,32},{32,48},{48,0},{1,17},{17,33},{33,49},{49,1},{2,18}... | collective-permute-start | bytes 1769480 | tf_op jit(solution)/shard_map/ppermute | solution.py:34
  40.8 50.4 %copy-start.1 = (bf16[384,768]{1,0:T(8,128)(2,1)}, bf16[384,768]{1,0:T(8,128)(2,1)S(1)}, u32[]{:S(2)}) copy-start(bf16[384,768]{1,0:T(8,128)(2,1)S(1)} %collective-permute-done.3.r0_ref) | copy-start | bytes 1769476
  40.8 50.4 %copy-start.2 = (bf16[384,768]{1,0:T(8,128)(2,1)}, bf16[384,768]{1,0:T(8,128)(2,1)S(1)}, u32[]{:S(2)}) copy-start(bf16[384,768]{1,0:T(8,128)(2,1)S(1)} %collective-permute-done.2.l0_ref) | copy-start | bytes 1769476
  50.5 40.7 %copy-start.3 = (bf16[384,768]{1,0:T(8,128)(2,1)}, bf16[384,768]{1,0:T(8,128)(2,1)S(1)}, u32[]{:S(2)}) copy-start(bf16[384,768]{1,0:T(8,128)(2,1)S(1)} %collective-permute-done.1.r1_ref) | copy-start | bytes 1769476
  50.5 40.7 %copy-start.4 = (bf16[384,768]{1,0:T(8,128)(2,1)}, bf16[384,768]{1,0:T(8,128)(2,1)S(1)}, u32[]{:S(2)}) copy-start(bf16[384,768]{1,0:T(8,128)(2,1)S(1)} %collective-permute-done.l1_ref) | copy-start | bytes 1769476
  50.6 94.2 %reduce-scatter.2.cloned.1.call-start = ((), (), s32[]{:S(2)}) async-start(), calls=%async_computation.4 | async-start | bytes 3932160 | tf_op jit(solution)/shard_map/reduce_scatter | solution.py:116
  52.2 45.6 %collective-permute-start.5 = (bf16[384,384]{1,0:T(8,128)(2,1)}, bf16[384,384]{1,0:T(8,128)(2,1)S(1)}, u32[]{:S(2)}, u32[]{:S(2)}) collective-permute-start(bf16[384,384]{1,0:T(8,128)(2,1)} %slice.29), channel_id=1, source_target_pairs={{0,48},{16,0},{32,16},{48,32},{1,49},{17,1},{33,17},{49,33},{2,50}... | collective-permute-start | bytes 884744 | tf_op jit(solution)/shard_map/ppermute | solution.py:45
  52.3 45.6 %collective-permute-start.4 = (bf16[384,384]{1,0:T(8,128)(2,1)}, bf16[384,384]{1,0:T(8,128)(2,1)S(1)}, u32[]{:S(2)}, u32[]{:S(2)}) collective-permute-start(bf16[384,384]{1,0:T(8,128)(2,1)} %slice.28), channel_id=1, source_target_pairs={{0,16},{16,32},{32,48},{48,0},{1,17},{17,33},{33,49},{49,1},{2,18}... | collective-permute-start | bytes 884744 | tf_op jit(solution)/shard_map/ppermute | solution.py:44
  57.0 40.9 %collective-permute-start.7 = (bf16[384,384]{1,0:T(8,128)(2,1)}, bf16[384,384]{1,0:T(8,128)(2,1)S(1)}, u32[]{:S(2)}, u32[]{:S(2)}) collective-permute-start(bf16[384,384]{1,0:T(8,128)(2,1)} %slice.31), channel_id=1, source_target_pairs={{0,48},{16,0},{32,16},{48,32},{1,49},{17,1},{33,17},{49,33},{2,50}... | collective-permute-start | bytes 884744 | tf_op jit(solution)/shard_map/ppermute | solution.py:45
  57.0 40.9 %collective-permute-start.6 = (bf16[384,384]{1,0:T(8,128)(2,1)}, bf16[384,384]{1,0:T(8,128)(2,1)S(1)}, u32[]{:S(2)}, u32[]{:S(2)}) collective-permute-start(bf16[384,384]{1,0:T(8,128)(2,1)} %slice.30), channel_id=1, source_target_pairs={{0,16},{16,32},{32,48},{48,0},{1,17},{17,33},{33,49},{49,1},{2,18}... | collective-permute-start | bytes 884744 | tf_op jit(solution)/shard_map/ppermute | solution.py:44
  97.9 0.7 copy-start.5
  97.9 0.8 copy-start.6
  97.9 0.9 copy-start.7
  98.8 0.7 copy-start.8
Sparse Core Ops, SparseCore 0:
  50.7 40.4 all-gather.1
  105.3 39.4 reduce-scatter.1

commit v10 on v6

--- a/solution.py
+++ b/solution.py
@@ -39,7 +39,7 @@
     return block, from_right, far_low, far_high, from_left
 
 
-def pieces_kernel(a_ref, w0_ref, w1_ref, w2lo_ref, w2hi_ref, w3_ref, o_ref):
+def pieces_kernel(a_ref, w0_ref, w1_ref, w2lo_ref, w2hi_ref, w3_ref, lo_ref, hi_ref):
     k = w0_ref.shape[0]
     half = w2lo_ref.shape[1]
     a = a_ref[...]
@@ -47,24 +47,42 @@
     base = base + jnp.dot(a[:, k:2 * k], w1_ref[...], preferred_element_type=jnp.float32)
     base = base + jnp.dot(a[:, 3 * k:4 * k], w3_ref[...], preferred_element_type=jnp.float32)
     far = a[:, 2 * k:3 * k]
-    o_ref[:, 0:half] = base[:, 0:half] + jnp.dot(far, w2lo_ref[...], preferred_element_type=jnp.float32)
-    o_ref[:, half:] = base[:, half:] + jnp.dot(far, w2hi_ref[...], preferred_element_type=jnp.float32)
+    lo_ref[...] = base[:, 0:half] + jnp.dot(far, w2lo_ref[...], preferred_element_type=jnp.float32)
+    hi_ref[...] = base[:, half:] + jnp.dot(far, w2hi_ref[...], preferred_element_type=jnp.float32)
 
 
 def dot_pieces(a, pieces, tile=128):
     m, kk = a.shape
     n = pieces[0].shape[1]
     full = lambda p: pl.BlockSpec(p.shape, lambda i: (0, 0))
+    half_spec = pl.BlockSpec((tile, n // 2), lambda i: (i, 0))
+    half_shape = jax.ShapeDtypeStruct((m, n // 2), jnp.float32)
     return pl.pallas_call(
         pieces_kernel,
         grid=(m // tile,),
         in_specs=[pl.BlockSpec((tile, kk), lambda i: (i, 0))] + [full(p) for p in pieces],
-        out_specs=pl.BlockSpec((tile, n), lambda i: (i, 0)),
-        out_shape=jax.ShapeDtypeStruct((m, n), jnp.float32),
+        out_specs=(half_spec, half_spec),
+        out_shape=(half_shape, half_shape),
         cost_estimate=pl.CostEstimate(
             flops=2 * m * kk * n, transcendentals=0, bytes_accessed=a.size * 2 + sum(p.size * 2 for p in pieces) + m * n * 4
         ),
     )(a, *pieces)
+
+
+def ring_reduce_scatter(x, axis, n):
+    me = lax.axis_index(axis)
+    half = x.shape[2] // 2
+    out = []
+    for step_dir, cols in ((1, slice(0, half)), (-1, slice(half, None))):
+        part = x[:, :, cols]
+        perm = [(i, (i + step_dir) % n) for i in range(n)]
+        acc = lax.dynamic_index_in_dim(part, (me - step_dir) % n, 0, keepdims=False)
+        for k in range(n - 1):
+            got = lax.ppermute(acc, axis, perm)
+            seg = (me - step_dir * (k + 2)) % n
+            acc = got + lax.dynamic_index_in_dim(part, seg, 0, keepdims=False)
+        out.append(acc)
+    return jnp.concatenate(out, axis=1)
 
 
 def per_device(q_seq, k_seq, v_seq, resid, ln_gain, w_up, n_x):
@@ -88,8 +106,10 @@
     part = part.reshape(n_y, chunk, part.shape[1])
     tokens = lax.all_gather(part, "col", axis=1, tiled=True)
     tokens = tokens.reshape(-1, tokens.shape[-1])
-    partial = dot_pieces(tokens, pieces)
-    product = lax.psum_scatter(partial, "ry", scatter_dimension=0, tiled=True)
+    low, high = dot_pieces(tokens, pieces)
+    product_low = lax.psum_scatter(low, "ry", scatter_dimension=0, tiled=True)
+    product_high = ring_reduce_scatter(high.reshape(n_y, -1, high.shape[1]), "ry", n_y)
+    product = jnp.concatenate([product_low, product_high], axis=1)
     return jax.nn.gelu(product, approximate=True).astype(jnp.bfloat16)
 
 

time: 139 us -> 135 us (0.971); the launches traced: 138 us -> 135 us
  waiting for transfers between devices: 82 us -> 73 us
  starting transfers between devices: 14.6 us -> 20.6 us
    reduce_scatter x1, waiting for transfers between devices: 35.3 us -> 0.02 us  [per_device(): product_low = lax.psum_scatter(low, 'ry', scatter_dimension=0, tiled=True)]
    ppermute x1, waiting for transfers between devices: 0.01 us -> 25.3 us  [ring_pieces(): from_left = lax.ppermute(block, axis, to_right)]
    ppermute x1, waiting for transfers between devices: 25.3 us -> 0.01 us  [ring_pieces(): from_right = lax.ppermute(block, axis, to_left)]
    ppermute x0 -> x6, waiting for transfers between devices: none -> 23.5 us  [ring_reduce_scatter(): got = lax.ppermute(acc, axis, perm)]
    ppermute x1, waiting for transfers between devices: 0.01 us -> 11.7 us  [ring_pieces(): far_low = lax.ppermute(from_left[:, :half], axis, to_right)]
    ppermute x1, waiting for transfers between devices: 11.6 us -> 2.63 us  [ring_pieces(): far_high = lax.ppermute(from_right[:, half:], axis, to_left)]
    ppermute x0 -> x6, starting transfers between devices: none -> 7.66 us  [ring_reduce_scatter(): got = lax.ppermute(acc, axis, perm)]
    ppermute x1, starting transfers between devices: 2.41 us -> 0.55 us  [ring_pieces(): from_left = lax.ppermute(block, axis, to_right)]
  transfers between devices with their start and end apart: 7 -> 13, of which waited for: 4 -> 10; matrix products, arithmetic and copies ran while one was open for 0% -> 0% of each run, Pallas kernels for 0% -> 0%
where the time goes in v10:
time: 135 us
  waiting for transfers between devices  73 us (54%)
  starting transfers between devices  20.6 us (15%)
  between operations  13.6 us (10%)
  blocking collectives  10.2 us (8%)
  Pallas kernels  7.52 us (6%)
  local copies, waits for them, and re-layouts  6.56 us (5%)
  other arithmetic  3.02 us (2%)
    ppermute x1, waiting for transfers between devices, ring_pieces(): from_left = lax.ppermute(block, axis, to_right)  25.3 us
    ppermute x6, waiting for transfers between devices, ring_reduce_scatter(): got = lax.ppermute(acc, axis, perm)  23.5 us
    ppermute x1, waiting for transfers between devices, ring_pieces(): far_low = lax.ppermute(from_left[:, :half], axis, to_right)  11.7 us
    all_to_all x1, blocking collectives, per_device(): part = lax.all_to_all(rolled, 'ry', split_axis=1, concat_axis=0, tiled=True)  10.2 us
    all_to_all x1, waiting for transfers between devices, per_device(): both = lax.all_to_all(both, 'col', split_axis=0, concat_axis=1, tiled=True)  9.87 us
    all_to_all x1, starting transfers between devices, per_device(): both = lax.all_to_all(both, 'col', split_axis=0, concat_axis=1, tiled=True)  8.57 us
    ppermute x6, starting transfers between devices, ring_reduce_scatter(): got = lax.ppermute(acc, axis, perm)  7.66 us
    pallas_call x1, Pallas kernels, dot_pieces(): pl.pallas_call(pieces_kernel, grid=(m // tile,), in_specs=[pl.BlockSpec((...  7.52 us
  transfers between devices with their start and end apart: 13, of which 10 were waited for; matrix products, arithmetic and copies ran while one was open for 0% of the time, Pallas kernels for 0%

profile of v10, /device:TPU:6, one launch (start us, length us, event | category | flops | bytes accessed | tf_op | source)
XLA Modules:
  0.0 135.0 jit_solution(18041996605387193850)
XLA Ops:
  6.6 1.0 copy.30
  7.6 1.0 copy.26
  8.6 1.0 copy.27
  11.2 8.6 %all-to-all-start = ((bf16[128,2,384]{2,1,0:T(2,128)(2,1)}), bf16[128,2,384]{2,1,0:T(2,128)(2,1)S(1)}, u32[]{:S(2)}, u32[]{:S(2)}) async-start(bf16[128,2,384]{2,1,0:T(2,128)(2,1)} %copy.33), calls=%async_computation | async-start | bytes 393216 | tf_op jit(solution)/shard_map/all_to_all | solution.py:92
  19.9 9.9 %all-to-all-done = bf16[128,2,384]{2,1,0:T(2,128)(2,1)S(1)} async-done(((bf16[128,2,384]{2,1,0:T(2,128)(2,1)}), bf16[128,2,384]{2,1,0:T(2,128)(2,1)S(1)}, u32[]{:S(2)}, u32[]{:S(2)}) %all-to-all-start) | async-done | bytes 196640 | tf_op jit(solution)/shard_map/all_to_all | solution.py:92
  30.6 10.2 %all_to_all.31 = bf16[8,4,1536]{2,0,1:T(8,128)(2,1)} all-to-all(bf16[8,4,1536]{2,0,1:T(8,128)(2,1)S(1)} %bitcast.48), channel_id=1, replica_groups=mesh['ry'=4,'rx'=4,'col'=16] {'ry'}, dimensions={1} | all-to-all | bytes 196608 | tf_op jit(solution)/shard_map/all_to_all | solution.py:105
  41.4 1.5 %collective-permute-start = (bf16[384,1536]{1,0:T(8,128)(2,1)S(1)}, bf16[384,1536]{1,0:T(8,128)(2,1)S(1)}, u32[]{:S(2)}, u32[]{:S(2)}) collective-permute-start(bf16[384,1536]{1,0:T(8,128)(2,1)S(1)} %copy-done.5), channel_id=1, source_target_pairs={{0,48},{16,0},{32,16},{48,32},{1,49},{17,1},{33,17},{49,33},{2,50}... | collective-permute-start | bytes 3538952 | tf_op jit(solution)/shard_map/ppermute | solution.py:35
  43.0 25.3 %collective-permute-done.1.w3_ref = bf16[384,1536]{1,0:T(8,128)(2,1)S(1)} collective-permute-done((bf16[384,1536]{1,0:T(8,128)(2,1)S(1)}, bf16[384,1536]{1,0:T(8,128)(2,1)S(1)}, u32[]{:S(2)}, u32[]{:S(2)}) %collective-permute-start.1) | collective-permute-done | bytes 1179680 | tf_op jit(solution)/shard_map/ppermute | solution.py:34
  68.3 1.8 %collective-permute-start.2 = (bf16[384,768]{1,0:T(8,128)(2,1)S(1)}, bf16[384,768]{1,0:T(8,128)(2,1)S(1)}, u32[]{:S(2)}, u32[]{:S(2)}) collective-permute-start(bf16[384,768]{1,0:T(8,128)(2,1)S(1)} %slice.26), channel_id=1, source_target_pairs={{0,16},{16,32},{32,48},{48,0},{1,17},{17,33},{33,49},{49,1},{2,18}... | collective-permute-start | bytes 1769480 | tf_op jit(solution)/shard_map/ppermute | solution.py:37
  70.5 11.7 %collective-permute-done.2.w2lo_ref = bf16[384,768]{1,0:T(8,128)(2,1)S(1)} collective-permute-done((bf16[384,768]{1,0:T(8,128)(2,1)S(1)}, bf16[384,768]{1,0:T(8,128)(2,1)S(1)}, u32[]{:S(2)}, u32[]{:S(2)}) %collective-permute-start.2) | collective-permute-done | bytes 589856 | tf_op jit(solution)/shard_map/ppermute | solution.py:37
  82.2 2.6 %collective-permute-done.3.w2hi_ref = bf16[384,768]{1,0:T(8,128)(2,1)S(1)} collective-permute-done((bf16[384,768]{1,0:T(8,128)(2,1)S(1)}, bf16[384,768]{1,0:T(8,128)(2,1)S(1)}, u32[]{:S(2)}, u32[]{:S(2)}) %collective-permute-start.3) | collective-permute-done | bytes 589856 | tf_op jit(solution)/shard_map/ppermute | solution.py:38
  85.7 7.5 %shard_map.64 = (f32[512,768]{1,0:T(8,128)}, f32[512,768]{1,0:T(8,128)}) custom-call(bf16[512,1536]{1,0:T(8,128)(2,1)} %bitcast.54, bf16[384,1536]{1,0:T(8,128)(2,1)} %w0_ref.1, bf16[384,1536]{1,0:T(8,128)(2,1)} %copy-done.2, bf16[384,768]{1,0:T(8,128)(2,1)} %copy-done.6, bf16[384,768]{1,0:T(8,128)(2,1)} %copy-done.7, bf16[384,1536]{1,0:T(8,128)(2,1)} %copy-done.1), custom_call_target="tpu_custom_call" | custom-call | flops 2415919104 | bytes 9437184 | tf_op jit(solution)/shard_map/pallas_call | solution.py:60
  93.3 1.4 %copy-done = f32[512,768]{1,0:T(8,128)S(1)} copy-done((f32[512,768]{1,0:T(8,128)S(1)}, f32[512,768]{1,0:T(8,128)}, u32[]{:S(2)}) %copy-start) | copy-done | bytes 1572888
  94.8 1.2 collective-permute-start.7
  97.0 5.8 %collective-permute-done.7 = f32[128,384]{1,0:T(8,128)S(1)} collective-permute-done((f32[128,384]{1,0:T(8,128)S(1)}, f32[128,384]{1,0:T(8,128)S(1)}, u32[]{:S(2)}, u32[]{:S(2)}) %collective-permute-start.7) | collective-permute-done | bytes 196640 | tf_op jit(solution)/shard_map/ppermute | solution.py:81
  102.8 1.9 %collective-permute-start.8 = (f32[128,384]{1,0:T(8,128)S(1)}, f32[128,384]{1,0:T(8,128)S(1)}, u32[]{:S(2)}, u32[]{:S(2)}) collective-permute-start(f32[128,384]{1,0:T(8,128)S(1)} %bitcast_add_fusion.2), channel_id=1, source_target_pairs={{0,192},{64,0},{128,64},{192,128},{1,193},{65,1},{129,65},{193,129... | collective-permute-start | bytes 589832 | tf_op jit(solution)/shard_map/ppermute | solution.py:81
  104.7 1.8 %collective-permute-done.4 = f32[128,384]{1,0:T(8,128)S(1)} collective-permute-done((f32[128,384]{1,0:T(8,128)S(1)}, f32[128,384]{1,0:T(8,128)S(1)}, u32[]{:S(2)}, u32[]{:S(2)}) %collective-permute-start.4) | collective-permute-done | bytes 196640 | tf_op jit(solution)/shard_map/ppermute | solution.py:81
  106.5 1.0 collective-permute-start.5
  107.5 6.6 %collective-permute-done.8 = f32[128,384]{1,0:T(8,128)S(1)} collective-permute-done((f32[128,384]{1,0:T(8,128)S(1)}, f32[128,384]{1,0:T(8,128)S(1)}, u32[]{:S(2)}, u32[]{:S(2)}) %collective-permute-start.8) | collective-permute-done | bytes 196640 | tf_op jit(solution)/shard_map/ppermute | solution.py:81
  114.1 2.5 %collective-permute-start.9 = (f32[128,384]{1,0:T(8,128)S(1)}, f32[128,384]{1,0:T(8,128)S(1)}, u32[]{:S(2)}, u32[]{:S(2)}) collective-permute-start(f32[128,384]{1,0:T(8,128)S(1)} %bitcast_add_fusion.1), channel_id=1, source_target_pairs={{0,192},{64,0},{128,64},{192,128},{1,193},{65,1},{129,65},{193,129... | collective-permute-start | bytes 589832 | tf_op jit(solution)/shard_map/ppermute | solution.py:81
  116.7 2.5 %collective-permute-done.5 = f32[128,384]{1,0:T(8,128)S(1)} collective-permute-done((f32[128,384]{1,0:T(8,128)S(1)}, f32[128,384]{1,0:T(8,128)S(1)}, u32[]{:S(2)}, u32[]{:S(2)}) %collective-permute-start.5) | collective-permute-done | bytes 196640 | tf_op jit(solution)/shard_map/ppermute | solution.py:81
  119.3 2.3 %collective-permute-done.9 = f32[128,384]{1,0:T(8,128)S(1)} collective-permute-done((f32[128,384]{1,0:T(8,128)S(1)}, f32[128,384]{1,0:T(8,128)S(1)}, u32[]{:S(2)}, u32[]{:S(2)}) %collective-permute-start.9) | collective-permute-done | bytes 196640 | tf_op jit(solution)/shard_map/ppermute | solution.py:81
  121.6 4.5 %collective-permute-done.6 = f32[128,384]{1,0:T(8,128)S(1)} collective-permute-done((f32[128,384]{1,0:T(8,128)S(1)}, f32[128,384]{1,0:T(8,128)S(1)}, u32[]{:S(2)}, u32[]{:S(2)}) %collective-permute-start.6) | collective-permute-done | bytes 196640 | tf_op jit(solution)/shard_map/ppermute | solution.py:81
  126.2 2.0 %fusion.11 = bf16[128,1536]{1,0:T(8,128)(2,1)} fusion(f32[128,384]{1,0:T(8,128)S(1)} %bitcast_add_fusion, f32[128,384]{1,0:T(8,128)S(1)} %bitcast_add_fusion.3, f32[128,768]{1,0:T(8,128)} %reduce-scatter.2.cloned.1.call-done), kind=kLoop, calls=%fused_computation.14 | loop fusion | flops 2162688 | bytes 1179648 | tf_op jit(solution)/shard_map/convert_element_type | solution.py:113
  (50 shorter events, 5.7 us)
Async XLA Ops:
  6.5 3.8 %copy-start.3 = (bf16[128,384]{1,0:T(8,128)(2,1)S(1)}, bf16[128,384]{1,0:T(8,128)(2,1)}, u32[]{:S(2)}) copy-start(bf16[128,384]{1,0:T(8,128)(2,1)} %param.9) | copy-start | bytes 294916
  8.6 11.3 %copy-start.4 = (f32[6144]{0:T(1024)S(1)}, f32[6144]{0:T(1024)}, u32[]{:S(2)}) copy-start(f32[6144]{0:T(1024)} %param.10) | copy-start | bytes 73732
  10.3 30.6 %copy-start.5 = (bf16[384,1536]{1,0:T(8,128)(2,1)S(1)}, bf16[384,1536]{1,0:T(8,128)(2,1)}, u32[]{:S(2)}) copy-start(bf16[384,1536]{1,0:T(8,128)(2,1)} %w0_ref.1) | copy-start | bytes 3538948
  11.2 18.5 %all-to-all-start = ((bf16[128,2,384]{2,1,0:T(2,128)(2,1)}), bf16[128,2,384]{2,1,0:T(2,128)(2,1)S(1)}, u32[]{:S(2)}, u32[]{:S(2)}) async-start(bf16[128,2,384]{2,1,0:T(2,128)(2,1)} %copy.33), calls=%async_computation | async-start | bytes 393216 | tf_op jit(solution)/shard_map/all_to_all | solution.py:92
  19.8 65.1 %all-gather.2.cloned.1.call-start = ((), (), s32[]{:S(2)}) async-start(), calls=%async_computation.3 | async-start | bytes 1671168 | tf_op jit(solution)/shard_map/all_gather | solution.py:107
  40.8 85.4 %reduce-scatter.2.cloned.1.call-start = ((), (), s32[]{:S(2)}) async-start(), calls=%async_computation.4 | async-start | bytes 1966080 | tf_op jit(solution)/shard_map/reduce_scatter | solution.py:110
  40.9 27.4 %collective-permute-start.1 = (bf16[384,1536]{1,0:T(8,128)(2,1)S(1)}, bf16[384,1536]{1,0:T(8,128)(2,1)S(1)}, u32[]{:S(2)}, u32[]{:S(2)}) collective-permute-start(bf16[384,1536]{1,0:T(8,128)(2,1)S(1)} %copy-done.5), channel_id=1, source_target_pairs={{0,16},{16,32},{32,48},{48,0},{1,17},{17,33},{33,49},{49,1},{2,18}... | collective-permute-start | bytes 3538952 | tf_op jit(solution)/shard_map/ppermute | solution.py:34
  41.4 28.6 %collective-permute-start = (bf16[384,1536]{1,0:T(8,128)(2,1)S(1)}, bf16[384,1536]{1,0:T(8,128)(2,1)S(1)}, u32[]{:S(2)}, u32[]{:S(2)}) collective-permute-start(bf16[384,1536]{1,0:T(8,128)(2,1)S(1)} %copy-done.5), channel_id=1, source_target_pairs={{0,48},{16,0},{32,16},{48,32},{1,49},{17,1},{33,17},{49,33},{2,50}... | collective-permute-start | bytes 3538952 | tf_op jit(solution)/shard_map/ppermute | solution.py:35
  68.3 16.6 %copy-start.1 = (bf16[384,1536]{1,0:T(8,128)(2,1)}, bf16[384,1536]{1,0:T(8,128)(2,1)S(1)}, u32[]{:S(2)}) copy-start(bf16[384,1536]{1,0:T(8,128)(2,1)S(1)} %collective-permute-done.1.w3_ref) | copy-start | bytes 3538948
  68.3 13.9 %collective-permute-start.2 = (bf16[384,768]{1,0:T(8,128)(2,1)S(1)}, bf16[384,768]{1,0:T(8,128)(2,1)S(1)}, u32[]{:S(2)}, u32[]{:S(2)}) collective-permute-start(bf16[384,768]{1,0:T(8,128)(2,1)S(1)} %slice.26), channel_id=1, source_target_pairs={{0,16},{16,32},{32,48},{48,0},{1,17},{17,33},{33,49},{49,1},{2,18}... | collective-permute-start | bytes 1769480 | tf_op jit(solution)/shard_map/ppermute | solution.py:37
  70.1 12.2 %copy-start.2 = (bf16[384,1536]{1,0:T(8,128)(2,1)}, bf16[384,1536]{1,0:T(8,128)(2,1)S(1)}, u32[]{:S(2)}) copy-start(bf16[384,1536]{1,0:T(8,128)(2,1)S(1)} %collective-permute-done.w1_ref) | copy-start | bytes 3538948
  70.1 14.7 %collective-permute-start.3 = (bf16[384,768]{1,0:T(8,128)(2,1)S(1)}, bf16[384,768]{1,0:T(8,128)(2,1)S(1)}, u32[]{:S(2)}, u32[]{:S(2)}) collective-permute-start(bf16[384,768]{1,0:T(8,128)(2,1)S(1)} %slice.27), channel_id=1, source_target_pairs={{0,48},{16,0},{32,16},{48,32},{1,49},{17,1},{33,17},{49,33},{2,50}... | collective-permute-start | bytes 1769480 | tf_op jit(solution)/shard_map/ppermute | solution.py:38
  82.2 2.6 %copy-start.6 = (bf16[384,768]{1,0:T(8,128)(2,1)}, bf16[384,768]{1,0:T(8,128)(2,1)S(1)}, u32[]{:S(2)}) copy-start(bf16[384,768]{1,0:T(8,128)(2,1)S(1)} %collective-permute-done.2.w2lo_ref) | copy-start | bytes 1769476
  84.9 0.9 copy-start.7
  93.2 1.4 %copy-start = (f32[512,768]{1,0:T(8,128)S(1)}, f32[512,768]{1,0:T(8,128)}, u32[]{:S(2)}) copy-start(f32[512,768]{1,0:T(8,128)} %get-tuple-element.8) | copy-start | bytes 4718596
  94.8 8.0 %collective-permute-start.7 = (f32[128,384]{1,0:T(8,128)S(1)}, f32[128,384]{1,0:T(8,128)S(1)}, u32[]{:S(2)}, u32[]{:S(2)}) collective-permute-start(f32[128,384]{1,0:T(8,128)S(1)} %dynamic-slice_bitcast_fusion), channel_id=1, source_target_pairs={{0,192},{64,0},{128,64},{192,128},{1,193},{65,1},{129,65},{193,129... | collective-permute-start | bytes 589832 | tf_op jit(solution)/shard_map/ppermute | solution.py:81
  96.1 10.4 %collective-permute-start.4 = (f32[128,384]{1,0:T(8,128)S(1)}, f32[128,384]{1,0:T(8,128)S(1)}, u32[]{:S(2)}, u32[]{:S(2)}) collective-permute-start(f32[128,384]{1,0:T(8,128)S(1)} %dynamic-slice_bitcast_fusion.1), channel_id=1, source_target_pairs={{0,64},{64,128},{128,192},{192,0},{1,65},{65,129},{129,193},{193,1... | collective-permute-start | bytes 589832 | tf_op jit(solution)/shard_map/ppermute | solution.py:81
  102.8 11.3 %collective-permute-start.8 = (f32[128,384]{1,0:T(8,128)S(1)}, f32[128,384]{1,0:T(8,128)S(1)}, u32[]{:S(2)}, u32[]{:S(2)}) collective-permute-start(f32[128,384]{1,0:T(8,128)S(1)} %bitcast_add_fusion.2), channel_id=1, source_target_pairs={{0,192},{64,0},{128,64},{192,128},{1,193},{65,1},{129,65},{193,129... | collective-permute-start | bytes 589832 | tf_op jit(solution)/shard_map/ppermute | solution.py:81
  106.5 12.6 %collective-permute-start.5 = (f32[128,384]{1,0:T(8,128)S(1)}, f32[128,384]{1,0:T(8,128)S(1)}, u32[]{:S(2)}, u32[]{:S(2)}) collective-permute-start(f32[128,384]{1,0:T(8,128)S(1)} %bitcast_add_fusion.5), channel_id=1, source_target_pairs={{0,64},{64,128},{128,192},{192,0},{1,65},{65,129},{129,193},{193,1... | collective-permute-start | bytes 589832 | tf_op jit(solution)/shard_map/ppermute | solution.py:81
  114.1 7.5 %collective-permute-start.9 = (f32[128,384]{1,0:T(8,128)S(1)}, f32[128,384]{1,0:T(8,128)S(1)}, u32[]{:S(2)}, u32[]{:S(2)}) collective-permute-start(f32[128,384]{1,0:T(8,128)S(1)} %bitcast_add_fusion.1), channel_id=1, source_target_pairs={{0,192},{64,0},{128,64},{192,128},{1,193},{65,1},{129,65},{193,129... | collective-permute-start | bytes 589832 | tf_op jit(solution)/shard_map/ppermute | solution.py:81
  119.2 7.0 %collective-permute-start.6 = (f32[128,384]{1,0:T(8,128)S(1)}, f32[128,384]{1,0:T(8,128)S(1)}, u32[]{:S(2)}, u32[]{:S(2)}) collective-permute-start(f32[128,384]{1,0:T(8,128)S(1)} %bitcast_add_fusion.4), channel_id=1, source_target_pairs={{0,64},{64,128},{128,192},{192,0},{1,65},{65,129},{129,193},{193,1... | collective-permute-start | bytes 589832 | tf_op jit(solution)/shard_map/ppermute | solution.py:81
Sparse Core Ops, SparseCore 0:
  40.9 34.6 all-gather.1
  93.4 29.5 reduce-scatter.1

commit v11 on v10

--- a/solution.py
+++ b/solution.py
@@ -104,12 +104,13 @@
     rolled = lax.dynamic_slice_in_dim(doubled, lax.axis_index("rx"), n_x, axis=2).reshape(chunk, full_width)
     part = lax.all_to_all(rolled, "ry", split_axis=1, concat_axis=0, tiled=True)
     part = part.reshape(n_y, chunk, part.shape[1])
-    tokens = lax.all_gather(part, "col", axis=1, tiled=True)
+    n_col = lax.axis_size("col")
+    spread_out = jnp.broadcast_to(part[:, None], (part.shape[0], n_col) + part.shape[1:])
+    tokens = lax.all_to_all(spread_out, "col", split_axis=1, concat_axis=1, tiled=True)
     tokens = tokens.reshape(-1, tokens.shape[-1])
     low, high = dot_pieces(tokens, pieces)
-    product_low = lax.psum_scatter(low, "ry", scatter_dimension=0, tiled=True)
-    product_high = ring_reduce_scatter(high.reshape(n_y, -1, high.shape[1]), "ry", n_y)
-    product = jnp.concatenate([product_low, product_high], axis=1)
+    partial = jnp.concatenate([low, high], axis=1)
+    product = ring_reduce_scatter(partial.reshape(n_y, -1, partial.shape[1]), "ry", n_y)
     return jax.nn.gelu(product, approximate=True).astype(jnp.bfloat16)
 
 

time: 135 us -> 135 us (level)
  between operations: 13.6 us -> 0.19 us
  other arithmetic: 3.02 us -> 11.8 us
  starting transfers between devices: 20.6 us -> 24.9 us
  waiting for transfers between devices: 73 us -> 69.8 us
  local copies, waits for them, and re-layouts: 6.56 us -> 9.71 us
    ppermute x1, waiting for transfers between devices: 11.7 us -> 4.08 us  [ring_pieces(): far_low = lax.ppermute(from_left[:, :half], axis, to_right)]
    add x6, other arithmetic: 0.14 us -> 7.72 us  [ring_reduce_scatter(): acc = got + lax.dynamic_index_in_dim(part, seg, 0, keepdims=False)]
    all_to_all x0 -> x1, waiting for transfers between devices: none -> 6.34 us  [per_device(): lax.all_to_all(spread_out, 'col', split_axis=1, concat_axis=1, tiled=True)]
    all_to_all x0 -> x1, starting transfers between devices: none -> 3.84 us  [per_device(): lax.all_to_all(spread_out, 'col', split_axis=1, concat_axis=1, tiled=True)]
    ppermute x6, waiting for transfers between devices: 23.5 us -> 19.8 us  [ring_reduce_scatter(): got = lax.ppermute(acc, axis, perm)]
    concatenate x0 -> x1, other arithmetic: none -> 2.17 us  [per_device(): partial = jnp.concatenate([low, high], axis=1)]
    unnamed x20 -> x16, local copies, waits for them, and re-layouts: 5.32 us -> 4.96 us
  transfers between devices with their start and end apart: 13 -> 12, of which waited for: 10 -> 10; matrix products, arithmetic and copies ran while one was open for 0% -> 7% of each run, Pallas kernels for 0% -> 0%
where the time goes in v11:
time: 135 us; the launch traced here: 134 us
  waiting for transfers between devices  69.8 us (52%)
  starting transfers between devices  24.9 us (18%)
  other arithmetic  11.8 us (9%)
  blocking collectives  10.1 us (7%)
  local copies, waits for them, and re-layouts  9.71 us (7%)
  Pallas kernels  7.51 us (6%)
    ppermute x1, waiting for transfers between devices, ring_pieces(): from_left = lax.ppermute(block, axis, to_right)  26.1 us
    ppermute x6, waiting for transfers between devices, ring_reduce_scatter(): got = lax.ppermute(acc, axis, perm)  19.8 us
    all_to_all x1, blocking collectives, per_device(): part = lax.all_to_all(rolled, 'ry', split_axis=1, concat_axis=0, tiled=True)  10.1 us
    all_to_all x1, waiting for transfers between devices, per_device(): both = lax.all_to_all(both, 'col', split_axis=0, concat_axis=1, tiled=True)  9.92 us
    all_to_all x1, starting transfers between devices, per_device(): both = lax.all_to_all(both, 'col', split_axis=0, concat_axis=1, tiled=True)  8.57 us
    ppermute x6, starting transfers between devices, ring_reduce_scatter(): got = lax.ppermute(acc, axis, perm)  8.24 us
    add x6, other arithmetic, ring_reduce_scatter(): acc = got + lax.dynamic_index_in_dim(part, seg, 0, keepdims=False)  7.72 us
    pallas_call x1, Pallas kernels, dot_pieces(): pl.pallas_call(pieces_kernel, grid=(m // tile,), in_specs=[pl.BlockSpec((...  7.51 us
  transfers between devices with their start and end apart: 12, of which 10 were waited for; matrix products, arithmetic and copies ran while one was open for 7% of the time, Pallas kernels for 0%

profile of v11, /device:TPU:6, one launch (start us, length us, event | category | flops | bytes accessed | tf_op | source)
XLA Modules:
  0.0 134.4 jit_solution(13616830219587625715)
XLA Ops:
  0.0 1.0 copy.31
  4.7 8.6 %all-to-all-start = ((bf16[128,2,384]{2,1,0:T(2,128)(2,1)}), bf16[128,2,384]{2,1,0:T(2,128)(2,1)S(1)}, u32[]{:S(2)}, u32[]{:S(2)}) async-start(bf16[128,2,384]{2,1,0:T(2,128)(2,1)} %copy.34), calls=%async_computation | async-start | bytes 393216 | tf_op jit(solution)/shard_map/all_to_all | solution.py:92
  13.3 9.9 %all-to-all-done = bf16[128,2,384]{2,1,0:T(2,128)(2,1)S(1)} async-done(((bf16[128,2,384]{2,1,0:T(2,128)(2,1)}), bf16[128,2,384]{2,1,0:T(2,128)(2,1)S(1)}, u32[]{:S(2)}, u32[]{:S(2)}) %all-to-all-start) | async-done | bytes 196640 | tf_op jit(solution)/shard_map/all_to_all | solution.py:92
  24.0 10.1 %all_to_all.36 = bf16[8,4,1536]{2,0,1:T(8,128)(2,1)S(1)} all-to-all(bf16[8,4,1536]{2,0,1:T(8,128)(2,1)S(1)} %bitcast.48), channel_id=1, replica_groups=mesh['ry'=4,'rx'=4,'col'=16] {'ry'}, dimensions={1} | all-to-all | bytes 196608 | tf_op jit(solution)/shard_map/all_to_all | solution.py:105
  34.1 1.3 broadcast_in_dim.16
  35.4 3.8 %all-to-all-start.2 = ((bf16[4,16,8,1536]{3,2,0,1:T(8,128)(2,1)}), bf16[4,16,8,1536]{3,2,0,1:T(8,128)(2,1)S(1)}, u32[]{:S(2)}, u32[]{:S(2)}) async-start(bf16[4,16,8,1536]{3,2,0,1:T(8,128)(2,1)} %broadcast_in_dim.16), calls=%async_computation.2 | async-start | bytes 3145728 | tf_op jit(solution)/shard_map/all_to_all | solution.py:109
  39.9 1.5 %collective-permute-start = (bf16[384,1536]{1,0:T(8,128)(2,1)S(1)}, bf16[384,1536]{1,0:T(8,128)(2,1)S(1)}, u32[]{:S(2)}, u32[]{:S(2)}) collective-permute-start(bf16[384,1536]{1,0:T(8,128)(2,1)S(1)} %copy-done.4), channel_id=1, source_target_pairs={{0,48},{16,0},{32,16},{48,32},{1,49},{17,1},{33,17},{49,33},{2,50}... | collective-permute-start | bytes 3538952 | tf_op jit(solution)/shard_map/ppermute | solution.py:35
  41.4 26.1 %collective-permute-done.1.w3_ref = bf16[384,1536]{1,0:T(8,128)(2,1)S(1)} collective-permute-done((bf16[384,1536]{1,0:T(8,128)(2,1)S(1)}, bf16[384,1536]{1,0:T(8,128)(2,1)S(1)}, u32[]{:S(2)}, u32[]{:S(2)}) %collective-permute-start.1) | collective-permute-done | bytes 1179680 | tf_op jit(solution)/shard_map/ppermute | solution.py:34
  67.6 1.8 %collective-permute-start.2 = (bf16[384,768]{1,0:T(8,128)(2,1)S(1)}, bf16[384,768]{1,0:T(8,128)(2,1)}, u32[]{:S(2)}, u32[]{:S(2)}) collective-permute-start(bf16[384,768]{1,0:T(8,128)(2,1)S(1)} %slice.26), channel_id=1, source_target_pairs={{0,16},{16,32},{32,48},{48,0},{1,17},{17,33},{33,49},{49,1},{2,18}... | collective-permute-start | bytes 1769480 | tf_op jit(solution)/shard_map/ppermute | solution.py:37
  70.8 6.3 %all-to-all-done.2 = bf16[4,16,8,1536]{3,2,0,1:T(8,128)(2,1)S(1)} async-done(((bf16[4,16,8,1536]{3,2,0,1:T(8,128)(2,1)}), bf16[4,16,8,1536]{3,2,0,1:T(8,128)(2,1)S(1)}, u32[]{:S(2)}, u32[]{:S(2)}) %all-to-all-start.2) | async-done | bytes 1572896 | tf_op jit(solution)/shard_map/all_to_all | solution.py:109
  77.1 1.3 copy.35
  78.4 4.1 %collective-permute-done.2.w2lo_ref = bf16[384,768]{1,0:T(8,128)(2,1)} collective-permute-done((bf16[384,768]{1,0:T(8,128)(2,1)S(1)}, bf16[384,768]{1,0:T(8,128)(2,1)}, u32[]{:S(2)}, u32[]{:S(2)}) %collective-permute-start.2) | collective-permute-done | bytes 589856 | tf_op jit(solution)/shard_map/ppermute | solution.py:37
  82.5 3.6 %collective-permute-done.3.w2hi_ref = bf16[384,768]{1,0:T(8,128)(2,1)S(1)} collective-permute-done((bf16[384,768]{1,0:T(8,128)(2,1)S(1)}, bf16[384,768]{1,0:T(8,128)(2,1)S(1)}, u32[]{:S(2)}, u32[]{:S(2)}) %collective-permute-start.3) | collective-permute-done | bytes 589856 | tf_op jit(solution)/shard_map/ppermute | solution.py:38
  86.9 7.5 %shard_map.64 = (f32[512,768]{1,0:T(8,128)}, f32[512,768]{1,0:T(8,128)}) custom-call(bf16[512,1536]{1,0:T(8,128)(2,1)} %bitcast.46, bf16[384,1536]{1,0:T(8,128)(2,1)} %w0_ref.1, bf16[384,1536]{1,0:T(8,128)(2,1)} %copy-done.1, bf16[384,768]{1,0:T(8,128)(2,1)} %collective-permute-done.2.w2lo_ref, bf16[384,768]{1,0:T(8,128)(2,1)} %copy-done.5, ...), custom_call_target="tpu_custom_call" | custom-call | flops 2415919104 | bytes 9437184 | tf_op jit(solution)/shard_map/pallas_call | solution.py:60
  94.4 2.2 %pad_maximum_fusion = f32[512,1536]{1,0:T(8,128)S(1)} fusion(f32[512,768]{1,0:T(8,128)} %get-tuple-element.8, f32[512,768]{1,0:T(8,128)} %get-tuple-element.7), kind=kLoop, calls=%fused_computation.1 | loop fusion | flops 786432 | bytes 6291456 | tf_op jit(solution)/shard_map/concatenate | solution.py:112
  96.9 1.2 collective-permute-start.7
  99.8 6.6 %collective-permute-done.7 = f32[128,768]{1,0:T(8,128)} collective-permute-done((f32[128,768]{1,0:T(8,128)S(1)}, f32[128,768]{1,0:T(8,128)}, u32[]{:S(2)}, u32[]{:S(2)}) %collective-permute-start.7) | collective-permute-done | bytes 393248 | tf_op jit(solution)/shard_map/ppermute | solution.py:81
  107.4 2.5 %collective-permute-start.8 = (f32[128,768]{1,0:T(8,128)S(1)}, f32[128,768]{1,0:T(8,128)}, u32[]{:S(2)}, u32[]{:S(2)}) collective-permute-start(f32[128,768]{1,0:T(8,128)S(1)} %bitcast_add_fusion.2), channel_id=1, source_target_pairs={{0,192},{64,0},{128,64},{192,128},{1,193},{65,1},{129,65},{193,129... | collective-permute-start | bytes 1179656 | tf_op jit(solution)/shard_map/ppermute | solution.py:81
  109.9 1.8 %bitcast_add_fusion.5 = f32[128,768]{1,0:T(8,128)} fusion(f32[128,768]{1,0:T(8,128)} %collective-permute-done.4, f32[4,128,768]{2,1,0:T(8,128)S(1)} %get-tuple-element.12, s32[]{:T(128)S(6)} %select_n.72), kind=kLoop, calls=%fused_computation.21 | loop fusion | flops 98304 | bytes 1179652 | tf_op jit(solution)/shard_map/add | solution.py:83
  111.7 4.3 %collective-permute-done.8 = f32[128,768]{1,0:T(8,128)} collective-permute-done((f32[128,768]{1,0:T(8,128)S(1)}, f32[128,768]{1,0:T(8,128)}, u32[]{:S(2)}, u32[]{:S(2)}) %collective-permute-start.8) | collective-permute-done | bytes 393248 | tf_op jit(solution)/shard_map/ppermute | solution.py:81
  117.0 3.7 %collective-permute-start.9 = (f32[128,768]{1,0:T(8,128)S(1)}, f32[128,768]{1,0:T(8,128)}, u32[]{:S(2)}, u32[]{:S(2)}) collective-permute-start(f32[128,768]{1,0:T(8,128)S(1)} %bitcast_add_fusion.1), channel_id=1, source_target_pairs={{0,192},{64,0},{128,64},{192,128},{1,193},{65,1},{129,65},{193,129... | collective-permute-start | bytes 1179656 | tf_op jit(solution)/shard_map/ppermute | solution.py:81
  121.3 1.8 %bitcast_add_fusion.4 = f32[128,768]{1,0:T(8,128)} fusion(f32[128,768]{1,0:T(8,128)} %collective-permute-done.5, f32[4,128,768]{2,1,0:T(8,128)S(1)} %get-tuple-element.12, s32[]{:T(128)S(6)} %select_n.74), kind=kLoop, calls=%fused_computation.20 | loop fusion | flops 98304 | bytes 1179652 | tf_op jit(solution)/shard_map/add | solution.py:83
  123.1 2.9 %collective-permute-done.9 = f32[128,768]{1,0:T(8,128)} collective-permute-done((f32[128,768]{1,0:T(8,128)S(1)}, f32[128,768]{1,0:T(8,128)}, u32[]{:S(2)}, u32[]{:S(2)}) %collective-permute-start.9) | collective-permute-done | bytes 393248 | tf_op jit(solution)/shard_map/ppermute | solution.py:81
  127.0 5.3 %collective-permute-done.6 = f32[128,768]{1,0:T(8,128)} collective-permute-done((f32[128,768]{1,0:T(8,128)}, f32[128,768]{1,0:T(8,128)}, u32[]{:S(2)}, u32[]{:S(2)}) %collective-permute-start.6) | collective-permute-done | bytes 393248 | tf_op jit(solution)/shard_map/ppermute | solution.py:81
  (45 shorter events, 14.9 us)
Async XLA Ops:
  0.0 3.8 %copy-start.2 = (bf16[128,384]{1,0:T(8,128)(2,1)S(1)}, bf16[128,384]{1,0:T(8,128)(2,1)}, u32[]{:S(2)}) copy-start(bf16[128,384]{1,0:T(8,128)(2,1)} %param.9) | copy-start | bytes 294916
  2.1 11.2 %copy-start.3 = (f32[6144]{0:T(1024)S(1)}, f32[6144]{0:T(1024)}, u32[]{:S(2)}) copy-start(f32[6144]{0:T(1024)} %param.10) | copy-start | bytes 73732
  4.7 18.5 %all-to-all-start = ((bf16[128,2,384]{2,1,0:T(2,128)(2,1)}), bf16[128,2,384]{2,1,0:T(2,128)(2,1)S(1)}, u32[]{:S(2)}, u32[]{:S(2)}) async-start(bf16[128,2,384]{2,1,0:T(2,128)(2,1)} %copy.34), calls=%async_computation | async-start | bytes 393216 | tf_op jit(solution)/shard_map/all_to_all | solution.py:92
  35.4 3.9 %copy-start.4 = (bf16[384,1536]{1,0:T(8,128)(2,1)S(1)}, bf16[384,1536]{1,0:T(8,128)(2,1)}, u32[]{:S(2)}) copy-start(bf16[384,1536]{1,0:T(8,128)(2,1)} %w0_ref.1) | copy-start | bytes 3538948
  35.4 41.7 %all-to-all-start.2 = ((bf16[4,16,8,1536]{3,2,0,1:T(8,128)(2,1)}), bf16[4,16,8,1536]{3,2,0,1:T(8,128)(2,1)S(1)}, u32[]{:S(2)}, u32[]{:S(2)}) async-start(bf16[4,16,8,1536]{3,2,0,1:T(8,128)(2,1)} %broadcast_in_dim.16), calls=%async_computation.2 | async-start | bytes 3145728 | tf_op jit(solution)/shard_map/all_to_all | solution.py:109
  39.3 28.2 %collective-permute-start.1 = (bf16[384,1536]{1,0:T(8,128)(2,1)S(1)}, bf16[384,1536]{1,0:T(8,128)(2,1)S(1)}, u32[]{:S(2)}, u32[]{:S(2)}) collective-permute-start(bf16[384,1536]{1,0:T(8,128)(2,1)S(1)} %copy-done.4), channel_id=1, source_target_pairs={{0,16},{16,32},{32,48},{48,0},{1,17},{17,33},{33,49},{49,1},{2,18}... | collective-permute-start | bytes 3538952 | tf_op jit(solution)/shard_map/ppermute | solution.py:34
  39.9 29.5 %collective-permute-start = (bf16[384,1536]{1,0:T(8,128)(2,1)S(1)}, bf16[384,1536]{1,0:T(8,128)(2,1)S(1)}, u32[]{:S(2)}, u32[]{:S(2)}) collective-permute-start(bf16[384,1536]{1,0:T(8,128)(2,1)S(1)} %copy-done.4), channel_id=1, source_target_pairs={{0,48},{16,0},{32,16},{48,32},{1,49},{17,1},{33,17},{49,33},{2,50}... | collective-permute-start | bytes 3538952 | tf_op jit(solution)/shard_map/ppermute | solution.py:35
  67.5 1.8 %copy-start = (bf16[384,1536]{1,0:T(8,128)(2,1)}, bf16[384,1536]{1,0:T(8,128)(2,1)S(1)}, u32[]{:S(2)}) copy-start(bf16[384,1536]{1,0:T(8,128)(2,1)S(1)} %collective-permute-done.1.w3_ref) | copy-start | bytes 3538948
  67.6 14.9 %collective-permute-start.2 = (bf16[384,768]{1,0:T(8,128)(2,1)S(1)}, bf16[384,768]{1,0:T(8,128)(2,1)}, u32[]{:S(2)}, u32[]{:S(2)}) collective-permute-start(bf16[384,768]{1,0:T(8,128)(2,1)S(1)} %slice.26), channel_id=1, source_target_pairs={{0,16},{16,32},{32,48},{48,0},{1,17},{17,33},{33,49},{49,1},{2,18}... | collective-permute-start | bytes 1769480 | tf_op jit(solution)/shard_map/ppermute | solution.py:37
  69.4 1.1 copy-start.1
  70.4 15.6 %collective-permute-start.3 = (bf16[384,768]{1,0:T(8,128)(2,1)S(1)}, bf16[384,768]{1,0:T(8,128)(2,1)S(1)}, u32[]{:S(2)}, u32[]{:S(2)}) collective-permute-start(bf16[384,768]{1,0:T(8,128)(2,1)S(1)} %slice.27), channel_id=1, source_target_pairs={{0,48},{16,0},{32,16},{48,32},{1,49},{17,1},{33,17},{49,33},{2,50}... | collective-permute-start | bytes 1769480 | tf_op jit(solution)/shard_map/ppermute | solution.py:38
  86.1 0.8 copy-start.5
  96.9 9.5 %collective-permute-start.7 = (f32[128,768]{1,0:T(8,128)S(1)}, f32[128,768]{1,0:T(8,128)}, u32[]{:S(2)}, u32[]{:S(2)}) collective-permute-start(f32[128,768]{1,0:T(8,128)S(1)} %dynamic-slice_bitcast_fusion), channel_id=1, source_target_pairs={{0,192},{64,0},{128,64},{192,128},{1,193},{65,1},{129,65},{193,129... | collective-permute-start | bytes 1179656 | tf_op jit(solution)/shard_map/ppermute | solution.py:81
  98.9 11.0 %collective-permute-start.4 = (f32[128,768]{1,0:T(8,128)}, f32[128,768]{1,0:T(8,128)}, u32[]{:S(2)}, u32[]{:S(2)}) collective-permute-start(f32[128,768]{1,0:T(8,128)} %dynamic-slice_bitcast_fusion.1), channel_id=1, source_target_pairs={{0,64},{64,128},{128,192},{192,0},{1,65},{65,129},{129,193},{193,1... | collective-permute-start | bytes 1179656 | tf_op jit(solution)/shard_map/ppermute | solution.py:81
  107.4 8.5 %collective-permute-start.8 = (f32[128,768]{1,0:T(8,128)S(1)}, f32[128,768]{1,0:T(8,128)}, u32[]{:S(2)}, u32[]{:S(2)}) collective-permute-start(f32[128,768]{1,0:T(8,128)S(1)} %bitcast_add_fusion.2), channel_id=1, source_target_pairs={{0,192},{64,0},{128,64},{192,128},{1,193},{65,1},{129,65},{193,129... | collective-permute-start | bytes 1179656 | tf_op jit(solution)/shard_map/ppermute | solution.py:81
  111.7 9.6 %collective-permute-start.5 = (f32[128,768]{1,0:T(8,128)}, f32[128,768]{1,0:T(8,128)}, u32[]{:S(2)}, u32[]{:S(2)}) collective-permute-start(f32[128,768]{1,0:T(8,128)} %bitcast_add_fusion.5), channel_id=1, source_target_pairs={{0,64},{64,128},{128,192},{192,0},{1,65},{65,129},{129,193},{193,1... | collective-permute-start | bytes 1179656 | tf_op jit(solution)/shard_map/ppermute | solution.py:81
  117.0 9.0 %collective-permute-start.9 = (f32[128,768]{1,0:T(8,128)S(1)}, f32[128,768]{1,0:T(8,128)}, u32[]{:S(2)}, u32[]{:S(2)}) collective-permute-start(f32[128,768]{1,0:T(8,128)S(1)} %bitcast_add_fusion.1), channel_id=1, source_target_pairs={{0,192},{64,0},{128,64},{192,128},{1,193},{65,1},{129,65},{193,129... | collective-permute-start | bytes 1179656 | tf_op jit(solution)/shard_map/ppermute | solution.py:81
  123.1 9.3 %collective-permute-start.6 = (f32[128,768]{1,0:T(8,128)}, f32[128,768]{1,0:T(8,128)}, u32[]{:S(2)}, u32[]{:S(2)}) collective-permute-start(f32[128,768]{1,0:T(8,128)} %bitcast_add_fusion.4), channel_id=1, source_target_pairs={{0,64},{64,128},{128,192},{192,0},{1,65},{65,129},{129,193},{193,1... | collective-permute-start | bytes 1179656 | tf_op jit(solution)/shard_map/ppermute | solution.py:81

commit v12 on v11

--- a/solution.py
+++ b/solution.py
@@ -39,42 +39,46 @@
     return block, from_right, far_low, far_high, from_left
 
 
-def pieces_kernel(a_ref, w0_ref, w1_ref, w2lo_ref, w2hi_ref, w3_ref, lo_ref, hi_ref):
+def pieces_kernel(a_ref, w0_ref, w1_ref, w2lo_ref, w2hi_ref, w3_ref, *o_refs):
     k = w0_ref.shape[0]
     half = w2lo_ref.shape[1]
+    quarter = o_refs[0].shape[1]
     a = a_ref[...]
     base = jnp.dot(a[:, 0:k], w0_ref[...], preferred_element_type=jnp.float32)
     base = base + jnp.dot(a[:, k:2 * k], w1_ref[...], preferred_element_type=jnp.float32)
     base = base + jnp.dot(a[:, 3 * k:4 * k], w3_ref[...], preferred_element_type=jnp.float32)
     far = a[:, 2 * k:3 * k]
-    lo_ref[...] = base[:, 0:half] + jnp.dot(far, w2lo_ref[...], preferred_element_type=jnp.float32)
-    hi_ref[...] = base[:, half:] + jnp.dot(far, w2hi_ref[...], preferred_element_type=jnp.float32)
+    low = base[:, 0:half] + jnp.dot(far, w2lo_ref[...], preferred_element_type=jnp.float32)
+    high = base[:, half:] + jnp.dot(far, w2hi_ref[...], preferred_element_type=jnp.float32)
+    for q, o_ref in enumerate(o_refs):
+        source = low if q < 2 else high
+        start = (q % 2) * quarter
+        o_ref[...] = source[:, start:start + quarter]
 
 
 def dot_pieces(a, pieces, tile=128):
     m, kk = a.shape
     n = pieces[0].shape[1]
     full = lambda p: pl.BlockSpec(p.shape, lambda i: (0, 0))
-    half_spec = pl.BlockSpec((tile, n // 2), lambda i: (i, 0))
-    half_shape = jax.ShapeDtypeStruct((m, n // 2), jnp.float32)
+    spec = pl.BlockSpec((tile, n // 4), lambda i: (i, 0))
+    shape = jax.ShapeDtypeStruct((m, n // 4), jnp.float32)
     return pl.pallas_call(
         pieces_kernel,
         grid=(m // tile,),
         in_specs=[pl.BlockSpec((tile, kk), lambda i: (i, 0))] + [full(p) for p in pieces],
-        out_specs=(half_spec, half_spec),
-        out_shape=(half_shape, half_shape),
+        out_specs=(spec,) * 4,
+        out_shape=(shape,) * 4,
         cost_estimate=pl.CostEstimate(
             flops=2 * m * kk * n, transcendentals=0, bytes_accessed=a.size * 2 + sum(p.size * 2 for p in pieces) + m * n * 4
         ),
     )(a, *pieces)
 
 
-def ring_reduce_scatter(x, axis, n):
+def ring_reduce_scatter(parts, axis, n):
     me = lax.axis_index(axis)
-    half = x.shape[2] // 2
     out = []
-    for step_dir, cols in ((1, slice(0, half)), (-1, slice(half, None))):
-        part = x[:, :, cols]
+    for index, part in enumerate(parts):
+        step_dir = 1 if index % 2 == 0 else -1
         perm = [(i, (i + step_dir) % n) for i in range(n)]
         acc = lax.dynamic_index_in_dim(part, (me - step_dir) % n, 0, keepdims=False)
         for k in range(n - 1):
@@ -108,9 +112,8 @@
     spread_out = jnp.broadcast_to(part[:, None], (part.shape[0], n_col) + part.shape[1:])
     tokens = lax.all_to_all(spread_out, "col", split_axis=1, concat_axis=1, tiled=True)
     tokens = tokens.reshape(-1, tokens.shape[-1])
-    low, high = dot_pieces(tokens, pieces)
-    partial = jnp.concatenate([low, high], axis=1)
-    product = ring_reduce_scatter(partial.reshape(n_y, -1, partial.shape[1]), "ry", n_y)
+    quarters = dot_pieces(tokens, pieces)
+    product = ring_reduce_scatter([q.reshape(n_y, -1, q.shape[1]) for q in quarters], "ry", n_y)
     return jax.nn.gelu(product, approximate=True).astype(jnp.bfloat16)
 
 

time: 135 us -> 129 us (0.956)
  starting transfers between devices: 24.9 us -> 35.8 us
  waiting for transfers between devices: 69.8 us -> 59 us
  other arithmetic: 11.8 us -> 3.09 us
  local copies, waits for them, and re-layouts: 9.71 us -> 12.6 us
    ppermute x6 -> x12, starting transfers between devices: 8.24 us -> 19.2 us  [ring_reduce_scatter(): got = lax.ppermute(acc, axis, perm)]
    ppermute x6 -> x12, waiting for transfers between devices: 19.8 us -> 8.94 us  [ring_reduce_scatter(): got = lax.ppermute(acc, axis, perm)]
    add x6 -> x12, other arithmetic: 7.72 us -> 1.22 us  [ring_reduce_scatter(): acc = got + lax.dynamic_index_in_dim(part, seg, 0, keepdims=False)]
    squeeze x2 -> x4, local copies, waits for them, and re-layouts: 0.81 us -> 3.96 us  [ring_reduce_scatter(): acc = lax.dynamic_index_in_dim(part, (me - step_dir) % n, 0, keepdims=False)]
    concatenate x1 -> x0, other arithmetic: 2.17 us -> none  [per_device(): partial = jnp.concatenate([low, high], axis=1)]
    unnamed x16 -> x24, local copies, waits for them, and re-layouts: 4.96 us -> 4.95 us
  transfers between devices with their start and end apart: 12 -> 18, of which waited for: 10 -> 12; matrix products, arithmetic and copies ran while one was open for 7% -> 4% of each run, Pallas kernels for 0% -> 0%
where the time goes in v12:
time: 129 us
  waiting for transfers between devices  59 us (46%)
  starting transfers between devices  35.8 us (28%)
  local copies, waits for them, and re-layouts  12.6 us (10%)
  blocking collectives  10.1 us (8%)
  Pallas kernels  7.51 us (6%)
  other arithmetic  3.09 us (2%)
    ppermute x1, waiting for transfers between devices, ring_pieces(): from_left = lax.ppermute(block, axis, to_right)  26.1 us
    ppermute x12, starting transfers between devices, ring_reduce_scatter(): got = lax.ppermute(acc, axis, perm)  19.2 us
    all_to_all x1, blocking collectives, per_device(): part = lax.all_to_all(rolled, 'ry', split_axis=1, concat_axis=0, tiled=True)  10.1 us
    all_to_all x1, waiting for transfers between devices, per_device(): both = lax.all_to_all(both, 'col', split_axis=0, concat_axis=1, tiled=True)  9.92 us
    ppermute x12, waiting for transfers between devices, ring_reduce_scatter(): got = lax.ppermute(acc, axis, perm)  8.94 us
    all_to_all x1, starting transfers between devices, per_device(): both = lax.all_to_all(both, 'col', split_axis=0, concat_axis=1, tiled=True)  8.57 us
    pallas_call x1, Pallas kernels, dot_pieces(): pl.pallas_call(pieces_kernel, grid=(m // tile,), in_specs=[pl.BlockSpec((...  7.51 us
    all_to_all x1, waiting for transfers between devices, per_device(): lax.all_to_all(spread_out, 'col', split_axis=1, concat_axis=1, tiled=True)  6.4 us
  transfers between devices with their start and end apart: 18, of which 12 were waited for; matrix products, arithmetic and copies ran while one was open for 4% of the time, Pallas kernels for 0%

profile of v12, /device:TPU:6, one launch (start us, length us, event | category | flops | bytes accessed | tf_op | source)
XLA Modules:
  0.0 128.9 jit_solution(2977992547192080264)
XLA Ops:
  0.0 1.0 copy.31
  4.7 8.6 %all-to-all-start = ((bf16[128,2,384]{2,1,0:T(2,128)(2,1)}), bf16[128,2,384]{2,1,0:T(2,128)(2,1)S(1)}, u32[]{:S(2)}, u32[]{:S(2)}) async-start(bf16[128,2,384]{2,1,0:T(2,128)(2,1)} %copy.34), calls=%async_computation | async-start | bytes 393216 | tf_op jit(solution)/shard_map/all_to_all | solution.py:96
  13.3 9.9 %all-to-all-done = bf16[128,2,384]{2,1,0:T(2,128)(2,1)S(1)} async-done(((bf16[128,2,384]{2,1,0:T(2,128)(2,1)}), bf16[128,2,384]{2,1,0:T(2,128)(2,1)S(1)}, u32[]{:S(2)}, u32[]{:S(2)}) %all-to-all-start) | async-done | bytes 196640 | tf_op jit(solution)/shard_map/all_to_all | solution.py:96
  24.0 10.1 %all_to_all.36 = bf16[8,4,1536]{2,0,1:T(8,128)(2,1)S(1)} all-to-all(bf16[8,4,1536]{2,0,1:T(8,128)(2,1)S(1)} %bitcast.82), channel_id=1, replica_groups=mesh['ry'=4,'rx'=4,'col'=16] {'ry'}, dimensions={1} | all-to-all | bytes 196608 | tf_op jit(solution)/shard_map/all_to_all | solution.py:109
  34.1 1.3 %broadcast_in_dim.16 = bf16[4,16,8,1536]{3,2,0,1:T(8,128)(2,1)} broadcast(bf16[4,8,1536]{2,1,0:T(8,128)(2,1)S(1)} %bitcast.83), dimensions={0,2,3} | broadcast | bytes 1671168 | tf_op jit(solution)/shard_map/broadcast_in_dim | solution.py:112
  35.5 3.8 %all-to-all-start.2 = ((bf16[4,16,8,1536]{3,2,0,1:T(8,128)(2,1)}), bf16[4,16,8,1536]{3,2,0,1:T(8,128)(2,1)S(1)}, u32[]{:S(2)}, u32[]{:S(2)}) async-start(bf16[4,16,8,1536]{3,2,0,1:T(8,128)(2,1)} %broadcast_in_dim.16), calls=%async_computation.2 | async-start | bytes 3145728 | tf_op jit(solution)/shard_map/all_to_all | solution.py:113
  39.9 1.5 %collective-permute-start = (bf16[384,1536]{1,0:T(8,128)(2,1)S(1)}, bf16[384,1536]{1,0:T(8,128)(2,1)S(1)}, u32[]{:S(2)}, u32[]{:S(2)}) collective-permute-start(bf16[384,1536]{1,0:T(8,128)(2,1)S(1)} %copy-done.8), channel_id=1, source_target_pairs={{0,48},{16,0},{32,16},{48,32},{1,49},{17,1},{33,17},{49,33},{2,50}... | collective-permute-start | bytes 3538952 | tf_op jit(solution)/shard_map/ppermute | solution.py:35
  41.4 26.1 %collective-permute-done.1.w3_ref = bf16[384,1536]{1,0:T(8,128)(2,1)S(1)} collective-permute-done((bf16[384,1536]{1,0:T(8,128)(2,1)S(1)}, bf16[384,1536]{1,0:T(8,128)(2,1)S(1)}, u32[]{:S(2)}, u32[]{:S(2)}) %collective-permute-start.1) | collective-permute-done | bytes 1179680 | tf_op jit(solution)/shard_map/ppermute | solution.py:34
  67.6 1.8 %collective-permute-start.2 = (bf16[384,768]{1,0:T(8,128)(2,1)S(1)}, bf16[384,768]{1,0:T(8,128)(2,1)}, u32[]{:S(2)}, u32[]{:S(2)}) collective-permute-start(bf16[384,768]{1,0:T(8,128)(2,1)S(1)} %slice.18), channel_id=1, source_target_pairs={{0,16},{16,32},{32,48},{48,0},{1,17},{17,33},{33,49},{49,1},{2,18}... | collective-permute-start | bytes 1769480 | tf_op jit(solution)/shard_map/ppermute | solution.py:37
  70.7 6.4 %all-to-all-done.2 = bf16[4,16,8,1536]{3,2,0,1:T(8,128)(2,1)S(1)} async-done(((bf16[4,16,8,1536]{3,2,0,1:T(8,128)(2,1)}), bf16[4,16,8,1536]{3,2,0,1:T(8,128)(2,1)S(1)}, u32[]{:S(2)}, u32[]{:S(2)}) %all-to-all-start.2) | async-done | bytes 1572896 | tf_op jit(solution)/shard_map/all_to_all | solution.py:113
  77.1 1.3 %copy.35 = bf16[4,16,8,1536]{3,2,1,0:T(8,128)(2,1)} copy(bf16[4,16,8,1536]{3,2,0,1:T(8,128)(2,1)S(1)} %all-to-all-done.2) | data formatting | bytes 3145728 | tf_op jit(solution)/shard_map/all_to_all | solution.py:113
  78.4 4.1 %collective-permute-done.2.w2lo_ref = bf16[384,768]{1,0:T(8,128)(2,1)} collective-permute-done((bf16[384,768]{1,0:T(8,128)(2,1)S(1)}, bf16[384,768]{1,0:T(8,128)(2,1)}, u32[]{:S(2)}, u32[]{:S(2)}) %collective-permute-start.2) | collective-permute-done | bytes 589856 | tf_op jit(solution)/shard_map/ppermute | solution.py:37
  82.5 3.5 %collective-permute-done.3.w2hi_ref = bf16[384,768]{1,0:T(8,128)(2,1)S(1)} collective-permute-done((bf16[384,768]{1,0:T(8,128)(2,1)S(1)}, bf16[384,768]{1,0:T(8,128)(2,1)S(1)}, u32[]{:S(2)}, u32[]{:S(2)}) %collective-permute-start.3) | collective-permute-done | bytes 589856 | tf_op jit(solution)/shard_map/ppermute | solution.py:38
  86.9 7.5 %shard_map.64 = (f32[512,384]{1,0:T(8,128)}, f32[512,384]{1,0:T(8,128)}, f32[512,384]{1,0:T(8,128)}, f32[512,384]{1,0:T(8,128)}) custom-call(bf16[512,1536]{1,0:T(8,128)(2,1)} %bitcast.64, bf16[384,1536]{1,0:T(8,128)(2,1)} %w0_ref.1, bf16[384,1536]{1,0:T(8,128)(2,1)} %copy-done.5, bf16[384,768]{1,0:T(8,128)(2,1)} %collective-permute-done.2.w2lo_ref, ...), custom_call_target="tpu_custom_call" | custom-call | flops 2415919104 | bytes 9437184 | tf_op jit(solution)/shard_map/pallas_call | solution.py:65
  94.4 1.1 dynamic-slice_bitcast_fusion
  95.5 1.2 collective-permute-start.13
  99.6 2.5 %collective-permute-start.7 = (f32[128,384]{1,0:T(8,128)S(1)}, f32[128,384]{1,0:T(8,128)S(1)}, u32[]{:S(2)}, u32[]{:S(2)}) collective-permute-start(f32[128,384]{1,0:T(8,128)S(1)} %dynamic-slice_bitcast_fusion.2), channel_id=1, source_target_pairs={{0,192},{64,0},{128,64},{192,128},{1,193},{65,1},{129,65},{193,129... | collective-permute-start | bytes 589832 | tf_op jit(solution)/shard_map/ppermute | solution.py:85
  104.1 3.3 %collective-permute-start.14 = (f32[128,384]{1,0:T(8,128)S(1)}, f32[128,384]{1,0:T(8,128)S(1)}, u32[]{:S(2)}, u32[]{:S(2)}) collective-permute-start(f32[128,384]{1,0:T(8,128)S(1)} %bitcast_add_fusion.2), channel_id=1, source_target_pairs={{0,192},{64,0},{128,64},{192,128},{1,193},{65,1},{129,65},{193,129... | collective-permute-start | bytes 589832 | tf_op jit(solution)/shard_map/ppermute | solution.py:85
  107.6 3.3 %collective-permute-start.8 = (f32[128,384]{1,0:T(8,128)S(1)}, f32[128,384]{1,0:T(8,128)S(1)}, u32[]{:S(2)}, u32[]{:S(2)}) collective-permute-start(f32[128,384]{1,0:T(8,128)S(1)} %bitcast_add_fusion.8), channel_id=1, source_target_pairs={{0,192},{64,0},{128,64},{192,128},{1,193},{65,1},{129,65},{193,129... | collective-permute-start | bytes 589832 | tf_op jit(solution)/shard_map/ppermute | solution.py:85
  112.4 3.8 %collective-permute-start.15 = (f32[128,384]{1,0:T(8,128)S(1)}, f32[128,384]{1,0:T(8,128)S(1)}, u32[]{:S(2)}, u32[]{:S(2)}) collective-permute-start(f32[128,384]{1,0:T(8,128)S(1)} %bitcast_add_fusion.1), channel_id=1, source_target_pairs={{0,192},{64,0},{128,64},{192,128},{1,193},{65,1},{129,65},{193,129... | collective-permute-start | bytes 589832 | tf_op jit(solution)/shard_map/ppermute | solution.py:85
  116.7 3.6 %collective-permute-start.9 = (f32[128,384]{1,0:T(8,128)S(1)}, f32[128,384]{1,0:T(8,128)S(1)}, u32[]{:S(2)}, u32[]{:S(2)}) collective-permute-start(f32[128,384]{1,0:T(8,128)S(1)} %bitcast_add_fusion.7), channel_id=1, source_target_pairs={{0,192},{64,0},{128,64},{192,128},{1,193},{65,1},{129,65},{193,129... | collective-permute-start | bytes 589832 | tf_op jit(solution)/shard_map/ppermute | solution.py:85
  121.1 2.5 %collective-permute-done.9 = f32[128,384]{1,0:T(8,128)S(1)} collective-permute-done((f32[128,384]{1,0:T(8,128)S(1)}, f32[128,384]{1,0:T(8,128)S(1)}, u32[]{:S(2)}, u32[]{:S(2)}) %collective-permute-start.9) | collective-permute-done | bytes 196640 | tf_op jit(solution)/shard_map/ppermute | solution.py:85
  123.5 1.2 collective-permute-done.12
  124.8 3.1 %collective-permute-done.6 = f32[128,384]{1,0:T(8,128)S(1)} collective-permute-done((f32[128,384]{1,0:T(8,128)S(1)}, f32[128,384]{1,0:T(8,128)S(1)}, u32[]{:S(2)}, u32[]{:S(2)}) %collective-permute-start.6) | collective-permute-done | bytes 196640 | tf_op jit(solution)/shard_map/ppermute | solution.py:85
  (71 shorter events, 16.0 us)
Async XLA Ops:
  2.1 11.2 %copy-start.7 = (f32[6144]{0:T(1024)S(1)}, f32[6144]{0:T(1024)}, u32[]{:S(2)}) copy-start(f32[6144]{0:T(1024)} %param.10) | copy-start | bytes 73732
  4.7 18.5 %all-to-all-start = ((bf16[128,2,384]{2,1,0:T(2,128)(2,1)}), bf16[128,2,384]{2,1,0:T(2,128)(2,1)S(1)}, u32[]{:S(2)}, u32[]{:S(2)}) async-start(bf16[128,2,384]{2,1,0:T(2,128)(2,1)} %copy.34), calls=%async_computation | async-start | bytes 393216 | tf_op jit(solution)/shard_map/all_to_all | solution.py:96
  35.5 3.9 %copy-start.8 = (bf16[384,1536]{1,0:T(8,128)(2,1)S(1)}, bf16[384,1536]{1,0:T(8,128)(2,1)}, u32[]{:S(2)}) copy-start(bf16[384,1536]{1,0:T(8,128)(2,1)} %w0_ref.1) | copy-start | bytes 3538948
  35.5 41.7 %all-to-all-start.2 = ((bf16[4,16,8,1536]{3,2,0,1:T(8,128)(2,1)}), bf16[4,16,8,1536]{3,2,0,1:T(8,128)(2,1)S(1)}, u32[]{:S(2)}, u32[]{:S(2)}) async-start(bf16[4,16,8,1536]{3,2,0,1:T(8,128)(2,1)} %broadcast_in_dim.16), calls=%async_computation.2 | async-start | bytes 3145728 | tf_op jit(solution)/shard_map/all_to_all | solution.py:113
  39.3 28.2 %collective-permute-start.1 = (bf16[384,1536]{1,0:T(8,128)(2,1)S(1)}, bf16[384,1536]{1,0:T(8,128)(2,1)S(1)}, u32[]{:S(2)}, u32[]{:S(2)}) collective-permute-start(bf16[384,1536]{1,0:T(8,128)(2,1)S(1)} %copy-done.8), channel_id=1, source_target_pairs={{0,16},{16,32},{32,48},{48,0},{1,17},{17,33},{33,49},{49,1},{2,18}... | collective-permute-start | bytes 3538952 | tf_op jit(solution)/shard_map/ppermute | solution.py:34
  39.9 29.5 %collective-permute-start = (bf16[384,1536]{1,0:T(8,128)(2,1)S(1)}, bf16[384,1536]{1,0:T(8,128)(2,1)S(1)}, u32[]{:S(2)}, u32[]{:S(2)}) collective-permute-start(bf16[384,1536]{1,0:T(8,128)(2,1)S(1)} %copy-done.8), channel_id=1, source_target_pairs={{0,48},{16,0},{32,16},{48,32},{1,49},{17,1},{33,17},{49,33},{2,50}... | collective-permute-start | bytes 3538952 | tf_op jit(solution)/shard_map/ppermute | solution.py:35
  67.6 14.9 %collective-permute-start.2 = (bf16[384,768]{1,0:T(8,128)(2,1)S(1)}, bf16[384,768]{1,0:T(8,128)(2,1)}, u32[]{:S(2)}, u32[]{:S(2)}) collective-permute-start(bf16[384,768]{1,0:T(8,128)(2,1)S(1)} %slice.18), channel_id=1, source_target_pairs={{0,16},{16,32},{32,48},{48,0},{1,17},{17,33},{33,49},{49,1},{2,18}... | collective-permute-start | bytes 1769480 | tf_op jit(solution)/shard_map/ppermute | solution.py:37
  70.4 15.6 %collective-permute-start.3 = (bf16[384,768]{1,0:T(8,128)(2,1)S(1)}, bf16[384,768]{1,0:T(8,128)(2,1)S(1)}, u32[]{:S(2)}, u32[]{:S(2)}) collective-permute-start(bf16[384,768]{1,0:T(8,128)(2,1)S(1)} %slice.19), channel_id=1, source_target_pairs={{0,48},{16,0},{32,16},{48,32},{1,49},{17,1},{33,17},{49,33},{2,50}... | collective-permute-start | bytes 1769480 | tf_op jit(solution)/shard_map/ppermute | solution.py:38
  94.4 13.0 %copy-start.1 = (f32[512,384]{1,0:T(8,128)S(1)}, f32[512,384]{1,0:T(8,128)}, u32[]{:S(2)}) copy-start(f32[512,384]{1,0:T(8,128)} %get-tuple-element.11) | copy-start | bytes 2359300
  94.4 13.1 %copy-start.2 = (f32[512,384]{1,0:T(8,128)S(1)}, f32[512,384]{1,0:T(8,128)}, u32[]{:S(2)}) copy-start(f32[512,384]{1,0:T(8,128)} %get-tuple-element.10) | copy-start | bytes 2359300
  95.5 16.3 %copy-start = (f32[512,384]{1,0:T(8,128)S(1)}, f32[512,384]{1,0:T(8,128)}, u32[]{:S(2)}) copy-start(f32[512,384]{1,0:T(8,128)} %get-tuple-element.9) | copy-start | bytes 2359300
  95.5 7.6 %collective-permute-start.13 = (f32[128,384]{1,0:T(8,128)S(1)}, f32[128,384]{1,0:T(8,128)S(1)}, u32[]{:S(2)}, u32[]{:S(2)}) collective-permute-start(f32[128,384]{1,0:T(8,128)S(1)} %dynamic-slice_bitcast_fusion), channel_id=1, source_target_pairs={{0,192},{64,0},{128,64},{192,128},{1,193},{65,1},{129,65},{193,129... | collective-permute-start | bytes 589832 | tf_op jit(solution)/shard_map/ppermute | solution.py:85
  97.7 9.7 %collective-permute-start.10 = (f32[128,384]{1,0:T(8,128)S(1)}, f32[128,384]{1,0:T(8,128)S(1)}, u32[]{:S(2)}, u32[]{:S(2)}) collective-permute-start(f32[128,384]{1,0:T(8,128)S(1)} %dynamic-slice_bitcast_fusion.1), channel_id=1, source_target_pairs={{0,64},{64,128},{128,192},{192,0},{1,65},{65,129},{129,193},{193,1... | collective-permute-start | bytes 589832 | tf_op jit(solution)/shard_map/ppermute | solution.py:85
  98.6 13.7 %copy-start.3 = (f32[512,384]{1,0:T(8,128)S(1)}, f32[512,384]{1,0:T(8,128)}, u32[]{:S(2)}) copy-start(f32[512,384]{1,0:T(8,128)} %get-tuple-element.12) | copy-start | bytes 2359300
  99.6 7.9 %collective-permute-start.7 = (f32[128,384]{1,0:T(8,128)S(1)}, f32[128,384]{1,0:T(8,128)S(1)}, u32[]{:S(2)}, u32[]{:S(2)}) collective-permute-start(f32[128,384]{1,0:T(8,128)S(1)} %dynamic-slice_bitcast_fusion.2), channel_id=1, source_target_pairs={{0,192},{64,0},{128,64},{192,128},{1,193},{65,1},{129,65},{193,129... | collective-permute-start | bytes 589832 | tf_op jit(solution)/shard_map/ppermute | solution.py:85
  103.0 8.8 %collective-permute-start.4 = (f32[128,384]{1,0:T(8,128)S(1)}, f32[128,384]{1,0:T(8,128)S(1)}, u32[]{:S(2)}, u32[]{:S(2)}) collective-permute-start(f32[128,384]{1,0:T(8,128)S(1)} %dynamic-slice_bitcast_fusion.3), channel_id=1, source_target_pairs={{0,64},{64,128},{128,192},{192,0},{1,65},{65,129},{129,193},{193,1... | collective-permute-start | bytes 589832 | tf_op jit(solution)/shard_map/ppermute | solution.py:85
  104.1 8.2 %collective-permute-start.14 = (f32[128,384]{1,0:T(8,128)S(1)}, f32[128,384]{1,0:T(8,128)S(1)}, u32[]{:S(2)}, u32[]{:S(2)}) collective-permute-start(f32[128,384]{1,0:T(8,128)S(1)} %bitcast_add_fusion.2), channel_id=1, source_target_pairs={{0,192},{64,0},{128,64},{192,128},{1,193},{65,1},{129,65},{193,129... | collective-permute-start | bytes 589832 | tf_op jit(solution)/shard_map/ppermute | solution.py:85
  107.4 9.1 %collective-permute-start.11 = (f32[128,384]{1,0:T(8,128)S(1)}, f32[128,384]{1,0:T(8,128)S(1)}, u32[]{:S(2)}, u32[]{:S(2)}) collective-permute-start(f32[128,384]{1,0:T(8,128)S(1)} %bitcast_add_fusion.5), channel_id=1, source_target_pairs={{0,64},{64,128},{128,192},{192,0},{1,65},{65,129},{129,193},{193,1... | collective-permute-start | bytes 589832 | tf_op jit(solution)/shard_map/ppermute | solution.py:85
  107.6 9.1 %collective-permute-start.8 = (f32[128,384]{1,0:T(8,128)S(1)}, f32[128,384]{1,0:T(8,128)S(1)}, u32[]{:S(2)}, u32[]{:S(2)}) collective-permute-start(f32[128,384]{1,0:T(8,128)S(1)} %bitcast_add_fusion.8), channel_id=1, source_target_pairs={{0,192},{64,0},{128,64},{192,128},{1,193},{65,1},{129,65},{193,129... | collective-permute-start | bytes 589832 | tf_op jit(solution)/shard_map/ppermute | solution.py:85
  111.9 9.0 %collective-permute-start.5 = (f32[128,384]{1,0:T(8,128)S(1)}, f32[128,384]{1,0:T(8,128)S(1)}, u32[]{:S(2)}, u32[]{:S(2)}) collective-permute-start(f32[128,384]{1,0:T(8,128)S(1)} %bitcast_add_fusion.11), channel_id=1, source_target_pairs={{0,64},{64,128},{128,192},{192,0},{1,65},{65,129},{129,193},{193,1... | collective-permute-start | bytes 589832 | tf_op jit(solution)/shard_map/ppermute | solution.py:85
  112.4 8.7 %collective-permute-start.15 = (f32[128,384]{1,0:T(8,128)S(1)}, f32[128,384]{1,0:T(8,128)S(1)}, u32[]{:S(2)}, u32[]{:S(2)}) collective-permute-start(f32[128,384]{1,0:T(8,128)S(1)} %bitcast_add_fusion.1), channel_id=1, source_target_pairs={{0,192},{64,0},{128,64},{192,128},{1,193},{65,1},{129,65},{193,129... | collective-permute-start | bytes 589832 | tf_op jit(solution)/shard_map/ppermute | solution.py:85
  116.6 8.2 %collective-permute-start.12 = (f32[128,384]{1,0:T(8,128)S(1)}, f32[128,384]{1,0:T(8,128)S(1)}, u32[]{:S(2)}, u32[]{:S(2)}) collective-permute-start(f32[128,384]{1,0:T(8,128)S(1)} %bitcast_add_fusion.4), channel_id=1, source_target_pairs={{0,64},{64,128},{128,192},{192,0},{1,65},{65,129},{129,193},{193,1... | collective-permute-start | bytes 589832 | tf_op jit(solution)/shard_map/ppermute | solution.py:85
  116.7 6.8 %collective-permute-start.9 = (f32[128,384]{1,0:T(8,128)S(1)}, f32[128,384]{1,0:T(8,128)S(1)}, u32[]{:S(2)}, u32[]{:S(2)}) collective-permute-start(f32[128,384]{1,0:T(8,128)S(1)} %bitcast_add_fusion.7), channel_id=1, source_target_pairs={{0,192},{64,0},{128,64},{192,128},{1,193},{65,1},{129,65},{193,129... | collective-permute-start | bytes 589832 | tf_op jit(solution)/shard_map/ppermute | solution.py:85
  120.9 7.0 %collective-permute-start.6 = (f32[128,384]{1,0:T(8,128)S(1)}, f32[128,384]{1,0:T(8,128)S(1)}, u32[]{:S(2)}, u32[]{:S(2)}) collective-permute-start(f32[128,384]{1,0:T(8,128)S(1)} %bitcast_add_fusion.10), channel_id=1, source_target_pairs={{0,64},{64,128},{128,192},{192,0},{1,65},{65,129},{129,193},{193,1... | collective-permute-start | bytes 589832 | tf_op jit(solution)/shard_map/ppermute | solution.py:85
  (4 other events, 7.5 us)

commit v13 on v12

--- a/solution.py
+++ b/solution.py
@@ -11,20 +11,23 @@
 
 def attention_block(query, keys, values):
     seq, width = query.shape
-    heads = width // HD
-    qshaped = query.reshape(seq, heads, HD)
-    kshaped = keys.reshape(seq, heads, HD)
-    vshaped = values.reshape(seq, heads, HD)
-    scores = jnp.einsum("qhd,khd->hqk", qshaped, kshaped, preferred_element_type=jnp.float32)
-    scores = scores * (1.0 / math.sqrt(HD))
     rows_idx = lax.broadcasted_iota(jnp.int32, (seq, seq), 0)
     cols_idx = lax.broadcasted_iota(jnp.int32, (seq, seq), 1)
-    scores = jnp.where((rows_idx >= cols_idx)[None], scores, -1e30)
-    highest = jnp.max(scores, axis=-1, keepdims=True)
-    expo = jnp.exp(scores - highest)
-    prob = (expo / jnp.sum(expo, axis=-1, keepdims=True)).astype(jnp.bfloat16)
-    output = jnp.einsum("hqk,khd->qhd", prob, vshaped, preferred_element_type=jnp.float32)
-    return output.astype(jnp.bfloat16).reshape(seq, width)
+    causal = rows_idx >= cols_idx
+    outputs = []
+    for head in range(width // HD):
+        cols = slice(head * HD, (head + 1) * HD)
+        scores = lax.dot_general(
+            query[:, cols], keys[:, cols], (((1,), (1,)), ((), ())), preferred_element_type=jnp.float32
+        )
+        scores = scores * (1.0 / math.sqrt(HD))
+        scores = jnp.where(causal, scores, -1e30)
+        highest = jnp.max(scores, axis=-1, keepdims=True)
+        expo = jnp.exp(scores - highest)
+        prob = (expo / jnp.sum(expo, axis=-1, keepdims=True)).astype(jnp.bfloat16)
+        output = jnp.dot(prob, values[:, cols], preferred_element_type=jnp.float32)
+        outputs.append(output.astype(jnp.bfloat16))
+    return jnp.concatenate(outputs, axis=1)
 
 
 def ring_pieces(block, axis):

time: 129 us -> 132 us (1.023)
  matrix products: 0.43 us -> 5.79 us
  local copies, waits for them, and re-layouts: 12.6 us -> 9.54 us
    dot_general x2 -> x6, matrix products: 0.43 us -> 5.79 us  [the longest x3 2.89 us: attention_block(): output = jnp.dot(prob, values[:, cols], preferred_element_type=jnp.float32)]
    unnamed x24 -> x21, local copies, waits for them, and re-layouts: 4.95 us -> 1.99 us
where the time goes in v13:
time: 132 us; the launch traced here: 131 us
  waiting for transfers between devices  58.9 us (45%)
  starting transfers between devices  35.8 us (27%)
  blocking collectives  10.1 us (8%)
  local copies, waits for them, and re-layouts  9.54 us (7%)
  Pallas kernels  7.53 us (6%)
  matrix products  5.79 us (4%)
  other arithmetic  2.74 us (2%)
    ppermute x1, waiting for transfers between devices, ring_pieces(): from_left = lax.ppermute(block, axis, to_right)  26.1 us
    ppermute x12, starting transfers between devices, ring_reduce_scatter(): got = lax.ppermute(acc, axis, perm)  19.2 us
    all_to_all x1, blocking collectives, per_device(): part = lax.all_to_all(rolled, 'ry', split_axis=1, concat_axis=0, tiled=True)  10.1 us
    all_to_all x1, waiting for transfers between devices, per_device(): both = lax.all_to_all(both, 'col', split_axis=0, concat_axis=1, tiled=True)  9.92 us
    ppermute x12, waiting for transfers between devices, ring_reduce_scatter(): got = lax.ppermute(acc, axis, perm)  8.9 us
    all_to_all x1, starting transfers between devices, per_device(): both = lax.all_to_all(both, 'col', split_axis=0, concat_axis=1, tiled=True)  8.57 us
    pallas_call x1, Pallas kernels, dot_pieces(): pl.pallas_call(pieces_kernel, grid=(m // tile,), in_specs=[pl.BlockSpec((...  7.53 us
    all_to_all x1, waiting for transfers between devices, per_device(): lax.all_to_all(spread_out, 'col', split_axis=1, concat_axis=1, tiled=True)  6.39 us
  transfers between devices with their start and end apart: 18, of which 12 were waited for; matrix products, arithmetic and copies ran while one was open for 4% of the time, Pallas kernels for 0%

profile of v13, /device:TPU:6, one launch (start us, length us, event | category | flops | bytes accessed | tf_op | source)
XLA Modules:
  0.0 130.8 jit_solution(15462542170024825062)
XLA Ops:
  7.0 8.6 %all-to-all-start = ((bf16[128,2,384]{2,1,0:T(2,128)(2,1)}), bf16[128,2,384]{2,1,0:T(2,128)(2,1)S(1)}, u32[]{:S(2)}, u32[]{:S(2)}) async-start(bf16[128,2,384]{2,1,0:T(2,128)(2,1)} %copy.12), calls=%async_computation | async-start | bytes 393216 | tf_op jit(solution)/shard_map/all_to_all | solution.py:99
  15.6 9.9 %all-to-all-done = bf16[128,2,384]{2,1,0:T(2,128)(2,1)S(1)} async-done(((bf16[128,2,384]{2,1,0:T(2,128)(2,1)}), bf16[128,2,384]{2,1,0:T(2,128)(2,1)S(1)}, u32[]{:S(2)}, u32[]{:S(2)}) %all-to-all-start) | async-done | bytes 196640 | tf_op jit(solution)/shard_map/all_to_all | solution.py:99
  25.9 10.1 %all_to_all.36 = bf16[8,4,1536]{2,0,1:T(8,128)(2,1)S(1)} all-to-all(bf16[8,4,1536]{2,0,1:T(8,128)(2,1)S(1)} %bitcast.67), channel_id=1, replica_groups=mesh['ry'=4,'rx'=4,'col'=16] {'ry'}, dimensions={1} | all-to-all | bytes 196608 | tf_op jit(solution)/shard_map/all_to_all | solution.py:112
  36.0 1.3 %broadcast_in_dim.9 = bf16[4,16,8,1536]{3,2,0,1:T(8,128)(2,1)} broadcast(bf16[4,8,1536]{2,1,0:T(8,128)(2,1)S(1)} %bitcast.68), dimensions={0,2,3} | broadcast | bytes 1671168 | tf_op jit(solution)/shard_map/broadcast_in_dim | solution.py:115
  37.4 3.8 %all-to-all-start.2 = ((bf16[4,16,8,1536]{3,2,0,1:T(8,128)(2,1)}), bf16[4,16,8,1536]{3,2,0,1:T(8,128)(2,1)S(1)}, u32[]{:S(2)}, u32[]{:S(2)}) async-start(bf16[4,16,8,1536]{3,2,0,1:T(8,128)(2,1)} %broadcast_in_dim.9), calls=%async_computation.2 | async-start | bytes 3145728 | tf_op jit(solution)/shard_map/all_to_all | solution.py:116
  41.8 1.5 %collective-permute-start = (bf16[384,1536]{1,0:T(8,128)(2,1)S(1)}, bf16[384,1536]{1,0:T(8,128)(2,1)S(1)}, u32[]{:S(2)}, u32[]{:S(2)}) collective-permute-start(bf16[384,1536]{1,0:T(8,128)(2,1)S(1)} %copy-done.8), channel_id=1, source_target_pairs={{0,48},{16,0},{32,16},{48,32},{1,49},{17,1},{33,17},{49,33},{2,50}... | collective-permute-start | bytes 3538952 | tf_op jit(solution)/shard_map/ppermute | solution.py:38
  43.3 26.1 %collective-permute-done.1.w3_ref = bf16[384,1536]{1,0:T(8,128)(2,1)S(1)} collective-permute-done((bf16[384,1536]{1,0:T(8,128)(2,1)S(1)}, bf16[384,1536]{1,0:T(8,128)(2,1)S(1)}, u32[]{:S(2)}, u32[]{:S(2)}) %collective-permute-start.1) | collective-permute-done | bytes 1179680 | tf_op jit(solution)/shard_map/ppermute | solution.py:37
  69.5 1.8 %collective-permute-start.2 = (bf16[384,768]{1,0:T(8,128)(2,1)S(1)}, bf16[384,768]{1,0:T(8,128)(2,1)}, u32[]{:S(2)}, u32[]{:S(2)}) collective-permute-start(bf16[384,768]{1,0:T(8,128)(2,1)S(1)} %slice.54), channel_id=1, source_target_pairs={{0,16},{16,32},{32,48},{48,0},{1,17},{17,33},{33,49},{49,1},{2,18}... | collective-permute-start | bytes 1769480 | tf_op jit(solution)/shard_map/ppermute | solution.py:40
  72.6 6.4 %all-to-all-done.2 = bf16[4,16,8,1536]{3,2,0,1:T(8,128)(2,1)S(1)} async-done(((bf16[4,16,8,1536]{3,2,0,1:T(8,128)(2,1)}), bf16[4,16,8,1536]{3,2,0,1:T(8,128)(2,1)S(1)}, u32[]{:S(2)}, u32[]{:S(2)}) %all-to-all-start.2) | async-done | bytes 1572896 | tf_op jit(solution)/shard_map/all_to_all | solution.py:116
  79.0 1.3 %copy.14 = bf16[4,16,8,1536]{3,2,1,0:T(8,128)(2,1)} copy(bf16[4,16,8,1536]{3,2,0,1:T(8,128)(2,1)S(1)} %all-to-all-done.2) | data formatting | bytes 3145728 | tf_op jit(solution)/shard_map/all_to_all | solution.py:116
  80.3 4.1 %collective-permute-done.2.w2lo_ref = bf16[384,768]{1,0:T(8,128)(2,1)} collective-permute-done((bf16[384,768]{1,0:T(8,128)(2,1)S(1)}, bf16[384,768]{1,0:T(8,128)(2,1)}, u32[]{:S(2)}, u32[]{:S(2)}) %collective-permute-start.2) | collective-permute-done | bytes 589856 | tf_op jit(solution)/shard_map/ppermute | solution.py:40
  84.4 3.5 %collective-permute-done.3.w2hi_ref = bf16[384,768]{1,0:T(8,128)(2,1)S(1)} collective-permute-done((bf16[384,768]{1,0:T(8,128)(2,1)S(1)}, bf16[384,768]{1,0:T(8,128)(2,1)S(1)}, u32[]{:S(2)}, u32[]{:S(2)}) %collective-permute-start.3) | collective-permute-done | bytes 589856 | tf_op jit(solution)/shard_map/ppermute | solution.py:41
  88.8 7.5 %shard_map.64 = (f32[512,384]{1,0:T(8,128)}, f32[512,384]{1,0:T(8,128)}, f32[512,384]{1,0:T(8,128)}, f32[512,384]{1,0:T(8,128)}) custom-call(bf16[512,1536]{1,0:T(8,128)(2,1)} %bitcast.48, bf16[384,1536]{1,0:T(8,128)(2,1)} %w0_ref.1, bf16[384,1536]{1,0:T(8,128)(2,1)} %copy-done.5, bf16[384,768]{1,0:T(8,128)(2,1)} %collective-permute-done.2.w2lo_ref, ...), custom_call_target="tpu_custom_call" | custom-call | flops 2415919104 | bytes 9437184 | tf_op jit(solution)/shard_map/pallas_call | solution.py:68
  96.3 1.1 dynamic-slice_bitcast_fusion
  97.4 1.2 collective-permute-start.13
  100.5 1.0 dynamic-slice_bitcast_fusion.2
  101.6 2.5 %collective-permute-start.7 = (f32[128,384]{1,0:T(8,128)S(1)}, f32[128,384]{1,0:T(8,128)S(1)}, u32[]{:S(2)}, u32[]{:S(2)}) collective-permute-start(f32[128,384]{1,0:T(8,128)S(1)} %dynamic-slice_bitcast_fusion.2), channel_id=1, source_target_pairs={{0,192},{64,0},{128,64},{192,128},{1,193},{65,1},{129,65},{193,129... | collective-permute-start | bytes 589832 | tf_op jit(solution)/shard_map/ppermute | solution.py:88
  106.0 3.3 %collective-permute-start.14 = (f32[128,384]{1,0:T(8,128)S(1)}, f32[128,384]{1,0:T(8,128)S(1)}, u32[]{:S(2)}, u32[]{:S(2)}) collective-permute-start(f32[128,384]{1,0:T(8,128)S(1)} %bitcast_add_fusion.2), channel_id=1, source_target_pairs={{0,192},{64,0},{128,64},{192,128},{1,193},{65,1},{129,65},{193,129... | collective-permute-start | bytes 589832 | tf_op jit(solution)/shard_map/ppermute | solution.py:88
  109.5 3.3 %collective-permute-start.8 = (f32[128,384]{1,0:T(8,128)S(1)}, f32[128,384]{1,0:T(8,128)S(1)}, u32[]{:S(2)}, u32[]{:S(2)}) collective-permute-start(f32[128,384]{1,0:T(8,128)S(1)} %bitcast_add_fusion.8), channel_id=1, source_target_pairs={{0,192},{64,0},{128,64},{192,128},{1,193},{65,1},{129,65},{193,129... | collective-permute-start | bytes 589832 | tf_op jit(solution)/shard_map/ppermute | solution.py:88
  114.3 3.8 %collective-permute-start.15 = (f32[128,384]{1,0:T(8,128)S(1)}, f32[128,384]{1,0:T(8,128)S(1)}, u32[]{:S(2)}, u32[]{:S(2)}) collective-permute-start(f32[128,384]{1,0:T(8,128)S(1)} %bitcast_add_fusion.1), channel_id=1, source_target_pairs={{0,192},{64,0},{128,64},{192,128},{1,193},{65,1},{129,65},{193,129... | collective-permute-start | bytes 589832 | tf_op jit(solution)/shard_map/ppermute | solution.py:88
  118.6 3.7 %collective-permute-start.9 = (f32[128,384]{1,0:T(8,128)S(1)}, f32[128,384]{1,0:T(8,128)S(1)}, u32[]{:S(2)}, u32[]{:S(2)}) collective-permute-start(f32[128,384]{1,0:T(8,128)S(1)} %bitcast_add_fusion.7), channel_id=1, source_target_pairs={{0,192},{64,0},{128,64},{192,128},{1,193},{65,1},{129,65},{193,129... | collective-permute-start | bytes 589832 | tf_op jit(solution)/shard_map/ppermute | solution.py:88
  123.0 2.5 %collective-permute-done.9 = f32[128,384]{1,0:T(8,128)S(1)} collective-permute-done((f32[128,384]{1,0:T(8,128)S(1)}, f32[128,384]{1,0:T(8,128)S(1)}, u32[]{:S(2)}, u32[]{:S(2)}) %collective-permute-start.9) | collective-permute-done | bytes 196640 | tf_op jit(solution)/shard_map/ppermute | solution.py:88
  125.5 1.2 collective-permute-done.12
  126.7 3.1 %collective-permute-done.6 = f32[128,384]{1,0:T(8,128)S(1)} collective-permute-done((f32[128,384]{1,0:T(8,128)S(1)}, f32[128,384]{1,0:T(8,128)S(1)}, u32[]{:S(2)}, u32[]{:S(2)}) %collective-permute-start.6) | collective-permute-done | bytes 196640 | tf_op jit(solution)/shard_map/ppermute | solution.py:88
  (74 shorter events, 17.9 us)
Async XLA Ops:
  0.0 5.9 %copy-start.6 = (bf16[128,384]{1,0:T(8,128)(2,1)S(1)}, bf16[128,384]{1,0:T(8,128)(2,1)}, u32[]{:S(2)}) copy-start(bf16[128,384]{1,0:T(8,128)(2,1)} %param.9) | copy-start | bytes 294916
  0.0 15.6 %copy-start.7 = (f32[6144]{0:T(1024)S(1)}, f32[6144]{0:T(1024)}, u32[]{:S(2)}) copy-start(f32[6144]{0:T(1024)} %param.10) | copy-start | bytes 73732
  7.0 18.5 %all-to-all-start = ((bf16[128,2,384]{2,1,0:T(2,128)(2,1)}), bf16[128,2,384]{2,1,0:T(2,128)(2,1)S(1)}, u32[]{:S(2)}, u32[]{:S(2)}) async-start(bf16[128,2,384]{2,1,0:T(2,128)(2,1)} %copy.12), calls=%async_computation | async-start | bytes 393216 | tf_op jit(solution)/shard_map/all_to_all | solution.py:99
  37.4 41.7 %all-to-all-start.2 = ((bf16[4,16,8,1536]{3,2,0,1:T(8,128)(2,1)}), bf16[4,16,8,1536]{3,2,0,1:T(8,128)(2,1)S(1)}, u32[]{:S(2)}, u32[]{:S(2)}) async-start(bf16[4,16,8,1536]{3,2,0,1:T(8,128)(2,1)} %broadcast_in_dim.9), calls=%async_computation.2 | async-start | bytes 3145728 | tf_op jit(solution)/shard_map/all_to_all | solution.py:116
  41.2 28.2 %collective-permute-start.1 = (bf16[384,1536]{1,0:T(8,128)(2,1)S(1)}, bf16[384,1536]{1,0:T(8,128)(2,1)S(1)}, u32[]{:S(2)}, u32[]{:S(2)}) collective-permute-start(bf16[384,1536]{1,0:T(8,128)(2,1)S(1)} %copy-done.8), channel_id=1, source_target_pairs={{0,16},{16,32},{32,48},{48,0},{1,17},{17,33},{33,49},{49,1},{2,18}... | collective-permute-start | bytes 3538952 | tf_op jit(solution)/shard_map/ppermute | solution.py:37
  41.8 29.5 %collective-permute-start = (bf16[384,1536]{1,0:T(8,128)(2,1)S(1)}, bf16[384,1536]{1,0:T(8,128)(2,1)S(1)}, u32[]{:S(2)}, u32[]{:S(2)}) collective-permute-start(bf16[384,1536]{1,0:T(8,128)(2,1)S(1)} %copy-done.8), channel_id=1, source_target_pairs={{0,48},{16,0},{32,16},{48,32},{1,49},{17,1},{33,17},{49,33},{2,50}... | collective-permute-start | bytes 3538952 | tf_op jit(solution)/shard_map/ppermute | solution.py:38
  69.5 14.9 %collective-permute-start.2 = (bf16[384,768]{1,0:T(8,128)(2,1)S(1)}, bf16[384,768]{1,0:T(8,128)(2,1)}, u32[]{:S(2)}, u32[]{:S(2)}) collective-permute-start(bf16[384,768]{1,0:T(8,128)(2,1)S(1)} %slice.54), channel_id=1, source_target_pairs={{0,16},{16,32},{32,48},{48,0},{1,17},{17,33},{33,49},{49,1},{2,18}... | collective-permute-start | bytes 1769480 | tf_op jit(solution)/shard_map/ppermute | solution.py:40
  72.3 15.6 %collective-permute-start.3 = (bf16[384,768]{1,0:T(8,128)(2,1)S(1)}, bf16[384,768]{1,0:T(8,128)(2,1)S(1)}, u32[]{:S(2)}, u32[]{:S(2)}) collective-permute-start(bf16[384,768]{1,0:T(8,128)(2,1)S(1)} %slice.55), channel_id=1, source_target_pairs={{0,48},{16,0},{32,16},{48,32},{1,49},{17,1},{33,17},{49,33},{2,50}... | collective-permute-start | bytes 1769480 | tf_op jit(solution)/shard_map/ppermute | solution.py:41
  96.3 13.0 %copy-start.1 = (f32[512,384]{1,0:T(8,128)S(1)}, f32[512,384]{1,0:T(8,128)}, u32[]{:S(2)}) copy-start(f32[512,384]{1,0:T(8,128)} %get-tuple-element.11) | copy-start | bytes 2359300
  96.3 13.1 %copy-start.2 = (f32[512,384]{1,0:T(8,128)S(1)}, f32[512,384]{1,0:T(8,128)}, u32[]{:S(2)}) copy-start(f32[512,384]{1,0:T(8,128)} %get-tuple-element.10) | copy-start | bytes 2359300
  97.4 16.3 %copy-start = (f32[512,384]{1,0:T(8,128)S(1)}, f32[512,384]{1,0:T(8,128)}, u32[]{:S(2)}) copy-start(f32[512,384]{1,0:T(8,128)} %get-tuple-element.9) | copy-start | bytes 2359300
  97.4 7.6 %collective-permute-start.13 = (f32[128,384]{1,0:T(8,128)S(1)}, f32[128,384]{1,0:T(8,128)S(1)}, u32[]{:S(2)}, u32[]{:S(2)}) collective-permute-start(f32[128,384]{1,0:T(8,128)S(1)} %dynamic-slice_bitcast_fusion), channel_id=1, source_target_pairs={{0,192},{64,0},{128,64},{192,128},{1,193},{65,1},{129,65},{193,129... | collective-permute-start | bytes 589832 | tf_op jit(solution)/shard_map/ppermute | solution.py:88
  99.6 9.7 %collective-permute-start.10 = (f32[128,384]{1,0:T(8,128)S(1)}, f32[128,384]{1,0:T(8,128)S(1)}, u32[]{:S(2)}, u32[]{:S(2)}) collective-permute-start(f32[128,384]{1,0:T(8,128)S(1)} %dynamic-slice_bitcast_fusion.1), channel_id=1, source_target_pairs={{0,64},{64,128},{128,192},{192,0},{1,65},{65,129},{129,193},{193,1... | collective-permute-start | bytes 589832 | tf_op jit(solution)/shard_map/ppermute | solution.py:88
  100.5 13.7 %copy-start.3 = (f32[512,384]{1,0:T(8,128)S(1)}, f32[512,384]{1,0:T(8,128)}, u32[]{:S(2)}) copy-start(f32[512,384]{1,0:T(8,128)} %get-tuple-element.12) | copy-start | bytes 2359300
  101.6 7.9 %collective-permute-start.7 = (f32[128,384]{1,0:T(8,128)S(1)}, f32[128,384]{1,0:T(8,128)S(1)}, u32[]{:S(2)}, u32[]{:S(2)}) collective-permute-start(f32[128,384]{1,0:T(8,128)S(1)} %dynamic-slice_bitcast_fusion.2), channel_id=1, source_target_pairs={{0,192},{64,0},{128,64},{192,128},{1,193},{65,1},{129,65},{193,129... | collective-permute-start | bytes 589832 | tf_op jit(solution)/shard_map/ppermute | solution.py:88
  105.0 8.8 %collective-permute-start.4 = (f32[128,384]{1,0:T(8,128)S(1)}, f32[128,384]{1,0:T(8,128)S(1)}, u32[]{:S(2)}, u32[]{:S(2)}) collective-permute-start(f32[128,384]{1,0:T(8,128)S(1)} %dynamic-slice_bitcast_fusion.3), channel_id=1, source_target_pairs={{0,64},{64,128},{128,192},{192,0},{1,65},{65,129},{129,193},{193,1... | collective-permute-start | bytes 589832 | tf_op jit(solution)/shard_map/ppermute | solution.py:88
  106.0 8.3 %collective-permute-start.14 = (f32[128,384]{1,0:T(8,128)S(1)}, f32[128,384]{1,0:T(8,128)S(1)}, u32[]{:S(2)}, u32[]{:S(2)}) collective-permute-start(f32[128,384]{1,0:T(8,128)S(1)} %bitcast_add_fusion.2), channel_id=1, source_target_pairs={{0,192},{64,0},{128,64},{192,128},{1,193},{65,1},{129,65},{193,129... | collective-permute-start | bytes 589832 | tf_op jit(solution)/shard_map/ppermute | solution.py:88
  109.3 9.1 %collective-permute-start.11 = (f32[128,384]{1,0:T(8,128)S(1)}, f32[128,384]{1,0:T(8,128)S(1)}, u32[]{:S(2)}, u32[]{:S(2)}) collective-permute-start(f32[128,384]{1,0:T(8,128)S(1)} %bitcast_add_fusion.5), channel_id=1, source_target_pairs={{0,64},{64,128},{128,192},{192,0},{1,65},{65,129},{129,193},{193,1... | collective-permute-start | bytes 589832 | tf_op jit(solution)/shard_map/ppermute | solution.py:88
  109.5 9.1 %collective-permute-start.8 = (f32[128,384]{1,0:T(8,128)S(1)}, f32[128,384]{1,0:T(8,128)S(1)}, u32[]{:S(2)}, u32[]{:S(2)}) collective-permute-start(f32[128,384]{1,0:T(8,128)S(1)} %bitcast_add_fusion.8), channel_id=1, source_target_pairs={{0,192},{64,0},{128,64},{192,128},{1,193},{65,1},{129,65},{193,129... | collective-permute-start | bytes 589832 | tf_op jit(solution)/shard_map/ppermute | solution.py:88
  113.8 9.1 %collective-permute-start.5 = (f32[128,384]{1,0:T(8,128)S(1)}, f32[128,384]{1,0:T(8,128)S(1)}, u32[]{:S(2)}, u32[]{:S(2)}) collective-permute-start(f32[128,384]{1,0:T(8,128)S(1)} %bitcast_add_fusion.11), channel_id=1, source_target_pairs={{0,64},{64,128},{128,192},{192,0},{1,65},{65,129},{129,193},{193,1... | collective-permute-start | bytes 589832 | tf_op jit(solution)/shard_map/ppermute | solution.py:88
  114.3 8.6 %collective-permute-start.15 = (f32[128,384]{1,0:T(8,128)S(1)}, f32[128,384]{1,0:T(8,128)S(1)}, u32[]{:S(2)}, u32[]{:S(2)}) collective-permute-start(f32[128,384]{1,0:T(8,128)S(1)} %bitcast_add_fusion.1), channel_id=1, source_target_pairs={{0,192},{64,0},{128,64},{192,128},{1,193},{65,1},{129,65},{193,129... | collective-permute-start | bytes 589832 | tf_op jit(solution)/shard_map/ppermute | solution.py:88
  118.5 8.2 %collective-permute-start.12 = (f32[128,384]{1,0:T(8,128)S(1)}, f32[128,384]{1,0:T(8,128)S(1)}, u32[]{:S(2)}, u32[]{:S(2)}) collective-permute-start(f32[128,384]{1,0:T(8,128)S(1)} %bitcast_add_fusion.4), channel_id=1, source_target_pairs={{0,64},{64,128},{128,192},{192,0},{1,65},{65,129},{129,193},{193,1... | collective-permute-start | bytes 589832 | tf_op jit(solution)/shard_map/ppermute | solution.py:88
  118.6 6.9 %collective-permute-start.9 = (f32[128,384]{1,0:T(8,128)S(1)}, f32[128,384]{1,0:T(8,128)S(1)}, u32[]{:S(2)}, u32[]{:S(2)}) collective-permute-start(f32[128,384]{1,0:T(8,128)S(1)} %bitcast_add_fusion.7), channel_id=1, source_target_pairs={{0,192},{64,0},{128,64},{192,128},{1,193},{65,1},{129,65},{193,129... | collective-permute-start | bytes 589832 | tf_op jit(solution)/shard_map/ppermute | solution.py:88
  122.8 7.0 %collective-permute-start.6 = (f32[128,384]{1,0:T(8,128)S(1)}, f32[128,384]{1,0:T(8,128)S(1)}, u32[]{:S(2)}, u32[]{:S(2)}) collective-permute-start(f32[128,384]{1,0:T(8,128)S(1)} %bitcast_add_fusion.10), channel_id=1, source_target_pairs={{0,64},{64,128},{128,192},{192,0},{1,65},{65,129},{129,193},{193,1... | collective-permute-start | bytes 589832 | tf_op jit(solution)/shard_map/ppermute | solution.py:88
  (4 other events, 7.5 us)

commit v14 on v12

--- a/solution.py
+++ b/solution.py
@@ -56,7 +56,7 @@
         o_ref[...] = source[:, start:start + quarter]
 
 
-def dot_pieces(a, pieces, tile=128):
+def dot_pieces(a, pieces, tile=256):
     m, kk = a.shape
     n = pieces[0].shape[1]
     full = lambda p: pl.BlockSpec(p.shape, lambda i: (0, 0))

time: 129 us -> 129 us (level)
  transfers between devices with their start and end apart: 18 -> 18, of which waited for: 12 -> 13; matrix products, arithmetic and copies ran while one was open for 4% -> 4% of each run, Pallas kernels for 0% -> 0%
where the time goes in v14:
time: 129 us
  waiting for transfers between devices  58.8 us (46%)
  starting transfers between devices  36 us (28%)
  local copies, waits for them, and re-layouts  12.6 us (10%)
  blocking collectives  10.1 us (8%)
  Pallas kernels  7.17 us (6%)
  other arithmetic  3.09 us (2%)
    ppermute x1, waiting for transfers between devices, ring_pieces(): from_left = lax.ppermute(block, axis, to_right)  26.1 us
    ppermute x12, starting transfers between devices, ring_reduce_scatter(): got = lax.ppermute(acc, axis, perm)  19.3 us
    all_to_all x1, blocking collectives, per_device(): part = lax.all_to_all(rolled, 'ry', split_axis=1, concat_axis=0, tiled=True)  10.1 us
    all_to_all x1, waiting for transfers between devices, per_device(): both = lax.all_to_all(both, 'col', split_axis=0, concat_axis=1, tiled=True)  9.92 us
    ppermute x12, waiting for transfers between devices, ring_reduce_scatter(): got = lax.ppermute(acc, axis, perm)  8.81 us
    all_to_all x1, starting transfers between devices, per_device(): both = lax.all_to_all(both, 'col', split_axis=0, concat_axis=1, tiled=True)  8.57 us
    pallas_call x1, Pallas kernels, dot_pieces(): pl.pallas_call(pieces_kernel, grid=(m // tile,), in_specs=[pl.BlockSpec((...  7.17 us
    all_to_all x1, waiting for transfers between devices, per_device(): lax.all_to_all(spread_out, 'col', split_axis=1, concat_axis=1, tiled=True)  6.4 us
  transfers between devices with their start and end apart: 18, of which 13 were waited for; matrix products, arithmetic and copies ran while one was open for 4% of the time, Pallas kernels for 0%

profile of v14, /device:TPU:6, one launch (start us, length us, event | category | flops | bytes accessed | tf_op | source)
XLA Modules:
  0.0 128.6 jit_solution(13277958050524245544)
XLA Ops:
  0.0 1.0 copy.31
  2.1 1.0 copy.28
  4.7 8.6 %all-to-all-start = ((bf16[128,2,384]{2,1,0:T(2,128)(2,1)}), bf16[128,2,384]{2,1,0:T(2,128)(2,1)S(1)}, u32[]{:S(2)}, u32[]{:S(2)}) async-start(bf16[128,2,384]{2,1,0:T(2,128)(2,1)} %copy.34), calls=%async_computation | async-start | bytes 393216 | tf_op jit(solution)/shard_map/all_to_all | solution.py:96
  13.3 9.9 %all-to-all-done = bf16[128,2,384]{2,1,0:T(2,128)(2,1)S(1)} async-done(((bf16[128,2,384]{2,1,0:T(2,128)(2,1)}), bf16[128,2,384]{2,1,0:T(2,128)(2,1)S(1)}, u32[]{:S(2)}, u32[]{:S(2)}) %all-to-all-start) | async-done | bytes 196640 | tf_op jit(solution)/shard_map/all_to_all | solution.py:96
  24.0 10.1 %all_to_all.36 = bf16[8,4,1536]{2,0,1:T(8,128)(2,1)S(1)} all-to-all(bf16[8,4,1536]{2,0,1:T(8,128)(2,1)S(1)} %bitcast.82), channel_id=1, replica_groups=mesh['ry'=4,'rx'=4,'col'=16] {'ry'}, dimensions={1} | all-to-all | bytes 196608 | tf_op jit(solution)/shard_map/all_to_all | solution.py:109
  34.1 1.3 %broadcast_in_dim.16 = bf16[4,16,8,1536]{3,2,0,1:T(8,128)(2,1)} broadcast(bf16[4,8,1536]{2,1,0:T(8,128)(2,1)S(1)} %bitcast.83), dimensions={0,2,3} | broadcast | bytes 1671168 | tf_op jit(solution)/shard_map/broadcast_in_dim | solution.py:112
  35.5 3.8 %all-to-all-start.2 = ((bf16[4,16,8,1536]{3,2,0,1:T(8,128)(2,1)}), bf16[4,16,8,1536]{3,2,0,1:T(8,128)(2,1)S(1)}, u32[]{:S(2)}, u32[]{:S(2)}) async-start(bf16[4,16,8,1536]{3,2,0,1:T(8,128)(2,1)} %broadcast_in_dim.16), calls=%async_computation.2 | async-start | bytes 3145728 | tf_op jit(solution)/shard_map/all_to_all | solution.py:113
  39.9 1.5 %collective-permute-start = (bf16[384,1536]{1,0:T(8,128)(2,1)S(1)}, bf16[384,1536]{1,0:T(8,128)(2,1)S(1)}, u32[]{:S(2)}, u32[]{:S(2)}) collective-permute-start(bf16[384,1536]{1,0:T(8,128)(2,1)S(1)} %copy-done.8), channel_id=1, source_target_pairs={{0,48},{16,0},{32,16},{48,32},{1,49},{17,1},{33,17},{49,33},{2,50}... | collective-permute-start | bytes 3538952 | tf_op jit(solution)/shard_map/ppermute | solution.py:35
  41.4 26.1 %collective-permute-done.1.w3_ref = bf16[384,1536]{1,0:T(8,128)(2,1)S(1)} collective-permute-done((bf16[384,1536]{1,0:T(8,128)(2,1)S(1)}, bf16[384,1536]{1,0:T(8,128)(2,1)S(1)}, u32[]{:S(2)}, u32[]{:S(2)}) %collective-permute-start.1) | collective-permute-done | bytes 1179680 | tf_op jit(solution)/shard_map/ppermute | solution.py:34
  67.6 1.8 %collective-permute-start.2 = (bf16[384,768]{1,0:T(8,128)(2,1)S(1)}, bf16[384,768]{1,0:T(8,128)(2,1)}, u32[]{:S(2)}, u32[]{:S(2)}) collective-permute-start(bf16[384,768]{1,0:T(8,128)(2,1)S(1)} %slice.18), channel_id=1, source_target_pairs={{0,16},{16,32},{32,48},{48,0},{1,17},{17,33},{33,49},{49,1},{2,18}... | collective-permute-start | bytes 1769480 | tf_op jit(solution)/shard_map/ppermute | solution.py:37
  70.7 6.4 %all-to-all-done.2 = bf16[4,16,8,1536]{3,2,0,1:T(8,128)(2,1)S(1)} async-done(((bf16[4,16,8,1536]{3,2,0,1:T(8,128)(2,1)}), bf16[4,16,8,1536]{3,2,0,1:T(8,128)(2,1)S(1)}, u32[]{:S(2)}, u32[]{:S(2)}) %all-to-all-start.2) | async-done | bytes 1572896 | tf_op jit(solution)/shard_map/all_to_all | solution.py:113
  77.1 1.3 %copy.35 = bf16[4,16,8,1536]{3,2,1,0:T(8,128)(2,1)} copy(bf16[4,16,8,1536]{3,2,0,1:T(8,128)(2,1)S(1)} %all-to-all-done.2) | data formatting | bytes 3145728 | tf_op jit(solution)/shard_map/all_to_all | solution.py:113
  78.4 4.1 %collective-permute-done.2.w2lo_ref = bf16[384,768]{1,0:T(8,128)(2,1)} collective-permute-done((bf16[384,768]{1,0:T(8,128)(2,1)S(1)}, bf16[384,768]{1,0:T(8,128)(2,1)}, u32[]{:S(2)}, u32[]{:S(2)}) %collective-permute-start.2) | collective-permute-done | bytes 589856 | tf_op jit(solution)/shard_map/ppermute | solution.py:37
  82.5 3.5 %collective-permute-done.3.w2hi_ref = bf16[384,768]{1,0:T(8,128)(2,1)S(1)} collective-permute-done((bf16[384,768]{1,0:T(8,128)(2,1)S(1)}, bf16[384,768]{1,0:T(8,128)(2,1)S(1)}, u32[]{:S(2)}, u32[]{:S(2)}) %collective-permute-start.3) | collective-permute-done | bytes 589856 | tf_op jit(solution)/shard_map/ppermute | solution.py:38
  86.9 7.2 %shard_map.64 = (f32[512,384]{1,0:T(8,128)}, f32[512,384]{1,0:T(8,128)}, f32[512,384]{1,0:T(8,128)}, f32[512,384]{1,0:T(8,128)}) custom-call(bf16[512,1536]{1,0:T(8,128)(2,1)} %bitcast.64, bf16[384,1536]{1,0:T(8,128)(2,1)} %w0_ref.1, bf16[384,1536]{1,0:T(8,128)(2,1)} %copy-done.5, bf16[384,768]{1,0:T(8,128)(2,1)} %collective-permute-done.2.w2lo_ref, ...), custom_call_target="tpu_custom_call" | custom-call | flops 2415919104 | bytes 9437184 | tf_op jit(solution)/shard_map/pallas_call | solution.py:65
  94.1 1.1 dynamic-slice_bitcast_fusion
  95.2 1.2 collective-permute-start.13
  99.3 2.5 %collective-permute-start.7 = (f32[128,384]{1,0:T(8,128)S(1)}, f32[128,384]{1,0:T(8,128)S(1)}, u32[]{:S(2)}, u32[]{:S(2)}) collective-permute-start(f32[128,384]{1,0:T(8,128)S(1)} %dynamic-slice_bitcast_fusion.2), channel_id=1, source_target_pairs={{0,192},{64,0},{128,64},{192,128},{1,193},{65,1},{129,65},{193,129... | collective-permute-start | bytes 589832 | tf_op jit(solution)/shard_map/ppermute | solution.py:85
  103.8 3.3 %collective-permute-start.14 = (f32[128,384]{1,0:T(8,128)S(1)}, f32[128,384]{1,0:T(8,128)S(1)}, u32[]{:S(2)}, u32[]{:S(2)}) collective-permute-start(f32[128,384]{1,0:T(8,128)S(1)} %bitcast_add_fusion.2), channel_id=1, source_target_pairs={{0,192},{64,0},{128,64},{192,128},{1,193},{65,1},{129,65},{193,129... | collective-permute-start | bytes 589832 | tf_op jit(solution)/shard_map/ppermute | solution.py:85
  107.2 3.5 %collective-permute-start.8 = (f32[128,384]{1,0:T(8,128)S(1)}, f32[128,384]{1,0:T(8,128)S(1)}, u32[]{:S(2)}, u32[]{:S(2)}) collective-permute-start(f32[128,384]{1,0:T(8,128)S(1)} %bitcast_add_fusion.8), channel_id=1, source_target_pairs={{0,192},{64,0},{128,64},{192,128},{1,193},{65,1},{129,65},{193,129... | collective-permute-start | bytes 589832 | tf_op jit(solution)/shard_map/ppermute | solution.py:85
  112.3 3.8 %collective-permute-start.15 = (f32[128,384]{1,0:T(8,128)S(1)}, f32[128,384]{1,0:T(8,128)S(1)}, u32[]{:S(2)}, u32[]{:S(2)}) collective-permute-start(f32[128,384]{1,0:T(8,128)S(1)} %bitcast_add_fusion.1), channel_id=1, source_target_pairs={{0,192},{64,0},{128,64},{192,128},{1,193},{65,1},{129,65},{193,129... | collective-permute-start | bytes 589832 | tf_op jit(solution)/shard_map/ppermute | solution.py:85
  116.6 3.8 %collective-permute-start.9 = (f32[128,384]{1,0:T(8,128)S(1)}, f32[128,384]{1,0:T(8,128)S(1)}, u32[]{:S(2)}, u32[]{:S(2)}) collective-permute-start(f32[128,384]{1,0:T(8,128)S(1)} %bitcast_add_fusion.7), channel_id=1, source_target_pairs={{0,192},{64,0},{128,64},{192,128},{1,193},{65,1},{129,65},{193,129... | collective-permute-start | bytes 589832 | tf_op jit(solution)/shard_map/ppermute | solution.py:85
  120.7 2.8 %collective-permute-done.9 = f32[128,384]{1,0:T(8,128)S(1)} collective-permute-done((f32[128,384]{1,0:T(8,128)S(1)}, f32[128,384]{1,0:T(8,128)S(1)}, u32[]{:S(2)}, u32[]{:S(2)}) %collective-permute-start.9) | collective-permute-done | bytes 196640 | tf_op jit(solution)/shard_map/ppermute | solution.py:85
  124.4 3.1 %collective-permute-done.6 = f32[128,384]{1,0:T(8,128)S(1)} collective-permute-done((f32[128,384]{1,0:T(8,128)S(1)}, f32[128,384]{1,0:T(8,128)S(1)}, u32[]{:S(2)}, u32[]{:S(2)}) %collective-permute-start.6) | collective-permute-done | bytes 196640 | tf_op jit(solution)/shard_map/ppermute | solution.py:85
  (71 shorter events, 15.6 us)
Async XLA Ops:
  2.1 11.2 %copy-start.7 = (f32[6144]{0:T(1024)S(1)}, f32[6144]{0:T(1024)}, u32[]{:S(2)}) copy-start(f32[6144]{0:T(1024)} %param.10) | copy-start | bytes 73732
  4.7 18.5 %all-to-all-start = ((bf16[128,2,384]{2,1,0:T(2,128)(2,1)}), bf16[128,2,384]{2,1,0:T(2,128)(2,1)S(1)}, u32[]{:S(2)}, u32[]{:S(2)}) async-start(bf16[128,2,384]{2,1,0:T(2,128)(2,1)} %copy.34), calls=%async_computation | async-start | bytes 393216 | tf_op jit(solution)/shard_map/all_to_all | solution.py:96
  35.5 3.9 %copy-start.8 = (bf16[384,1536]{1,0:T(8,128)(2,1)S(1)}, bf16[384,1536]{1,0:T(8,128)(2,1)}, u32[]{:S(2)}) copy-start(bf16[384,1536]{1,0:T(8,128)(2,1)} %w0_ref.1) | copy-start | bytes 3538948
  35.5 41.7 %all-to-all-start.2 = ((bf16[4,16,8,1536]{3,2,0,1:T(8,128)(2,1)}), bf16[4,16,8,1536]{3,2,0,1:T(8,128)(2,1)S(1)}, u32[]{:S(2)}, u32[]{:S(2)}) async-start(bf16[4,16,8,1536]{3,2,0,1:T(8,128)(2,1)} %broadcast_in_dim.16), calls=%async_computation.2 | async-start | bytes 3145728 | tf_op jit(solution)/shard_map/all_to_all | solution.py:113
  39.3 28.2 %collective-permute-start.1 = (bf16[384,1536]{1,0:T(8,128)(2,1)S(1)}, bf16[384,1536]{1,0:T(8,128)(2,1)S(1)}, u32[]{:S(2)}, u32[]{:S(2)}) collective-permute-start(bf16[384,1536]{1,0:T(8,128)(2,1)S(1)} %copy-done.8), channel_id=1, source_target_pairs={{0,16},{16,32},{32,48},{48,0},{1,17},{17,33},{33,49},{49,1},{2,18}... | collective-permute-start | bytes 3538952 | tf_op jit(solution)/shard_map/ppermute | solution.py:34
  39.9 29.5 %collective-permute-start = (bf16[384,1536]{1,0:T(8,128)(2,1)S(1)}, bf16[384,1536]{1,0:T(8,128)(2,1)S(1)}, u32[]{:S(2)}, u32[]{:S(2)}) collective-permute-start(bf16[384,1536]{1,0:T(8,128)(2,1)S(1)} %copy-done.8), channel_id=1, source_target_pairs={{0,48},{16,0},{32,16},{48,32},{1,49},{17,1},{33,17},{49,33},{2,50}... | collective-permute-start | bytes 3538952 | tf_op jit(solution)/shard_map/ppermute | solution.py:35
  67.6 14.9 %collective-permute-start.2 = (bf16[384,768]{1,0:T(8,128)(2,1)S(1)}, bf16[384,768]{1,0:T(8,128)(2,1)}, u32[]{:S(2)}, u32[]{:S(2)}) collective-permute-start(bf16[384,768]{1,0:T(8,128)(2,1)S(1)} %slice.18), channel_id=1, source_target_pairs={{0,16},{16,32},{32,48},{48,0},{1,17},{17,33},{33,49},{49,1},{2,18}... | collective-permute-start | bytes 1769480 | tf_op jit(solution)/shard_map/ppermute | solution.py:37
  70.4 15.6 %collective-permute-start.3 = (bf16[384,768]{1,0:T(8,128)(2,1)S(1)}, bf16[384,768]{1,0:T(8,128)(2,1)S(1)}, u32[]{:S(2)}, u32[]{:S(2)}) collective-permute-start(bf16[384,768]{1,0:T(8,128)(2,1)S(1)} %slice.19), channel_id=1, source_target_pairs={{0,48},{16,0},{32,16},{48,32},{1,49},{17,1},{33,17},{49,33},{2,50}... | collective-permute-start | bytes 1769480 | tf_op jit(solution)/shard_map/ppermute | solution.py:38
  94.1 13.0 %copy-start.1 = (f32[512,384]{1,0:T(8,128)S(1)}, f32[512,384]{1,0:T(8,128)}, u32[]{:S(2)}) copy-start(f32[512,384]{1,0:T(8,128)} %get-tuple-element.11) | copy-start | bytes 2359300
  94.1 13.1 %copy-start.2 = (f32[512,384]{1,0:T(8,128)S(1)}, f32[512,384]{1,0:T(8,128)}, u32[]{:S(2)}) copy-start(f32[512,384]{1,0:T(8,128)} %get-tuple-element.10) | copy-start | bytes 2359300
  95.2 16.3 %copy-start = (f32[512,384]{1,0:T(8,128)S(1)}, f32[512,384]{1,0:T(8,128)}, u32[]{:S(2)}) copy-start(f32[512,384]{1,0:T(8,128)} %get-tuple-element.9) | copy-start | bytes 2359300
  95.2 7.6 %collective-permute-start.13 = (f32[128,384]{1,0:T(8,128)S(1)}, f32[128,384]{1,0:T(8,128)S(1)}, u32[]{:S(2)}, u32[]{:S(2)}) collective-permute-start(f32[128,384]{1,0:T(8,128)S(1)} %dynamic-slice_bitcast_fusion), channel_id=1, source_target_pairs={{0,192},{64,0},{128,64},{192,128},{1,193},{65,1},{129,65},{193,129... | collective-permute-start | bytes 589832 | tf_op jit(solution)/shard_map/ppermute | solution.py:85
  97.4 9.7 %collective-permute-start.10 = (f32[128,384]{1,0:T(8,128)S(1)}, f32[128,384]{1,0:T(8,128)S(1)}, u32[]{:S(2)}, u32[]{:S(2)}) collective-permute-start(f32[128,384]{1,0:T(8,128)S(1)} %dynamic-slice_bitcast_fusion.1), channel_id=1, source_target_pairs={{0,64},{64,128},{128,192},{192,0},{1,65},{65,129},{129,193},{193,1... | collective-permute-start | bytes 589832 | tf_op jit(solution)/shard_map/ppermute | solution.py:85
  98.3 14.0 %copy-start.3 = (f32[512,384]{1,0:T(8,128)S(1)}, f32[512,384]{1,0:T(8,128)}, u32[]{:S(2)}) copy-start(f32[512,384]{1,0:T(8,128)} %get-tuple-element.12) | copy-start | bytes 2359300
  99.3 7.9 %collective-permute-start.7 = (f32[128,384]{1,0:T(8,128)S(1)}, f32[128,384]{1,0:T(8,128)S(1)}, u32[]{:S(2)}, u32[]{:S(2)}) collective-permute-start(f32[128,384]{1,0:T(8,128)S(1)} %dynamic-slice_bitcast_fusion.2), channel_id=1, source_target_pairs={{0,192},{64,0},{128,64},{192,128},{1,193},{65,1},{129,65},{193,129... | collective-permute-start | bytes 589832 | tf_op jit(solution)/shard_map/ppermute | solution.py:85
  102.7 8.8 %collective-permute-start.4 = (f32[128,384]{1,0:T(8,128)S(1)}, f32[128,384]{1,0:T(8,128)S(1)}, u32[]{:S(2)}, u32[]{:S(2)}) collective-permute-start(f32[128,384]{1,0:T(8,128)S(1)} %dynamic-slice_bitcast_fusion.3), channel_id=1, source_target_pairs={{0,64},{64,128},{128,192},{192,0},{1,65},{65,129},{129,193},{193,1... | collective-permute-start | bytes 589832 | tf_op jit(solution)/shard_map/ppermute | solution.py:85
  103.8 8.5 %collective-permute-start.14 = (f32[128,384]{1,0:T(8,128)S(1)}, f32[128,384]{1,0:T(8,128)S(1)}, u32[]{:S(2)}, u32[]{:S(2)}) collective-permute-start(f32[128,384]{1,0:T(8,128)S(1)} %bitcast_add_fusion.2), channel_id=1, source_target_pairs={{0,192},{64,0},{128,64},{192,128},{1,193},{65,1},{129,65},{193,129... | collective-permute-start | bytes 589832 | tf_op jit(solution)/shard_map/ppermute | solution.py:85
  107.1 9.1 %collective-permute-start.11 = (f32[128,384]{1,0:T(8,128)S(1)}, f32[128,384]{1,0:T(8,128)S(1)}, u32[]{:S(2)}, u32[]{:S(2)}) collective-permute-start(f32[128,384]{1,0:T(8,128)S(1)} %bitcast_add_fusion.5), channel_id=1, source_target_pairs={{0,64},{64,128},{128,192},{192,0},{1,65},{65,129},{129,193},{193,1... | collective-permute-start | bytes 589832 | tf_op jit(solution)/shard_map/ppermute | solution.py:85
  107.2 9.3 %collective-permute-start.8 = (f32[128,384]{1,0:T(8,128)S(1)}, f32[128,384]{1,0:T(8,128)S(1)}, u32[]{:S(2)}, u32[]{:S(2)}) collective-permute-start(f32[128,384]{1,0:T(8,128)S(1)} %bitcast_add_fusion.8), channel_id=1, source_target_pairs={{0,192},{64,0},{128,64},{192,128},{1,193},{65,1},{129,65},{193,129... | collective-permute-start | bytes 589832 | tf_op jit(solution)/shard_map/ppermute | solution.py:85
  111.5 9.0 %collective-permute-start.5 = (f32[128,384]{1,0:T(8,128)S(1)}, f32[128,384]{1,0:T(8,128)S(1)}, u32[]{:S(2)}, u32[]{:S(2)}) collective-permute-start(f32[128,384]{1,0:T(8,128)S(1)} %bitcast_add_fusion.11), channel_id=1, source_target_pairs={{0,64},{64,128},{128,192},{192,0},{1,65},{65,129},{129,193},{193,1... | collective-permute-start | bytes 589832 | tf_op jit(solution)/shard_map/ppermute | solution.py:85
  112.3 8.3 %collective-permute-start.15 = (f32[128,384]{1,0:T(8,128)S(1)}, f32[128,384]{1,0:T(8,128)S(1)}, u32[]{:S(2)}, u32[]{:S(2)}) collective-permute-start(f32[128,384]{1,0:T(8,128)S(1)} %bitcast_add_fusion.1), channel_id=1, source_target_pairs={{0,192},{64,0},{128,64},{192,128},{1,193},{65,1},{129,65},{193,129... | collective-permute-start | bytes 589832 | tf_op jit(solution)/shard_map/ppermute | solution.py:85
  116.2 8.2 %collective-permute-start.12 = (f32[128,384]{1,0:T(8,128)S(1)}, f32[128,384]{1,0:T(8,128)S(1)}, u32[]{:S(2)}, u32[]{:S(2)}) collective-permute-start(f32[128,384]{1,0:T(8,128)S(1)} %bitcast_add_fusion.4), channel_id=1, source_target_pairs={{0,64},{64,128},{128,192},{192,0},{1,65},{65,129},{129,193},{193,1... | collective-permute-start | bytes 589832 | tf_op jit(solution)/shard_map/ppermute | solution.py:85
  116.6 7.0 %collective-permute-start.9 = (f32[128,384]{1,0:T(8,128)S(1)}, f32[128,384]{1,0:T(8,128)S(1)}, u32[]{:S(2)}, u32[]{:S(2)}) collective-permute-start(f32[128,384]{1,0:T(8,128)S(1)} %bitcast_add_fusion.7), channel_id=1, source_target_pairs={{0,192},{64,0},{128,64},{192,128},{1,193},{65,1},{129,65},{193,129... | collective-permute-start | bytes 589832 | tf_op jit(solution)/shard_map/ppermute | solution.py:85
  120.6 7.0 %collective-permute-start.6 = (f32[128,384]{1,0:T(8,128)S(1)}, f32[128,384]{1,0:T(8,128)S(1)}, u32[]{:S(2)}, u32[]{:S(2)}) collective-permute-start(f32[128,384]{1,0:T(8,128)S(1)} %bitcast_add_fusion.10), channel_id=1, source_target_pairs={{0,64},{64,128},{128,192},{192,0},{1,65},{65,129},{129,193},{193,1... | collective-permute-start | bytes 589832 | tf_op jit(solution)/shard_map/ppermute | solution.py:85
  (4 other events, 7.5 us)

commit v15 on v14

--- a/solution.py
+++ b/solution.py
@@ -39,39 +39,60 @@
     return block, from_right, far_low, far_high, from_left
 
 
-def pieces_kernel(a_ref, w0_ref, w1_ref, w2lo_ref, w2hi_ref, w3_ref, *o_refs):
+def near_kernel(a_ref, w0_ref, w1_ref, w3_ref, *o_refs):
     k = w0_ref.shape[0]
-    half = w2lo_ref.shape[1]
     quarter = o_refs[0].shape[1]
     a = a_ref[...]
     base = jnp.dot(a[:, 0:k], w0_ref[...], preferred_element_type=jnp.float32)
     base = base + jnp.dot(a[:, k:2 * k], w1_ref[...], preferred_element_type=jnp.float32)
     base = base + jnp.dot(a[:, 3 * k:4 * k], w3_ref[...], preferred_element_type=jnp.float32)
-    far = a[:, 2 * k:3 * k]
-    low = base[:, 0:half] + jnp.dot(far, w2lo_ref[...], preferred_element_type=jnp.float32)
-    high = base[:, half:] + jnp.dot(far, w2hi_ref[...], preferred_element_type=jnp.float32)
     for q, o_ref in enumerate(o_refs):
+        o_ref[...] = base[:, q * quarter:(q + 1) * quarter]
+
+
+def far_kernel(a_ref, w2lo_ref, w2hi_ref, *refs):
+    k = w2lo_ref.shape[0]
+    acc_refs, o_refs = refs[:4], refs[4:]
+    quarter = o_refs[0].shape[1]
+    far = a_ref[:, 2 * k:3 * k]
+    low = jnp.dot(far, w2lo_ref[...], preferred_element_type=jnp.float32)
+    high = jnp.dot(far, w2hi_ref[...], preferred_element_type=jnp.float32)
+    for q, (acc_ref, o_ref) in enumerate(zip(acc_refs, o_refs)):
         source = low if q < 2 else high
         start = (q % 2) * quarter
-        o_ref[...] = source[:, start:start + quarter]
+        o_ref[...] = acc_ref[...] + source[:, start:start + quarter]
 
 
 def dot_pieces(a, pieces, tile=256):
     m, kk = a.shape
     n = pieces[0].shape[1]
+    own, right, far_low, far_high, left = pieces
     full = lambda p: pl.BlockSpec(p.shape, lambda i: (0, 0))
     spec = pl.BlockSpec((tile, n // 4), lambda i: (i, 0))
     shape = jax.ShapeDtypeStruct((m, n // 4), jnp.float32)
-    return pl.pallas_call(
-        pieces_kernel,
+    a_spec = pl.BlockSpec((tile, kk), lambda i: (i, 0))
+    near_w = (own, right, left)
+    quarters = pl.pallas_call(
+        near_kernel,
         grid=(m // tile,),
-        in_specs=[pl.BlockSpec((tile, kk), lambda i: (i, 0))] + [full(p) for p in pieces],
+        in_specs=[a_spec] + [full(p) for p in near_w],
         out_specs=(spec,) * 4,
         out_shape=(shape,) * 4,
         cost_estimate=pl.CostEstimate(
-            flops=2 * m * kk * n, transcendentals=0, bytes_accessed=a.size * 2 + sum(p.size * 2 for p in pieces) + m * n * 4
+            flops=2 * m * 3 * own.size, transcendentals=0, bytes_accessed=a.size * 2 + 3 * own.size * 2 + m * n * 4
         ),
-    )(a, *pieces)
+    )(a, *near_w)
+    return pl.pallas_call(
+        far_kernel,
+        grid=(m // tile,),
+        in_specs=[a_spec, full(far_low), full(far_high)] + [spec] * 4,
+        out_specs=(spec,) * 4,
+        out_shape=(shape,) * 4,
+        input_output_aliases={3: 0, 4: 1, 5: 2, 6: 3},
+        cost_estimate=pl.CostEstimate(
+            flops=2 * m * own.size, transcendentals=0, bytes_accessed=a.size * 2 + own.size * 2 + 2 * m * n * 4
+        ),
+    )(a, far_low, far_high, *quarters)
 
 
 def ring_reduce_scatter(parts, axis, n):

time: 129 us -> 128 us (level)
  waiting for transfers between devices: 58.8 us -> 53.1 us
  Pallas kernels: 7.17 us -> 10.4 us
  local copies, waits for them, and re-layouts: 12.6 us -> 14.5 us
    ppermute x1, waiting for transfers between devices: 4.06 us -> 0.01 us  [ring_pieces(): far_low = lax.ppermute(from_left[:, :half], axis, to_right)]
    pallas_call x1 -> x2, Pallas kernels: 7.17 us -> 10.4 us  [the longest x1 5.98 us: dot_pieces(): pl.pallas_call(near_kernel, grid=(m // tile,), in_specs=[a_spec] + [full(...]
    all_to_all x1, waiting for transfers between devices: 6.4 us -> 4.4 us  [per_device(): lax.all_to_all(spread_out, 'col', split_axis=1, concat_axis=1, tiled=True)]
  transfers between devices with their start and end apart: 18 -> 18, of which waited for: 13 -> 12; matrix products, arithmetic and copies ran while one was open for 4% -> 5% of each run, Pallas kernels for 0% -> 5%
where the time goes in v15:
time: 128 us
  waiting for transfers between devices  53.1 us (41%)
  starting transfers between devices  35.8 us (28%)
  local copies, waits for them, and re-layouts  14.5 us (11%)
  Pallas kernels  10.4 us (8%)
  blocking collectives  10.1 us (8%)
  other arithmetic  3.11 us (2%)
    ppermute x1, waiting for transfers between devices, ring_pieces(): from_left = lax.ppermute(block, axis, to_right)  26.3 us
    ppermute x12, starting transfers between devices, ring_reduce_scatter(): got = lax.ppermute(acc, axis, perm)  19.3 us
    all_to_all x1, blocking collectives, per_device(): part = lax.all_to_all(rolled, 'ry', split_axis=1, concat_axis=0, tiled=True)  10.1 us
    all_to_all x1, waiting for transfers between devices, per_device(): both = lax.all_to_all(both, 'col', split_axis=0, concat_axis=1, tiled=True)  9.92 us
    ppermute x12, waiting for transfers between devices, ring_reduce_scatter(): got = lax.ppermute(acc, axis, perm)  8.79 us
    all_to_all x1, starting transfers between devices, per_device(): both = lax.all_to_all(both, 'col', split_axis=0, concat_axis=1, tiled=True)  8.57 us
    pallas_call x1, Pallas kernels, dot_pieces(): pl.pallas_call(near_kernel, grid=(m // tile,), in_specs=[a_spec] + [full(...  5.98 us
    unnamed x24, local copies, waits for them, and re-layouts  5.98 us
  transfers between devices with their start and end apart: 18, of which 12 were waited for; matrix products, arithmetic and copies ran while one was open for 5% of the time, Pallas kernels for 5%

profile of v15, /device:TPU:6, one launch (start us, length us, event | category | flops | bytes accessed | tf_op | source)
XLA Modules:
  0.0 127.8 jit_solution(10817817884951241452)
XLA Ops:
  0.0 1.0 copy.35
  4.7 8.6 %all-to-all-start = ((bf16[128,2,384]{2,1,0:T(2,128)(2,1)}), bf16[128,2,384]{2,1,0:T(2,128)(2,1)S(1)}, u32[]{:S(2)}, u32[]{:S(2)}) async-start(bf16[128,2,384]{2,1,0:T(2,128)(2,1)} %copy.38), calls=%async_computation | async-start | bytes 393216 | tf_op jit(solution)/shard_map/all_to_all | solution.py:117
  13.3 9.9 %all-to-all-done = bf16[128,2,384]{2,1,0:T(2,128)(2,1)S(1)} async-done(((bf16[128,2,384]{2,1,0:T(2,128)(2,1)}), bf16[128,2,384]{2,1,0:T(2,128)(2,1)S(1)}, u32[]{:S(2)}, u32[]{:S(2)}) %all-to-all-start) | async-done | bytes 196640 | tf_op jit(solution)/shard_map/all_to_all | solution.py:117
  24.0 10.1 %all_to_all.36 = bf16[8,4,1536]{2,0,1:T(8,128)(2,1)S(1)} all-to-all(bf16[8,4,1536]{2,0,1:T(8,128)(2,1)S(1)} %bitcast.83), channel_id=1, replica_groups=mesh['ry'=4,'rx'=4,'col'=16] {'ry'}, dimensions={1} | all-to-all | bytes 196608 | tf_op jit(solution)/shard_map/all_to_all | solution.py:130
  34.1 1.3 %broadcast_in_dim.16 = bf16[4,16,8,1536]{3,2,0,1:T(8,128)(2,1)} broadcast(bf16[4,8,1536]{2,1,0:T(8,128)(2,1)S(1)} %bitcast.84), dimensions={0,2,3} | broadcast | bytes 1671168 | tf_op jit(solution)/shard_map/broadcast_in_dim | solution.py:133
  35.5 3.7 %all-to-all-start.2 = ((bf16[4,16,8,1536]{3,2,0,1:T(8,128)(2,1)}), bf16[4,16,8,1536]{3,2,0,1:T(8,128)(2,1)S(1)}, u32[]{:S(2)}, u32[]{:S(2)}) async-start(bf16[4,16,8,1536]{3,2,0,1:T(8,128)(2,1)} %broadcast_in_dim.16), calls=%async_computation.2 | async-start | bytes 3145728 | tf_op jit(solution)/shard_map/all_to_all | solution.py:134
  39.7 1.5 %collective-permute-start.2 = (bf16[384,1536]{1,0:T(8,128)(2,1)}, bf16[384,1536]{1,0:T(8,128)(2,1)S(1)}, u32[]{:S(2)}, u32[]{:S(2)}) collective-permute-start(bf16[384,1536]{1,0:T(8,128)(2,1)} %w0_ref.1), channel_id=1, source_target_pairs={{0,48},{16,0},{32,16},{48,32},{1,49},{17,1},{33,17},{49,33},{2,50}... | collective-permute-start | bytes 3538952 | tf_op jit(solution)/shard_map/ppermute | solution.py:35
  41.3 26.3 %collective-permute-done.w3_ref = bf16[384,1536]{1,0:T(8,128)(2,1)S(1)} collective-permute-done((bf16[384,1536]{1,0:T(8,128)(2,1)}, bf16[384,1536]{1,0:T(8,128)(2,1)S(1)}, u32[]{:S(2)}, u32[]{:S(2)}) %collective-permute-start) | collective-permute-done | bytes 1179680 | tf_op jit(solution)/shard_map/ppermute | solution.py:34
  67.6 1.0 copy-done.6
  68.6 1.8 %collective-permute-start.1 = (bf16[384,768]{1,0:T(8,128)(2,1)S(1)}, bf16[384,768]{1,0:T(8,128)(2,1)S(1)}, u32[]{:S(2)}, u32[]{:S(2)}) collective-permute-start(bf16[384,768]{1,0:T(8,128)(2,1)S(1)} %slice.18), channel_id=1, source_target_pairs={{0,16},{16,32},{32,48},{48,0},{1,17},{17,33},{33,49},{49,1},{2,18}... | collective-permute-start | bytes 1769480 | tf_op jit(solution)/shard_map/ppermute | solution.py:37
  72.6 4.4 %all-to-all-done.2 = bf16[4,16,8,1536]{3,2,0,1:T(8,128)(2,1)S(1)} async-done(((bf16[4,16,8,1536]{3,2,0,1:T(8,128)(2,1)}), bf16[4,16,8,1536]{3,2,0,1:T(8,128)(2,1)S(1)}, u32[]{:S(2)}, u32[]{:S(2)}) %all-to-all-start.2) | async-done | bytes 1572896 | tf_op jit(solution)/shard_map/all_to_all | solution.py:134
  77.0 1.3 %copy.39 = bf16[4,16,8,1536]{3,2,1,0:T(8,128)(2,1)} copy(bf16[4,16,8,1536]{3,2,0,1:T(8,128)(2,1)S(1)} %all-to-all-done.2) | data formatting | bytes 3145728 | tf_op jit(solution)/shard_map/all_to_all | solution.py:134
  78.3 6.0 %shard_map.64 = (f32[512,384]{1,0:T(8,128)}, f32[512,384]{1,0:T(8,128)}, f32[512,384]{1,0:T(8,128)}, f32[512,384]{1,0:T(8,128)}) custom-call(bf16[512,1536]{1,0:T(8,128)(2,1)} %bitcast.63, bf16[384,1536]{1,0:T(8,128)(2,1)} %w0_ref.1, bf16[384,1536]{1,0:T(8,128)(2,1)} %copy-done.7, bf16[384,1536]{1,0:T(8,128)(2,1)} %copy-done.6), custom_call_target="tpu_custom_call" | custom-call | flops 1811939328 | bytes 8257536 | tf_op jit(solution)/shard_map/pallas_call | solution.py:75
  84.3 3.7 %collective-permute-done.3.w2hi_ref = bf16[384,768]{1,0:T(8,128)(2,1)S(1)} collective-permute-done((bf16[384,768]{1,0:T(8,128)(2,1)}, bf16[384,768]{1,0:T(8,128)(2,1)S(1)}, u32[]{:S(2)}, u32[]{:S(2)}) %collective-permute-start.3) | collective-permute-done | bytes 589856 | tf_op jit(solution)/shard_map/ppermute | solution.py:38
  88.9 4.4 %shard_map.65 = (f32[512,384]{1,0:T(8,128)}, f32[512,384]{1,0:T(8,128)}, f32[512,384]{1,0:T(8,128)}, f32[512,384]{1,0:T(8,128)}) custom-call(bf16[512,1536]{1,0:T(8,128)(2,1)} %bitcast.64, bf16[384,768]{1,0:T(8,128)(2,1)} %copy-done.4, bf16[384,768]{1,0:T(8,128)(2,1)} %copy-done.5, ...), custom_call_target="tpu_custom_call", output_to_operand_aliasing={{0}: (3, {}), {1}: (4, {}), {2}: (5, {}), {3}: (6, {})} | custom-call | flops 603979776 | bytes 9043968 | tf_op jit(solution)/shard_map/pallas_call | solution.py:85
  93.3 1.1 dynamic-slice_bitcast_fusion
  94.4 1.2 collective-permute-start.13
  98.5 2.5 %collective-permute-start.7 = (f32[128,384]{1,0:T(8,128)S(1)}, f32[128,384]{1,0:T(8,128)S(1)}, u32[]{:S(2)}, u32[]{:S(2)}) collective-permute-start(f32[128,384]{1,0:T(8,128)S(1)} %dynamic-slice_bitcast_fusion.2), channel_id=1, source_target_pairs={{0,192},{64,0},{128,64},{192,128},{1,193},{65,1},{129,65},{193,129... | collective-permute-start | bytes 589832 | tf_op jit(solution)/shard_map/ppermute | solution.py:106
  103.0 3.3 %collective-permute-start.14 = (f32[128,384]{1,0:T(8,128)S(1)}, f32[128,384]{1,0:T(8,128)S(1)}, u32[]{:S(2)}, u32[]{:S(2)}) collective-permute-start(f32[128,384]{1,0:T(8,128)S(1)} %bitcast_add_fusion.2), channel_id=1, source_target_pairs={{0,192},{64,0},{128,64},{192,128},{1,193},{65,1},{129,65},{193,129... | collective-permute-start | bytes 589832 | tf_op jit(solution)/shard_map/ppermute | solution.py:106
  106.4 3.5 %collective-permute-start.8 = (f32[128,384]{1,0:T(8,128)S(1)}, f32[128,384]{1,0:T(8,128)S(1)}, u32[]{:S(2)}, u32[]{:S(2)}) collective-permute-start(f32[128,384]{1,0:T(8,128)S(1)} %bitcast_add_fusion.8), channel_id=1, source_target_pairs={{0,192},{64,0},{128,64},{192,128},{1,193},{65,1},{129,65},{193,129... | collective-permute-start | bytes 589832 | tf_op jit(solution)/shard_map/ppermute | solution.py:106
  111.4 3.8 %collective-permute-start.15 = (f32[128,384]{1,0:T(8,128)S(1)}, f32[128,384]{1,0:T(8,128)S(1)}, u32[]{:S(2)}, u32[]{:S(2)}) collective-permute-start(f32[128,384]{1,0:T(8,128)S(1)} %bitcast_add_fusion.1), channel_id=1, source_target_pairs={{0,192},{64,0},{128,64},{192,128},{1,193},{65,1},{129,65},{193,129... | collective-permute-start | bytes 589832 | tf_op jit(solution)/shard_map/ppermute | solution.py:106
  115.7 3.8 %collective-permute-start.9 = (f32[128,384]{1,0:T(8,128)S(1)}, f32[128,384]{1,0:T(8,128)S(1)}, u32[]{:S(2)}, u32[]{:S(2)}) collective-permute-start(f32[128,384]{1,0:T(8,128)S(1)} %bitcast_add_fusion.7), channel_id=1, source_target_pairs={{0,192},{64,0},{128,64},{192,128},{1,193},{65,1},{129,65},{193,129... | collective-permute-start | bytes 589832 | tf_op jit(solution)/shard_map/ppermute | solution.py:106
  119.9 2.7 %collective-permute-done.9 = f32[128,384]{1,0:T(8,128)S(1)} collective-permute-done((f32[128,384]{1,0:T(8,128)S(1)}, f32[128,384]{1,0:T(8,128)S(1)}, u32[]{:S(2)}, u32[]{:S(2)}) %collective-permute-start.9) | collective-permute-done | bytes 196640 | tf_op jit(solution)/shard_map/ppermute | solution.py:106
  123.6 3.1 %collective-permute-done.6 = f32[128,384]{1,0:T(8,128)S(1)} collective-permute-done((f32[128,384]{1,0:T(8,128)S(1)}, f32[128,384]{1,0:T(8,128)S(1)}, u32[]{:S(2)}, u32[]{:S(2)}) %collective-permute-start.6) | collective-permute-done | bytes 196640 | tf_op jit(solution)/shard_map/ppermute | solution.py:106
  (72 shorter events, 17.5 us)
Async XLA Ops:
  0.0 3.8 %copy-start.8 = (bf16[128,384]{1,0:T(8,128)(2,1)S(1)}, bf16[128,384]{1,0:T(8,128)(2,1)}, u32[]{:S(2)}) copy-start(bf16[128,384]{1,0:T(8,128)(2,1)} %param.9) | copy-start | bytes 294916
  2.1 11.2 %copy-start.9 = (f32[6144]{0:T(1024)S(1)}, f32[6144]{0:T(1024)}, u32[]{:S(2)}) copy-start(f32[6144]{0:T(1024)} %param.10) | copy-start | bytes 73732
  4.7 18.5 %all-to-all-start = ((bf16[128,2,384]{2,1,0:T(2,128)(2,1)}), bf16[128,2,384]{2,1,0:T(2,128)(2,1)S(1)}, u32[]{:S(2)}, u32[]{:S(2)}) async-start(bf16[128,2,384]{2,1,0:T(2,128)(2,1)} %copy.38), calls=%async_computation | async-start | bytes 393216 | tf_op jit(solution)/shard_map/all_to_all | solution.py:117
  35.5 41.5 %all-to-all-start.2 = ((bf16[4,16,8,1536]{3,2,0,1:T(8,128)(2,1)}), bf16[4,16,8,1536]{3,2,0,1:T(8,128)(2,1)S(1)}, u32[]{:S(2)}, u32[]{:S(2)}) async-start(bf16[4,16,8,1536]{3,2,0,1:T(8,128)(2,1)} %broadcast_in_dim.16), calls=%async_computation.2 | async-start | bytes 3145728 | tf_op jit(solution)/shard_map/all_to_all | solution.py:134
  39.2 28.4 %collective-permute-start = (bf16[384,1536]{1,0:T(8,128)(2,1)}, bf16[384,1536]{1,0:T(8,128)(2,1)S(1)}, u32[]{:S(2)}, u32[]{:S(2)}) collective-permute-start(bf16[384,1536]{1,0:T(8,128)(2,1)} %w0_ref.1), channel_id=1, source_target_pairs={{0,16},{16,32},{32,48},{48,0},{1,17},{17,33},{33,49},{49,1},{2,18}... | collective-permute-start | bytes 3538952 | tf_op jit(solution)/shard_map/ppermute | solution.py:34
  39.7 30.7 %collective-permute-start.2 = (bf16[384,1536]{1,0:T(8,128)(2,1)}, bf16[384,1536]{1,0:T(8,128)(2,1)S(1)}, u32[]{:S(2)}, u32[]{:S(2)}) collective-permute-start(bf16[384,1536]{1,0:T(8,128)(2,1)} %w0_ref.1), channel_id=1, source_target_pairs={{0,48},{16,0},{32,16},{48,32},{1,49},{17,1},{33,17},{49,33},{2,50}... | collective-permute-start | bytes 3538952 | tf_op jit(solution)/shard_map/ppermute | solution.py:35
  68.6 15.7 %collective-permute-start.1 = (bf16[384,768]{1,0:T(8,128)(2,1)S(1)}, bf16[384,768]{1,0:T(8,128)(2,1)S(1)}, u32[]{:S(2)}, u32[]{:S(2)}) collective-permute-start(bf16[384,768]{1,0:T(8,128)(2,1)S(1)} %slice.18), channel_id=1, source_target_pairs={{0,16},{16,32},{32,48},{48,0},{1,17},{17,33},{33,49},{49,1},{2,18}... | collective-permute-start | bytes 1769480 | tf_op jit(solution)/shard_map/ppermute | solution.py:37
  72.3 15.8 %collective-permute-start.3 = (bf16[384,768]{1,0:T(8,128)(2,1)}, bf16[384,768]{1,0:T(8,128)(2,1)S(1)}, u32[]{:S(2)}, u32[]{:S(2)}) collective-permute-start(bf16[384,768]{1,0:T(8,128)(2,1)} %slice.19), channel_id=1, source_target_pairs={{0,48},{16,0},{32,16},{48,32},{1,49},{17,1},{33,17},{49,33},{2,50}... | collective-permute-start | bytes 1769480 | tf_op jit(solution)/shard_map/ppermute | solution.py:38
  93.3 13.0 %copy-start.2 = (f32[512,384]{1,0:T(8,128)S(1)}, f32[512,384]{1,0:T(8,128)}, u32[]{:S(2)}) copy-start(f32[512,384]{1,0:T(8,128)} %get-tuple-element.19) | copy-start | bytes 2359300
  93.3 13.1 %copy-start.1 = (f32[512,384]{1,0:T(8,128)S(1)}, f32[512,384]{1,0:T(8,128)}, u32[]{:S(2)}) copy-start(f32[512,384]{1,0:T(8,128)} %get-tuple-element.18) | copy-start | bytes 2359300
  94.4 16.4 %copy-start = (f32[512,384]{1,0:T(8,128)S(1)}, f32[512,384]{1,0:T(8,128)}, u32[]{:S(2)}) copy-start(f32[512,384]{1,0:T(8,128)} %get-tuple-element.17) | copy-start | bytes 2359300
  94.4 7.6 %collective-permute-start.13 = (f32[128,384]{1,0:T(8,128)S(1)}, f32[128,384]{1,0:T(8,128)S(1)}, u32[]{:S(2)}, u32[]{:S(2)}) collective-permute-start(f32[128,384]{1,0:T(8,128)S(1)} %dynamic-slice_bitcast_fusion), channel_id=1, source_target_pairs={{0,192},{64,0},{128,64},{192,128},{1,193},{65,1},{129,65},{193,129... | collective-permute-start | bytes 589832 | tf_op jit(solution)/shard_map/ppermute | solution.py:106
  96.6 9.7 %collective-permute-start.10 = (f32[128,384]{1,0:T(8,128)S(1)}, f32[128,384]{1,0:T(8,128)S(1)}, u32[]{:S(2)}, u32[]{:S(2)}) collective-permute-start(f32[128,384]{1,0:T(8,128)S(1)} %dynamic-slice_bitcast_fusion.1), channel_id=1, source_target_pairs={{0,64},{64,128},{128,192},{192,0},{1,65},{65,129},{129,193},{193,1... | collective-permute-start | bytes 589832 | tf_op jit(solution)/shard_map/ppermute | solution.py:106
  97.5 13.9 %copy-start.3 = (f32[512,384]{1,0:T(8,128)S(1)}, f32[512,384]{1,0:T(8,128)}, u32[]{:S(2)}) copy-start(f32[512,384]{1,0:T(8,128)} %get-tuple-element.20) | copy-start | bytes 2359300
  98.5 7.9 %collective-permute-start.7 = (f32[128,384]{1,0:T(8,128)S(1)}, f32[128,384]{1,0:T(8,128)S(1)}, u32[]{:S(2)}, u32[]{:S(2)}) collective-permute-start(f32[128,384]{1,0:T(8,128)S(1)} %dynamic-slice_bitcast_fusion.2), channel_id=1, source_target_pairs={{0,192},{64,0},{128,64},{192,128},{1,193},{65,1},{129,65},{193,129... | collective-permute-start | bytes 589832 | tf_op jit(solution)/shard_map/ppermute | solution.py:106
  101.9 8.9 %collective-permute-start.4 = (f32[128,384]{1,0:T(8,128)S(1)}, f32[128,384]{1,0:T(8,128)S(1)}, u32[]{:S(2)}, u32[]{:S(2)}) collective-permute-start(f32[128,384]{1,0:T(8,128)S(1)} %dynamic-slice_bitcast_fusion.3), channel_id=1, source_target_pairs={{0,64},{64,128},{128,192},{192,0},{1,65},{65,129},{129,193},{193,1... | collective-permute-start | bytes 589832 | tf_op jit(solution)/shard_map/ppermute | solution.py:106
  103.0 8.4 %collective-permute-start.14 = (f32[128,384]{1,0:T(8,128)S(1)}, f32[128,384]{1,0:T(8,128)S(1)}, u32[]{:S(2)}, u32[]{:S(2)}) collective-permute-start(f32[128,384]{1,0:T(8,128)S(1)} %bitcast_add_fusion.2), channel_id=1, source_target_pairs={{0,192},{64,0},{128,64},{192,128},{1,193},{65,1},{129,65},{193,129... | collective-permute-start | bytes 589832 | tf_op jit(solution)/shard_map/ppermute | solution.py:106
  106.3 9.1 %collective-permute-start.11 = (f32[128,384]{1,0:T(8,128)S(1)}, f32[128,384]{1,0:T(8,128)S(1)}, u32[]{:S(2)}, u32[]{:S(2)}) collective-permute-start(f32[128,384]{1,0:T(8,128)S(1)} %bitcast_add_fusion.5), channel_id=1, source_target_pairs={{0,64},{64,128},{128,192},{192,0},{1,65},{65,129},{129,193},{193,1... | collective-permute-start | bytes 589832 | tf_op jit(solution)/shard_map/ppermute | solution.py:106
  106.4 9.2 %collective-permute-start.8 = (f32[128,384]{1,0:T(8,128)S(1)}, f32[128,384]{1,0:T(8,128)S(1)}, u32[]{:S(2)}, u32[]{:S(2)}) collective-permute-start(f32[128,384]{1,0:T(8,128)S(1)} %bitcast_add_fusion.8), channel_id=1, source_target_pairs={{0,192},{64,0},{128,64},{192,128},{1,193},{65,1},{129,65},{193,129... | collective-permute-start | bytes 589832 | tf_op jit(solution)/shard_map/ppermute | solution.py:106
  110.8 9.0 %collective-permute-start.5 = (f32[128,384]{1,0:T(8,128)S(1)}, f32[128,384]{1,0:T(8,128)S(1)}, u32[]{:S(2)}, u32[]{:S(2)}) collective-permute-start(f32[128,384]{1,0:T(8,128)S(1)} %bitcast_add_fusion.11), channel_id=1, source_target_pairs={{0,64},{64,128},{128,192},{192,0},{1,65},{65,129},{129,193},{193,1... | collective-permute-start | bytes 589832 | tf_op jit(solution)/shard_map/ppermute | solution.py:106
  111.4 8.4 %collective-permute-start.15 = (f32[128,384]{1,0:T(8,128)S(1)}, f32[128,384]{1,0:T(8,128)S(1)}, u32[]{:S(2)}, u32[]{:S(2)}) collective-permute-start(f32[128,384]{1,0:T(8,128)S(1)} %bitcast_add_fusion.1), channel_id=1, source_target_pairs={{0,192},{64,0},{128,64},{192,128},{1,193},{65,1},{129,65},{193,129... | collective-permute-start | bytes 589832 | tf_op jit(solution)/shard_map/ppermute | solution.py:106
  115.4 8.2 %collective-permute-start.12 = (f32[128,384]{1,0:T(8,128)S(1)}, f32[128,384]{1,0:T(8,128)S(1)}, u32[]{:S(2)}, u32[]{:S(2)}) collective-permute-start(f32[128,384]{1,0:T(8,128)S(1)} %bitcast_add_fusion.4), channel_id=1, source_target_pairs={{0,64},{64,128},{128,192},{192,0},{1,65},{65,129},{129,193},{193,1... | collective-permute-start | bytes 589832 | tf_op jit(solution)/shard_map/ppermute | solution.py:106
  115.7 7.0 %collective-permute-start.9 = (f32[128,384]{1,0:T(8,128)S(1)}, f32[128,384]{1,0:T(8,128)S(1)}, u32[]{:S(2)}, u32[]{:S(2)}) collective-permute-start(f32[128,384]{1,0:T(8,128)S(1)} %bitcast_add_fusion.7), channel_id=1, source_target_pairs={{0,192},{64,0},{128,64},{192,128},{1,193},{65,1},{129,65},{193,129... | collective-permute-start | bytes 589832 | tf_op jit(solution)/shard_map/ppermute | solution.py:106
  119.8 7.0 %collective-permute-start.6 = (f32[128,384]{1,0:T(8,128)S(1)}, f32[128,384]{1,0:T(8,128)S(1)}, u32[]{:S(2)}, u32[]{:S(2)}) collective-permute-start(f32[128,384]{1,0:T(8,128)S(1)} %bitcast_add_fusion.10), channel_id=1, source_target_pairs={{0,64},{64,128},{128,192},{192,0},{1,65},{65,129},{129,193},{193,1... | collective-permute-start | bytes 589832 | tf_op jit(solution)/shard_map/ppermute | solution.py:106
  (4 other events, 6.6 us)

commit v16 on v15

--- a/solution.py
+++ b/solution.py
@@ -134,7 +134,15 @@
     tokens = lax.all_to_all(spread_out, "col", split_axis=1, concat_axis=1, tiled=True)
     tokens = tokens.reshape(-1, tokens.shape[-1])
     quarters = dot_pieces(tokens, pieces)
-    product = ring_reduce_scatter([q.reshape(n_y, -1, q.shape[1]) for q in quarters], "ry", n_y)
+    segments = [q.reshape(n_y, 2, -1, q.shape[1]) for q in quarters]
+    halves = [seg[:, h] for seg in segments for h in range(2)]
+    summed = ring_reduce_scatter(halves, "ry", n_y)
+    width = quarters[0].shape[1]
+    product = jnp.concatenate(
+        [jnp.concatenate([summed[:, (2 * q) * width:(2 * q + 1) * width], summed[:, (2 * q + 1) * width:(2 * q + 2) * width]], axis=0)
+         for q in range(4)],
+        axis=1,
+    )
     return jax.nn.gelu(product, approximate=True).astype(jnp.bfloat16)
 
 

time: 128 us -> 141 us (1.10)
  starting transfers between devices: 35.8 us -> 55.1 us
  waiting for transfers between devices: 53.1 us -> 50 us
  local copies, waits for them, and re-layouts: 14.5 us -> 12.1 us
    ppermute x12 -> x24, starting transfers between devices: 19.3 us -> 38.6 us  [ring_reduce_scatter(): got = lax.ppermute(acc, axis, perm)]
    squeeze x4 -> x8, local copies, waits for them, and re-layouts: 3.95 us -> 0.1 us  [ring_reduce_scatter(): acc = lax.dynamic_index_in_dim(part, (me - step_dir) % n, 0, keepdims=False)]
    ppermute x12 -> x24, waiting for transfers between devices: 8.79 us -> 5.72 us  [ring_reduce_scatter(): got = lax.ppermute(acc, axis, perm)]
    unnamed x24 -> x22, local copies, waits for them, and re-layouts: 5.98 us -> 6 us
  transfers between devices with their start and end apart: 18 -> 30, of which waited for: 12 -> 6; matrix products, arithmetic and copies ran while one was open for 5% -> 2% of each run, Pallas kernels for 5% -> 4%
where the time goes in v16:
time: 141 us
  starting transfers between devices  55.1 us (39%)
  waiting for transfers between devices  50 us (35%)
  local copies, waits for them, and re-layouts  12.1 us (9%)
  Pallas kernels  10.5 us (7%)
  blocking collectives  10.1 us (7%)
  other arithmetic  2.24 us (2%)
    ppermute x24, starting transfers between devices, ring_reduce_scatter(): got = lax.ppermute(acc, axis, perm)  38.6 us
    ppermute x1, waiting for transfers between devices, ring_pieces(): from_left = lax.ppermute(block, axis, to_right)  26.3 us
    all_to_all x1, blocking collectives, per_device(): part = lax.all_to_all(rolled, 'ry', split_axis=1, concat_axis=0, tiled=True)  10.1 us
    all_to_all x1, waiting for transfers between devices, per_device(): both = lax.all_to_all(both, 'col', split_axis=0, concat_axis=1, tiled=True)  9.92 us
    all_to_all x1, starting transfers between devices, per_device(): both = lax.all_to_all(both, 'col', split_axis=0, concat_axis=1, tiled=True)  8.57 us
    pallas_call x1, Pallas kernels, dot_pieces(): pl.pallas_call(near_kernel, grid=(m // tile,), in_specs=[a_spec] + [full(...  6.01 us
    unnamed x22, local copies, waits for them, and re-layouts  6 us
    ppermute x24, waiting for transfers between devices, ring_reduce_scatter(): got = lax.ppermute(acc, axis, perm)  5.72 us
  transfers between devices with their start and end apart: 30, of which 6 were waited for; matrix products, arithmetic and copies ran while one was open for 2% of the time, Pallas kernels for 4%

profile of v16, /device:TPU:6, one launch (start us, length us, event | category | flops | bytes accessed | tf_op | source)
XLA Modules:
  0.0 141.1 jit_solution(6629066597667438873)
XLA Ops:
  4.7 8.6 %all-to-all-start = ((bf16[128,2,384]{2,1,0:T(2,128)(2,1)}), bf16[128,2,384]{2,1,0:T(2,128)(2,1)S(1)}, u32[]{:S(2)}, u32[]{:S(2)}) async-start(bf16[128,2,384]{2,1,0:T(2,128)(2,1)} %copy.38), calls=%async_computation | async-start | bytes 393216 | tf_op jit(solution)/shard_map/all_to_all | solution.py:117
  13.3 9.9 %all-to-all-done = bf16[128,2,384]{2,1,0:T(2,128)(2,1)S(1)} async-done(((bf16[128,2,384]{2,1,0:T(2,128)(2,1)}), bf16[128,2,384]{2,1,0:T(2,128)(2,1)S(1)}, u32[]{:S(2)}, u32[]{:S(2)}) %all-to-all-start) | async-done | bytes 196640 | tf_op jit(solution)/shard_map/all_to_all | solution.py:117
  24.0 10.1 %all_to_all.36 = bf16[8,4,1536]{2,0,1:T(8,128)(2,1)S(1)} all-to-all(bf16[8,4,1536]{2,0,1:T(8,128)(2,1)S(1)} %bitcast.103), channel_id=1, replica_groups=mesh['ry'=4,'rx'=4,'col'=16] {'ry'}, dimensions={1} | all-to-all | bytes 196608 | tf_op jit(solution)/shard_map/all_to_all | solution.py:130
  35.5 3.7 %all-to-all-start.2 = ((bf16[4,16,8,1536]{3,2,0,1:T(8,128)(2,1)}), bf16[4,16,8,1536]{3,2,0,1:T(8,128)(2,1)S(1)}, u32[]{:S(2)}, u32[]{:S(2)}) async-start(bf16[4,16,8,1536]{3,2,0,1:T(8,128)(2,1)} %broadcast_in_dim.16), calls=%async_computation.2 | async-start | bytes 3145728 | tf_op jit(solution)/shard_map/all_to_all | solution.py:134
  39.7 1.5 %collective-permute-start.2 = (bf16[384,1536]{1,0:T(8,128)(2,1)}, bf16[384,1536]{1,0:T(8,128)(2,1)S(1)}, u32[]{:S(2)}, u32[]{:S(2)}) collective-permute-start(bf16[384,1536]{1,0:T(8,128)(2,1)} %w0_ref.1), channel_id=1, source_target_pairs={{0,48},{16,0},{32,16},{48,32},{1,49},{17,1},{33,17},{49,33},{2,50}... | collective-permute-start | bytes 3538952 | tf_op jit(solution)/shard_map/ppermute | solution.py:35
  41.3 26.3 %collective-permute-done.w3_ref = bf16[384,1536]{1,0:T(8,128)(2,1)S(1)} collective-permute-done((bf16[384,1536]{1,0:T(8,128)(2,1)}, bf16[384,1536]{1,0:T(8,128)(2,1)S(1)}, u32[]{:S(2)}, u32[]{:S(2)}) %collective-permute-start) | collective-permute-done | bytes 1179680 | tf_op jit(solution)/shard_map/ppermute | solution.py:34
  68.7 1.8 %collective-permute-start.1 = (bf16[384,768]{1,0:T(8,128)(2,1)S(1)}, bf16[384,768]{1,0:T(8,128)(2,1)S(1)}, u32[]{:S(2)}, u32[]{:S(2)}) collective-permute-start(bf16[384,768]{1,0:T(8,128)(2,1)S(1)} %slice.50), channel_id=1, source_target_pairs={{0,16},{16,32},{32,48},{48,0},{1,17},{17,33},{33,49},{49,1},{2,18}... | collective-permute-start | bytes 1769480 | tf_op jit(solution)/shard_map/ppermute | solution.py:37
  72.7 4.3 %all-to-all-done.2 = bf16[4,16,8,1536]{3,2,0,1:T(8,128)(2,1)S(1)} async-done(((bf16[4,16,8,1536]{3,2,0,1:T(8,128)(2,1)}), bf16[4,16,8,1536]{3,2,0,1:T(8,128)(2,1)S(1)}, u32[]{:S(2)}, u32[]{:S(2)}) %all-to-all-start.2) | async-done | bytes 1572896 | tf_op jit(solution)/shard_map/all_to_all | solution.py:134
  78.3 6.0 %shard_map.64 = (f32[512,384]{1,0:T(8,128)}, f32[512,384]{1,0:T(8,128)}, f32[512,384]{1,0:T(8,128)}, f32[512,384]{1,0:T(8,128)}) custom-call(bf16[512,1536]{1,0:T(8,128)(2,1)} %bitcast.95, bf16[384,1536]{1,0:T(8,128)(2,1)} %w0_ref.1, bf16[384,1536]{1,0:T(8,128)(2,1)} %copy-done.6, bf16[384,1536]{1,0:T(8,128)(2,1)} %copy-done.5), custom_call_target="tpu_custom_call" | custom-call | flops 1811939328 | bytes 8257536 | tf_op jit(solution)/shard_map/pallas_call | solution.py:75
  84.3 3.8 %collective-permute-done.3.w2hi_ref = bf16[384,768]{1,0:T(8,128)(2,1)S(1)} collective-permute-done((bf16[384,768]{1,0:T(8,128)(2,1)}, bf16[384,768]{1,0:T(8,128)(2,1)S(1)}, u32[]{:S(2)}, u32[]{:S(2)}) %collective-permute-start.3) | collective-permute-done | bytes 589856 | tf_op jit(solution)/shard_map/ppermute | solution.py:38
  88.9 4.5 %shard_map.65 = (f32[512,384]{1,0:T(8,128)}, f32[512,384]{1,0:T(8,128)}, f32[512,384]{1,0:T(8,128)}, f32[512,384]{1,0:T(8,128)}) custom-call(bf16[512,1536]{1,0:T(8,128)(2,1)} %bitcast.96, bf16[384,768]{1,0:T(8,128)(2,1)} %copy-done.3, bf16[384,768]{1,0:T(8,128)(2,1)} %copy-done.4, ...), custom_call_target="tpu_custom_call", output_to_operand_aliasing={{0}: (3, {}), {1}: (4, {}), {2}: (5, {}), {3}: (6, {})} | custom-call | flops 603979776 | bytes 9043968 | tf_op jit(solution)/shard_map/pallas_call | solution.py:85
  96.9 2.5 %collective-permute-start.19 = (f32[64,384]{1,0:T(8,128)S(1)}, f32[64,384]{1,0:T(8,128)S(1)}, u32[]{:S(2)}, u32[]{:S(2)}) collective-permute-start(f32[64,384]{1,0:T(8,128)S(1)} %dynamic-slice_bitcast_fusion.2), channel_id=1, source_target_pairs={{0,192},{64,0},{128,64},{192,128},{1,193},{65,1},{129,65},{193,129... | collective-permute-start | bytes 294920 | tf_op jit(solution)/shard_map/ppermute | solution.py:106
  99.6 3.3 %collective-permute-start.13 = (f32[64,384]{1,0:T(8,128)S(1)}, f32[64,384]{1,0:T(8,128)S(1)}, u32[]{:S(2)}, u32[]{:S(2)}) collective-permute-start(f32[64,384]{1,0:T(8,128)S(1)} %dynamic-slice_bitcast_fusion.4), channel_id=1, source_target_pairs={{0,192},{64,0},{128,64},{192,128},{1,193},{65,1},{129,65},{193,129... | collective-permute-start | bytes 294920 | tf_op jit(solution)/shard_map/ppermute | solution.py:106
  103.1 3.5 %collective-permute-start.7 = (f32[64,384]{1,0:T(8,128)S(1)}, f32[64,384]{1,0:T(8,128)S(1)}, u32[]{:S(2)}, u32[]{:S(2)}) collective-permute-start(f32[64,384]{1,0:T(8,128)S(1)} %dynamic-slice_bitcast_fusion.6), channel_id=1, source_target_pairs={{0,192},{64,0},{128,64},{192,128},{1,193},{65,1},{129,65},{193,129... | collective-permute-start | bytes 294920 | tf_op jit(solution)/shard_map/ppermute | solution.py:106
  106.8 3.3 %collective-permute-start.26 = (f32[64,384]{1,0:T(8,128)S(1)}, f32[64,384]{1,0:T(8,128)S(1)}, u32[]{:S(2)}, u32[]{:S(2)}) collective-permute-start(f32[64,384]{1,0:T(8,128)S(1)} %bitcast_add_fusion.2), channel_id=1, source_target_pairs={{0,192},{64,0},{128,64},{192,128},{1,193},{65,1},{129,65},{193,129... | collective-permute-start | bytes 294920 | tf_op jit(solution)/shard_map/ppermute | solution.py:106
  110.2 3.3 %collective-permute-start.20 = (f32[64,384]{1,0:T(8,128)S(1)}, f32[64,384]{1,0:T(8,128)S(1)}, u32[]{:S(2)}, u32[]{:S(2)}) collective-permute-start(f32[64,384]{1,0:T(8,128)S(1)} %bitcast_add_fusion.8), channel_id=1, source_target_pairs={{0,192},{64,0},{128,64},{192,128},{1,193},{65,1},{129,65},{193,129... | collective-permute-start | bytes 294920 | tf_op jit(solution)/shard_map/ppermute | solution.py:106
  113.6 3.3 %collective-permute-start.14 = (f32[64,384]{1,0:T(8,128)S(1)}, f32[64,384]{1,0:T(8,128)S(1)}, u32[]{:S(2)}, u32[]{:S(2)}) collective-permute-start(f32[64,384]{1,0:T(8,128)S(1)} %bitcast_add_fusion.14), channel_id=1, source_target_pairs={{0,192},{64,0},{128,64},{192,128},{1,193},{65,1},{129,65},{193,129... | collective-permute-start | bytes 294920 | tf_op jit(solution)/shard_map/ppermute | solution.py:106
  117.1 3.3 %collective-permute-start.8 = (f32[64,384]{1,0:T(8,128)S(1)}, f32[64,384]{1,0:T(8,128)S(1)}, u32[]{:S(2)}, u32[]{:S(2)}) collective-permute-start(f32[64,384]{1,0:T(8,128)S(1)} %bitcast_add_fusion.20), channel_id=1, source_target_pairs={{0,192},{64,0},{128,64},{192,128},{1,193},{65,1},{129,65},{193,129... | collective-permute-start | bytes 294920 | tf_op jit(solution)/shard_map/ppermute | solution.py:106
  120.5 3.3 %collective-permute-start.27 = (f32[64,384]{1,0:T(8,128)S(1)}, f32[64,384]{1,0:T(8,128)S(1)}, u32[]{:S(2)}, u32[]{:S(2)}) collective-permute-start(f32[64,384]{1,0:T(8,128)S(1)} %bitcast_add_fusion.1), channel_id=1, source_target_pairs={{0,192},{64,0},{128,64},{192,128},{1,193},{65,1},{129,65},{193,129... | collective-permute-start | bytes 294920 | tf_op jit(solution)/shard_map/ppermute | solution.py:106
  124.0 3.3 %collective-permute-start.21 = (f32[64,384]{1,0:T(8,128)S(1)}, f32[64,384]{1,0:T(8,128)S(1)}, u32[]{:S(2)}, u32[]{:S(2)}) collective-permute-start(f32[64,384]{1,0:T(8,128)S(1)} %bitcast_add_fusion.7), channel_id=1, source_target_pairs={{0,192},{64,0},{128,64},{192,128},{1,193},{65,1},{129,65},{193,129... | collective-permute-start | bytes 294920 | tf_op jit(solution)/shard_map/ppermute | solution.py:106
  127.4 3.3 %collective-permute-start.15 = (f32[64,384]{1,0:T(8,128)S(1)}, f32[64,384]{1,0:T(8,128)S(1)}, u32[]{:S(2)}, u32[]{:S(2)}) collective-permute-start(f32[64,384]{1,0:T(8,128)S(1)} %bitcast_add_fusion.13), channel_id=1, source_target_pairs={{0,192},{64,0},{128,64},{192,128},{1,193},{65,1},{129,65},{193,129... | collective-permute-start | bytes 294920 | tf_op jit(solution)/shard_map/ppermute | solution.py:106
  130.9 3.3 %collective-permute-start.9 = (f32[64,384]{1,0:T(8,128)S(1)}, f32[64,384]{1,0:T(8,128)S(1)}, u32[]{:S(2)}, u32[]{:S(2)}) collective-permute-start(f32[64,384]{1,0:T(8,128)S(1)} %bitcast_add_fusion.19), channel_id=1, source_target_pairs={{0,192},{64,0},{128,64},{192,128},{1,193},{65,1},{129,65},{193,129... | collective-permute-start | bytes 294920 | tf_op jit(solution)/shard_map/ppermute | solution.py:106
  134.4 2.3 %collective-permute-done.12 = f32[64,384]{1,0:T(8,128)S(1)} collective-permute-done((f32[64,384]{1,0:T(8,128)S(1)}, f32[64,384]{1,0:T(8,128)S(1)}, u32[]{:S(2)}, u32[]{:S(2)}) %collective-permute-start.12) | collective-permute-done | bytes 98336 | tf_op jit(solution)/shard_map/ppermute | solution.py:106
  136.7 3.4 %collective-permute-done.6 = f32[64,384]{1,0:T(8,128)S(1)} collective-permute-done((f32[64,384]{1,0:T(8,128)S(1)}, f32[64,384]{1,0:T(8,128)S(1)}, u32[]{:S(2)}, u32[]{:S(2)}) %collective-permute-start.6) | collective-permute-done | bytes 98336 | tf_op jit(solution)/shard_map/ppermute | solution.py:106
  (114 shorter events, 18.8 us)
Async XLA Ops:
  4.7 18.5 %all-to-all-start = ((bf16[128,2,384]{2,1,0:T(2,128)(2,1)}), bf16[128,2,384]{2,1,0:T(2,128)(2,1)S(1)}, u32[]{:S(2)}, u32[]{:S(2)}) async-start(bf16[128,2,384]{2,1,0:T(2,128)(2,1)} %copy.38), calls=%async_computation | async-start | bytes 393216 | tf_op jit(solution)/shard_map/all_to_all | solution.py:117
  35.5 41.5 %all-to-all-start.2 = ((bf16[4,16,8,1536]{3,2,0,1:T(8,128)(2,1)}), bf16[4,16,8,1536]{3,2,0,1:T(8,128)(2,1)S(1)}, u32[]{:S(2)}, u32[]{:S(2)}) async-start(bf16[4,16,8,1536]{3,2,0,1:T(8,128)(2,1)} %broadcast_in_dim.16), calls=%async_computation.2 | async-start | bytes 3145728 | tf_op jit(solution)/shard_map/all_to_all | solution.py:134
  39.2 28.4 %collective-permute-start = (bf16[384,1536]{1,0:T(8,128)(2,1)}, bf16[384,1536]{1,0:T(8,128)(2,1)S(1)}, u32[]{:S(2)}, u32[]{:S(2)}) collective-permute-start(bf16[384,1536]{1,0:T(8,128)(2,1)} %w0_ref.1), channel_id=1, source_target_pairs={{0,16},{16,32},{32,48},{48,0},{1,17},{17,33},{33,49},{49,1},{2,18}... | collective-permute-start | bytes 3538952 | tf_op jit(solution)/shard_map/ppermute | solution.py:34
  39.7 30.7 %collective-permute-start.2 = (bf16[384,1536]{1,0:T(8,128)(2,1)}, bf16[384,1536]{1,0:T(8,128)(2,1)S(1)}, u32[]{:S(2)}, u32[]{:S(2)}) collective-permute-start(bf16[384,1536]{1,0:T(8,128)(2,1)} %w0_ref.1), channel_id=1, source_target_pairs={{0,48},{16,0},{32,16},{48,32},{1,49},{17,1},{33,17},{49,33},{2,50}... | collective-permute-start | bytes 3538952 | tf_op jit(solution)/shard_map/ppermute | solution.py:35
  68.7 15.7 %collective-permute-start.1 = (bf16[384,768]{1,0:T(8,128)(2,1)S(1)}, bf16[384,768]{1,0:T(8,128)(2,1)S(1)}, u32[]{:S(2)}, u32[]{:S(2)}) collective-permute-start(bf16[384,768]{1,0:T(8,128)(2,1)S(1)} %slice.50), channel_id=1, source_target_pairs={{0,16},{16,32},{32,48},{48,0},{1,17},{17,33},{33,49},{49,1},{2,18}... | collective-permute-start | bytes 1769480 | tf_op jit(solution)/shard_map/ppermute | solution.py:37
  72.3 15.8 %collective-permute-start.3 = (bf16[384,768]{1,0:T(8,128)(2,1)}, bf16[384,768]{1,0:T(8,128)(2,1)S(1)}, u32[]{:S(2)}, u32[]{:S(2)}) collective-permute-start(bf16[384,768]{1,0:T(8,128)(2,1)} %slice.51), channel_id=1, source_target_pairs={{0,48},{16,0},{32,16},{48,32},{1,49},{17,1},{33,17},{49,33},{2,50}... | collective-permute-start | bytes 1769480 | tf_op jit(solution)/shard_map/ppermute | solution.py:38
  94.7 8.3 %collective-permute-start.25 = (f32[64,384]{1,0:T(8,128)S(1)}, f32[64,384]{1,0:T(8,128)S(1)}, u32[]{:S(2)}, u32[]{:S(2)}) collective-permute-start(f32[64,384]{1,0:T(8,128)S(1)} %dynamic-slice_bitcast_fusion), channel_id=1, source_target_pairs={{0,192},{64,0},{128,64},{192,128},{1,193},{65,1},{129,65},{193,129... | collective-permute-start | bytes 294920 | tf_op jit(solution)/shard_map/ppermute | solution.py:106
  95.9 10.7 %collective-permute-start.22 = (f32[64,384]{1,0:T(8,128)S(1)}, f32[64,384]{1,0:T(8,128)S(1)}, u32[]{:S(2)}, u32[]{:S(2)}) collective-permute-start(f32[64,384]{1,0:T(8,128)S(1)} %dynamic-slice_bitcast_fusion.1), channel_id=1, source_target_pairs={{0,64},{64,128},{128,192},{192,0},{1,65},{65,129},{129,193},{193,1... | collective-permute-start | bytes 294920 | tf_op jit(solution)/shard_map/ppermute | solution.py:106
  99.4 7.3 %collective-permute-start.16 = (f32[64,384]{1,0:T(8,128)S(1)}, f32[64,384]{1,0:T(8,128)S(1)}, u32[]{:S(2)}, u32[]{:S(2)}) collective-permute-start(f32[64,384]{1,0:T(8,128)S(1)} %dynamic-slice_bitcast_fusion.3), channel_id=1, source_target_pairs={{0,64},{64,128},{128,192},{192,0},{1,65},{65,129},{129,193},{193,1... | collective-permute-start | bytes 294920 | tf_op jit(solution)/shard_map/ppermute | solution.py:106
  99.6 10.5 %collective-permute-start.13 = (f32[64,384]{1,0:T(8,128)S(1)}, f32[64,384]{1,0:T(8,128)S(1)}, u32[]{:S(2)}, u32[]{:S(2)}) collective-permute-start(f32[64,384]{1,0:T(8,128)S(1)} %dynamic-slice_bitcast_fusion.4), channel_id=1, source_target_pairs={{0,192},{64,0},{128,64},{192,128},{1,193},{65,1},{129,65},{193,129... | collective-permute-start | bytes 294920 | tf_op jit(solution)/shard_map/ppermute | solution.py:106
  103.0 7.2 %collective-permute-start.10 = (f32[64,384]{1,0:T(8,128)S(1)}, f32[64,384]{1,0:T(8,128)S(1)}, u32[]{:S(2)}, u32[]{:S(2)}) collective-permute-start(f32[64,384]{1,0:T(8,128)S(1)} %dynamic-slice_bitcast_fusion.5), channel_id=1, source_target_pairs={{0,64},{64,128},{128,192},{192,0},{1,65},{65,129},{129,193},{193,1... | collective-permute-start | bytes 294920 | tf_op jit(solution)/shard_map/ppermute | solution.py:106
  103.1 10.4 %collective-permute-start.7 = (f32[64,384]{1,0:T(8,128)S(1)}, f32[64,384]{1,0:T(8,128)S(1)}, u32[]{:S(2)}, u32[]{:S(2)}) collective-permute-start(f32[64,384]{1,0:T(8,128)S(1)} %dynamic-slice_bitcast_fusion.6), channel_id=1, source_target_pairs={{0,192},{64,0},{128,64},{192,128},{1,193},{65,1},{129,65},{193,129... | collective-permute-start | bytes 294920 | tf_op jit(solution)/shard_map/ppermute | solution.py:106
  106.6 7.0 %collective-permute-start.4 = (f32[64,384]{1,0:T(8,128)S(1)}, f32[64,384]{1,0:T(8,128)S(1)}, u32[]{:S(2)}, u32[]{:S(2)}) collective-permute-start(f32[64,384]{1,0:T(8,128)S(1)} %dynamic-slice_bitcast_fusion.7), channel_id=1, source_target_pairs={{0,64},{64,128},{128,192},{192,0},{1,65},{65,129},{129,193},{193,1... | collective-permute-start | bytes 294920 | tf_op jit(solution)/shard_map/ppermute | solution.py:106
  106.8 10.2 %collective-permute-start.26 = (f32[64,384]{1,0:T(8,128)S(1)}, f32[64,384]{1,0:T(8,128)S(1)}, u32[]{:S(2)}, u32[]{:S(2)}) collective-permute-start(f32[64,384]{1,0:T(8,128)S(1)} %bitcast_add_fusion.2), channel_id=1, source_target_pairs={{0,192},{64,0},{128,64},{192,128},{1,193},{65,1},{129,65},{193,129... | collective-permute-start | bytes 294920 | tf_op jit(solution)/shard_map/ppermute | solution.py:106
  110.1 10.3 %collective-permute-start.23 = (f32[64,384]{1,0:T(8,128)S(1)}, f32[64,384]{1,0:T(8,128)S(1)}, u32[]{:S(2)}, u32[]{:S(2)}) collective-permute-start(f32[64,384]{1,0:T(8,128)S(1)} %bitcast_add_fusion.5), channel_id=1, source_target_pairs={{0,64},{64,128},{128,192},{192,0},{1,65},{65,129},{129,193},{193,1... | collective-permute-start | bytes 294920 | tf_op jit(solution)/shard_map/ppermute | solution.py:106
  113.5 7.0 %collective-permute-start.17 = (f32[64,384]{1,0:T(8,128)S(1)}, f32[64,384]{1,0:T(8,128)S(1)}, u32[]{:S(2)}, u32[]{:S(2)}) collective-permute-start(f32[64,384]{1,0:T(8,128)S(1)} %bitcast_add_fusion.11), channel_id=1, source_target_pairs={{0,64},{64,128},{128,192},{192,0},{1,65},{65,129},{129,193},{193,1... | collective-permute-start | bytes 294920 | tf_op jit(solution)/shard_map/ppermute | solution.py:106
  113.6 10.2 %collective-permute-start.14 = (f32[64,384]{1,0:T(8,128)S(1)}, f32[64,384]{1,0:T(8,128)S(1)}, u32[]{:S(2)}, u32[]{:S(2)}) collective-permute-start(f32[64,384]{1,0:T(8,128)S(1)} %bitcast_add_fusion.14), channel_id=1, source_target_pairs={{0,192},{64,0},{128,64},{192,128},{1,193},{65,1},{129,65},{193,129... | collective-permute-start | bytes 294920 | tf_op jit(solution)/shard_map/ppermute | solution.py:106
  117.0 7.0 %collective-permute-start.11 = (f32[64,384]{1,0:T(8,128)S(1)}, f32[64,384]{1,0:T(8,128)S(1)}, u32[]{:S(2)}, u32[]{:S(2)}) collective-permute-start(f32[64,384]{1,0:T(8,128)S(1)} %bitcast_add_fusion.17), channel_id=1, source_target_pairs={{0,64},{64,128},{128,192},{192,0},{1,65},{65,129},{129,193},{193,1... | collective-permute-start | bytes 294920 | tf_op jit(solution)/shard_map/ppermute | solution.py:106
  117.1 10.2 %collective-permute-start.8 = (f32[64,384]{1,0:T(8,128)S(1)}, f32[64,384]{1,0:T(8,128)S(1)}, u32[]{:S(2)}, u32[]{:S(2)}) collective-permute-start(f32[64,384]{1,0:T(8,128)S(1)} %bitcast_add_fusion.20), channel_id=1, source_target_pairs={{0,192},{64,0},{128,64},{192,128},{1,193},{65,1},{129,65},{193,129... | collective-permute-start | bytes 294920 | tf_op jit(solution)/shard_map/ppermute | solution.py:106
  120.4 7.0 %collective-permute-start.5 = (f32[64,384]{1,0:T(8,128)S(1)}, f32[64,384]{1,0:T(8,128)S(1)}, u32[]{:S(2)}, u32[]{:S(2)}) collective-permute-start(f32[64,384]{1,0:T(8,128)S(1)} %bitcast_add_fusion.23), channel_id=1, source_target_pairs={{0,64},{64,128},{128,192},{192,0},{1,65},{65,129},{129,193},{193,1... | collective-permute-start | bytes 294920 | tf_op jit(solution)/shard_map/ppermute | solution.py:106
  120.5 10.2 %collective-permute-start.27 = (f32[64,384]{1,0:T(8,128)S(1)}, f32[64,384]{1,0:T(8,128)S(1)}, u32[]{:S(2)}, u32[]{:S(2)}) collective-permute-start(f32[64,384]{1,0:T(8,128)S(1)} %bitcast_add_fusion.1), channel_id=1, source_target_pairs={{0,192},{64,0},{128,64},{192,128},{1,193},{65,1},{129,65},{193,129... | collective-permute-start | bytes 294920 | tf_op jit(solution)/shard_map/ppermute | solution.py:106
  123.9 10.3 %collective-permute-start.24 = (f32[64,384]{1,0:T(8,128)S(1)}, f32[64,384]{1,0:T(8,128)S(1)}, u32[]{:S(2)}, u32[]{:S(2)}) collective-permute-start(f32[64,384]{1,0:T(8,128)S(1)} %bitcast_add_fusion.4), channel_id=1, source_target_pairs={{0,64},{64,128},{128,192},{192,0},{1,65},{65,129},{129,193},{193,1... | collective-permute-start | bytes 294920 | tf_op jit(solution)/shard_map/ppermute | solution.py:106
  127.3 7.0 %collective-permute-start.18 = (f32[64,384]{1,0:T(8,128)S(1)}, f32[64,384]{1,0:T(8,128)S(1)}, u32[]{:S(2)}, u32[]{:S(2)}) collective-permute-start(f32[64,384]{1,0:T(8,128)S(1)} %bitcast_add_fusion.10), channel_id=1, source_target_pairs={{0,64},{64,128},{128,192},{192,0},{1,65},{65,129},{129,193},{193,1... | collective-permute-start | bytes 294920 | tf_op jit(solution)/shard_map/ppermute | solution.py:106
  127.4 6.9 %collective-permute-start.15 = (f32[64,384]{1,0:T(8,128)S(1)}, f32[64,384]{1,0:T(8,128)S(1)}, u32[]{:S(2)}, u32[]{:S(2)}) collective-permute-start(f32[64,384]{1,0:T(8,128)S(1)} %bitcast_add_fusion.13), channel_id=1, source_target_pairs={{0,192},{64,0},{128,64},{192,128},{1,193},{65,1},{129,65},{193,129... | collective-permute-start | bytes 294920 | tf_op jit(solution)/shard_map/ppermute | solution.py:106
  (15 other events, 73.5 us)

commit v17 on v15

--- a/solution.py
+++ b/solution.py
@@ -127,11 +127,11 @@
     grouped = normed.reshape(chunk, n_y, n_x, block)
     doubled = jnp.concatenate([grouped, grouped], axis=2)
     rolled = lax.dynamic_slice_in_dim(doubled, lax.axis_index("rx"), n_x, axis=2).reshape(chunk, full_width)
-    part = lax.all_to_all(rolled, "ry", split_axis=1, concat_axis=0, tiled=True)
-    part = part.reshape(n_y, chunk, part.shape[1])
     n_col = lax.axis_size("col")
-    spread_out = jnp.broadcast_to(part[:, None], (part.shape[0], n_col) + part.shape[1:])
-    tokens = lax.all_to_all(spread_out, "col", split_axis=1, concat_axis=1, tiled=True)
+    groups = rolled.reshape(chunk, n_y, -1).transpose(1, 0, 2)
+    spread_out = jnp.broadcast_to(groups[:, None], (n_y, n_col) + groups.shape[1:])
+    spread_out = spread_out.reshape((n_y * n_col,) + groups.shape[1:])
+    tokens = lax.all_to_all(spread_out, ("ry", "col"), split_axis=0, concat_axis=0, tiled=True)
     tokens = tokens.reshape(-1, tokens.shape[-1])
     quarters = dot_pieces(tokens, pieces)
     product = ring_reduce_scatter([q.reshape(n_y, -1, q.shape[1]) for q in quarters], "ry", n_y)

time: 128 us -> 122 us (0.953)
  blocking collectives: 10.1 us -> 0 us
  starting transfers between devices: 35.8 us -> 41.2 us
    all_to_all x1 -> x0, blocking collectives: 10.1 us -> none  [per_device(): part = lax.all_to_all(rolled, 'ry', split_axis=1, concat_axis=0, tiled=True)]
    all_to_all x1, starting transfers between devices: 3.71 us -> 6.77 us  [per_device(): lax.all_to_all(spread_out, ('ry', 'col'), split_axis=0, concat_axis=0, ti...]
    ppermute x12, starting transfers between devices: 19.3 us -> 21.7 us  [ring_reduce_scatter(): got = lax.ppermute(acc, axis, perm)]
    ppermute x1, waiting for transfers between devices: 3.72 us -> 1.85 us  [ring_pieces(): far_high = lax.ppermute(from_right[:, half:], axis, to_left)]
    all_to_all x1, waiting for transfers between devices: 4.4 us -> 6.24 us  [per_device(): lax.all_to_all(spread_out, ('ry', 'col'), split_axis=0, concat_axis=0, ti...]
    all_to_all x1 -> x0, local copies, waits for them, and re-layouts: 1.32 us -> none  [per_device(): lax.all_to_all(spread_out, 'col', split_axis=1, concat_axis=1, tiled=True)]
    unnamed x24 -> x26, local copies, waits for them, and re-layouts: 5.98 us -> 7.15 us
  transfers between devices with their start and end apart: 18 -> 18, of which waited for: 12 -> 12; matrix products, arithmetic and copies ran while one was open for 5% -> 3% of each run, Pallas kernels for 5% -> 5%
where the time goes in v17:
time: 122 us
  waiting for transfers between devices  52.6 us (43%)
  starting transfers between devices  41.2 us (34%)
  local copies, waits for them, and re-layouts  13.4 us (11%)
  Pallas kernels  10.4 us (9%)
  other arithmetic  3.17 us (3%)
    ppermute x1, waiting for transfers between devices, ring_pieces(): from_left = lax.ppermute(block, axis, to_right)  26.1 us
    ppermute x12, starting transfers between devices, ring_reduce_scatter(): got = lax.ppermute(acc, axis, perm)  21.7 us
    all_to_all x1, waiting for transfers between devices, per_device(): both = lax.all_to_all(both, 'col', split_axis=0, concat_axis=1, tiled=True)  9.92 us
    all_to_all x1, starting transfers between devices, per_device(): both = lax.all_to_all(both, 'col', split_axis=0, concat_axis=1, tiled=True)  8.57 us
    ppermute x12, waiting for transfers between devices, ring_reduce_scatter(): got = lax.ppermute(acc, axis, perm)  8.48 us
    unnamed x26, local copies, waits for them, and re-layouts  7.15 us
    all_to_all x1, starting transfers between devices, per_device(): lax.all_to_all(spread_out, ('ry', 'col'), split_axis=0, concat_axis=0, ti...  6.77 us
    all_to_all x1, waiting for transfers between devices, per_device(): lax.all_to_all(spread_out, ('ry', 'col'), split_axis=0, concat_axis=0, ti...  6.24 us
  transfers between devices with their start and end apart: 18, of which 12 were waited for; matrix products, arithmetic and copies ran while one was open for 3% of the time, Pallas kernels for 5%

profile of v17, /device:TPU:6, one launch (start us, length us, event | category | flops | bytes accessed | tf_op | source)
XLA Modules:
  0.0 121.5 jit_solution(14035413023300657386)
XLA Ops:
  0.0 1.0 copy.34
  4.7 8.6 %all-to-all-start = ((bf16[128,2,384]{2,1,0:T(2,128)(2,1)}), bf16[128,2,384]{2,1,0:T(2,128)(2,1)S(1)}, u32[]{:S(2)}, u32[]{:S(2)}) async-start(bf16[128,2,384]{2,1,0:T(2,128)(2,1)} %copy.37), calls=%async_computation | async-start | bytes 393216 | tf_op jit(solution)/shard_map/all_to_all | solution.py:117
  13.3 9.9 %all-to-all-done = bf16[128,2,384]{2,1,0:T(2,128)(2,1)S(1)} async-done(((bf16[128,2,384]{2,1,0:T(2,128)(2,1)}), bf16[128,2,384]{2,1,0:T(2,128)(2,1)S(1)}, u32[]{:S(2)}, u32[]{:S(2)}) %all-to-all-start) | async-done | bytes 196640 | tf_op jit(solution)/shard_map/all_to_all | solution.py:117
  24.0 1.3 %broadcast_in_dim.16 = bf16[4,16,8,1536]{3,2,1,0:T(8,128)(2,1)} broadcast(bf16[4,8,1536]{2,1,0:T(8,128)(2,1)S(1)} %bitcast.85), dimensions={0,2,3} | broadcast | bytes 1671168 | tf_op jit(solution)/shard_map/broadcast_in_dim | solution.py:132
  25.3 6.8 %all-to-all-start.1 = ((bf16[64,8,1536]{2,1,0:T(8,128)(2,1)}), bf16[64,8,1536]{2,1,0:T(8,128)(2,1)S(1)}, u32[]{:S(2)}, u32[]{:S(2)}) async-start(bf16[64,8,1536]{2,1,0:T(8,128)(2,1)} %bitcast.11), calls=%async_computation.1 | async-start | bytes 3145728 | tf_op jit(solution)/shard_map/all_to_all | solution.py:134
  32.6 1.5 %collective-permute-start.2 = (bf16[384,1536]{1,0:T(8,128)(2,1)}, bf16[384,1536]{1,0:T(8,128)(2,1)S(1)}, u32[]{:S(2)}, u32[]{:S(2)}) collective-permute-start(bf16[384,1536]{1,0:T(8,128)(2,1)} %w0_ref.1), channel_id=1, source_target_pairs={{0,48},{16,0},{32,16},{48,32},{1,49},{17,1},{33,17},{49,33},{2,50}... | collective-permute-start | bytes 3538952 | tf_op jit(solution)/shard_map/ppermute | solution.py:35
  34.2 26.1 %collective-permute-done.w3_ref = bf16[384,1536]{1,0:T(8,128)(2,1)S(1)} collective-permute-done((bf16[384,1536]{1,0:T(8,128)(2,1)}, bf16[384,1536]{1,0:T(8,128)(2,1)S(1)}, u32[]{:S(2)}, u32[]{:S(2)}) %collective-permute-start) | collective-permute-done | bytes 1179680 | tf_op jit(solution)/shard_map/ppermute | solution.py:34
  60.3 1.0 copy-done.7
  61.4 1.8 %collective-permute-start.1 = (bf16[384,768]{1,0:T(8,128)(2,1)S(1)}, bf16[384,768]{1,0:T(8,128)(2,1)S(1)}, u32[]{:S(2)}, u32[]{:S(2)}) collective-permute-start(bf16[384,768]{1,0:T(8,128)(2,1)S(1)} %slice.18), channel_id=1, source_target_pairs={{0,16},{16,32},{32,48},{48,0},{1,17},{17,33},{33,49},{49,1},{2,18}... | collective-permute-start | bytes 1769480 | tf_op jit(solution)/shard_map/ppermute | solution.py:37
  65.3 6.2 %all-to-all-done.1 = bf16[64,8,1536]{2,1,0:T(8,128)(2,1)S(1)} async-done(((bf16[64,8,1536]{2,1,0:T(8,128)(2,1)}), bf16[64,8,1536]{2,1,0:T(8,128)(2,1)S(1)}, u32[]{:S(2)}, u32[]{:S(2)}) %all-to-all-start.1) | async-done | bytes 1572896 | tf_op jit(solution)/shard_map/all_to_all | solution.py:134
  71.6 1.2 copy-done
  72.7 6.0 %shard_map.64 = (f32[512,384]{1,0:T(8,128)}, f32[512,384]{1,0:T(8,128)}, f32[512,384]{1,0:T(8,128)}, f32[512,384]{1,0:T(8,128)}) custom-call(bf16[512,1536]{1,0:T(8,128)(2,1)} %bitcast.65, bf16[384,1536]{1,0:T(8,128)(2,1)} %w0_ref.1, bf16[384,1536]{1,0:T(8,128)(2,1)} %copy-done.8, bf16[384,1536]{1,0:T(8,128)(2,1)} %copy-done.7), custom_call_target="tpu_custom_call" | custom-call | flops 1811939328 | bytes 8257536 | tf_op jit(solution)/shard_map/pallas_call | solution.py:75
  78.7 1.9 %collective-permute-done.3.w2hi_ref = bf16[384,768]{1,0:T(8,128)(2,1)S(1)} collective-permute-done((bf16[384,768]{1,0:T(8,128)(2,1)}, bf16[384,768]{1,0:T(8,128)(2,1)S(1)}, u32[]{:S(2)}, u32[]{:S(2)}) %collective-permute-start.3) | collective-permute-done | bytes 589856 | tf_op jit(solution)/shard_map/ppermute | solution.py:38
  81.4 4.4 %shard_map.65 = (f32[512,384]{1,0:T(8,128)}, f32[512,384]{1,0:T(8,128)}, f32[512,384]{1,0:T(8,128)}, f32[512,384]{1,0:T(8,128)}) custom-call(bf16[512,1536]{1,0:T(8,128)(2,1)} %bitcast.66, bf16[384,768]{1,0:T(8,128)(2,1)} %copy-done.5, bf16[384,768]{1,0:T(8,128)(2,1)} %copy-done.6, ...), custom_call_target="tpu_custom_call", output_to_operand_aliasing={{0}: (3, {}), {1}: (4, {}), {2}: (5, {}), {3}: (6, {})} | custom-call | flops 603979776 | bytes 9043968 | tf_op jit(solution)/shard_map/pallas_call | solution.py:85
  85.8 1.1 dynamic-slice_bitcast_fusion
  86.9 3.3 %collective-permute-start.13 = (f32[128,384]{1,0:T(8,128)S(1)}, f32[128,384]{1,0:T(8,128)S(1)}, u32[]{:S(2)}, u32[]{:S(2)}) collective-permute-start(f32[128,384]{1,0:T(8,128)S(1)} %dynamic-slice_bitcast_fusion), channel_id=1, source_target_pairs={{0,192},{64,0},{128,64},{192,128},{1,193},{65,1},{129,65},{193,129... | collective-permute-start | bytes 589832 | tf_op jit(solution)/shard_map/ppermute | solution.py:106
  92.2 3.3 %collective-permute-start.7 = (f32[128,384]{1,0:T(8,128)S(1)}, f32[128,384]{1,0:T(8,128)S(1)}, u32[]{:S(2)}, u32[]{:S(2)}) collective-permute-start(f32[128,384]{1,0:T(8,128)S(1)} %dynamic-slice_bitcast_fusion.2), channel_id=1, source_target_pairs={{0,192},{64,0},{128,64},{192,128},{1,193},{65,1},{129,65},{193,129... | collective-permute-start | bytes 589832 | tf_op jit(solution)/shard_map/ppermute | solution.py:106
  96.7 3.3 %collective-permute-start.14 = (f32[128,384]{1,0:T(8,128)S(1)}, f32[128,384]{1,0:T(8,128)S(1)}, u32[]{:S(2)}, u32[]{:S(2)}) collective-permute-start(f32[128,384]{1,0:T(8,128)S(1)} %bitcast_add_fusion.2), channel_id=1, source_target_pairs={{0,192},{64,0},{128,64},{192,128},{1,193},{65,1},{129,65},{193,129... | collective-permute-start | bytes 589832 | tf_op jit(solution)/shard_map/ppermute | solution.py:106
  100.3 3.7 %collective-permute-start.8 = (f32[128,384]{1,0:T(8,128)S(1)}, f32[128,384]{1,0:T(8,128)S(1)}, u32[]{:S(2)}, u32[]{:S(2)}) collective-permute-start(f32[128,384]{1,0:T(8,128)S(1)} %bitcast_add_fusion.8), channel_id=1, source_target_pairs={{0,192},{64,0},{128,64},{192,128},{1,193},{65,1},{129,65},{193,129... | collective-permute-start | bytes 589832 | tf_op jit(solution)/shard_map/ppermute | solution.py:106
  104.2 1.1 collective-permute-done.14
  105.3 3.8 %collective-permute-start.15 = (f32[128,384]{1,0:T(8,128)S(1)}, f32[128,384]{1,0:T(8,128)S(1)}, u32[]{:S(2)}, u32[]{:S(2)}) collective-permute-start(f32[128,384]{1,0:T(8,128)S(1)} %bitcast_add_fusion.1), channel_id=1, source_target_pairs={{0,192},{64,0},{128,64},{192,128},{1,193},{65,1},{129,65},{193,129... | collective-permute-start | bytes 589832 | tf_op jit(solution)/shard_map/ppermute | solution.py:106
  109.5 3.8 %collective-permute-start.9 = (f32[128,384]{1,0:T(8,128)S(1)}, f32[128,384]{1,0:T(8,128)S(1)}, u32[]{:S(2)}, u32[]{:S(2)}) collective-permute-start(f32[128,384]{1,0:T(8,128)S(1)} %bitcast_add_fusion.7), channel_id=1, source_target_pairs={{0,192},{64,0},{128,64},{192,128},{1,193},{65,1},{129,65},{193,129... | collective-permute-start | bytes 589832 | tf_op jit(solution)/shard_map/ppermute | solution.py:106
  113.7 2.8 %collective-permute-done.9 = f32[128,384]{1,0:T(8,128)S(1)} collective-permute-done((f32[128,384]{1,0:T(8,128)S(1)}, f32[128,384]{1,0:T(8,128)S(1)}, u32[]{:S(2)}, u32[]{:S(2)}) %collective-permute-start.9) | collective-permute-done | bytes 196640 | tf_op jit(solution)/shard_map/ppermute | solution.py:106
  117.3 3.2 %collective-permute-done.6 = f32[128,384]{1,0:T(8,128)S(1)} collective-permute-done((f32[128,384]{1,0:T(8,128)S(1)}, f32[128,384]{1,0:T(8,128)S(1)}, u32[]{:S(2)}, u32[]{:S(2)}) %collective-permute-start.6) | collective-permute-done | bytes 196640 | tf_op jit(solution)/shard_map/ppermute | solution.py:106
  (72 shorter events, 14.3 us)
Async XLA Ops:
  0.0 3.8 %copy-start.9 = (bf16[128,384]{1,0:T(8,128)(2,1)S(1)}, bf16[128,384]{1,0:T(8,128)(2,1)}, u32[]{:S(2)}) copy-start(bf16[128,384]{1,0:T(8,128)(2,1)} %param.9) | copy-start | bytes 294916
  3.4 9.9 %copy-start.10 = (f32[6144]{0:T(1024)S(1)}, f32[6144]{0:T(1024)}, u32[]{:S(2)}) copy-start(f32[6144]{0:T(1024)} %param.10) | copy-start | bytes 73732
  4.7 18.5 %all-to-all-start = ((bf16[128,2,384]{2,1,0:T(2,128)(2,1)}), bf16[128,2,384]{2,1,0:T(2,128)(2,1)S(1)}, u32[]{:S(2)}, u32[]{:S(2)}) async-start(bf16[128,2,384]{2,1,0:T(2,128)(2,1)} %copy.37), calls=%async_computation | async-start | bytes 393216 | tf_op jit(solution)/shard_map/all_to_all | solution.py:117
  25.3 46.3 %all-to-all-start.1 = ((bf16[64,8,1536]{2,1,0:T(8,128)(2,1)}), bf16[64,8,1536]{2,1,0:T(8,128)(2,1)S(1)}, u32[]{:S(2)}, u32[]{:S(2)}) async-start(bf16[64,8,1536]{2,1,0:T(8,128)(2,1)} %bitcast.11), calls=%async_computation.1 | async-start | bytes 3145728 | tf_op jit(solution)/shard_map/all_to_all | solution.py:134
  32.1 28.2 %collective-permute-start = (bf16[384,1536]{1,0:T(8,128)(2,1)}, bf16[384,1536]{1,0:T(8,128)(2,1)S(1)}, u32[]{:S(2)}, u32[]{:S(2)}) collective-permute-start(bf16[384,1536]{1,0:T(8,128)(2,1)} %w0_ref.1), channel_id=1, source_target_pairs={{0,16},{16,32},{32,48},{48,0},{1,17},{17,33},{33,49},{49,1},{2,18}... | collective-permute-start | bytes 3538952 | tf_op jit(solution)/shard_map/ppermute | solution.py:34
  32.6 30.5 %collective-permute-start.2 = (bf16[384,1536]{1,0:T(8,128)(2,1)}, bf16[384,1536]{1,0:T(8,128)(2,1)S(1)}, u32[]{:S(2)}, u32[]{:S(2)}) collective-permute-start(bf16[384,1536]{1,0:T(8,128)(2,1)} %w0_ref.1), channel_id=1, source_target_pairs={{0,48},{16,0},{32,16},{48,32},{1,49},{17,1},{33,17},{49,33},{2,50}... | collective-permute-start | bytes 3538952 | tf_op jit(solution)/shard_map/ppermute | solution.py:35
  61.4 17.4 %collective-permute-start.1 = (bf16[384,768]{1,0:T(8,128)(2,1)S(1)}, bf16[384,768]{1,0:T(8,128)(2,1)S(1)}, u32[]{:S(2)}, u32[]{:S(2)}) collective-permute-start(bf16[384,768]{1,0:T(8,128)(2,1)S(1)} %slice.18), channel_id=1, source_target_pairs={{0,16},{16,32},{32,48},{48,0},{1,17},{17,33},{33,49},{49,1},{2,18}... | collective-permute-start | bytes 1769480 | tf_op jit(solution)/shard_map/ppermute | solution.py:37
  65.0 15.6 %collective-permute-start.3 = (bf16[384,768]{1,0:T(8,128)(2,1)}, bf16[384,768]{1,0:T(8,128)(2,1)S(1)}, u32[]{:S(2)}, u32[]{:S(2)}) collective-permute-start(bf16[384,768]{1,0:T(8,128)(2,1)} %slice.19), channel_id=1, source_target_pairs={{0,48},{16,0},{32,16},{48,32},{1,49},{17,1},{33,17},{49,33},{2,50}... | collective-permute-start | bytes 1769480 | tf_op jit(solution)/shard_map/ppermute | solution.py:38
  85.8 9.7 %copy-start.1 = (f32[512,384]{1,0:T(8,128)S(1)}, f32[512,384]{1,0:T(8,128)}, u32[]{:S(2)}) copy-start(f32[512,384]{1,0:T(8,128)} %get-tuple-element.17) | copy-start | bytes 2359300
  85.8 14.1 %copy-start.3 = (f32[512,384]{1,0:T(8,128)S(1)}, f32[512,384]{1,0:T(8,128)}, u32[]{:S(2)}) copy-start(f32[512,384]{1,0:T(8,128)} %get-tuple-element.19) | copy-start | bytes 2359300
  86.9 8.7 %collective-permute-start.13 = (f32[128,384]{1,0:T(8,128)S(1)}, f32[128,384]{1,0:T(8,128)S(1)}, u32[]{:S(2)}, u32[]{:S(2)}) collective-permute-start(f32[128,384]{1,0:T(8,128)S(1)} %dynamic-slice_bitcast_fusion), channel_id=1, source_target_pairs={{0,192},{64,0},{128,64},{192,128},{1,193},{65,1},{129,65},{193,129... | collective-permute-start | bytes 589832 | tf_op jit(solution)/shard_map/ppermute | solution.py:106
  90.2 10.1 %copy-start.2 = (f32[512,384]{1,0:T(8,128)S(1)}, f32[512,384]{1,0:T(8,128)}, u32[]{:S(2)}) copy-start(f32[512,384]{1,0:T(8,128)} %get-tuple-element.18) | copy-start | bytes 2359300
  91.2 8.7 %collective-permute-start.10 = (f32[128,384]{1,0:T(8,128)S(1)}, f32[128,384]{1,0:T(8,128)S(1)}, u32[]{:S(2)}, u32[]{:S(2)}) collective-permute-start(f32[128,384]{1,0:T(8,128)S(1)} %dynamic-slice_bitcast_fusion.1), channel_id=1, source_target_pairs={{0,64},{64,128},{128,192},{192,0},{1,65},{65,129},{129,193},{193,1... | collective-permute-start | bytes 589832 | tf_op jit(solution)/shard_map/ppermute | solution.py:106
  92.2 8.0 %collective-permute-start.7 = (f32[128,384]{1,0:T(8,128)S(1)}, f32[128,384]{1,0:T(8,128)S(1)}, u32[]{:S(2)}, u32[]{:S(2)}) collective-permute-start(f32[128,384]{1,0:T(8,128)S(1)} %dynamic-slice_bitcast_fusion.2), channel_id=1, source_target_pairs={{0,192},{64,0},{128,64},{192,128},{1,193},{65,1},{129,65},{193,129... | collective-permute-start | bytes 589832 | tf_op jit(solution)/shard_map/ppermute | solution.py:106
  95.6 9.7 %copy-start.4 = (f32[512,384]{1,0:T(8,128)S(1)}, f32[512,384]{1,0:T(8,128)}, u32[]{:S(2)}) copy-start(f32[512,384]{1,0:T(8,128)} %get-tuple-element.20) | copy-start | bytes 2359300
  95.6 8.5 %collective-permute-start.4 = (f32[128,384]{1,0:T(8,128)S(1)}, f32[128,384]{1,0:T(8,128)S(1)}, u32[]{:S(2)}, u32[]{:S(2)}) collective-permute-start(f32[128,384]{1,0:T(8,128)S(1)} %dynamic-slice_bitcast_fusion.3), channel_id=1, source_target_pairs={{0,64},{64,128},{128,192},{192,0},{1,65},{65,129},{129,193},{193,1... | collective-permute-start | bytes 589832 | tf_op jit(solution)/shard_map/ppermute | solution.py:106
  96.7 8.6 %collective-permute-start.14 = (f32[128,384]{1,0:T(8,128)S(1)}, f32[128,384]{1,0:T(8,128)S(1)}, u32[]{:S(2)}, u32[]{:S(2)}) collective-permute-start(f32[128,384]{1,0:T(8,128)S(1)} %bitcast_add_fusion.2), channel_id=1, source_target_pairs={{0,192},{64,0},{128,64},{192,128},{1,193},{65,1},{129,65},{193,129... | collective-permute-start | bytes 589832 | tf_op jit(solution)/shard_map/ppermute | solution.py:106
  100.0 9.3 %collective-permute-start.11 = (f32[128,384]{1,0:T(8,128)S(1)}, f32[128,384]{1,0:T(8,128)S(1)}, u32[]{:S(2)}, u32[]{:S(2)}) collective-permute-start(f32[128,384]{1,0:T(8,128)S(1)} %bitcast_add_fusion.5), channel_id=1, source_target_pairs={{0,64},{64,128},{128,192},{192,0},{1,65},{65,129},{129,193},{193,1... | collective-permute-start | bytes 589832 | tf_op jit(solution)/shard_map/ppermute | solution.py:106
  100.3 9.2 %collective-permute-start.8 = (f32[128,384]{1,0:T(8,128)S(1)}, f32[128,384]{1,0:T(8,128)S(1)}, u32[]{:S(2)}, u32[]{:S(2)}) collective-permute-start(f32[128,384]{1,0:T(8,128)S(1)} %bitcast_add_fusion.8), channel_id=1, source_target_pairs={{0,192},{64,0},{128,64},{192,128},{1,193},{65,1},{129,65},{193,129... | collective-permute-start | bytes 589832 | tf_op jit(solution)/shard_map/ppermute | solution.py:106
  104.1 9.4 %collective-permute-start.5 = (f32[128,384]{1,0:T(8,128)S(1)}, f32[128,384]{1,0:T(8,128)S(1)}, u32[]{:S(2)}, u32[]{:S(2)}) collective-permute-start(f32[128,384]{1,0:T(8,128)S(1)} %bitcast_add_fusion.11), channel_id=1, source_target_pairs={{0,64},{64,128},{128,192},{192,0},{1,65},{65,129},{129,193},{193,1... | collective-permute-start | bytes 589832 | tf_op jit(solution)/shard_map/ppermute | solution.py:106
  105.3 8.3 %collective-permute-start.15 = (f32[128,384]{1,0:T(8,128)S(1)}, f32[128,384]{1,0:T(8,128)S(1)}, u32[]{:S(2)}, u32[]{:S(2)}) collective-permute-start(f32[128,384]{1,0:T(8,128)S(1)} %bitcast_add_fusion.1), channel_id=1, source_target_pairs={{0,192},{64,0},{128,64},{192,128},{1,193},{65,1},{129,65},{193,129... | collective-permute-start | bytes 589832 | tf_op jit(solution)/shard_map/ppermute | solution.py:106
  109.3 8.0 %collective-permute-start.12 = (f32[128,384]{1,0:T(8,128)S(1)}, f32[128,384]{1,0:T(8,128)S(1)}, u32[]{:S(2)}, u32[]{:S(2)}) collective-permute-start(f32[128,384]{1,0:T(8,128)S(1)} %bitcast_add_fusion.4), channel_id=1, source_target_pairs={{0,64},{64,128},{128,192},{192,0},{1,65},{65,129},{129,193},{193,1... | collective-permute-start | bytes 589832 | tf_op jit(solution)/shard_map/ppermute | solution.py:106
  109.5 7.0 %collective-permute-start.9 = (f32[128,384]{1,0:T(8,128)S(1)}, f32[128,384]{1,0:T(8,128)S(1)}, u32[]{:S(2)}, u32[]{:S(2)}) collective-permute-start(f32[128,384]{1,0:T(8,128)S(1)} %bitcast_add_fusion.7), channel_id=1, source_target_pairs={{0,192},{64,0},{128,64},{192,128},{1,193},{65,1},{129,65},{193,129... | collective-permute-start | bytes 589832 | tf_op jit(solution)/shard_map/ppermute | solution.py:106
  113.5 7.0 %collective-permute-start.6 = (f32[128,384]{1,0:T(8,128)S(1)}, f32[128,384]{1,0:T(8,128)S(1)}, u32[]{:S(2)}, u32[]{:S(2)}) collective-permute-start(f32[128,384]{1,0:T(8,128)S(1)} %bitcast_add_fusion.10), channel_id=1, source_target_pairs={{0,64},{64,128},{128,192},{192,0},{1,65},{65,129},{129,193},{193,1... | collective-permute-start | bytes 589832 | tf_op jit(solution)/shard_map/ppermute | solution.py:106
  (5 other events, 5.9 us)

commit v18 on v17

--- a/solution.py
+++ b/solution.py
@@ -50,17 +50,16 @@
         o_ref[...] = base[:, q * quarter:(q + 1) * quarter]
 
 
-def far_kernel(a_ref, w2lo_ref, w2hi_ref, *refs):
+def far_kernel(a_ref, w2lo_ref, w2hi_ref, *o_refs):
     k = w2lo_ref.shape[0]
-    acc_refs, o_refs = refs[:4], refs[4:]
     quarter = o_refs[0].shape[1]
     far = a_ref[:, 2 * k:3 * k]
     low = jnp.dot(far, w2lo_ref[...], preferred_element_type=jnp.float32)
     high = jnp.dot(far, w2hi_ref[...], preferred_element_type=jnp.float32)
-    for q, (acc_ref, o_ref) in enumerate(zip(acc_refs, o_refs)):
+    for q, o_ref in enumerate(o_refs):
         source = low if q < 2 else high
         start = (q % 2) * quarter
-        o_ref[...] = acc_ref[...] + source[:, start:start + quarter]
+        o_ref[...] = source[:, start:start + quarter]
 
 
 def dot_pieces(a, pieces, tile=256):
@@ -82,31 +81,33 @@
             flops=2 * m * 3 * own.size, transcendentals=0, bytes_accessed=a.size * 2 + 3 * own.size * 2 + m * n * 4
         ),
     )(a, *near_w)
-    return pl.pallas_call(
+    far_quarters = pl.pallas_call(
         far_kernel,
         grid=(m // tile,),
-        in_specs=[a_spec, full(far_low), full(far_high)] + [spec] * 4,
+        in_specs=[a_spec, full(far_low), full(far_high)],
         out_specs=(spec,) * 4,
         out_shape=(shape,) * 4,
-        input_output_aliases={3: 0, 4: 1, 5: 2, 6: 3},
         cost_estimate=pl.CostEstimate(
-            flops=2 * m * own.size, transcendentals=0, bytes_accessed=a.size * 2 + own.size * 2 + 2 * m * n * 4
+            flops=2 * m * own.size, transcendentals=0, bytes_accessed=a.size * 2 + own.size * 2 + m * n * 4
         ),
-    )(a, far_low, far_high, *quarters)
+    )(a, far_low, far_high)
+    return quarters, far_quarters
 
 
-def ring_reduce_scatter(parts, axis, n):
+def ring_reduce_scatter(parts, others, axis, n, finish):
     me = lax.axis_index(axis)
     out = []
-    for index, part in enumerate(parts):
+    for index, (part, other) in enumerate(zip(parts, others)):
         step_dir = 1 if index % 2 == 0 else -1
         perm = [(i, (i + step_dir) % n) for i in range(n)]
-        acc = lax.dynamic_index_in_dim(part, (me - step_dir) % n, 0, keepdims=False)
+        own = lambda seg: lax.dynamic_index_in_dim(part, seg, 0, keepdims=False) + lax.dynamic_index_in_dim(
+            other, seg, 0, keepdims=False
+        )
+        acc = own((me - step_dir) % n)
         for k in range(n - 1):
             got = lax.ppermute(acc, axis, perm)
-            seg = (me - step_dir * (k + 2)) % n
-            acc = got + lax.dynamic_index_in_dim(part, seg, 0, keepdims=False)
-        out.append(acc)
+            acc = got + own((me - step_dir * (k + 2)) % n)
+        out.append(finish(acc))
     return jnp.concatenate(out, axis=1)
 
 
@@ -133,9 +134,10 @@
     spread_out = spread_out.reshape((n_y * n_col,) + groups.shape[1:])
     tokens = lax.all_to_all(spread_out, ("ry", "col"), split_axis=0, concat_axis=0, tiled=True)
     tokens = tokens.reshape(-1, tokens.shape[-1])
-    quarters = dot_pieces(tokens, pieces)
-    product = ring_reduce_scatter([q.reshape(n_y, -1, q.shape[1]) for q in quarters], "ry", n_y)
-    return jax.nn.gelu(product, approximate=True).astype(jnp.bfloat16)
+    near, far = dot_pieces(tokens, pieces)
+    segments = lambda qs: [q.reshape(n_y, -1, q.shape[1]) for q in qs]
+    finish = lambda u: jax.nn.gelu(u, approximate=True).astype(jnp.bfloat16)
+    return ring_reduce_scatter(segments(near), segments(far), "ry", n_y, finish)
 
 
 def solution(mesh):

time: 122 us -> 119 us (0.975)
  local copies, waits for them, and re-layouts: 13.4 us -> 7.84 us
  other arithmetic: 3.17 us -> 5.39 us
    ppermute x1, waiting for transfers between devices: 26.1 us -> 0.01 us  [ring_pieces(): from_left = lax.ppermute(block, axis, to_right)]
    ppermute x1, waiting for transfers between devices: 0.01 us -> 26.1 us  [ring_pieces(): from_right = lax.ppermute(block, axis, to_left)]
    squeeze x4 -> x0, local copies, waits for them, and re-layouts: 3.04 us -> none  [ring_reduce_scatter(): acc = lax.dynamic_index_in_dim(part, (me - step_dir) % n, 0, keepdims=False)]
    ppermute x12, waiting for transfers between devices: 8.48 us -> 11.5 us  [ring_reduce_scatter(): got = lax.ppermute(acc, axis, perm)]
    ppermute x12, starting transfers between devices: 21.7 us -> 18.8 us  [ring_reduce_scatter(): got = lax.ppermute(acc, axis, perm)]
    add x12, other arithmetic: 1.29 us -> 3.37 us  [the longest x4 3.1 us: ring_reduce_scatter(): lax.dynamic_index_in_dim(part, seg, 0, keepdims=False)]
    ppermute x1, starting transfers between devices: 0.56 us -> 2.41 us  [ring_pieces(): from_left = lax.ppermute(block, axis, to_right)]
    ppermute x1, waiting for transfers between devices: 1.85 us -> 0.01 us  [ring_pieces(): far_high = lax.ppermute(from_right[:, half:], axis, to_left)]
  transfers between devices with their start and end apart: 18 -> 18, of which waited for: 12 -> 10; matrix products, arithmetic and copies ran while one was open for 3% -> 2% of each run, Pallas kernels for 5% -> 5%
where the time goes in v18:
time: 119 us; the launch traced here: 117 us
  waiting for transfers between devices  53.1 us (45%)
  starting transfers between devices  40.7 us (34%)
  Pallas kernels  9.7 us (8%)
  local copies, waits for them, and re-layouts  7.84 us (7%)
  other arithmetic  5.39 us (5%)
    ppermute x1, waiting for transfers between devices, ring_pieces(): from_right = lax.ppermute(block, axis, to_left)  26.1 us
    ppermute x12, starting transfers between devices, ring_reduce_scatter(): got = lax.ppermute(acc, axis, perm)  18.8 us
    ppermute x12, waiting for transfers between devices, ring_reduce_scatter(): got = lax.ppermute(acc, axis, perm)  11.5 us
    all_to_all x1, waiting for transfers between devices, per_device(): both = lax.all_to_all(both, 'col', split_axis=0, concat_axis=1, tiled=True)  9.92 us
    all_to_all x1, starting transfers between devices, per_device(): both = lax.all_to_all(both, 'col', split_axis=0, concat_axis=1, tiled=True)  8.57 us
    all_to_all x1, starting transfers between devices, per_device(): lax.all_to_all(spread_out, ('ry', 'col'), split_axis=0, concat_axis=0, ti...  6.77 us
    pallas_call x1, Pallas kernels, dot_pieces(): pl.pallas_call(near_kernel, grid=(m // tile,), in_specs=[a_spec] + [full(...  5.99 us
    all_to_all x1, waiting for transfers between devices, per_device(): lax.all_to_all(spread_out, ('ry', 'col'), split_axis=0, concat_axis=0, ti...  5.54 us
  transfers between devices with their start and end apart: 18, of which 10 were waited for; matrix products, arithmetic and copies ran while one was open for 2% of the time, Pallas kernels for 5%

profile of v18, /device:TPU:6, one launch (start us, length us, event | category | flops | bytes accessed | tf_op | source)
XLA Modules:
  0.0 117.4 jit_solution(671972126132124488)
XLA Ops:
  4.7 8.6 %all-to-all-start = ((bf16[128,2,384]{2,1,0:T(2,128)(2,1)}), bf16[128,2,384]{2,1,0:T(2,128)(2,1)S(1)}, u32[]{:S(2)}, u32[]{:S(2)}) async-start(bf16[128,2,384]{2,1,0:T(2,128)(2,1)} %copy.33), calls=%async_computation | async-start | bytes 393216 | tf_op jit(solution)/shard_map/all_to_all | solution.py:118
  13.3 9.9 %all-to-all-done = bf16[128,2,384]{2,1,0:T(2,128)(2,1)S(1)} async-done(((bf16[128,2,384]{2,1,0:T(2,128)(2,1)}), bf16[128,2,384]{2,1,0:T(2,128)(2,1)S(1)}, u32[]{:S(2)}, u32[]{:S(2)}) %all-to-all-start) | async-done | bytes 196640 | tf_op jit(solution)/shard_map/all_to_all | solution.py:118
  24.0 1.3 %broadcast_in_dim.16 = bf16[4,16,8,1536]{3,2,1,0:T(8,128)(2,1)} broadcast(bf16[4,8,1536]{2,1,0:T(8,128)(2,1)S(1)} %bitcast.113), dimensions={0,2,3} | broadcast | bytes 1671168 | tf_op jit(solution)/shard_map/broadcast_in_dim | solution.py:133
  25.3 6.8 %all-to-all-start.1 = ((bf16[64,8,1536]{2,1,0:T(8,128)(2,1)}), bf16[64,8,1536]{2,1,0:T(8,128)(2,1)S(1)}, u32[]{:S(2)}, u32[]{:S(2)}) async-start(bf16[64,8,1536]{2,1,0:T(8,128)(2,1)} %bitcast.11), calls=%async_computation.1 | async-start | bytes 3145728 | tf_op jit(solution)/shard_map/all_to_all | solution.py:135
  33.0 2.4 %collective-permute-start.1 = (bf16[384,1536]{1,0:T(8,128)(2,1)}, bf16[384,1536]{1,0:T(8,128)(2,1)S(1)}, u32[]{:S(2)}, u32[]{:S(2)}) collective-permute-start(bf16[384,1536]{1,0:T(8,128)(2,1)} %w0_ref.1), channel_id=1, source_target_pairs={{0,16},{16,32},{32,48},{48,0},{1,17},{17,33},{33,49},{49,1},{2,18}... | collective-permute-start | bytes 3538952 | tf_op jit(solution)/shard_map/ppermute | solution.py:34
  35.4 26.1 %collective-permute-done.w1_ref = bf16[384,1536]{1,0:T(8,128)(2,1)S(1)} collective-permute-done((bf16[384,1536]{1,0:T(8,128)(2,1)}, bf16[384,1536]{1,0:T(8,128)(2,1)S(1)}, u32[]{:S(2)}, u32[]{:S(2)}) %collective-permute-start) | collective-permute-done | bytes 1179680 | tf_op jit(solution)/shard_map/ppermute | solution.py:35
  61.6 1.1 copy-done.10
  62.9 3.1 %collective-permute-start.2 = (bf16[384,768]{1,0:T(8,128)(2,1)S(1)}, bf16[384,768]{1,0:T(8,128)(2,1)}, u32[]{:S(2)}, u32[]{:S(2)}) collective-permute-start(bf16[384,768]{1,0:T(8,128)(2,1)S(1)} %slice.18), channel_id=1, source_target_pairs={{0,16},{16,32},{32,48},{48,0},{1,17},{17,33},{33,49},{49,1},{2,18}... | collective-permute-start | bytes 1769480 | tf_op jit(solution)/shard_map/ppermute | solution.py:37
  66.0 5.5 %all-to-all-done.1 = bf16[64,8,1536]{2,1,0:T(8,128)(2,1)S(1)} async-done(((bf16[64,8,1536]{2,1,0:T(8,128)(2,1)}), bf16[64,8,1536]{2,1,0:T(8,128)(2,1)S(1)}, u32[]{:S(2)}, u32[]{:S(2)}) %all-to-all-start.1) | async-done | bytes 1572896 | tf_op jit(solution)/shard_map/all_to_all | solution.py:135
  71.6 1.2 copy-done
  72.7 6.0 %shard_map.64 = (f32[512,384]{1,0:T(8,128)}, f32[512,384]{1,0:T(8,128)}, f32[512,384]{1,0:T(8,128)}, f32[512,384]{1,0:T(8,128)}) custom-call(bf16[512,1536]{1,0:T(8,128)(2,1)} %bitcast.77, bf16[384,1536]{1,0:T(8,128)(2,1)} %w0_ref.1, bf16[384,1536]{1,0:T(8,128)(2,1)} %copy-done.9, bf16[384,1536]{1,0:T(8,128)(2,1)} %copy-done.10), custom_call_target="tpu_custom_call" | custom-call | flops 1811939328 | bytes 8257536 | tf_op jit(solution)/shard_map/pallas_call | solution.py:74
  78.7 3.7 %shard_map.65 = (f32[512,384]{1,0:T(8,128)}, f32[512,384]{1,0:T(8,128)}, f32[512,384]{1,0:T(8,128)}, f32[512,384]{1,0:T(8,128)}) custom-call(bf16[512,1536]{1,0:T(8,128)(2,1)} %bitcast.78, bf16[384,768]{1,0:T(8,128)(2,1)} %collective-permute-done.2.w2lo_ref, bf16[384,768]{1,0:T(8,128)(2,1)} %collective-permute-done.3.w2hi_ref), custom_call_target="tpu_custom_call" | custom-call | flops 603979776 | bytes 5898240 | tf_op jit(solution)/shard_map/pallas_call | solution.py:84
  85.4 1.6 %collective-permute-start.4 = (f32[128,384]{1,0:T(8,128)S(1)}, f32[128,384]{1,0:T(8,128)S(1)}, u32[]{:S(2)}, u32[]{:S(2)}) collective-permute-start(f32[128,384]{1,0:T(8,128)S(1)} %add_bitcast_fusion.3), channel_id=1, source_target_pairs={{0,64},{64,128},{128,192},{192,0},{1,65},{65,129},{129,193},{193,1... | collective-permute-start | bytes 589832 | tf_op jit(solution)/shard_map/ppermute | solution.py:108
  87.9 1.8 %collective-permute-start.13 = (f32[128,384]{1,0:T(8,128)S(1)}, f32[128,384]{1,0:T(8,128)S(1)}, u32[]{:S(2)}, u32[]{:S(2)}) collective-permute-start(f32[128,384]{1,0:T(8,128)S(1)} %add_bitcast_fusion), channel_id=1, source_target_pairs={{0,192},{64,0},{128,64},{192,128},{1,193},{65,1},{129,65},{193,129... | collective-permute-start | bytes 589832 | tf_op jit(solution)/shard_map/ppermute | solution.py:108
  89.8 1.4 %collective-permute-start.7 = (f32[128,384]{1,0:T(8,128)S(1)}, f32[128,384]{1,0:T(8,128)S(1)}, u32[]{:S(2)}, u32[]{:S(2)}) collective-permute-start(f32[128,384]{1,0:T(8,128)S(1)} %add_bitcast_fusion.2), channel_id=1, source_target_pairs={{0,192},{64,0},{128,64},{192,128},{1,193},{65,1},{129,65},{193,129... | collective-permute-start | bytes 589832 | tf_op jit(solution)/shard_map/ppermute | solution.py:108
  91.2 1.4 %collective-permute-done.10 = f32[128,384]{1,0:T(8,128)S(1)} collective-permute-done((f32[128,384]{1,0:T(8,128)S(1)}, f32[128,384]{1,0:T(8,128)S(1)}, u32[]{:S(2)}, u32[]{:S(2)}) %collective-permute-start.10) | collective-permute-done | bytes 196640 | tf_op jit(solution)/shard_map/ppermute | solution.py:108
  92.8 4.1 %collective-permute-done.4 = f32[128,384]{1,0:T(8,128)S(1)} collective-permute-done((f32[128,384]{1,0:T(8,128)S(1)}, f32[128,384]{1,0:T(8,128)S(1)}, u32[]{:S(2)}, u32[]{:S(2)}) %collective-permute-start.4) | collective-permute-done | bytes 196640 | tf_op jit(solution)/shard_map/ppermute | solution.py:108
  97.2 3.3 %collective-permute-start.14 = (f32[128,384]{1,0:T(8,128)S(1)}, f32[128,384]{1,0:T(8,128)S(1)}, u32[]{:S(2)}, u32[]{:S(2)}) collective-permute-start(f32[128,384]{1,0:T(8,128)S(1)} %bitcast_add_fusion.2), channel_id=1, source_target_pairs={{0,192},{64,0},{128,64},{192,128},{1,193},{65,1},{129,65},{193,129... | collective-permute-start | bytes 589832 | tf_op jit(solution)/shard_map/ppermute | solution.py:108
  100.5 2.2 %collective-permute-start.8 = (f32[128,384]{1,0:T(8,128)S(1)}, f32[128,384]{1,0:T(8,128)S(1)}, u32[]{:S(2)}, u32[]{:S(2)}) collective-permute-start(f32[128,384]{1,0:T(8,128)S(1)} %bitcast_add_fusion.8), channel_id=1, source_target_pairs={{0,192},{64,0},{128,64},{192,128},{1,193},{65,1},{129,65},{193,129... | collective-permute-start | bytes 589832 | tf_op jit(solution)/shard_map/ppermute | solution.py:108
  102.8 1.9 %collective-permute-done.5 = f32[128,384]{1,0:T(8,128)S(1)} collective-permute-done((f32[128,384]{1,0:T(8,128)S(1)}, f32[128,384]{1,0:T(8,128)S(1)}, u32[]{:S(2)}, u32[]{:S(2)}) %collective-permute-start.5) | collective-permute-done | bytes 196640 | tf_op jit(solution)/shard_map/ppermute | solution.py:108
  105.2 3.4 %collective-permute-start.15 = (f32[128,384]{1,0:T(8,128)S(1)}, f32[128,384]{1,0:T(8,128)S(1)}, u32[]{:S(2)}, u32[]{:S(2)}) collective-permute-start(f32[128,384]{1,0:T(8,128)S(1)} %bitcast_add_fusion.1), channel_id=1, source_target_pairs={{0,192},{64,0},{128,64},{192,128},{1,193},{65,1},{129,65},{193,129... | collective-permute-start | bytes 589832 | tf_op jit(solution)/shard_map/ppermute | solution.py:108
  109.0 3.8 %collective-permute-start.9 = (f32[128,384]{1,0:T(8,128)S(1)}, f32[128,384]{1,0:T(8,128)S(1)}, u32[]{:S(2)}, u32[]{:S(2)}) collective-permute-start(f32[128,384]{1,0:T(8,128)S(1)} %bitcast_add_fusion.7), channel_id=1, source_target_pairs={{0,192},{64,0},{128,64},{192,128},{1,193},{65,1},{129,65},{193,129... | collective-permute-start | bytes 589832 | tf_op jit(solution)/shard_map/ppermute | solution.py:108
  112.8 1.8 %collective-permute-done.6 = f32[128,384]{1,0:T(8,128)S(1)} collective-permute-done((f32[128,384]{1,0:T(8,128)S(1)}, f32[128,384]{1,0:T(8,128)S(1)}, u32[]{:S(2)}, u32[]{:S(2)}) %collective-permute-start.6) | collective-permute-done | bytes 196640 | tf_op jit(solution)/shard_map/ppermute | solution.py:108
  114.8 1.8 %collective-permute-done.9 = f32[128,384]{1,0:T(8,128)S(1)} collective-permute-done((f32[128,384]{1,0:T(8,128)S(1)}, f32[128,384]{1,0:T(8,128)S(1)}, u32[]{:S(2)}, u32[]{:S(2)}) %collective-permute-start.9) | collective-permute-done | bytes 196640 | tf_op jit(solution)/shard_map/ppermute | solution.py:108
  (76 shorter events, 13.1 us)
Async XLA Ops:
  3.4 9.9 %copy-start.12 = (f32[6144]{0:T(1024)S(1)}, f32[6144]{0:T(1024)}, u32[]{:S(2)}) copy-start(f32[6144]{0:T(1024)} %param.10) | copy-start | bytes 73732
  4.7 18.5 %all-to-all-start = ((bf16[128,2,384]{2,1,0:T(2,128)(2,1)}), bf16[128,2,384]{2,1,0:T(2,128)(2,1)S(1)}, u32[]{:S(2)}, u32[]{:S(2)}) async-start(bf16[128,2,384]{2,1,0:T(2,128)(2,1)} %copy.33), calls=%async_computation | async-start | bytes 393216 | tf_op jit(solution)/shard_map/all_to_all | solution.py:118
  25.3 46.3 %all-to-all-start.1 = ((bf16[64,8,1536]{2,1,0:T(8,128)(2,1)}), bf16[64,8,1536]{2,1,0:T(8,128)(2,1)S(1)}, u32[]{:S(2)}, u32[]{:S(2)}) async-start(bf16[64,8,1536]{2,1,0:T(8,128)(2,1)} %bitcast.11), calls=%async_computation.1 | async-start | bytes 3145728 | tf_op jit(solution)/shard_map/all_to_all | solution.py:135
  32.1 29.4 %collective-permute-start = (bf16[384,1536]{1,0:T(8,128)(2,1)}, bf16[384,1536]{1,0:T(8,128)(2,1)S(1)}, u32[]{:S(2)}, u32[]{:S(2)}) collective-permute-start(bf16[384,1536]{1,0:T(8,128)(2,1)} %w0_ref.1), channel_id=1, source_target_pairs={{0,48},{16,0},{32,16},{48,32},{1,49},{17,1},{33,17},{49,33},{2,50}... | collective-permute-start | bytes 3538952 | tf_op jit(solution)/shard_map/ppermute | solution.py:35
  33.0 28.7 %collective-permute-start.1 = (bf16[384,1536]{1,0:T(8,128)(2,1)}, bf16[384,1536]{1,0:T(8,128)(2,1)S(1)}, u32[]{:S(2)}, u32[]{:S(2)}) collective-permute-start(bf16[384,1536]{1,0:T(8,128)(2,1)} %w0_ref.1), channel_id=1, source_target_pairs={{0,16},{16,32},{32,48},{48,0},{1,17},{17,33},{33,49},{49,1},{2,18}... | collective-permute-start | bytes 3538952 | tf_op jit(solution)/shard_map/ppermute | solution.py:34
  61.5 17.2 %collective-permute-start.3 = (bf16[384,768]{1,0:T(8,128)(2,1)S(1)}, bf16[384,768]{1,0:T(8,128)(2,1)}, u32[]{:S(2)}, u32[]{:S(2)}) collective-permute-start(bf16[384,768]{1,0:T(8,128)(2,1)S(1)} %slice.19), channel_id=1, source_target_pairs={{0,48},{16,0},{32,16},{48,32},{1,49},{17,1},{33,17},{49,33},{2,50}... | collective-permute-start | bytes 1769480 | tf_op jit(solution)/shard_map/ppermute | solution.py:38
  62.9 15.8 %collective-permute-start.2 = (bf16[384,768]{1,0:T(8,128)(2,1)S(1)}, bf16[384,768]{1,0:T(8,128)(2,1)}, u32[]{:S(2)}, u32[]{:S(2)}) collective-permute-start(bf16[384,768]{1,0:T(8,128)(2,1)S(1)} %slice.18), channel_id=1, source_target_pairs={{0,16},{16,32},{32,48},{48,0},{1,17},{17,33},{33,49},{49,1},{2,18}... | collective-permute-start | bytes 1769480 | tf_op jit(solution)/shard_map/ppermute | solution.py:37
  78.7 8.2 %copy-start.2 = (f32[512,384]{1,0:T(8,128)S(1)}, f32[512,384]{1,0:T(8,128)}, u32[]{:S(2)}) copy-start(f32[512,384]{1,0:T(8,128)} %get-tuple-element.19) | copy-start | bytes 2359300
  82.5 7.3 %copy-start.3 = (f32[512,384]{1,0:T(8,128)S(1)}, f32[512,384]{1,0:T(8,128)}, u32[]{:S(2)}) copy-start(f32[512,384]{1,0:T(8,128)} %get-tuple-element.16) | copy-start | bytes 2359300
  82.5 10.1 %copy-start.8 = (f32[512,384]{1,0:T(8,128)S(1)}, f32[512,384]{1,0:T(8,128)}, u32[]{:S(2)}) copy-start(f32[512,384]{1,0:T(8,128)} %get-tuple-element.18) | copy-start | bytes 2359300
  83.6 9.0 %collective-permute-start.10 = (f32[128,384]{1,0:T(8,128)S(1)}, f32[128,384]{1,0:T(8,128)S(1)}, u32[]{:S(2)}, u32[]{:S(2)}) collective-permute-start(f32[128,384]{1,0:T(8,128)S(1)} %add_bitcast_fusion.1), channel_id=1, source_target_pairs={{0,64},{64,128},{128,192},{192,0},{1,65},{65,129},{129,193},{193,1... | collective-permute-start | bytes 589832 | tf_op jit(solution)/shard_map/ppermute | solution.py:108
  84.4 12.4 %copy-start.7 = (f32[512,384]{1,0:T(8,128)S(1)}, f32[512,384]{1,0:T(8,128)}, u32[]{:S(2)}) copy-start(f32[512,384]{1,0:T(8,128)} %get-tuple-element.14) | copy-start | bytes 2359300
  85.4 11.4 %collective-permute-start.4 = (f32[128,384]{1,0:T(8,128)S(1)}, f32[128,384]{1,0:T(8,128)S(1)}, u32[]{:S(2)}, u32[]{:S(2)}) collective-permute-start(f32[128,384]{1,0:T(8,128)S(1)} %add_bitcast_fusion.3), channel_id=1, source_target_pairs={{0,64},{64,128},{128,192},{192,0},{1,65},{65,129},{129,193},{193,1... | collective-permute-start | bytes 589832 | tf_op jit(solution)/shard_map/ppermute | solution.py:108
  87.9 9.2 %copy-start.5 = (f32[512,384]{1,0:T(8,128)S(1)}, f32[512,384]{1,0:T(8,128)}, u32[]{:S(2)}) copy-start(f32[512,384]{1,0:T(8,128)} %get-tuple-element.20) | copy-start | bytes 2359300
  87.9 9.2 %collective-permute-start.13 = (f32[128,384]{1,0:T(8,128)S(1)}, f32[128,384]{1,0:T(8,128)S(1)}, u32[]{:S(2)}, u32[]{:S(2)}) collective-permute-start(f32[128,384]{1,0:T(8,128)S(1)} %add_bitcast_fusion), channel_id=1, source_target_pairs={{0,192},{64,0},{128,64},{192,128},{1,193},{65,1},{129,65},{193,129... | collective-permute-start | bytes 589832 | tf_op jit(solution)/shard_map/ppermute | solution.py:108
  89.8 10.7 %collective-permute-start.7 = (f32[128,384]{1,0:T(8,128)S(1)}, f32[128,384]{1,0:T(8,128)S(1)}, u32[]{:S(2)}, u32[]{:S(2)}) collective-permute-start(f32[128,384]{1,0:T(8,128)S(1)} %add_bitcast_fusion.2), channel_id=1, source_target_pairs={{0,192},{64,0},{128,64},{192,128},{1,193},{65,1},{129,65},{193,129... | collective-permute-start | bytes 589832 | tf_op jit(solution)/shard_map/ppermute | solution.py:108
  92.7 10.0 %collective-permute-start.11 = (f32[128,384]{1,0:T(8,128)S(1)}, f32[128,384]{1,0:T(8,128)S(1)}, u32[]{:S(2)}, u32[]{:S(2)}) collective-permute-start(f32[128,384]{1,0:T(8,128)S(1)} %bitcast_add_fusion.5), channel_id=1, source_target_pairs={{0,64},{64,128},{128,192},{192,0},{1,65},{65,129},{129,193},{193,1... | collective-permute-start | bytes 589832 | tf_op jit(solution)/shard_map/ppermute | solution.py:108
  96.9 7.8 %collective-permute-start.5 = (f32[128,384]{1,0:T(8,128)S(1)}, f32[128,384]{1,0:T(8,128)S(1)}, u32[]{:S(2)}, u32[]{:S(2)}) collective-permute-start(f32[128,384]{1,0:T(8,128)S(1)} %bitcast_add_fusion.11), channel_id=1, source_target_pairs={{0,64},{64,128},{128,192},{192,0},{1,65},{65,129},{129,193},{193,1... | collective-permute-start | bytes 589832 | tf_op jit(solution)/shard_map/ppermute | solution.py:108
  97.2 7.9 %collective-permute-start.14 = (f32[128,384]{1,0:T(8,128)S(1)}, f32[128,384]{1,0:T(8,128)S(1)}, u32[]{:S(2)}, u32[]{:S(2)}) collective-permute-start(f32[128,384]{1,0:T(8,128)S(1)} %bitcast_add_fusion.2), channel_id=1, source_target_pairs={{0,192},{64,0},{128,64},{192,128},{1,193},{65,1},{129,65},{193,129... | collective-permute-start | bytes 589832 | tf_op jit(solution)/shard_map/ppermute | solution.py:108
  100.5 8.4 %collective-permute-start.8 = (f32[128,384]{1,0:T(8,128)S(1)}, f32[128,384]{1,0:T(8,128)S(1)}, u32[]{:S(2)}, u32[]{:S(2)}) collective-permute-start(f32[128,384]{1,0:T(8,128)S(1)} %bitcast_add_fusion.8), channel_id=1, source_target_pairs={{0,192},{64,0},{128,64},{192,128},{1,193},{65,1},{129,65},{193,129... | collective-permute-start | bytes 589832 | tf_op jit(solution)/shard_map/ppermute | solution.py:108
  102.7 10.0 %collective-permute-start.12 = (f32[128,384]{1,0:T(8,128)S(1)}, f32[128,384]{1,0:T(8,128)S(1)}, u32[]{:S(2)}, u32[]{:S(2)}) collective-permute-start(f32[128,384]{1,0:T(8,128)S(1)} %bitcast_add_fusion.4), channel_id=1, source_target_pairs={{0,64},{64,128},{128,192},{192,0},{1,65},{65,129},{129,193},{193,1... | collective-permute-start | bytes 589832 | tf_op jit(solution)/shard_map/ppermute | solution.py:108
  104.7 9.9 %collective-permute-start.6 = (f32[128,384]{1,0:T(8,128)S(1)}, f32[128,384]{1,0:T(8,128)S(1)}, u32[]{:S(2)}, u32[]{:S(2)}) collective-permute-start(f32[128,384]{1,0:T(8,128)S(1)} %bitcast_add_fusion.10), channel_id=1, source_target_pairs={{0,64},{64,128},{128,192},{192,0},{1,65},{65,129},{129,193},{193,1... | collective-permute-start | bytes 589832 | tf_op jit(solution)/shard_map/ppermute | solution.py:108
  105.2 9.5 %collective-permute-start.15 = (f32[128,384]{1,0:T(8,128)S(1)}, f32[128,384]{1,0:T(8,128)S(1)}, u32[]{:S(2)}, u32[]{:S(2)}) collective-permute-start(f32[128,384]{1,0:T(8,128)S(1)} %bitcast_add_fusion.1), channel_id=1, source_target_pairs={{0,192},{64,0},{128,64},{192,128},{1,193},{65,1},{129,65},{193,129... | collective-permute-start | bytes 589832 | tf_op jit(solution)/shard_map/ppermute | solution.py:108
  109.0 7.6 %collective-permute-start.9 = (f32[128,384]{1,0:T(8,128)S(1)}, f32[128,384]{1,0:T(8,128)S(1)}, u32[]{:S(2)}, u32[]{:S(2)}) collective-permute-start(f32[128,384]{1,0:T(8,128)S(1)} %bitcast_add_fusion.7), channel_id=1, source_target_pairs={{0,192},{64,0},{128,64},{192,128},{1,193},{65,1},{129,65},{193,129... | collective-permute-start | bytes 589832 | tf_op jit(solution)/shard_map/ppermute | solution.py:108
  (7 other events, 24.2 us)

commit v19 on v18

--- a/solution.py
+++ b/solution.py
@@ -62,7 +62,7 @@
         o_ref[...] = source[:, start:start + quarter]
 
 
-def dot_pieces(a, pieces, tile=256):
+def dot_pieces(a, pieces, tile=512):
     m, kk = a.shape
     n = pieces[0].shape[1]
     own, right, far_low, far_high, left = pieces

time: 119 us -> 119 us (level)
  transfers between devices with their start and end apart: 18 -> 18, of which waited for: 10 -> 9; matrix products, arithmetic and copies ran while one was open for 2% -> 2% of each run, Pallas kernels for 5% -> 5%
where the time goes in v19:
time: 119 us; the launch traced here: 118 us
  waiting for transfers between devices  53.7 us (45%)
  starting transfers between devices  40.1 us (34%)
  Pallas kernels  10.2 us (9%)
  local copies, waits for them, and re-layouts  7.84 us (7%)
  other arithmetic  5.39 us (5%)
    ppermute x1, waiting for transfers between devices, ring_pieces(): from_right = lax.ppermute(block, axis, to_left)  26.1 us
    ppermute x12, starting transfers between devices, ring_reduce_scatter(): got = lax.ppermute(acc, axis, perm)  18.2 us
    ppermute x12, waiting for transfers between devices, ring_reduce_scatter(): got = lax.ppermute(acc, axis, perm)  12.1 us
    all_to_all x1, waiting for transfers between devices, per_device(): both = lax.all_to_all(both, 'col', split_axis=0, concat_axis=1, tiled=True)  9.92 us
    all_to_all x1, starting transfers between devices, per_device(): both = lax.all_to_all(both, 'col', split_axis=0, concat_axis=1, tiled=True)  8.57 us
    all_to_all x1, starting transfers between devices, per_device(): lax.all_to_all(spread_out, ('ry', 'col'), split_axis=0, concat_axis=0, ti...  6.77 us
    pallas_call x1, Pallas kernels, dot_pieces(): pl.pallas_call(near_kernel, grid=(m // tile,), in_specs=[a_spec] + [full(...  6.24 us
    all_to_all x1, waiting for transfers between devices, per_device(): lax.all_to_all(spread_out, ('ry', 'col'), split_axis=0, concat_axis=0, ti...  5.54 us
  transfers between devices with their start and end apart: 18, of which 9 were waited for; matrix products, arithmetic and copies ran while one was open for 2% of the time, Pallas kernels for 5%

profile of v19, /device:TPU:6, one launch (start us, length us, event | category | flops | bytes accessed | tf_op | source)
XLA Modules:
  0.0 118.0 jit_solution(12597086128491147646)
XLA Ops:
  4.7 8.6 %all-to-all-start = ((bf16[128,2,384]{2,1,0:T(2,128)(2,1)}), bf16[128,2,384]{2,1,0:T(2,128)(2,1)S(1)}, u32[]{:S(2)}, u32[]{:S(2)}) async-start(bf16[128,2,384]{2,1,0:T(2,128)(2,1)} %copy.33), calls=%async_computation | async-start | bytes 393216 | tf_op jit(solution)/shard_map/all_to_all | solution.py:118
  13.3 9.9 %all-to-all-done = bf16[128,2,384]{2,1,0:T(2,128)(2,1)S(1)} async-done(((bf16[128,2,384]{2,1,0:T(2,128)(2,1)}), bf16[128,2,384]{2,1,0:T(2,128)(2,1)S(1)}, u32[]{:S(2)}, u32[]{:S(2)}) %all-to-all-start) | async-done | bytes 196640 | tf_op jit(solution)/shard_map/all_to_all | solution.py:118
  24.0 1.3 %broadcast_in_dim.16 = bf16[4,16,8,1536]{3,2,1,0:T(8,128)(2,1)} broadcast(bf16[4,8,1536]{2,1,0:T(8,128)(2,1)S(1)} %bitcast.113), dimensions={0,2,3} | broadcast | bytes 1671168 | tf_op jit(solution)/shard_map/broadcast_in_dim | solution.py:133
  25.3 6.8 %all-to-all-start.1 = ((bf16[64,8,1536]{2,1,0:T(8,128)(2,1)}), bf16[64,8,1536]{2,1,0:T(8,128)(2,1)S(1)}, u32[]{:S(2)}, u32[]{:S(2)}) async-start(bf16[64,8,1536]{2,1,0:T(8,128)(2,1)} %bitcast.11), calls=%async_computation.1 | async-start | bytes 3145728 | tf_op jit(solution)/shard_map/all_to_all | solution.py:135
  33.0 2.4 %collective-permute-start.1 = (bf16[384,1536]{1,0:T(8,128)(2,1)}, bf16[384,1536]{1,0:T(8,128)(2,1)S(1)}, u32[]{:S(2)}, u32[]{:S(2)}) collective-permute-start(bf16[384,1536]{1,0:T(8,128)(2,1)} %w0_ref.1), channel_id=1, source_target_pairs={{0,16},{16,32},{32,48},{48,0},{1,17},{17,33},{33,49},{49,1},{2,18}... | collective-permute-start | bytes 3538952 | tf_op jit(solution)/shard_map/ppermute | solution.py:34
  35.4 26.1 %collective-permute-done.w1_ref = bf16[384,1536]{1,0:T(8,128)(2,1)S(1)} collective-permute-done((bf16[384,1536]{1,0:T(8,128)(2,1)}, bf16[384,1536]{1,0:T(8,128)(2,1)S(1)}, u32[]{:S(2)}, u32[]{:S(2)}) %collective-permute-start) | collective-permute-done | bytes 1179680 | tf_op jit(solution)/shard_map/ppermute | solution.py:35
  61.6 1.1 copy-done.10
  62.9 3.1 %collective-permute-start.2 = (bf16[384,768]{1,0:T(8,128)(2,1)S(1)}, bf16[384,768]{1,0:T(8,128)(2,1)}, u32[]{:S(2)}, u32[]{:S(2)}) collective-permute-start(bf16[384,768]{1,0:T(8,128)(2,1)S(1)} %slice.18), channel_id=1, source_target_pairs={{0,16},{16,32},{32,48},{48,0},{1,17},{17,33},{33,49},{49,1},{2,18}... | collective-permute-start | bytes 1769480 | tf_op jit(solution)/shard_map/ppermute | solution.py:37
  66.0 5.5 %all-to-all-done.1 = bf16[64,8,1536]{2,1,0:T(8,128)(2,1)S(1)} async-done(((bf16[64,8,1536]{2,1,0:T(8,128)(2,1)}), bf16[64,8,1536]{2,1,0:T(8,128)(2,1)S(1)}, u32[]{:S(2)}, u32[]{:S(2)}) %all-to-all-start.1) | async-done | bytes 1572896 | tf_op jit(solution)/shard_map/all_to_all | solution.py:135
  71.6 1.2 copy-done
  72.7 6.2 %shard_map.64 = (f32[512,384]{1,0:T(8,128)}, f32[512,384]{1,0:T(8,128)}, f32[512,384]{1,0:T(8,128)}, f32[512,384]{1,0:T(8,128)}) custom-call(bf16[512,1536]{1,0:T(8,128)(2,1)} %bitcast.77, bf16[384,1536]{1,0:T(8,128)(2,1)} %w0_ref.1, bf16[384,1536]{1,0:T(8,128)(2,1)} %copy-done.9, bf16[384,1536]{1,0:T(8,128)(2,1)} %copy-done.10), custom_call_target="tpu_custom_call" | custom-call | flops 1811939328 | bytes 8257536 | tf_op jit(solution)/shard_map/pallas_call | solution.py:74
  79.0 4.0 %shard_map.65 = (f32[512,384]{1,0:T(8,128)}, f32[512,384]{1,0:T(8,128)}, f32[512,384]{1,0:T(8,128)}, f32[512,384]{1,0:T(8,128)}) custom-call(bf16[512,1536]{1,0:T(8,128)(2,1)} %bitcast.78, bf16[384,768]{1,0:T(8,128)(2,1)} %collective-permute-done.2.w2lo_ref, bf16[384,768]{1,0:T(8,128)(2,1)} %collective-permute-done.3.w2hi_ref), custom_call_target="tpu_custom_call" | custom-call | flops 603979776 | bytes 5898240 | tf_op jit(solution)/shard_map/pallas_call | solution.py:84
  85.9 1.4 %collective-permute-start.4 = (f32[128,384]{1,0:T(8,128)S(1)}, f32[128,384]{1,0:T(8,128)S(1)}, u32[]{:S(2)}, u32[]{:S(2)}) collective-permute-start(f32[128,384]{1,0:T(8,128)S(1)} %add_bitcast_fusion.3), channel_id=1, source_target_pairs={{0,64},{64,128},{128,192},{192,0},{1,65},{65,129},{129,193},{193,1... | collective-permute-start | bytes 589832 | tf_op jit(solution)/shard_map/ppermute | solution.py:108
  88.2 2.0 %collective-permute-start.13 = (f32[128,384]{1,0:T(8,128)S(1)}, f32[128,384]{1,0:T(8,128)S(1)}, u32[]{:S(2)}, u32[]{:S(2)}) collective-permute-start(f32[128,384]{1,0:T(8,128)S(1)} %add_bitcast_fusion), channel_id=1, source_target_pairs={{0,192},{64,0},{128,64},{192,128},{1,193},{65,1},{129,65},{193,129... | collective-permute-start | bytes 589832 | tf_op jit(solution)/shard_map/ppermute | solution.py:108
  90.3 1.4 %collective-permute-start.7 = (f32[128,384]{1,0:T(8,128)S(1)}, f32[128,384]{1,0:T(8,128)S(1)}, u32[]{:S(2)}, u32[]{:S(2)}) collective-permute-start(f32[128,384]{1,0:T(8,128)S(1)} %add_bitcast_fusion.2), channel_id=1, source_target_pairs={{0,192},{64,0},{128,64},{192,128},{1,193},{65,1},{129,65},{193,129... | collective-permute-start | bytes 589832 | tf_op jit(solution)/shard_map/ppermute | solution.py:108
  91.7 1.4 %collective-permute-done.10 = f32[128,384]{1,0:T(8,128)S(1)} collective-permute-done((f32[128,384]{1,0:T(8,128)S(1)}, f32[128,384]{1,0:T(8,128)S(1)}, u32[]{:S(2)}, u32[]{:S(2)}) %collective-permute-start.10) | collective-permute-done | bytes 196640 | tf_op jit(solution)/shard_map/ppermute | solution.py:108
  93.4 3.8 %collective-permute-done.4 = f32[128,384]{1,0:T(8,128)S(1)} collective-permute-done((f32[128,384]{1,0:T(8,128)S(1)}, f32[128,384]{1,0:T(8,128)S(1)}, u32[]{:S(2)}, u32[]{:S(2)}) %collective-permute-start.4) | collective-permute-done | bytes 196640 | tf_op jit(solution)/shard_map/ppermute | solution.py:108
  97.5 3.3 %collective-permute-start.14 = (f32[128,384]{1,0:T(8,128)S(1)}, f32[128,384]{1,0:T(8,128)S(1)}, u32[]{:S(2)}, u32[]{:S(2)}) collective-permute-start(f32[128,384]{1,0:T(8,128)S(1)} %bitcast_add_fusion.2), channel_id=1, source_target_pairs={{0,192},{64,0},{128,64},{192,128},{1,193},{65,1},{129,65},{193,129... | collective-permute-start | bytes 589832 | tf_op jit(solution)/shard_map/ppermute | solution.py:108
  100.8 2.4 %collective-permute-start.8 = (f32[128,384]{1,0:T(8,128)S(1)}, f32[128,384]{1,0:T(8,128)S(1)}, u32[]{:S(2)}, u32[]{:S(2)}) collective-permute-start(f32[128,384]{1,0:T(8,128)S(1)} %bitcast_add_fusion.8), channel_id=1, source_target_pairs={{0,192},{64,0},{128,64},{192,128},{1,193},{65,1},{129,65},{193,129... | collective-permute-start | bytes 589832 | tf_op jit(solution)/shard_map/ppermute | solution.py:108
  103.3 1.9 %collective-permute-done.5 = f32[128,384]{1,0:T(8,128)S(1)} collective-permute-done((f32[128,384]{1,0:T(8,128)S(1)}, f32[128,384]{1,0:T(8,128)S(1)}, u32[]{:S(2)}, u32[]{:S(2)}) %collective-permute-start.5) | collective-permute-done | bytes 196640 | tf_op jit(solution)/shard_map/ppermute | solution.py:108
  105.4 3.2 %collective-permute-start.15 = (f32[128,384]{1,0:T(8,128)S(1)}, f32[128,384]{1,0:T(8,128)S(1)}, u32[]{:S(2)}, u32[]{:S(2)}) collective-permute-start(f32[128,384]{1,0:T(8,128)S(1)} %bitcast_add_fusion.1), channel_id=1, source_target_pairs={{0,192},{64,0},{128,64},{192,128},{1,193},{65,1},{129,65},{193,129... | collective-permute-start | bytes 589832 | tf_op jit(solution)/shard_map/ppermute | solution.py:108
  109.5 3.1 %collective-permute-start.9 = (f32[128,384]{1,0:T(8,128)S(1)}, f32[128,384]{1,0:T(8,128)S(1)}, u32[]{:S(2)}, u32[]{:S(2)}) collective-permute-start(f32[128,384]{1,0:T(8,128)S(1)} %bitcast_add_fusion.7), channel_id=1, source_target_pairs={{0,192},{64,0},{128,64},{192,128},{1,193},{65,1},{129,65},{193,129... | collective-permute-start | bytes 589832 | tf_op jit(solution)/shard_map/ppermute | solution.py:108
  112.7 2.4 %collective-permute-done.6 = f32[128,384]{1,0:T(8,128)S(1)} collective-permute-done((f32[128,384]{1,0:T(8,128)S(1)}, f32[128,384]{1,0:T(8,128)S(1)}, u32[]{:S(2)}, u32[]{:S(2)}) %collective-permute-start.6) | collective-permute-done | bytes 196640 | tf_op jit(solution)/shard_map/ppermute | solution.py:108
  115.3 1.7 %collective-permute-done.9 = f32[128,384]{1,0:T(8,128)S(1)} collective-permute-done((f32[128,384]{1,0:T(8,128)S(1)}, f32[128,384]{1,0:T(8,128)S(1)}, u32[]{:S(2)}, u32[]{:S(2)}) %collective-permute-start.9) | collective-permute-done | bytes 196640 | tf_op jit(solution)/shard_map/ppermute | solution.py:108
  (76 shorter events, 13.3 us)
Async XLA Ops:
  3.4 9.9 %copy-start.12 = (f32[6144]{0:T(1024)S(1)}, f32[6144]{0:T(1024)}, u32[]{:S(2)}) copy-start(f32[6144]{0:T(1024)} %param.10) | copy-start | bytes 73732
  4.7 18.5 %all-to-all-start = ((bf16[128,2,384]{2,1,0:T(2,128)(2,1)}), bf16[128,2,384]{2,1,0:T(2,128)(2,1)S(1)}, u32[]{:S(2)}, u32[]{:S(2)}) async-start(bf16[128,2,384]{2,1,0:T(2,128)(2,1)} %copy.33), calls=%async_computation | async-start | bytes 393216 | tf_op jit(solution)/shard_map/all_to_all | solution.py:118
  25.3 46.3 %all-to-all-start.1 = ((bf16[64,8,1536]{2,1,0:T(8,128)(2,1)}), bf16[64,8,1536]{2,1,0:T(8,128)(2,1)S(1)}, u32[]{:S(2)}, u32[]{:S(2)}) async-start(bf16[64,8,1536]{2,1,0:T(8,128)(2,1)} %bitcast.11), calls=%async_computation.1 | async-start | bytes 3145728 | tf_op jit(solution)/shard_map/all_to_all | solution.py:135
  32.1 29.4 %collective-permute-start = (bf16[384,1536]{1,0:T(8,128)(2,1)}, bf16[384,1536]{1,0:T(8,128)(2,1)S(1)}, u32[]{:S(2)}, u32[]{:S(2)}) collective-permute-start(bf16[384,1536]{1,0:T(8,128)(2,1)} %w0_ref.1), channel_id=1, source_target_pairs={{0,48},{16,0},{32,16},{48,32},{1,49},{17,1},{33,17},{49,33},{2,50}... | collective-permute-start | bytes 3538952 | tf_op jit(solution)/shard_map/ppermute | solution.py:35
  33.0 28.7 %collective-permute-start.1 = (bf16[384,1536]{1,0:T(8,128)(2,1)}, bf16[384,1536]{1,0:T(8,128)(2,1)S(1)}, u32[]{:S(2)}, u32[]{:S(2)}) collective-permute-start(bf16[384,1536]{1,0:T(8,128)(2,1)} %w0_ref.1), channel_id=1, source_target_pairs={{0,16},{16,32},{32,48},{48,0},{1,17},{17,33},{33,49},{49,1},{2,18}... | collective-permute-start | bytes 3538952 | tf_op jit(solution)/shard_map/ppermute | solution.py:34
  61.5 17.4 %collective-permute-start.3 = (bf16[384,768]{1,0:T(8,128)(2,1)S(1)}, bf16[384,768]{1,0:T(8,128)(2,1)}, u32[]{:S(2)}, u32[]{:S(2)}) collective-permute-start(bf16[384,768]{1,0:T(8,128)(2,1)S(1)} %slice.19), channel_id=1, source_target_pairs={{0,48},{16,0},{32,16},{48,32},{1,49},{17,1},{33,17},{49,33},{2,50}... | collective-permute-start | bytes 1769480 | tf_op jit(solution)/shard_map/ppermute | solution.py:38
  62.9 16.1 %collective-permute-start.2 = (bf16[384,768]{1,0:T(8,128)(2,1)S(1)}, bf16[384,768]{1,0:T(8,128)(2,1)}, u32[]{:S(2)}, u32[]{:S(2)}) collective-permute-start(bf16[384,768]{1,0:T(8,128)(2,1)S(1)} %slice.18), channel_id=1, source_target_pairs={{0,16},{16,32},{32,48},{48,0},{1,17},{17,33},{33,49},{49,1},{2,18}... | collective-permute-start | bytes 1769480 | tf_op jit(solution)/shard_map/ppermute | solution.py:37
  79.0 8.3 %copy-start.2 = (f32[512,384]{1,0:T(8,128)S(1)}, f32[512,384]{1,0:T(8,128)}, u32[]{:S(2)}) copy-start(f32[512,384]{1,0:T(8,128)} %get-tuple-element.19) | copy-start | bytes 2359300
  83.0 7.3 %copy-start.3 = (f32[512,384]{1,0:T(8,128)S(1)}, f32[512,384]{1,0:T(8,128)}, u32[]{:S(2)}) copy-start(f32[512,384]{1,0:T(8,128)} %get-tuple-element.16) | copy-start | bytes 2359300
  83.0 10.1 %copy-start.8 = (f32[512,384]{1,0:T(8,128)S(1)}, f32[512,384]{1,0:T(8,128)}, u32[]{:S(2)}) copy-start(f32[512,384]{1,0:T(8,128)} %get-tuple-element.18) | copy-start | bytes 2359300
  84.1 9.0 %collective-permute-start.10 = (f32[128,384]{1,0:T(8,128)S(1)}, f32[128,384]{1,0:T(8,128)S(1)}, u32[]{:S(2)}, u32[]{:S(2)}) collective-permute-start(f32[128,384]{1,0:T(8,128)S(1)} %add_bitcast_fusion.1), channel_id=1, source_target_pairs={{0,64},{64,128},{128,192},{192,0},{1,65},{65,129},{129,193},{193,1... | collective-permute-start | bytes 589832 | tf_op jit(solution)/shard_map/ppermute | solution.py:108
  84.9 12.4 %copy-start.7 = (f32[512,384]{1,0:T(8,128)S(1)}, f32[512,384]{1,0:T(8,128)}, u32[]{:S(2)}) copy-start(f32[512,384]{1,0:T(8,128)} %get-tuple-element.14) | copy-start | bytes 2359300
  85.9 11.4 %collective-permute-start.4 = (f32[128,384]{1,0:T(8,128)S(1)}, f32[128,384]{1,0:T(8,128)S(1)}, u32[]{:S(2)}, u32[]{:S(2)}) collective-permute-start(f32[128,384]{1,0:T(8,128)S(1)} %add_bitcast_fusion.3), channel_id=1, source_target_pairs={{0,64},{64,128},{128,192},{192,0},{1,65},{65,129},{129,193},{193,1... | collective-permute-start | bytes 589832 | tf_op jit(solution)/shard_map/ppermute | solution.py:108
  88.2 9.2 %copy-start.5 = (f32[512,384]{1,0:T(8,128)S(1)}, f32[512,384]{1,0:T(8,128)}, u32[]{:S(2)}) copy-start(f32[512,384]{1,0:T(8,128)} %get-tuple-element.20) | copy-start | bytes 2359300
  88.2 9.2 %collective-permute-start.13 = (f32[128,384]{1,0:T(8,128)S(1)}, f32[128,384]{1,0:T(8,128)S(1)}, u32[]{:S(2)}, u32[]{:S(2)}) collective-permute-start(f32[128,384]{1,0:T(8,128)S(1)} %add_bitcast_fusion), channel_id=1, source_target_pairs={{0,192},{64,0},{128,64},{192,128},{1,193},{65,1},{129,65},{193,129... | collective-permute-start | bytes 589832 | tf_op jit(solution)/shard_map/ppermute | solution.py:108
  90.3 10.5 %collective-permute-start.7 = (f32[128,384]{1,0:T(8,128)S(1)}, f32[128,384]{1,0:T(8,128)S(1)}, u32[]{:S(2)}, u32[]{:S(2)}) collective-permute-start(f32[128,384]{1,0:T(8,128)S(1)} %add_bitcast_fusion.2), channel_id=1, source_target_pairs={{0,192},{64,0},{128,64},{192,128},{1,193},{65,1},{129,65},{193,129... | collective-permute-start | bytes 589832 | tf_op jit(solution)/shard_map/ppermute | solution.py:108
  93.2 10.1 %collective-permute-start.11 = (f32[128,384]{1,0:T(8,128)S(1)}, f32[128,384]{1,0:T(8,128)S(1)}, u32[]{:S(2)}, u32[]{:S(2)}) collective-permute-start(f32[128,384]{1,0:T(8,128)S(1)} %bitcast_add_fusion.5), channel_id=1, source_target_pairs={{0,64},{64,128},{128,192},{192,0},{1,65},{65,129},{129,193},{193,1... | collective-permute-start | bytes 589832 | tf_op jit(solution)/shard_map/ppermute | solution.py:108
  97.3 7.9 %collective-permute-start.5 = (f32[128,384]{1,0:T(8,128)S(1)}, f32[128,384]{1,0:T(8,128)S(1)}, u32[]{:S(2)}, u32[]{:S(2)}) collective-permute-start(f32[128,384]{1,0:T(8,128)S(1)} %bitcast_add_fusion.11), channel_id=1, source_target_pairs={{0,64},{64,128},{128,192},{192,0},{1,65},{65,129},{129,193},{193,1... | collective-permute-start | bytes 589832 | tf_op jit(solution)/shard_map/ppermute | solution.py:108
  97.5 7.9 %collective-permute-start.14 = (f32[128,384]{1,0:T(8,128)S(1)}, f32[128,384]{1,0:T(8,128)S(1)}, u32[]{:S(2)}, u32[]{:S(2)}) collective-permute-start(f32[128,384]{1,0:T(8,128)S(1)} %bitcast_add_fusion.2), channel_id=1, source_target_pairs={{0,192},{64,0},{128,64},{192,128},{1,193},{65,1},{129,65},{193,129... | collective-permute-start | bytes 589832 | tf_op jit(solution)/shard_map/ppermute | solution.py:108
  100.8 8.7 %collective-permute-start.8 = (f32[128,384]{1,0:T(8,128)S(1)}, f32[128,384]{1,0:T(8,128)S(1)}, u32[]{:S(2)}, u32[]{:S(2)}) collective-permute-start(f32[128,384]{1,0:T(8,128)S(1)} %bitcast_add_fusion.8), channel_id=1, source_target_pairs={{0,192},{64,0},{128,64},{192,128},{1,193},{65,1},{129,65},{193,129... | collective-permute-start | bytes 589832 | tf_op jit(solution)/shard_map/ppermute | solution.py:108
  103.2 9.4 %collective-permute-start.12 = (f32[128,384]{1,0:T(8,128)S(1)}, f32[128,384]{1,0:T(8,128)S(1)}, u32[]{:S(2)}, u32[]{:S(2)}) collective-permute-start(f32[128,384]{1,0:T(8,128)S(1)} %bitcast_add_fusion.4), channel_id=1, source_target_pairs={{0,64},{64,128},{128,192},{192,0},{1,65},{65,129},{129,193},{193,1... | collective-permute-start | bytes 589832 | tf_op jit(solution)/shard_map/ppermute | solution.py:108
  105.2 9.9 %collective-permute-start.6 = (f32[128,384]{1,0:T(8,128)S(1)}, f32[128,384]{1,0:T(8,128)S(1)}, u32[]{:S(2)}, u32[]{:S(2)}) collective-permute-start(f32[128,384]{1,0:T(8,128)S(1)} %bitcast_add_fusion.10), channel_id=1, source_target_pairs={{0,64},{64,128},{128,192},{192,0},{1,65},{65,129},{129,193},{193,1... | collective-permute-start | bytes 589832 | tf_op jit(solution)/shard_map/ppermute | solution.py:108
  105.4 9.8 %collective-permute-start.15 = (f32[128,384]{1,0:T(8,128)S(1)}, f32[128,384]{1,0:T(8,128)S(1)}, u32[]{:S(2)}, u32[]{:S(2)}) collective-permute-start(f32[128,384]{1,0:T(8,128)S(1)} %bitcast_add_fusion.1), channel_id=1, source_target_pairs={{0,192},{64,0},{128,64},{192,128},{1,193},{65,1},{129,65},{193,129... | collective-permute-start | bytes 589832 | tf_op jit(solution)/shard_map/ppermute | solution.py:108
  109.5 7.5 %collective-permute-start.9 = (f32[128,384]{1,0:T(8,128)S(1)}, f32[128,384]{1,0:T(8,128)S(1)}, u32[]{:S(2)}, u32[]{:S(2)}) collective-permute-start(f32[128,384]{1,0:T(8,128)S(1)} %bitcast_add_fusion.7), channel_id=1, source_target_pairs={{0,192},{64,0},{128,64},{192,128},{1,193},{65,1},{129,65},{193,129... | collective-permute-start | bytes 589832 | tf_op jit(solution)/shard_map/ppermute | solution.py:108
  (7 other events, 24.6 us)

commit v20 on v18

--- a/solution.py
+++ b/solution.py
@@ -114,7 +114,7 @@
 def per_device(q_seq, k_seq, v_seq, resid, ln_gain, w_up, n_x):
     pieces = ring_pieces(w_up, "rx")
     attended = attention_block(q_seq, k_seq, v_seq)
-    both = jnp.stack([resid, attended], axis=1)
+    both = jnp.concatenate([resid, attended], axis=1)
     both = lax.all_to_all(both, "col", split_axis=0, concat_axis=1, tiled=True)
     chunk = both.shape[0]
     both = both.reshape(chunk, -1, 2, resid.shape[1])

time: 119 us -> 118 us (level)
    unnamed x30 -> x29, local copies, waits for them, and re-layouts: 5.48 us -> 5.47 us
where the time goes in v20:
time: 118 us; the launch traced here: 117 us
  waiting for transfers between devices  53.1 us (45%)
  starting transfers between devices  40.6 us (34%)
  Pallas kernels  9.7 us (8%)
  local copies, waits for them, and re-layouts  7.01 us (6%)
  other arithmetic  5.67 us (5%)
    ppermute x1, waiting for transfers between devices, ring_pieces(): from_right = lax.ppermute(block, axis, to_left)  26.1 us
    ppermute x12, starting transfers between devices, ring_reduce_scatter(): got = lax.ppermute(acc, axis, perm)  18.8 us
    ppermute x12, waiting for transfers between devices, ring_reduce_scatter(): got = lax.ppermute(acc, axis, perm)  11.5 us
    all_to_all x1, waiting for transfers between devices, per_device(): both = lax.all_to_all(both, 'col', split_axis=0, concat_axis=1, tiled=True)  9.92 us
    all_to_all x1, starting transfers between devices, per_device(): both = lax.all_to_all(both, 'col', split_axis=0, concat_axis=1, tiled=True)  8.57 us
    all_to_all x1, starting transfers between devices, per_device(): lax.all_to_all(spread_out, ('ry', 'col'), split_axis=0, concat_axis=0, ti...  6.78 us
    pallas_call x1, Pallas kernels, dot_pieces(): pl.pallas_call(near_kernel, grid=(m // tile,), in_specs=[a_spec] + [full(...  5.99 us
    all_to_all x1, waiting for transfers between devices, per_device(): lax.all_to_all(spread_out, ('ry', 'col'), split_axis=0, concat_axis=0, ti...  5.54 us
  transfers between devices with their start and end apart: 18, of which 10 were waited for; matrix products, arithmetic and copies ran while one was open for 2% of the time, Pallas kernels for 5%

profile of v20, /device:TPU:6, one launch (start us, length us, event | category | flops | bytes accessed | tf_op | source)
XLA Modules:
  0.0 116.9 jit_solution(11977798326374491893)
XLA Ops:
  4.6 8.6 %all-to-all-start = ((bf16[16,8,768]{2,1,0:T(8,128)(2,1)}), bf16[16,8,768]{2,1,0:T(8,128)(2,1)S(1)}, u32[]{:S(2)}, u32[]{:S(2)}) async-start(bf16[16,8,768]{2,1,0:T(8,128)(2,1)} %pad_maximum_fusion.1), calls=%async_computation | async-start | bytes 393216 | tf_op jit(solution)/shard_map/all_to_all | solution.py:118
  13.2 9.9 %all-to-all-done = bf16[16,8,768]{2,1,0:T(8,128)(2,1)S(1)} async-done(((bf16[16,8,768]{2,1,0:T(8,128)(2,1)}), bf16[16,8,768]{2,1,0:T(8,128)(2,1)S(1)}, u32[]{:S(2)}, u32[]{:S(2)}) %all-to-all-start) | async-done | bytes 196640 | tf_op jit(solution)/shard_map/all_to_all | solution.py:118
  23.5 1.3 %broadcast_in_dim.16 = bf16[4,16,8,1536]{3,2,1,0:T(8,128)(2,1)} broadcast(bf16[4,8,1536]{2,1,0:T(8,128)(2,1)S(1)} %bitcast.112), dimensions={0,2,3} | broadcast | bytes 1671168 | tf_op jit(solution)/shard_map/broadcast_in_dim | solution.py:133
  24.8 6.8 %all-to-all-start.1 = ((bf16[64,8,1536]{2,1,0:T(8,128)(2,1)}), bf16[64,8,1536]{2,1,0:T(8,128)(2,1)S(1)}, u32[]{:S(2)}, u32[]{:S(2)}) async-start(bf16[64,8,1536]{2,1,0:T(8,128)(2,1)} %bitcast.11), calls=%async_computation.1 | async-start | bytes 3145728 | tf_op jit(solution)/shard_map/all_to_all | solution.py:135
  32.5 2.4 %collective-permute-start.1 = (bf16[384,1536]{1,0:T(8,128)(2,1)}, bf16[384,1536]{1,0:T(8,128)(2,1)S(1)}, u32[]{:S(2)}, u32[]{:S(2)}) collective-permute-start(bf16[384,1536]{1,0:T(8,128)(2,1)} %w0_ref.1), channel_id=1, source_target_pairs={{0,16},{16,32},{32,48},{48,0},{1,17},{17,33},{33,49},{49,1},{2,18}... | collective-permute-start | bytes 3538952 | tf_op jit(solution)/shard_map/ppermute | solution.py:34
  34.9 26.1 %collective-permute-done.w1_ref = bf16[384,1536]{1,0:T(8,128)(2,1)S(1)} collective-permute-done((bf16[384,1536]{1,0:T(8,128)(2,1)}, bf16[384,1536]{1,0:T(8,128)(2,1)S(1)}, u32[]{:S(2)}, u32[]{:S(2)}) %collective-permute-start) | collective-permute-done | bytes 1179680 | tf_op jit(solution)/shard_map/ppermute | solution.py:35
  61.1 1.1 copy-done.10
  62.4 3.1 %collective-permute-start.2 = (bf16[384,768]{1,0:T(8,128)(2,1)S(1)}, bf16[384,768]{1,0:T(8,128)(2,1)}, u32[]{:S(2)}, u32[]{:S(2)}) collective-permute-start(bf16[384,768]{1,0:T(8,128)(2,1)S(1)} %slice.18), channel_id=1, source_target_pairs={{0,16},{16,32},{32,48},{48,0},{1,17},{17,33},{33,49},{49,1},{2,18}... | collective-permute-start | bytes 1769480 | tf_op jit(solution)/shard_map/ppermute | solution.py:37
  65.5 5.5 %all-to-all-done.1 = bf16[64,8,1536]{2,1,0:T(8,128)(2,1)S(1)} async-done(((bf16[64,8,1536]{2,1,0:T(8,128)(2,1)}), bf16[64,8,1536]{2,1,0:T(8,128)(2,1)S(1)}, u32[]{:S(2)}, u32[]{:S(2)}) %all-to-all-start.1) | async-done | bytes 1572896 | tf_op jit(solution)/shard_map/all_to_all | solution.py:135
  71.1 1.2 copy-done
  72.2 6.0 %shard_map.64 = (f32[512,384]{1,0:T(8,128)}, f32[512,384]{1,0:T(8,128)}, f32[512,384]{1,0:T(8,128)}, f32[512,384]{1,0:T(8,128)}) custom-call(bf16[512,1536]{1,0:T(8,128)(2,1)} %bitcast.76, bf16[384,1536]{1,0:T(8,128)(2,1)} %w0_ref.1, bf16[384,1536]{1,0:T(8,128)(2,1)} %copy-done.9, bf16[384,1536]{1,0:T(8,128)(2,1)} %copy-done.10), custom_call_target="tpu_custom_call" | custom-call | flops 1811939328 | bytes 8257536 | tf_op jit(solution)/shard_map/pallas_call | solution.py:74
  78.3 3.7 %shard_map.65 = (f32[512,384]{1,0:T(8,128)}, f32[512,384]{1,0:T(8,128)}, f32[512,384]{1,0:T(8,128)}, f32[512,384]{1,0:T(8,128)}) custom-call(bf16[512,1536]{1,0:T(8,128)(2,1)} %bitcast.77, bf16[384,768]{1,0:T(8,128)(2,1)} %collective-permute-done.2.w2lo_ref, bf16[384,768]{1,0:T(8,128)(2,1)} %collective-permute-done.3.w2hi_ref), custom_call_target="tpu_custom_call" | custom-call | flops 603979776 | bytes 5898240 | tf_op jit(solution)/shard_map/pallas_call | solution.py:84
  84.9 1.6 %collective-permute-start.4 = (f32[128,384]{1,0:T(8,128)S(1)}, f32[128,384]{1,0:T(8,128)S(1)}, u32[]{:S(2)}, u32[]{:S(2)}) collective-permute-start(f32[128,384]{1,0:T(8,128)S(1)} %add_bitcast_fusion.3), channel_id=1, source_target_pairs={{0,64},{64,128},{128,192},{192,0},{1,65},{65,129},{129,193},{193,1... | collective-permute-start | bytes 589832 | tf_op jit(solution)/shard_map/ppermute | solution.py:108
  87.4 1.8 %collective-permute-start.13 = (f32[128,384]{1,0:T(8,128)S(1)}, f32[128,384]{1,0:T(8,128)S(1)}, u32[]{:S(2)}, u32[]{:S(2)}) collective-permute-start(f32[128,384]{1,0:T(8,128)S(1)} %add_bitcast_fusion), channel_id=1, source_target_pairs={{0,192},{64,0},{128,64},{192,128},{1,193},{65,1},{129,65},{193,129... | collective-permute-start | bytes 589832 | tf_op jit(solution)/shard_map/ppermute | solution.py:108
  89.3 1.4 %collective-permute-start.7 = (f32[128,384]{1,0:T(8,128)S(1)}, f32[128,384]{1,0:T(8,128)S(1)}, u32[]{:S(2)}, u32[]{:S(2)}) collective-permute-start(f32[128,384]{1,0:T(8,128)S(1)} %add_bitcast_fusion.2), channel_id=1, source_target_pairs={{0,192},{64,0},{128,64},{192,128},{1,193},{65,1},{129,65},{193,129... | collective-permute-start | bytes 589832 | tf_op jit(solution)/shard_map/ppermute | solution.py:108
  90.7 1.4 %collective-permute-done.10 = f32[128,384]{1,0:T(8,128)S(1)} collective-permute-done((f32[128,384]{1,0:T(8,128)S(1)}, f32[128,384]{1,0:T(8,128)S(1)}, u32[]{:S(2)}, u32[]{:S(2)}) %collective-permute-start.10) | collective-permute-done | bytes 196640 | tf_op jit(solution)/shard_map/ppermute | solution.py:108
  92.2 4.1 %collective-permute-done.4 = f32[128,384]{1,0:T(8,128)S(1)} collective-permute-done((f32[128,384]{1,0:T(8,128)S(1)}, f32[128,384]{1,0:T(8,128)S(1)}, u32[]{:S(2)}, u32[]{:S(2)}) %collective-permute-start.4) | collective-permute-done | bytes 196640 | tf_op jit(solution)/shard_map/ppermute | solution.py:108
  96.5 3.5 %collective-permute-start.14 = (f32[128,384]{1,0:T(8,128)S(1)}, f32[128,384]{1,0:T(8,128)S(1)}, u32[]{:S(2)}, u32[]{:S(2)}) collective-permute-start(f32[128,384]{1,0:T(8,128)S(1)} %bitcast_add_fusion.2), channel_id=1, source_target_pairs={{0,192},{64,0},{128,64},{192,128},{1,193},{65,1},{129,65},{193,129... | collective-permute-start | bytes 589832 | tf_op jit(solution)/shard_map/ppermute | solution.py:108
  100.0 2.2 %collective-permute-start.8 = (f32[128,384]{1,0:T(8,128)S(1)}, f32[128,384]{1,0:T(8,128)S(1)}, u32[]{:S(2)}, u32[]{:S(2)}) collective-permute-start(f32[128,384]{1,0:T(8,128)S(1)} %bitcast_add_fusion.8), channel_id=1, source_target_pairs={{0,192},{64,0},{128,64},{192,128},{1,193},{65,1},{129,65},{193,129... | collective-permute-start | bytes 589832 | tf_op jit(solution)/shard_map/ppermute | solution.py:108
  102.3 1.9 %collective-permute-done.5 = f32[128,384]{1,0:T(8,128)S(1)} collective-permute-done((f32[128,384]{1,0:T(8,128)S(1)}, f32[128,384]{1,0:T(8,128)S(1)}, u32[]{:S(2)}, u32[]{:S(2)}) %collective-permute-start.5) | collective-permute-done | bytes 196640 | tf_op jit(solution)/shard_map/ppermute | solution.py:108
  104.7 3.4 %collective-permute-start.15 = (f32[128,384]{1,0:T(8,128)S(1)}, f32[128,384]{1,0:T(8,128)S(1)}, u32[]{:S(2)}, u32[]{:S(2)}) collective-permute-start(f32[128,384]{1,0:T(8,128)S(1)} %bitcast_add_fusion.1), channel_id=1, source_target_pairs={{0,192},{64,0},{128,64},{192,128},{1,193},{65,1},{129,65},{193,129... | collective-permute-start | bytes 589832 | tf_op jit(solution)/shard_map/ppermute | solution.py:108
  108.5 3.8 %collective-permute-start.9 = (f32[128,384]{1,0:T(8,128)S(1)}, f32[128,384]{1,0:T(8,128)S(1)}, u32[]{:S(2)}, u32[]{:S(2)}) collective-permute-start(f32[128,384]{1,0:T(8,128)S(1)} %bitcast_add_fusion.7), channel_id=1, source_target_pairs={{0,192},{64,0},{128,64},{192,128},{1,193},{65,1},{129,65},{193,129... | collective-permute-start | bytes 589832 | tf_op jit(solution)/shard_map/ppermute | solution.py:108
  112.3 1.8 %collective-permute-done.6 = f32[128,384]{1,0:T(8,128)S(1)} collective-permute-done((f32[128,384]{1,0:T(8,128)S(1)}, f32[128,384]{1,0:T(8,128)S(1)}, u32[]{:S(2)}, u32[]{:S(2)}) %collective-permute-start.6) | collective-permute-done | bytes 196640 | tf_op jit(solution)/shard_map/ppermute | solution.py:108
  114.3 1.8 %collective-permute-done.9 = f32[128,384]{1,0:T(8,128)S(1)} collective-permute-done((f32[128,384]{1,0:T(8,128)S(1)}, f32[128,384]{1,0:T(8,128)S(1)}, u32[]{:S(2)}, u32[]{:S(2)}) %collective-permute-start.9) | collective-permute-done | bytes 196640 | tf_op jit(solution)/shard_map/ppermute | solution.py:108
  (75 shorter events, 12.4 us)
Async XLA Ops:
  2.4 10.8 %copy-start.12 = (f32[6144]{0:T(1024)S(1)}, f32[6144]{0:T(1024)}, u32[]{:S(2)}) copy-start(f32[6144]{0:T(1024)} %param.10) | copy-start | bytes 73732
  4.6 18.5 %all-to-all-start = ((bf16[16,8,768]{2,1,0:T(8,128)(2,1)}), bf16[16,8,768]{2,1,0:T(8,128)(2,1)S(1)}, u32[]{:S(2)}, u32[]{:S(2)}) async-start(bf16[16,8,768]{2,1,0:T(8,128)(2,1)} %pad_maximum_fusion.1), calls=%async_computation | async-start | bytes 393216 | tf_op jit(solution)/shard_map/all_to_all | solution.py:118
  24.8 46.3 %all-to-all-start.1 = ((bf16[64,8,1536]{2,1,0:T(8,128)(2,1)}), bf16[64,8,1536]{2,1,0:T(8,128)(2,1)S(1)}, u32[]{:S(2)}, u32[]{:S(2)}) async-start(bf16[64,8,1536]{2,1,0:T(8,128)(2,1)} %bitcast.11), calls=%async_computation.1 | async-start | bytes 3145728 | tf_op jit(solution)/shard_map/all_to_all | solution.py:135
  31.6 29.4 %collective-permute-start = (bf16[384,1536]{1,0:T(8,128)(2,1)}, bf16[384,1536]{1,0:T(8,128)(2,1)S(1)}, u32[]{:S(2)}, u32[]{:S(2)}) collective-permute-start(bf16[384,1536]{1,0:T(8,128)(2,1)} %w0_ref.1), channel_id=1, source_target_pairs={{0,48},{16,0},{32,16},{48,32},{1,49},{17,1},{33,17},{49,33},{2,50}... | collective-permute-start | bytes 3538952 | tf_op jit(solution)/shard_map/ppermute | solution.py:35
  32.5 28.7 %collective-permute-start.1 = (bf16[384,1536]{1,0:T(8,128)(2,1)}, bf16[384,1536]{1,0:T(8,128)(2,1)S(1)}, u32[]{:S(2)}, u32[]{:S(2)}) collective-permute-start(bf16[384,1536]{1,0:T(8,128)(2,1)} %w0_ref.1), channel_id=1, source_target_pairs={{0,16},{16,32},{32,48},{48,0},{1,17},{17,33},{33,49},{49,1},{2,18}... | collective-permute-start | bytes 3538952 | tf_op jit(solution)/shard_map/ppermute | solution.py:34
  61.0 17.2 %collective-permute-start.3 = (bf16[384,768]{1,0:T(8,128)(2,1)S(1)}, bf16[384,768]{1,0:T(8,128)(2,1)}, u32[]{:S(2)}, u32[]{:S(2)}) collective-permute-start(bf16[384,768]{1,0:T(8,128)(2,1)S(1)} %slice.19), channel_id=1, source_target_pairs={{0,48},{16,0},{32,16},{48,32},{1,49},{17,1},{33,17},{49,33},{2,50}... | collective-permute-start | bytes 1769480 | tf_op jit(solution)/shard_map/ppermute | solution.py:38
  62.4 15.8 %collective-permute-start.2 = (bf16[384,768]{1,0:T(8,128)(2,1)S(1)}, bf16[384,768]{1,0:T(8,128)(2,1)}, u32[]{:S(2)}, u32[]{:S(2)}) collective-permute-start(bf16[384,768]{1,0:T(8,128)(2,1)S(1)} %slice.18), channel_id=1, source_target_pairs={{0,16},{16,32},{32,48},{48,0},{1,17},{17,33},{33,49},{49,1},{2,18}... | collective-permute-start | bytes 1769480 | tf_op jit(solution)/shard_map/ppermute | solution.py:37
  78.2 8.2 %copy-start.2 = (f32[512,384]{1,0:T(8,128)S(1)}, f32[512,384]{1,0:T(8,128)}, u32[]{:S(2)}) copy-start(f32[512,384]{1,0:T(8,128)} %get-tuple-element.19) | copy-start | bytes 2359300
  82.0 7.3 %copy-start.3 = (f32[512,384]{1,0:T(8,128)S(1)}, f32[512,384]{1,0:T(8,128)}, u32[]{:S(2)}) copy-start(f32[512,384]{1,0:T(8,128)} %get-tuple-element.16) | copy-start | bytes 2359300
  82.0 10.1 %copy-start.8 = (f32[512,384]{1,0:T(8,128)S(1)}, f32[512,384]{1,0:T(8,128)}, u32[]{:S(2)}) copy-start(f32[512,384]{1,0:T(8,128)} %get-tuple-element.18) | copy-start | bytes 2359300
  83.1 9.0 %collective-permute-start.10 = (f32[128,384]{1,0:T(8,128)S(1)}, f32[128,384]{1,0:T(8,128)S(1)}, u32[]{:S(2)}, u32[]{:S(2)}) collective-permute-start(f32[128,384]{1,0:T(8,128)S(1)} %add_bitcast_fusion.1), channel_id=1, source_target_pairs={{0,64},{64,128},{128,192},{192,0},{1,65},{65,129},{129,193},{193,1... | collective-permute-start | bytes 589832 | tf_op jit(solution)/shard_map/ppermute | solution.py:108
  83.9 12.4 %copy-start.7 = (f32[512,384]{1,0:T(8,128)S(1)}, f32[512,384]{1,0:T(8,128)}, u32[]{:S(2)}) copy-start(f32[512,384]{1,0:T(8,128)} %get-tuple-element.14) | copy-start | bytes 2359300
  84.9 11.4 %collective-permute-start.4 = (f32[128,384]{1,0:T(8,128)S(1)}, f32[128,384]{1,0:T(8,128)S(1)}, u32[]{:S(2)}, u32[]{:S(2)}) collective-permute-start(f32[128,384]{1,0:T(8,128)S(1)} %add_bitcast_fusion.3), channel_id=1, source_target_pairs={{0,64},{64,128},{128,192},{192,0},{1,65},{65,129},{129,193},{193,1... | collective-permute-start | bytes 589832 | tf_op jit(solution)/shard_map/ppermute | solution.py:108
  87.4 9.0 %copy-start.5 = (f32[512,384]{1,0:T(8,128)S(1)}, f32[512,384]{1,0:T(8,128)}, u32[]{:S(2)}) copy-start(f32[512,384]{1,0:T(8,128)} %get-tuple-element.20) | copy-start | bytes 2359300
  87.4 9.0 %collective-permute-start.13 = (f32[128,384]{1,0:T(8,128)S(1)}, f32[128,384]{1,0:T(8,128)S(1)}, u32[]{:S(2)}, u32[]{:S(2)}) collective-permute-start(f32[128,384]{1,0:T(8,128)S(1)} %add_bitcast_fusion), channel_id=1, source_target_pairs={{0,192},{64,0},{128,64},{192,128},{1,193},{65,1},{129,65},{193,129... | collective-permute-start | bytes 589832 | tf_op jit(solution)/shard_map/ppermute | solution.py:108
  89.3 10.7 %collective-permute-start.7 = (f32[128,384]{1,0:T(8,128)S(1)}, f32[128,384]{1,0:T(8,128)S(1)}, u32[]{:S(2)}, u32[]{:S(2)}) collective-permute-start(f32[128,384]{1,0:T(8,128)S(1)} %add_bitcast_fusion.2), channel_id=1, source_target_pairs={{0,192},{64,0},{128,64},{192,128},{1,193},{65,1},{129,65},{193,129... | collective-permute-start | bytes 589832 | tf_op jit(solution)/shard_map/ppermute | solution.py:108
  92.2 10.1 %collective-permute-start.11 = (f32[128,384]{1,0:T(8,128)S(1)}, f32[128,384]{1,0:T(8,128)S(1)}, u32[]{:S(2)}, u32[]{:S(2)}) collective-permute-start(f32[128,384]{1,0:T(8,128)S(1)} %bitcast_add_fusion.5), channel_id=1, source_target_pairs={{0,64},{64,128},{128,192},{192,0},{1,65},{65,129},{129,193},{193,1... | collective-permute-start | bytes 589832 | tf_op jit(solution)/shard_map/ppermute | solution.py:108
  96.4 7.8 %collective-permute-start.5 = (f32[128,384]{1,0:T(8,128)S(1)}, f32[128,384]{1,0:T(8,128)S(1)}, u32[]{:S(2)}, u32[]{:S(2)}) collective-permute-start(f32[128,384]{1,0:T(8,128)S(1)} %bitcast_add_fusion.11), channel_id=1, source_target_pairs={{0,64},{64,128},{128,192},{192,0},{1,65},{65,129},{129,193},{193,1... | collective-permute-start | bytes 589832 | tf_op jit(solution)/shard_map/ppermute | solution.py:108
  96.5 8.1 %collective-permute-start.14 = (f32[128,384]{1,0:T(8,128)S(1)}, f32[128,384]{1,0:T(8,128)S(1)}, u32[]{:S(2)}, u32[]{:S(2)}) collective-permute-start(f32[128,384]{1,0:T(8,128)S(1)} %bitcast_add_fusion.2), channel_id=1, source_target_pairs={{0,192},{64,0},{128,64},{192,128},{1,193},{65,1},{129,65},{193,129... | collective-permute-start | bytes 589832 | tf_op jit(solution)/shard_map/ppermute | solution.py:108
  100.0 8.4 %collective-permute-start.8 = (f32[128,384]{1,0:T(8,128)S(1)}, f32[128,384]{1,0:T(8,128)S(1)}, u32[]{:S(2)}, u32[]{:S(2)}) collective-permute-start(f32[128,384]{1,0:T(8,128)S(1)} %bitcast_add_fusion.8), channel_id=1, source_target_pairs={{0,192},{64,0},{128,64},{192,128},{1,193},{65,1},{129,65},{193,129... | collective-permute-start | bytes 589832 | tf_op jit(solution)/shard_map/ppermute | solution.py:108
  102.2 10.0 %collective-permute-start.12 = (f32[128,384]{1,0:T(8,128)S(1)}, f32[128,384]{1,0:T(8,128)S(1)}, u32[]{:S(2)}, u32[]{:S(2)}) collective-permute-start(f32[128,384]{1,0:T(8,128)S(1)} %bitcast_add_fusion.4), channel_id=1, source_target_pairs={{0,64},{64,128},{128,192},{192,0},{1,65},{65,129},{129,193},{193,1... | collective-permute-start | bytes 589832 | tf_op jit(solution)/shard_map/ppermute | solution.py:108
  104.2 9.9 %collective-permute-start.6 = (f32[128,384]{1,0:T(8,128)S(1)}, f32[128,384]{1,0:T(8,128)S(1)}, u32[]{:S(2)}, u32[]{:S(2)}) collective-permute-start(f32[128,384]{1,0:T(8,128)S(1)} %bitcast_add_fusion.10), channel_id=1, source_target_pairs={{0,64},{64,128},{128,192},{192,0},{1,65},{65,129},{129,193},{193,1... | collective-permute-start | bytes 589832 | tf_op jit(solution)/shard_map/ppermute | solution.py:108
  104.7 9.5 %collective-permute-start.15 = (f32[128,384]{1,0:T(8,128)S(1)}, f32[128,384]{1,0:T(8,128)S(1)}, u32[]{:S(2)}, u32[]{:S(2)}) collective-permute-start(f32[128,384]{1,0:T(8,128)S(1)} %bitcast_add_fusion.1), channel_id=1, source_target_pairs={{0,192},{64,0},{128,64},{192,128},{1,193},{65,1},{129,65},{193,129... | collective-permute-start | bytes 589832 | tf_op jit(solution)/shard_map/ppermute | solution.py:108
  108.5 7.6 %collective-permute-start.9 = (f32[128,384]{1,0:T(8,128)S(1)}, f32[128,384]{1,0:T(8,128)S(1)}, u32[]{:S(2)}, u32[]{:S(2)}) collective-permute-start(f32[128,384]{1,0:T(8,128)S(1)} %bitcast_add_fusion.7), channel_id=1, source_target_pairs={{0,192},{64,0},{128,64},{192,128},{1,193},{65,1},{129,65},{193,129... | collective-permute-start | bytes 589832 | tf_op jit(solution)/shard_map/ppermute | solution.py:108
  (7 other events, 23.3 us)

commit v21 on v20

--- a/solution.py
+++ b/solution.py
@@ -50,16 +50,12 @@
         o_ref[...] = base[:, q * quarter:(q + 1) * quarter]
 
 
-def far_kernel(a_ref, w2lo_ref, w2hi_ref, *o_refs):
-    k = w2lo_ref.shape[0]
+def far_kernel(a_ref, w2_ref, *o_refs):
+    k = w2_ref.shape[0]
     quarter = o_refs[0].shape[1]
-    far = a_ref[:, 2 * k:3 * k]
-    low = jnp.dot(far, w2lo_ref[...], preferred_element_type=jnp.float32)
-    high = jnp.dot(far, w2hi_ref[...], preferred_element_type=jnp.float32)
+    product = jnp.dot(a_ref[:, 2 * k:3 * k], w2_ref[...], preferred_element_type=jnp.float32)
     for q, o_ref in enumerate(o_refs):
-        source = low if q < 2 else high
-        start = (q % 2) * quarter
-        o_ref[...] = source[:, start:start + quarter]
+        o_ref[...] = product[:, q * quarter:(q + 1) * quarter]
 
 
 def dot_pieces(a, pieces, tile=256):
@@ -81,16 +77,18 @@
             flops=2 * m * 3 * own.size, transcendentals=0, bytes_accessed=a.size * 2 + 3 * own.size * 2 + m * n * 4
         ),
     )(a, *near_w)
-    far_quarters = pl.pallas_call(
-        far_kernel,
-        grid=(m // tile,),
-        in_specs=[a_spec, full(far_low), full(far_high)],
-        out_specs=(spec,) * 4,
-        out_shape=(shape,) * 4,
-        cost_estimate=pl.CostEstimate(
-            flops=2 * m * own.size, transcendentals=0, bytes_accessed=a.size * 2 + own.size * 2 + m * n * 4
-        ),
-    )(a, far_low, far_high)
+    far_quarters = ()
+    for far_half in (far_low, far_high):
+        far_quarters += pl.pallas_call(
+            far_kernel,
+            grid=(m // tile,),
+            in_specs=[a_spec, full(far_half)],
+            out_specs=(spec,) * 2,
+            out_shape=(shape,) * 2,
+            cost_estimate=pl.CostEstimate(
+                flops=2 * m * far_half.size, transcendentals=0, bytes_accessed=a.size * 2 + far_half.size * 2 + m * n * 2
+            ),
+        )(a, far_half)
     return quarters, far_quarters
 
 

time: 118 us -> 125 us (1.059)
  the two profiles are of different devices: /device:TPU:6 before, /device:TPU:24 now
where the time goes in v21:
time: 125 us; the launch traced here: 124 us
  waiting for transfers between devices  56 us (45%)
  starting transfers between devices  39.3 us (31%)
  Pallas kernels  12 us (10%)
  other arithmetic  8.19 us (7%)
  local copies, waits for them, and re-layouts  7.83 us (6%)
    ppermute x1, waiting for transfers between devices, ring_pieces(): from_left = lax.ppermute(block, axis, to_right)  26.2 us
    ppermute x12, starting transfers between devices, ring_reduce_scatter(): got = lax.ppermute(acc, axis, perm)  17.4 us
    ppermute x1, waiting for transfers between devices, ring_pieces(): far_low = lax.ppermute(from_left[:, :half], axis, to_right)  10.6 us
    all_to_all x1, waiting for transfers between devices, per_device(): both = lax.all_to_all(both, 'col', split_axis=0, concat_axis=1, tiled=True)  9.92 us
    ppermute x12, waiting for transfers between devices, ring_reduce_scatter(): got = lax.ppermute(acc, axis, perm)  9.24 us
    all_to_all x1, starting transfers between devices, per_device(): both = lax.all_to_all(both, 'col', split_axis=0, concat_axis=1, tiled=True)  8.57 us
    all_to_all x1, starting transfers between devices, per_device(): lax.all_to_all(spread_out, ('ry', 'col'), split_axis=0, concat_axis=0, ti...  6.75 us
    pallas_call x1, Pallas kernels, dot_pieces(): pl.pallas_call(near_kernel, grid=(m // tile,), in_specs=[a_spec] + [full(...  6.12 us
  transfers between devices with their start and end apart: 18, of which 13 were waited for; matrix products, arithmetic and copies ran while one was open for 6% of the time, Pallas kernels for 10%

profile of v21, /device:TPU:24, one launch (start us, length us, event | category | flops | bytes accessed | tf_op | source)
XLA Modules:
  0.0 124.1 jit_solution(7798843731131191692)
XLA Ops:
  1.0 1.0 copy.12
  4.6 8.6 %all-to-all-start = ((bf16[16,8,768]{2,1,0:T(8,128)(2,1)}), bf16[16,8,768]{2,1,0:T(8,128)(2,1)S(1)}, u32[]{:S(2)}, u32[]{:S(2)}) async-start(bf16[16,8,768]{2,1,0:T(8,128)(2,1)} %pad_maximum_fusion.1), calls=%async_computation | async-start | bytes 393216 | tf_op jit(solution)/shard_map/all_to_all | solution.py:116
  13.2 9.9 %all-to-all-done = bf16[16,8,768]{2,1,0:T(8,128)(2,1)S(1)} async-done(((bf16[16,8,768]{2,1,0:T(8,128)(2,1)}), bf16[16,8,768]{2,1,0:T(8,128)(2,1)S(1)}, u32[]{:S(2)}, u32[]{:S(2)}) %all-to-all-start) | async-done | bytes 196640 | tf_op jit(solution)/shard_map/all_to_all | solution.py:116
  23.5 1.3 %broadcast_in_dim.16 = bf16[4,16,8,1536]{3,2,1,0:T(8,128)(2,1)} broadcast(bf16[4,8,1536]{2,1,0:T(8,128)(2,1)S(1)} %bitcast.113), dimensions={0,2,3} | broadcast | bytes 1671168 | tf_op jit(solution)/shard_map/broadcast_in_dim | solution.py:131
  24.8 6.8 %all-to-all-start.1 = ((bf16[64,8,1536]{2,1,0:T(8,128)(2,1)}), bf16[64,8,1536]{2,1,0:T(8,128)(2,1)S(1)}, u32[]{:S(2)}, u32[]{:S(2)}) async-start(bf16[64,8,1536]{2,1,0:T(8,128)(2,1)} %bitcast.11), calls=%async_computation.1 | async-start | bytes 3145728 | tf_op jit(solution)/shard_map/all_to_all | solution.py:133
  31.5 1.6 %collective-permute-start.1 = (bf16[384,1536]{1,0:T(8,128)(2,1)}, bf16[384,1536]{1,0:T(8,128)(2,1)S(1)}, u32[]{:S(2)}, u32[]{:S(2)}) collective-permute-start(bf16[384,1536]{1,0:T(8,128)(2,1)} %w0_ref.1), channel_id=1, source_target_pairs={{0,16},{16,32},{32,48},{48,0},{1,17},{17,33},{33,49},{49,1},{2,18}... | collective-permute-start | bytes 3538952 | tf_op jit(solution)/shard_map/ppermute | solution.py:34
  33.1 1.7 %collective-permute-start = (bf16[384,1536]{1,0:T(8,128)(2,1)}, bf16[384,1536]{1,0:T(8,128)(2,1)S(1)}, u32[]{:S(2)}, u32[]{:S(2)}) collective-permute-start(bf16[384,1536]{1,0:T(8,128)(2,1)} %w0_ref.1), channel_id=1, source_target_pairs={{0,48},{16,0},{32,16},{48,32},{1,49},{17,1},{33,17},{49,33},{2,50}... | collective-permute-start | bytes 3538952 | tf_op jit(solution)/shard_map/ppermute | solution.py:35
  34.8 26.2 %collective-permute-done.1.w3_ref = bf16[384,1536]{1,0:T(8,128)(2,1)S(1)} collective-permute-done((bf16[384,1536]{1,0:T(8,128)(2,1)}, bf16[384,1536]{1,0:T(8,128)(2,1)S(1)}, u32[]{:S(2)}, u32[]{:S(2)}) %collective-permute-start.1) | collective-permute-done | bytes 1179680 | tf_op jit(solution)/shard_map/ppermute | solution.py:34
  63.4 3.0 %collective-permute-start.9 = (bf16[384,768]{1,0:T(8,128)(2,1)}, bf16[384,768]{1,0:T(8,128)(2,1)}, u32[]{:S(2)}, u32[]{:S(2)}) collective-permute-start(bf16[384,768]{1,0:T(8,128)(2,1)} %slice.19), channel_id=1, source_target_pairs={{0,48},{16,0},{32,16},{48,32},{1,49},{17,1},{33,17},{49,33},{2,50}... | collective-permute-start | bytes 1769480 | tf_op jit(solution)/shard_map/ppermute | solution.py:38
  66.3 10.6 %collective-permute-done.2.w2_ref = bf16[384,768]{1,0:T(8,128)(2,1)S(1)} collective-permute-done((bf16[384,768]{1,0:T(8,128)(2,1)S(1)}, bf16[384,768]{1,0:T(8,128)(2,1)S(1)}, u32[]{:S(2)}, u32[]{:S(2)}) %collective-permute-start.2) | collective-permute-done | bytes 589856 | tf_op jit(solution)/shard_map/ppermute | solution.py:37
  78.3 2.9 %shard_map.65 = (f32[512,384]{1,0:T(8,128)}, f32[512,384]{1,0:T(8,128)}) custom-call(bf16[512,1536]{1,0:T(8,128)(2,1)} %bitcast.76, bf16[384,768]{1,0:T(8,128)(2,1)} %copy-done.9), custom_call_target="tpu_custom_call" | custom-call | flops 301989888 | bytes 3735552 | tf_op jit(solution)/shard_map/pallas_call | solution.py:82
  81.2 6.1 %shard_map.64 = (f32[512,384]{1,0:T(8,128)}, f32[512,384]{1,0:T(8,128)}, f32[512,384]{1,0:T(8,128)}, f32[512,384]{1,0:T(8,128)}) custom-call(bf16[512,1536]{1,0:T(8,128)(2,1)} %bitcast.77, bf16[384,1536]{1,0:T(8,128)(2,1)} %w0_ref.1, bf16[384,1536]{1,0:T(8,128)(2,1)} %copy-done.11, bf16[384,1536]{1,0:T(8,128)(2,1)} %copy-done.10), custom_call_target="tpu_custom_call" | custom-call | flops 1811939328 | bytes 8257536 | tf_op jit(solution)/shard_map/pallas_call | solution.py:70
  87.3 1.6 %add_bitcast_fusion.3 = f32[128,384]{1,0:T(8,128)} fusion(f32[4,128,384]{2,1,0:T(8,128)S(1)} %bitcast.97, s32[]{:T(128)S(6)} %select_n.110, f32[4,128,384]{2,1,0:T(8,128)} %bitcast.105), kind=kLoop, calls=%fused_computation.66 | loop fusion | flops 49152 | bytes 589828 | tf_op jit(solution)/shard_map/add | solution.py:101
  90.0 2.1 %collective-permute-start.6 = (f32[128,384]{1,0:T(8,128)S(1)}, f32[128,384]{1,0:T(8,128)S(1)}, u32[]{:S(2)}, u32[]{:S(2)}) collective-permute-start(f32[128,384]{1,0:T(8,128)S(1)} %add_bitcast_fusion.2), channel_id=1, source_target_pairs={{0,192},{64,0},{128,64},{192,128},{1,193},{65,1},{129,65},{193,129... | collective-permute-start | bytes 589832 | tf_op jit(solution)/shard_map/ppermute | solution.py:106
  92.1 2.9 %shard_map.66 = (f32[512,384]{1,0:T(8,128)}, f32[512,384]{1,0:T(8,128)}) custom-call(bf16[512,1536]{1,0:T(8,128)(2,1)} %bitcast.78, bf16[384,768]{1,0:T(8,128)(2,1)} %collective-permute-done.9.w2_ref), custom_call_target="tpu_custom_call" | custom-call | flops 301989888 | bytes 3735552 | tf_op jit(solution)/shard_map/pallas_call | solution.py:82
  96.0 1.3 %collective-permute-start.10 = (f32[128,384]{1,0:T(8,128)S(1)}, f32[128,384]{1,0:T(8,128)S(1)}, u32[]{:S(2)}, u32[]{:S(2)}) collective-permute-start(f32[128,384]{1,0:T(8,128)S(1)} %add_bitcast_fusion.1), channel_id=1, source_target_pairs={{0,64},{64,128},{128,192},{192,0},{1,65},{65,129},{129,193},{193,1... | collective-permute-start | bytes 589832 | tf_op jit(solution)/shard_map/ppermute | solution.py:106
  99.2 1.1 bitcast_add_fusion.11
  100.3 2.6 %collective-permute-start.4 = (f32[128,384]{1,0:T(8,128)S(1)}, f32[128,384]{1,0:T(8,128)S(1)}, u32[]{:S(2)}, u32[]{:S(2)}) collective-permute-start(f32[128,384]{1,0:T(8,128)S(1)} %bitcast_add_fusion.11), channel_id=1, source_target_pairs={{0,64},{64,128},{128,192},{192,0},{1,65},{65,129},{129,193},{193,1... | collective-permute-start | bytes 589832 | tf_op jit(solution)/shard_map/ppermute | solution.py:106
  103.5 3.0 %collective-permute-start.11 = (f32[128,384]{1,0:T(8,128)S(1)}, f32[128,384]{1,0:T(8,128)S(1)}, u32[]{:S(2)}, u32[]{:S(2)}) collective-permute-start(f32[128,384]{1,0:T(8,128)S(1)} %bitcast_add_fusion.5), channel_id=1, source_target_pairs={{0,64},{64,128},{128,192},{192,0},{1,65},{65,129},{129,193},{193,1... | collective-permute-start | bytes 589832 | tf_op jit(solution)/shard_map/ppermute | solution.py:106
  106.8 1.4 %collective-permute-done.4 = f32[128,384]{1,0:T(8,128)S(1)} collective-permute-done((f32[128,384]{1,0:T(8,128)S(1)}, f32[128,384]{1,0:T(8,128)S(1)}, u32[]{:S(2)}, u32[]{:S(2)}) %collective-permute-start.4) | collective-permute-done | bytes 196640 | tf_op jit(solution)/shard_map/ppermute | solution.py:106
  108.2 3.6 %collective-permute-start.5 = (f32[128,384]{1,0:T(8,128)S(1)}, f32[128,384]{1,0:T(8,128)S(1)}, u32[]{:S(2)}, u32[]{:S(2)}) collective-permute-start(f32[128,384]{1,0:T(8,128)S(1)} %bitcast_add_fusion.10), channel_id=1, source_target_pairs={{0,64},{64,128},{128,192},{192,0},{1,65},{65,129},{129,193},{193,1... | collective-permute-start | bytes 589832 | tf_op jit(solution)/shard_map/ppermute | solution.py:106
  112.4 3.6 %collective-permute-start.12 = (f32[128,384]{1,0:T(8,128)S(1)}, f32[128,384]{1,0:T(8,128)S(1)}, u32[]{:S(2)}, u32[]{:S(2)}) collective-permute-start(f32[128,384]{1,0:T(8,128)S(1)} %bitcast_add_fusion.4), channel_id=1, source_target_pairs={{0,64},{64,128},{128,192},{192,0},{1,65},{65,129},{129,193},{193,1... | collective-permute-start | bytes 589832 | tf_op jit(solution)/shard_map/ppermute | solution.py:106
  116.6 2.6 %collective-permute-done.12 = f32[128,384]{1,0:T(8,128)S(1)} collective-permute-done((f32[128,384]{1,0:T(8,128)S(1)}, f32[128,384]{1,0:T(8,128)S(1)}, u32[]{:S(2)}, u32[]{:S(2)}) %collective-permute-start.12) | collective-permute-done | bytes 196640 | tf_op jit(solution)/shard_map/ppermute | solution.py:106
  120.1 3.0 %collective-permute-done.15 = f32[128,384]{1,0:T(8,128)S(1)} collective-permute-done((f32[128,384]{1,0:T(8,128)S(1)}, f32[128,384]{1,0:T(8,128)S(1)}, u32[]{:S(2)}, u32[]{:S(2)}) %collective-permute-start.15) | collective-permute-done | bytes 196640 | tf_op jit(solution)/shard_map/ppermute | solution.py:106
  (78 shorter events, 15.4 us)
Async XLA Ops:
  2.4 10.8 %copy-start.13 = (f32[6144]{0:T(1024)S(1)}, f32[6144]{0:T(1024)}, u32[]{:S(2)}) copy-start(f32[6144]{0:T(1024)} %param.10) | copy-start | bytes 73732
  4.6 18.5 %all-to-all-start = ((bf16[16,8,768]{2,1,0:T(8,128)(2,1)}), bf16[16,8,768]{2,1,0:T(8,128)(2,1)S(1)}, u32[]{:S(2)}, u32[]{:S(2)}) async-start(bf16[16,8,768]{2,1,0:T(8,128)(2,1)} %pad_maximum_fusion.1), calls=%async_computation | async-start | bytes 393216 | tf_op jit(solution)/shard_map/all_to_all | solution.py:116
  24.8 52.2 %all-to-all-start.1 = ((bf16[64,8,1536]{2,1,0:T(8,128)(2,1)}), bf16[64,8,1536]{2,1,0:T(8,128)(2,1)S(1)}, u32[]{:S(2)}, u32[]{:S(2)}) async-start(bf16[64,8,1536]{2,1,0:T(8,128)(2,1)} %bitcast.11), calls=%async_computation.1 | async-start | bytes 3145728 | tf_op jit(solution)/shard_map/all_to_all | solution.py:133
  31.5 29.5 %collective-permute-start.1 = (bf16[384,1536]{1,0:T(8,128)(2,1)}, bf16[384,1536]{1,0:T(8,128)(2,1)S(1)}, u32[]{:S(2)}, u32[]{:S(2)}) collective-permute-start(bf16[384,1536]{1,0:T(8,128)(2,1)} %w0_ref.1), channel_id=1, source_target_pairs={{0,16},{16,32},{32,48},{48,0},{1,17},{17,33},{33,49},{49,1},{2,18}... | collective-permute-start | bytes 3538952 | tf_op jit(solution)/shard_map/ppermute | solution.py:34
  33.1 28.4 %collective-permute-start = (bf16[384,1536]{1,0:T(8,128)(2,1)}, bf16[384,1536]{1,0:T(8,128)(2,1)S(1)}, u32[]{:S(2)}, u32[]{:S(2)}) collective-permute-start(bf16[384,1536]{1,0:T(8,128)(2,1)} %w0_ref.1), channel_id=1, source_target_pairs={{0,48},{16,0},{32,16},{48,32},{1,49},{17,1},{33,17},{49,33},{2,50}... | collective-permute-start | bytes 3538952 | tf_op jit(solution)/shard_map/ppermute | solution.py:35
  61.1 15.8 %collective-permute-start.2 = (bf16[384,768]{1,0:T(8,128)(2,1)S(1)}, bf16[384,768]{1,0:T(8,128)(2,1)S(1)}, u32[]{:S(2)}, u32[]{:S(2)}) collective-permute-start(bf16[384,768]{1,0:T(8,128)(2,1)S(1)} %slice.18), channel_id=1, source_target_pairs={{0,16},{16,32},{32,48},{48,0},{1,17},{17,33},{33,49},{49,1},{2,18}... | collective-permute-start | bytes 1769480 | tf_op jit(solution)/shard_map/ppermute | solution.py:37
  63.4 28.7 %collective-permute-start.9 = (bf16[384,768]{1,0:T(8,128)(2,1)}, bf16[384,768]{1,0:T(8,128)(2,1)}, u32[]{:S(2)}, u32[]{:S(2)}) collective-permute-start(bf16[384,768]{1,0:T(8,128)(2,1)} %slice.19), channel_id=1, source_target_pairs={{0,48},{16,0},{32,16},{48,32},{1,49},{17,1},{33,17},{49,33},{2,50}... | collective-permute-start | bytes 1769480 | tf_op jit(solution)/shard_map/ppermute | solution.py:38
  81.2 7.8 %copy-start.2 = (f32[512,384]{1,0:T(8,128)S(1)}, f32[512,384]{1,0:T(8,128)}, u32[]{:S(2)}) copy-start(f32[512,384]{1,0:T(8,128)} %get-tuple-element.16) | copy-start | bytes 2359300
  89.0 10.2 %collective-permute-start.3 = (f32[128,384]{1,0:T(8,128)}, f32[128,384]{1,0:T(8,128)}, u32[]{:S(2)}, u32[]{:S(2)}) collective-permute-start(f32[128,384]{1,0:T(8,128)} %add_bitcast_fusion.3), channel_id=1, source_target_pairs={{0,64},{64,128},{128,192},{192,0},{1,65},{65,129},{129,193},{193,1... | collective-permute-start | bytes 589832 | tf_op jit(solution)/shard_map/ppermute | solution.py:106
  90.0 12.8 %collective-permute-start.6 = (f32[128,384]{1,0:T(8,128)S(1)}, f32[128,384]{1,0:T(8,128)S(1)}, u32[]{:S(2)}, u32[]{:S(2)}) collective-permute-start(f32[128,384]{1,0:T(8,128)S(1)} %add_bitcast_fusion.2), channel_id=1, source_target_pairs={{0,192},{64,0},{128,64},{192,128},{1,193},{65,1},{129,65},{193,129... | collective-permute-start | bytes 589832 | tf_op jit(solution)/shard_map/ppermute | solution.py:106
  95.0 7.8 %copy-start.3 = (f32[512,384]{1,0:T(8,128)S(1)}, f32[512,384]{1,0:T(8,128)}, u32[]{:S(2)}) copy-start(f32[512,384]{1,0:T(8,128)} %get-tuple-element.15) | copy-start | bytes 2359300
  96.0 7.4 %copy-start.8 = (f32[512,384]{1,0:T(8,128)S(1)}, f32[512,384]{1,0:T(8,128)}, u32[]{:S(2)}) copy-start(f32[512,384]{1,0:T(8,128)} %get-tuple-element.18) | copy-start | bytes 2359300
  96.0 7.4 %collective-permute-start.10 = (f32[128,384]{1,0:T(8,128)S(1)}, f32[128,384]{1,0:T(8,128)S(1)}, u32[]{:S(2)}, u32[]{:S(2)}) collective-permute-start(f32[128,384]{1,0:T(8,128)S(1)} %add_bitcast_fusion.1), channel_id=1, source_target_pairs={{0,64},{64,128},{128,192},{192,0},{1,65},{65,129},{129,193},{193,1... | collective-permute-start | bytes 589832 | tf_op jit(solution)/shard_map/ppermute | solution.py:106
  98.3 8.3 %copy-start.6 = (f32[512,384]{1,0:T(8,128)S(1)}, f32[512,384]{1,0:T(8,128)}, u32[]{:S(2)}) copy-start(f32[512,384]{1,0:T(8,128)} %get-tuple-element.20) | copy-start | bytes 2359300
  98.3 8.3 %collective-permute-start.13 = (f32[128,384]{1,0:T(8,128)S(1)}, f32[128,384]{1,0:T(8,128)S(1)}, u32[]{:S(2)}, u32[]{:S(2)}) collective-permute-start(f32[128,384]{1,0:T(8,128)S(1)} %add_bitcast_fusion), channel_id=1, source_target_pairs={{0,192},{64,0},{128,64},{192,128},{1,193},{65,1},{129,65},{193,129... | collective-permute-start | bytes 589832 | tf_op jit(solution)/shard_map/ppermute | solution.py:106
  100.2 7.9 %copy-start.7 = (f32[512,384]{1,0:T(8,128)S(1)}, f32[512,384]{1,0:T(8,128)}, u32[]{:S(2)}) copy-start(f32[512,384]{1,0:T(8,128)} %get-tuple-element.13) | copy-start | bytes 2359300
  100.3 7.9 %collective-permute-start.4 = (f32[128,384]{1,0:T(8,128)S(1)}, f32[128,384]{1,0:T(8,128)S(1)}, u32[]{:S(2)}, u32[]{:S(2)}) collective-permute-start(f32[128,384]{1,0:T(8,128)S(1)} %bitcast_add_fusion.11), channel_id=1, source_target_pairs={{0,64},{64,128},{128,192},{192,0},{1,65},{65,129},{129,193},{193,1... | collective-permute-start | bytes 589832 | tf_op jit(solution)/shard_map/ppermute | solution.py:106
  102.9 9.1 %collective-permute-start.7 = (f32[128,384]{1,0:T(8,128)S(1)}, f32[128,384]{1,0:T(8,128)S(1)}, u32[]{:S(2)}, u32[]{:S(2)}) collective-permute-start(f32[128,384]{1,0:T(8,128)S(1)} %bitcast_add_fusion.8), channel_id=1, source_target_pairs={{0,192},{64,0},{128,64},{192,128},{1,193},{65,1},{129,65},{193,129... | collective-permute-start | bytes 589832 | tf_op jit(solution)/shard_map/ppermute | solution.py:106
  103.5 8.9 %collective-permute-start.11 = (f32[128,384]{1,0:T(8,128)S(1)}, f32[128,384]{1,0:T(8,128)S(1)}, u32[]{:S(2)}, u32[]{:S(2)}) collective-permute-start(f32[128,384]{1,0:T(8,128)S(1)} %bitcast_add_fusion.5), channel_id=1, source_target_pairs={{0,64},{64,128},{128,192},{192,0},{1,65},{65,129},{129,193},{193,1... | collective-permute-start | bytes 589832 | tf_op jit(solution)/shard_map/ppermute | solution.py:106
  106.7 9.5 %collective-permute-start.14 = (f32[128,384]{1,0:T(8,128)S(1)}, f32[128,384]{1,0:T(8,128)S(1)}, u32[]{:S(2)}, u32[]{:S(2)}) collective-permute-start(f32[128,384]{1,0:T(8,128)S(1)} %bitcast_add_fusion.2), channel_id=1, source_target_pairs={{0,192},{64,0},{128,64},{192,128},{1,193},{65,1},{129,65},{193,129... | collective-permute-start | bytes 589832 | tf_op jit(solution)/shard_map/ppermute | solution.py:106
  108.2 8.3 %collective-permute-start.5 = (f32[128,384]{1,0:T(8,128)S(1)}, f32[128,384]{1,0:T(8,128)S(1)}, u32[]{:S(2)}, u32[]{:S(2)}) collective-permute-start(f32[128,384]{1,0:T(8,128)S(1)} %bitcast_add_fusion.10), channel_id=1, source_target_pairs={{0,64},{64,128},{128,192},{192,0},{1,65},{65,129},{129,193},{193,1... | collective-permute-start | bytes 589832 | tf_op jit(solution)/shard_map/ppermute | solution.py:106
  112.0 8.0 %collective-permute-start.8 = (f32[128,384]{1,0:T(8,128)S(1)}, f32[128,384]{1,0:T(8,128)S(1)}, u32[]{:S(2)}, u32[]{:S(2)}) collective-permute-start(f32[128,384]{1,0:T(8,128)S(1)} %bitcast_add_fusion.7), channel_id=1, source_target_pairs={{0,192},{64,0},{128,64},{192,128},{1,193},{65,1},{129,65},{193,129... | collective-permute-start | bytes 589832 | tf_op jit(solution)/shard_map/ppermute | solution.py:106
  112.4 6.8 %collective-permute-start.12 = (f32[128,384]{1,0:T(8,128)S(1)}, f32[128,384]{1,0:T(8,128)S(1)}, u32[]{:S(2)}, u32[]{:S(2)}) collective-permute-start(f32[128,384]{1,0:T(8,128)S(1)} %bitcast_add_fusion.4), channel_id=1, source_target_pairs={{0,64},{64,128},{128,192},{192,0},{1,65},{65,129},{129,193},{193,1... | collective-permute-start | bytes 589832 | tf_op jit(solution)/shard_map/ppermute | solution.py:106
  116.2 7.0 %collective-permute-start.15 = (f32[128,384]{1,0:T(8,128)S(1)}, f32[128,384]{1,0:T(8,128)S(1)}, u32[]{:S(2)}, u32[]{:S(2)}) collective-permute-start(f32[128,384]{1,0:T(8,128)S(1)} %bitcast_add_fusion.1), channel_id=1, source_target_pairs={{0,192},{64,0},{128,64},{192,128},{1,193},{65,1},{129,65},{193,129... | collective-permute-start | bytes 589832 | tf_op jit(solution)/shard_map/ppermute | solution.py:106
  (8 other events, 26.9 us)

commit v22 on v20

--- a/solution.py
+++ b/solution.py
@@ -4,6 +4,7 @@
 import jax.numpy as jnp
 from jax import lax
 from jax.experimental import pallas as pl
+from jax.experimental.pallas import tpu as pltpu
 from jax.sharding import Mesh, PartitionSpec as P
 
 HD = 128
@@ -42,7 +43,8 @@
 def near_kernel(a_ref, w0_ref, w1_ref, w3_ref, *o_refs):
     k = w0_ref.shape[0]
     quarter = o_refs[0].shape[1]
-    a = a_ref[...]
+    rows = o_refs[0].shape[0]
+    a = a_ref[pl.ds(pl.multiple_of(pl.program_id(0) * rows, rows), rows), :]
     base = jnp.dot(a[:, 0:k], w0_ref[...], preferred_element_type=jnp.float32)
     base = base + jnp.dot(a[:, k:2 * k], w1_ref[...], preferred_element_type=jnp.float32)
     base = base + jnp.dot(a[:, 3 * k:4 * k], w3_ref[...], preferred_element_type=jnp.float32)
@@ -53,7 +55,8 @@
 def far_kernel(a_ref, w2lo_ref, w2hi_ref, *o_refs):
     k = w2lo_ref.shape[0]
     quarter = o_refs[0].shape[1]
-    far = a_ref[:, 2 * k:3 * k]
+    rows = o_refs[0].shape[0]
+    far = a_ref[pl.ds(pl.multiple_of(pl.program_id(0) * rows, rows), rows), 2 * k:3 * k]
     low = jnp.dot(far, w2lo_ref[...], preferred_element_type=jnp.float32)
     high = jnp.dot(far, w2hi_ref[...], preferred_element_type=jnp.float32)
     for q, o_ref in enumerate(o_refs):
@@ -69,7 +72,7 @@
     full = lambda p: pl.BlockSpec(p.shape, lambda i: (0, 0))
     spec = pl.BlockSpec((tile, n // 4), lambda i: (i, 0))
     shape = jax.ShapeDtypeStruct((m, n // 4), jnp.float32)
-    a_spec = pl.BlockSpec((tile, kk), lambda i: (i, 0))
+    a_spec = pl.BlockSpec(memory_space=pltpu.VMEM)
     near_w = (own, right, left)
     quarters = pl.pallas_call(
         near_kernel,

time: 118 us -> 119 us (level)
  no operation moved by 1% of the time
where the time goes in v22:
time: 119 us; the launch traced here: 118 us
  waiting for transfers between devices  53.2 us (45%)
  starting transfers between devices  40.6 us (34%)
  Pallas kernels  10.3 us (9%)
  local copies, waits for them, and re-layouts  7.01 us (6%)
  other arithmetic  5.67 us (5%)
    ppermute x1, waiting for transfers between devices, ring_pieces(): from_right = lax.ppermute(block, axis, to_left)  26.1 us
    ppermute x12, starting transfers between devices, ring_reduce_scatter(): got = lax.ppermute(acc, axis, perm)  18.7 us
    ppermute x12, waiting for transfers between devices, ring_reduce_scatter(): got = lax.ppermute(acc, axis, perm)  11.6 us
    all_to_all x1, waiting for transfers between devices, per_device(): both = lax.all_to_all(both, 'col', split_axis=0, concat_axis=1, tiled=True)  9.92 us
    all_to_all x1, starting transfers between devices, per_device(): both = lax.all_to_all(both, 'col', split_axis=0, concat_axis=1, tiled=True)  8.57 us
    all_to_all x1, starting transfers between devices, per_device(): lax.all_to_all(spread_out, ('ry', 'col'), split_axis=0, concat_axis=0, ti...  6.78 us
    pallas_call x1, Pallas kernels, dot_pieces(): pl.pallas_call(near_kernel, grid=(m // tile,), in_specs=[a_spec] + [full(...  6.23 us
    all_to_all x1, waiting for transfers between devices, per_device(): lax.all_to_all(spread_out, ('ry', 'col'), split_axis=0, concat_axis=0, ti...  5.54 us
  transfers between devices with their start and end apart: 18, of which 10 were waited for; matrix products, arithmetic and copies ran while one was open for 2% of the time, Pallas kernels for 5%

profile of v22, /device:TPU:6, one launch (start us, length us, event | category | flops | bytes accessed | tf_op | source)
XLA Modules:
  0.0 117.6 jit_solution(10600356600888481509)
XLA Ops:
  4.6 8.6 %all-to-all-start = ((bf16[16,8,768]{2,1,0:T(8,128)(2,1)}), bf16[16,8,768]{2,1,0:T(8,128)(2,1)S(1)}, u32[]{:S(2)}, u32[]{:S(2)}) async-start(bf16[16,8,768]{2,1,0:T(8,128)(2,1)} %pad_maximum_fusion.1), calls=%async_computation | async-start | bytes 393216 | tf_op jit(solution)/shard_map/all_to_all | solution.py:121
  13.2 9.9 %all-to-all-done = bf16[16,8,768]{2,1,0:T(8,128)(2,1)S(1)} async-done(((bf16[16,8,768]{2,1,0:T(8,128)(2,1)}), bf16[16,8,768]{2,1,0:T(8,128)(2,1)S(1)}, u32[]{:S(2)}, u32[]{:S(2)}) %all-to-all-start) | async-done | bytes 196640 | tf_op jit(solution)/shard_map/all_to_all | solution.py:121
  23.5 1.3 %broadcast_in_dim.16 = bf16[4,16,8,1536]{3,2,1,0:T(8,128)(2,1)} broadcast(bf16[4,8,1536]{2,1,0:T(8,128)(2,1)S(1)} %bitcast.112), dimensions={0,2,3} | broadcast | bytes 1671168 | tf_op jit(solution)/shard_map/broadcast_in_dim | solution.py:136
  24.8 6.8 %all-to-all-start.1 = ((bf16[64,8,1536]{2,1,0:T(8,128)(2,1)}), bf16[64,8,1536]{2,1,0:T(8,128)(2,1)S(1)}, u32[]{:S(2)}, u32[]{:S(2)}) async-start(bf16[64,8,1536]{2,1,0:T(8,128)(2,1)} %bitcast.11), calls=%async_computation.1 | async-start | bytes 3145728 | tf_op jit(solution)/shard_map/all_to_all | solution.py:138
  32.5 2.4 %collective-permute-start.1 = (bf16[384,1536]{1,0:T(8,128)(2,1)}, bf16[384,1536]{1,0:T(8,128)(2,1)S(1)}, u32[]{:S(2)}, u32[]{:S(2)}) collective-permute-start(bf16[384,1536]{1,0:T(8,128)(2,1)} %w0_ref.1), channel_id=1, source_target_pairs={{0,16},{16,32},{32,48},{48,0},{1,17},{17,33},{33,49},{49,1},{2,18}... | collective-permute-start | bytes 3538952 | tf_op jit(solution)/shard_map/ppermute | solution.py:35
  34.9 26.1 %collective-permute-done.w1_ref = bf16[384,1536]{1,0:T(8,128)(2,1)S(1)} collective-permute-done((bf16[384,1536]{1,0:T(8,128)(2,1)}, bf16[384,1536]{1,0:T(8,128)(2,1)S(1)}, u32[]{:S(2)}, u32[]{:S(2)}) %collective-permute-start) | collective-permute-done | bytes 1179680 | tf_op jit(solution)/shard_map/ppermute | solution.py:36
  61.1 1.1 copy-done.10
  62.4 3.1 %collective-permute-start.2 = (bf16[384,768]{1,0:T(8,128)(2,1)S(1)}, bf16[384,768]{1,0:T(8,128)(2,1)}, u32[]{:S(2)}, u32[]{:S(2)}) collective-permute-start(bf16[384,768]{1,0:T(8,128)(2,1)S(1)} %slice.18), channel_id=1, source_target_pairs={{0,16},{16,32},{32,48},{48,0},{1,17},{17,33},{33,49},{49,1},{2,18}... | collective-permute-start | bytes 1769480 | tf_op jit(solution)/shard_map/ppermute | solution.py:38
  65.5 5.5 %all-to-all-done.1 = bf16[64,8,1536]{2,1,0:T(8,128)(2,1)S(1)} async-done(((bf16[64,8,1536]{2,1,0:T(8,128)(2,1)}), bf16[64,8,1536]{2,1,0:T(8,128)(2,1)S(1)}, u32[]{:S(2)}, u32[]{:S(2)}) %all-to-all-start.1) | async-done | bytes 1572896 | tf_op jit(solution)/shard_map/all_to_all | solution.py:138
  71.1 1.2 copy-done
  72.2 6.2 %shard_map.64 = (f32[512,384]{1,0:T(8,128)}, f32[512,384]{1,0:T(8,128)}, f32[512,384]{1,0:T(8,128)}, f32[512,384]{1,0:T(8,128)}) custom-call(bf16[512,1536]{1,0:T(8,128)(2,1)} %bitcast.76, bf16[384,1536]{1,0:T(8,128)(2,1)} %w0_ref.1, bf16[384,1536]{1,0:T(8,128)(2,1)} %copy-done.9, bf16[384,1536]{1,0:T(8,128)(2,1)} %copy-done.10), custom_call_target="tpu_custom_call" | custom-call | flops 1811939328 | bytes 8257536 | tf_op jit(solution)/shard_map/pallas_call | solution.py:77
  78.5 4.1 %shard_map.65 = (f32[512,384]{1,0:T(8,128)}, f32[512,384]{1,0:T(8,128)}, f32[512,384]{1,0:T(8,128)}, f32[512,384]{1,0:T(8,128)}) custom-call(bf16[512,1536]{1,0:T(8,128)(2,1)} %bitcast.77, bf16[384,768]{1,0:T(8,128)(2,1)} %collective-permute-done.2.w2lo_ref, bf16[384,768]{1,0:T(8,128)(2,1)} %collective-permute-done.3.w2hi_ref), custom_call_target="tpu_custom_call" | custom-call | flops 603979776 | bytes 5898240 | tf_op jit(solution)/shard_map/pallas_call | solution.py:87
  85.5 1.3 %collective-permute-start.4 = (f32[128,384]{1,0:T(8,128)S(1)}, f32[128,384]{1,0:T(8,128)S(1)}, u32[]{:S(2)}, u32[]{:S(2)}) collective-permute-start(f32[128,384]{1,0:T(8,128)S(1)} %add_bitcast_fusion.3), channel_id=1, source_target_pairs={{0,64},{64,128},{128,192},{192,0},{1,65},{65,129},{129,193},{193,1... | collective-permute-start | bytes 589832 | tf_op jit(solution)/shard_map/ppermute | solution.py:111
  87.8 2.1 %collective-permute-start.13 = (f32[128,384]{1,0:T(8,128)S(1)}, f32[128,384]{1,0:T(8,128)S(1)}, u32[]{:S(2)}, u32[]{:S(2)}) collective-permute-start(f32[128,384]{1,0:T(8,128)S(1)} %add_bitcast_fusion), channel_id=1, source_target_pairs={{0,192},{64,0},{128,64},{192,128},{1,193},{65,1},{129,65},{193,129... | collective-permute-start | bytes 589832 | tf_op jit(solution)/shard_map/ppermute | solution.py:111
  89.9 1.4 %collective-permute-start.7 = (f32[128,384]{1,0:T(8,128)S(1)}, f32[128,384]{1,0:T(8,128)S(1)}, u32[]{:S(2)}, u32[]{:S(2)}) collective-permute-start(f32[128,384]{1,0:T(8,128)S(1)} %add_bitcast_fusion.2), channel_id=1, source_target_pairs={{0,192},{64,0},{128,64},{192,128},{1,193},{65,1},{129,65},{193,129... | collective-permute-start | bytes 589832 | tf_op jit(solution)/shard_map/ppermute | solution.py:111
  91.3 1.4 %collective-permute-done.10 = f32[128,384]{1,0:T(8,128)S(1)} collective-permute-done((f32[128,384]{1,0:T(8,128)S(1)}, f32[128,384]{1,0:T(8,128)S(1)}, u32[]{:S(2)}, u32[]{:S(2)}) %collective-permute-start.10) | collective-permute-done | bytes 196640 | tf_op jit(solution)/shard_map/ppermute | solution.py:111
  92.9 4.1 %collective-permute-done.4 = f32[128,384]{1,0:T(8,128)S(1)} collective-permute-done((f32[128,384]{1,0:T(8,128)S(1)}, f32[128,384]{1,0:T(8,128)S(1)}, u32[]{:S(2)}, u32[]{:S(2)}) %collective-permute-start.4) | collective-permute-done | bytes 196640 | tf_op jit(solution)/shard_map/ppermute | solution.py:111
  97.2 3.5 %collective-permute-start.14 = (f32[128,384]{1,0:T(8,128)S(1)}, f32[128,384]{1,0:T(8,128)S(1)}, u32[]{:S(2)}, u32[]{:S(2)}) collective-permute-start(f32[128,384]{1,0:T(8,128)S(1)} %bitcast_add_fusion.2), channel_id=1, source_target_pairs={{0,192},{64,0},{128,64},{192,128},{1,193},{65,1},{129,65},{193,129... | collective-permute-start | bytes 589832 | tf_op jit(solution)/shard_map/ppermute | solution.py:111
  100.6 2.2 %collective-permute-start.8 = (f32[128,384]{1,0:T(8,128)S(1)}, f32[128,384]{1,0:T(8,128)S(1)}, u32[]{:S(2)}, u32[]{:S(2)}) collective-permute-start(f32[128,384]{1,0:T(8,128)S(1)} %bitcast_add_fusion.8), channel_id=1, source_target_pairs={{0,192},{64,0},{128,64},{192,128},{1,193},{65,1},{129,65},{193,129... | collective-permute-start | bytes 589832 | tf_op jit(solution)/shard_map/ppermute | solution.py:111
  103.0 1.9 %collective-permute-done.5 = f32[128,384]{1,0:T(8,128)S(1)} collective-permute-done((f32[128,384]{1,0:T(8,128)S(1)}, f32[128,384]{1,0:T(8,128)S(1)}, u32[]{:S(2)}, u32[]{:S(2)}) %collective-permute-start.5) | collective-permute-done | bytes 196640 | tf_op jit(solution)/shard_map/ppermute | solution.py:111
  105.3 3.3 %collective-permute-start.15 = (f32[128,384]{1,0:T(8,128)S(1)}, f32[128,384]{1,0:T(8,128)S(1)}, u32[]{:S(2)}, u32[]{:S(2)}) collective-permute-start(f32[128,384]{1,0:T(8,128)S(1)} %bitcast_add_fusion.1), channel_id=1, source_target_pairs={{0,192},{64,0},{128,64},{192,128},{1,193},{65,1},{129,65},{193,129... | collective-permute-start | bytes 589832 | tf_op jit(solution)/shard_map/ppermute | solution.py:111
  109.0 3.8 %collective-permute-start.9 = (f32[128,384]{1,0:T(8,128)S(1)}, f32[128,384]{1,0:T(8,128)S(1)}, u32[]{:S(2)}, u32[]{:S(2)}) collective-permute-start(f32[128,384]{1,0:T(8,128)S(1)} %bitcast_add_fusion.7), channel_id=1, source_target_pairs={{0,192},{64,0},{128,64},{192,128},{1,193},{65,1},{129,65},{193,129... | collective-permute-start | bytes 589832 | tf_op jit(solution)/shard_map/ppermute | solution.py:111
  112.9 1.9 %collective-permute-done.6 = f32[128,384]{1,0:T(8,128)S(1)} collective-permute-done((f32[128,384]{1,0:T(8,128)S(1)}, f32[128,384]{1,0:T(8,128)S(1)}, u32[]{:S(2)}, u32[]{:S(2)}) %collective-permute-start.6) | collective-permute-done | bytes 196640 | tf_op jit(solution)/shard_map/ppermute | solution.py:111
  115.0 1.7 %collective-permute-done.9 = f32[128,384]{1,0:T(8,128)S(1)} collective-permute-done((f32[128,384]{1,0:T(8,128)S(1)}, f32[128,384]{1,0:T(8,128)S(1)}, u32[]{:S(2)}, u32[]{:S(2)}) %collective-permute-start.9) | collective-permute-done | bytes 196640 | tf_op jit(solution)/shard_map/ppermute | solution.py:111
  (75 shorter events, 12.4 us)
Async XLA Ops:
  2.4 10.8 %copy-start.12 = (f32[6144]{0:T(1024)S(1)}, f32[6144]{0:T(1024)}, u32[]{:S(2)}) copy-start(f32[6144]{0:T(1024)} %param.10) | copy-start | bytes 73732
  4.6 18.5 %all-to-all-start = ((bf16[16,8,768]{2,1,0:T(8,128)(2,1)}), bf16[16,8,768]{2,1,0:T(8,128)(2,1)S(1)}, u32[]{:S(2)}, u32[]{:S(2)}) async-start(bf16[16,8,768]{2,1,0:T(8,128)(2,1)} %pad_maximum_fusion.1), calls=%async_computation | async-start | bytes 393216 | tf_op jit(solution)/shard_map/all_to_all | solution.py:121
  24.8 46.3 %all-to-all-start.1 = ((bf16[64,8,1536]{2,1,0:T(8,128)(2,1)}), bf16[64,8,1536]{2,1,0:T(8,128)(2,1)S(1)}, u32[]{:S(2)}, u32[]{:S(2)}) async-start(bf16[64,8,1536]{2,1,0:T(8,128)(2,1)} %bitcast.11), calls=%async_computation.1 | async-start | bytes 3145728 | tf_op jit(solution)/shard_map/all_to_all | solution.py:138
  31.6 29.4 %collective-permute-start = (bf16[384,1536]{1,0:T(8,128)(2,1)}, bf16[384,1536]{1,0:T(8,128)(2,1)S(1)}, u32[]{:S(2)}, u32[]{:S(2)}) collective-permute-start(bf16[384,1536]{1,0:T(8,128)(2,1)} %w0_ref.1), channel_id=1, source_target_pairs={{0,48},{16,0},{32,16},{48,32},{1,49},{17,1},{33,17},{49,33},{2,50}... | collective-permute-start | bytes 3538952 | tf_op jit(solution)/shard_map/ppermute | solution.py:36
  32.5 28.7 %collective-permute-start.1 = (bf16[384,1536]{1,0:T(8,128)(2,1)}, bf16[384,1536]{1,0:T(8,128)(2,1)S(1)}, u32[]{:S(2)}, u32[]{:S(2)}) collective-permute-start(bf16[384,1536]{1,0:T(8,128)(2,1)} %w0_ref.1), channel_id=1, source_target_pairs={{0,16},{16,32},{32,48},{48,0},{1,17},{17,33},{33,49},{49,1},{2,18}... | collective-permute-start | bytes 3538952 | tf_op jit(solution)/shard_map/ppermute | solution.py:35
  61.0 17.4 %collective-permute-start.3 = (bf16[384,768]{1,0:T(8,128)(2,1)S(1)}, bf16[384,768]{1,0:T(8,128)(2,1)}, u32[]{:S(2)}, u32[]{:S(2)}) collective-permute-start(bf16[384,768]{1,0:T(8,128)(2,1)S(1)} %slice.19), channel_id=1, source_target_pairs={{0,48},{16,0},{32,16},{48,32},{1,49},{17,1},{33,17},{49,33},{2,50}... | collective-permute-start | bytes 1769480 | tf_op jit(solution)/shard_map/ppermute | solution.py:39
  62.4 16.1 %collective-permute-start.2 = (bf16[384,768]{1,0:T(8,128)(2,1)S(1)}, bf16[384,768]{1,0:T(8,128)(2,1)}, u32[]{:S(2)}, u32[]{:S(2)}) collective-permute-start(bf16[384,768]{1,0:T(8,128)(2,1)S(1)} %slice.18), channel_id=1, source_target_pairs={{0,16},{16,32},{32,48},{48,0},{1,17},{17,33},{33,49},{49,1},{2,18}... | collective-permute-start | bytes 1769480 | tf_op jit(solution)/shard_map/ppermute | solution.py:38
  78.5 8.3 %copy-start.2 = (f32[512,384]{1,0:T(8,128)S(1)}, f32[512,384]{1,0:T(8,128)}, u32[]{:S(2)}) copy-start(f32[512,384]{1,0:T(8,128)} %get-tuple-element.19) | copy-start | bytes 2359300
  82.6 7.3 %copy-start.3 = (f32[512,384]{1,0:T(8,128)S(1)}, f32[512,384]{1,0:T(8,128)}, u32[]{:S(2)}) copy-start(f32[512,384]{1,0:T(8,128)} %get-tuple-element.16) | copy-start | bytes 2359300
  82.6 10.1 %copy-start.8 = (f32[512,384]{1,0:T(8,128)S(1)}, f32[512,384]{1,0:T(8,128)}, u32[]{:S(2)}) copy-start(f32[512,384]{1,0:T(8,128)} %get-tuple-element.18) | copy-start | bytes 2359300
  83.7 9.0 %collective-permute-start.10 = (f32[128,384]{1,0:T(8,128)S(1)}, f32[128,384]{1,0:T(8,128)S(1)}, u32[]{:S(2)}, u32[]{:S(2)}) collective-permute-start(f32[128,384]{1,0:T(8,128)S(1)} %add_bitcast_fusion.1), channel_id=1, source_target_pairs={{0,64},{64,128},{128,192},{192,0},{1,65},{65,129},{129,193},{193,1... | collective-permute-start | bytes 589832 | tf_op jit(solution)/shard_map/ppermute | solution.py:111
  84.5 12.5 %copy-start.7 = (f32[512,384]{1,0:T(8,128)S(1)}, f32[512,384]{1,0:T(8,128)}, u32[]{:S(2)}) copy-start(f32[512,384]{1,0:T(8,128)} %get-tuple-element.14) | copy-start | bytes 2359300
  85.5 11.4 %collective-permute-start.4 = (f32[128,384]{1,0:T(8,128)S(1)}, f32[128,384]{1,0:T(8,128)S(1)}, u32[]{:S(2)}, u32[]{:S(2)}) collective-permute-start(f32[128,384]{1,0:T(8,128)S(1)} %add_bitcast_fusion.3), channel_id=1, source_target_pairs={{0,64},{64,128},{128,192},{192,0},{1,65},{65,129},{129,193},{193,1... | collective-permute-start | bytes 589832 | tf_op jit(solution)/shard_map/ppermute | solution.py:111
  87.8 9.3 %copy-start.5 = (f32[512,384]{1,0:T(8,128)S(1)}, f32[512,384]{1,0:T(8,128)}, u32[]{:S(2)}) copy-start(f32[512,384]{1,0:T(8,128)} %get-tuple-element.20) | copy-start | bytes 2359300
  87.8 9.3 %collective-permute-start.13 = (f32[128,384]{1,0:T(8,128)S(1)}, f32[128,384]{1,0:T(8,128)S(1)}, u32[]{:S(2)}, u32[]{:S(2)}) collective-permute-start(f32[128,384]{1,0:T(8,128)S(1)} %add_bitcast_fusion), channel_id=1, source_target_pairs={{0,192},{64,0},{128,64},{192,128},{1,193},{65,1},{129,65},{193,129... | collective-permute-start | bytes 589832 | tf_op jit(solution)/shard_map/ppermute | solution.py:111
  89.9 10.7 %collective-permute-start.7 = (f32[128,384]{1,0:T(8,128)S(1)}, f32[128,384]{1,0:T(8,128)S(1)}, u32[]{:S(2)}, u32[]{:S(2)}) collective-permute-start(f32[128,384]{1,0:T(8,128)S(1)} %add_bitcast_fusion.2), channel_id=1, source_target_pairs={{0,192},{64,0},{128,64},{192,128},{1,193},{65,1},{129,65},{193,129... | collective-permute-start | bytes 589832 | tf_op jit(solution)/shard_map/ppermute | solution.py:111
  92.8 10.0 %collective-permute-start.11 = (f32[128,384]{1,0:T(8,128)S(1)}, f32[128,384]{1,0:T(8,128)S(1)}, u32[]{:S(2)}, u32[]{:S(2)}) collective-permute-start(f32[128,384]{1,0:T(8,128)S(1)} %bitcast_add_fusion.5), channel_id=1, source_target_pairs={{0,64},{64,128},{128,192},{192,0},{1,65},{65,129},{129,193},{193,1... | collective-permute-start | bytes 589832 | tf_op jit(solution)/shard_map/ppermute | solution.py:111
  97.0 7.8 %collective-permute-start.5 = (f32[128,384]{1,0:T(8,128)S(1)}, f32[128,384]{1,0:T(8,128)S(1)}, u32[]{:S(2)}, u32[]{:S(2)}) collective-permute-start(f32[128,384]{1,0:T(8,128)S(1)} %bitcast_add_fusion.11), channel_id=1, source_target_pairs={{0,64},{64,128},{128,192},{192,0},{1,65},{65,129},{129,193},{193,1... | collective-permute-start | bytes 589832 | tf_op jit(solution)/shard_map/ppermute | solution.py:111
  97.2 8.1 %collective-permute-start.14 = (f32[128,384]{1,0:T(8,128)S(1)}, f32[128,384]{1,0:T(8,128)S(1)}, u32[]{:S(2)}, u32[]{:S(2)}) collective-permute-start(f32[128,384]{1,0:T(8,128)S(1)} %bitcast_add_fusion.2), channel_id=1, source_target_pairs={{0,192},{64,0},{128,64},{192,128},{1,193},{65,1},{129,65},{193,129... | collective-permute-start | bytes 589832 | tf_op jit(solution)/shard_map/ppermute | solution.py:111
  100.6 8.4 %collective-permute-start.8 = (f32[128,384]{1,0:T(8,128)S(1)}, f32[128,384]{1,0:T(8,128)S(1)}, u32[]{:S(2)}, u32[]{:S(2)}) collective-permute-start(f32[128,384]{1,0:T(8,128)S(1)} %bitcast_add_fusion.8), channel_id=1, source_target_pairs={{0,192},{64,0},{128,64},{192,128},{1,193},{65,1},{129,65},{193,129... | collective-permute-start | bytes 589832 | tf_op jit(solution)/shard_map/ppermute | solution.py:111
  102.9 9.9 %collective-permute-start.12 = (f32[128,384]{1,0:T(8,128)S(1)}, f32[128,384]{1,0:T(8,128)S(1)}, u32[]{:S(2)}, u32[]{:S(2)}) collective-permute-start(f32[128,384]{1,0:T(8,128)S(1)} %bitcast_add_fusion.4), channel_id=1, source_target_pairs={{0,64},{64,128},{128,192},{192,0},{1,65},{65,129},{129,193},{193,1... | collective-permute-start | bytes 589832 | tf_op jit(solution)/shard_map/ppermute | solution.py:111
  104.9 9.9 %collective-permute-start.6 = (f32[128,384]{1,0:T(8,128)S(1)}, f32[128,384]{1,0:T(8,128)S(1)}, u32[]{:S(2)}, u32[]{:S(2)}) collective-permute-start(f32[128,384]{1,0:T(8,128)S(1)} %bitcast_add_fusion.10), channel_id=1, source_target_pairs={{0,64},{64,128},{128,192},{192,0},{1,65},{65,129},{129,193},{193,1... | collective-permute-start | bytes 589832 | tf_op jit(solution)/shard_map/ppermute | solution.py:111
  105.3 9.6 %collective-permute-start.15 = (f32[128,384]{1,0:T(8,128)S(1)}, f32[128,384]{1,0:T(8,128)S(1)}, u32[]{:S(2)}, u32[]{:S(2)}) collective-permute-start(f32[128,384]{1,0:T(8,128)S(1)} %bitcast_add_fusion.1), channel_id=1, source_target_pairs={{0,192},{64,0},{128,64},{192,128},{1,193},{65,1},{129,65},{193,129... | collective-permute-start | bytes 589832 | tf_op jit(solution)/shard_map/ppermute | solution.py:111
  109.0 7.7 %collective-permute-start.9 = (f32[128,384]{1,0:T(8,128)S(1)}, f32[128,384]{1,0:T(8,128)S(1)}, u32[]{:S(2)}, u32[]{:S(2)}) collective-permute-start(f32[128,384]{1,0:T(8,128)S(1)} %bitcast_add_fusion.7), channel_id=1, source_target_pairs={{0,192},{64,0},{128,64},{192,128},{1,193},{65,1},{129,65},{193,129... | collective-permute-start | bytes 589832 | tf_op jit(solution)/shard_map/ppermute | solution.py:111
  (7 other events, 24.0 us)
